TPU v7x, 32 devices: a whole 2x2x4 slice. The times are simulated.
32 devices in a mesh: dp: 8 (over z, x), fsdp: 4 (over y, core).
Axes of the slice: x: 2, y: 2, z: 4, core: 2. Of those that a mesh axis runs over, the one named last changes fastest.
Arguments:
- inputs: bfloat16 [16384, 768], P(('dp', 'fsdp')), may hold values from -6 to 6
- cotangent: bfloat16 [16384, 768], P(('dp', 'fsdp')), may hold values from -6 to 6
- masked: int32 [32, 512], P(('dp', 'fsdp')), may hold values from 0 to 1, as said below
- query_weight: bfloat16 [768, 768], P(('dp', 'fsdp')), may hold values from -0.21875 to 0.21875
- query_bias: bfloat16 [768], P(('dp', 'fsdp')), may hold values from -3 to 3
- key_weight: bfloat16 [768, 768], P(('dp', 'fsdp')), may hold values from -0.21875 to 0.21875
- value_weight: bfloat16 [768, 768], P(('dp', 'fsdp')), may hold values from -0.21875 to 0.21875
- value_bias: bfloat16 [768], P(('dp', 'fsdp')), may hold values from -0.14941406 to 0.14941406
- output_weight: bfloat16 [768, 768], P(('dp', 'fsdp')), may hold values from -0.875 to 0.875
- output_bias: bfloat16 [768], P(('dp', 'fsdp')), may hold values from -0.5 to 0.5
- first_gain: bfloat16 [768], P(('dp', 'fsdp')), may hold values from 0.25 to 1.75
- first_shift: bfloat16 [768], P(('dp', 'fsdp')), may hold values from -0.5 to 0.5
- inner_weight: bfloat16 [768, 3072], P(('dp', 'fsdp')), may hold values from -0.21875 to 0.21875
- inner_bias: bfloat16 [3072], P(('dp', 'fsdp')), may hold values from -0.5 to 0.5
- outer_weight: bfloat16 [3072, 768], P(('dp', 'fsdp')), may hold values from -0.109375 to 0.109375
- outer_bias: bfloat16 [768], P(('dp', 'fsdp')), may hold values from -0.5 to 0.5
- second_gain: bfloat16 [768], P(('dp', 'fsdp')), may hold values from 0.25 to 1.75
- second_shift: bfloat16 [768], P(('dp', 'fsdp')), may hold values from -0.5 to 0.5
Outputs:
- outputs: bfloat16 [16384, 768], P(('dp', 'fsdp'))
- input_grad: bfloat16 [16384, 768], P(('dp', 'fsdp'))
- query_weight_grad: float32 [768, 768], P(('dp', 'fsdp'))
- query_bias_grad: float32 [768], P(('dp', 'fsdp'))
- key_weight_grad: float32 [768, 768], P(('dp', 'fsdp'))
- value_weight_grad: float32 [768, 768], P(('dp', 'fsdp'))
- value_bias_grad: float32 [768], P(('dp', 'fsdp'))
- output_weight_grad: float32 [768, 768], P(('dp', 'fsdp'))
- output_bias_grad: float32 [768], P(('dp', 'fsdp'))
- first_gain_grad: float32 [768], P(('dp', 'fsdp'))
- first_shift_grad: float32 [768], P(('dp', 'fsdp'))
- inner_weight_grad: float32 [768, 3072], P(('dp', 'fsdp'))
- inner_bias_grad: float32 [3072], P(('dp', 'fsdp'))
- outer_weight_grad: float32 [3072, 768], P(('dp', 'fsdp'))
- outer_bias_grad: float32 [768], P(('dp', 'fsdp'))
- second_gain_grad: float32 [768], P(('dp', 'fsdp'))
- second_shift_grad: float32 [768], P(('dp', 'fsdp'))
Inputs may be any that keep to these rules, and one draw needn't show every extreme that they name: `masked`: each sequence has 1 to 80 ones, in runs of 1 to 3 positions; some sequence has exactly 80.
All inputs are finite; a program needn't handle non-finite values.
Results may differ from a plain program's by a relative error of at most 0.02.
Values may be sent and summed in bfloat16 or wider, within the bound.
No kernel may reach another device: no remote copies, remote signals or barrier semaphores. Data moves between devices by JAX's collectives and lax.ppermute only.
A program may use at most 256 MiB of HBM per device.

v0:
```python
import jax
import jax.numpy as jnp
from jax import lax
from jax.sharding import PartitionSpec as P

HEADS = 12
SEQ = 512
LAYERS = 3


norm_epsilon = 1e-05


def product(left, right):
    return jnp.dot(left, right, preferred_element_type=jnp.float32)


def product_tn(left, right):
    return lax.dot_general(
        left, right, (((0,), (0,)), ((), ())), preferred_element_type=jnp.float32
    )


def product_nt(left, right):
    return lax.dot_general(
        left, right, (((1,), (1,)), ((), ())), preferred_element_type=jnp.float32
    )


def column_sums(values):
    return jnp.sum(values.astype(jnp.float32), axis=0)


def gelu_tanh(values):
    return jax.nn.gelu(values, approximate=True)


def layer_norm(summed, gain, shift):
    centre = summed - jnp.mean(summed, axis=-1, keepdims=True)
    inverse = lax.rsqrt(jnp.mean(centre * centre, axis=-1, keepdims=True) + norm_epsilon)
    normed = centre * inverse
    return (normed * gain.astype(jnp.float32) + shift.astype(jnp.float32), normed, inverse)


def norm_backward(upstream, normed, inverse, gain):
    scaled = upstream * gain.astype(jnp.float32)
    return inverse * (
        scaled
        - jnp.mean(scaled, axis=-1, keepdims=True)
        - normed * jnp.mean(scaled * normed, axis=-1, keepdims=True)
    )


def by_heads(rows):
    return rows.reshape(rows.shape[0], HEADS, rows.shape[1] // HEADS)


def by_sequence(rows):
    return rows.reshape(rows.shape[0] // SEQ, SEQ, rows.shape[1])


def flatten_rows(blocks):
    return blocks.reshape(-1, blocks.shape[-1])


def attend_forward(triple):
    query_rows, key_rows, value_rows = triple
    query_heads = by_heads(query_rows)
    key_heads = by_heads(key_rows)
    value_heads = by_heads(value_rows)
    scale = query_heads.shape[-1] ** (-0.5)
    scores = (
        jnp.einsum("qhd,khd->hqk", query_heads, key_heads, preferred_element_type=jnp.float32)
        * scale
    )
    top_score = jnp.max(scores, axis=-1, keepdims=True)
    weights = jnp.exp(scores - top_score)
    totals = jnp.sum(weights, axis=-1, keepdims=True)
    probs = (weights / totals).astype(jnp.bfloat16)
    context = jnp.einsum("hqk,khd->qhd", probs, value_heads, preferred_element_type=jnp.float32)
    return (context.reshape(query_rows.shape), (top_score + jnp.log(totals))[..., 0])


def attend_backward(packed):
    query_rows, key_rows, value_rows, log_total, context_grad = packed
    query_heads = by_heads(query_rows)
    key_heads = by_heads(key_rows)
    value_heads = by_heads(value_rows)
    grad_heads = by_heads(context_grad)
    scale = query_heads.shape[-1] ** (-0.5)
    scores = (
        jnp.einsum("qhd,khd->hqk", query_heads, key_heads, preferred_element_type=jnp.float32)
        * scale
    )
    probs = jnp.exp(scores - log_total[..., None])
    prob_grad = jnp.einsum(
        "qhd,khd->hqk", grad_heads, value_heads, preferred_element_type=jnp.float32
    )
    value_grad = jnp.einsum(
        "hqk,qhd->khd", probs.astype(jnp.bfloat16), grad_heads, preferred_element_type=jnp.float32
    )
    score_grad = (probs * (prob_grad - jnp.sum(probs * prob_grad, axis=-1, keepdims=True))).astype(
        jnp.bfloat16
    )
    query_grad = (
        jnp.einsum("hqk,khd->qhd", score_grad, key_heads, preferred_element_type=jnp.float32)
        * scale
    )
    key_grad = (
        jnp.einsum("hqk,qhd->khd", score_grad, query_heads, preferred_element_type=jnp.float32)
        * scale
    )
    row_shape = query_rows.shape
    return (
        query_grad.reshape(row_shape).astype(jnp.bfloat16),
        key_grad.reshape(row_shape).astype(jnp.bfloat16),
        value_grad.reshape(row_shape).astype(jnp.bfloat16),
    )


def layer_forward(weights, hidden_state):
    (
        query_weight,
        query_bias,
        key_weight,
        value_weight,
        value_bias,
        output_weight,
        output_bias,
        first_gain,
        first_shift,
        inner_weight,
        inner_bias,
        outer_weight,
        outer_bias,
        second_gain,
        second_shift,
    ) = weights
    rows_low = hidden_state.astype(jnp.bfloat16)
    query_rows = (product(rows_low, query_weight) + query_bias.astype(jnp.float32)).astype(
        jnp.bfloat16
    )
    key_rows = product(rows_low, key_weight).astype(jnp.bfloat16)
    value_rows = (product(rows_low, value_weight) + value_bias.astype(jnp.float32)).astype(
        jnp.bfloat16
    )
    context, log_total = lax.map(
        attend_forward, (by_sequence(query_rows), by_sequence(key_rows), by_sequence(value_rows))
    )
    context_low = flatten_rows(context).astype(jnp.bfloat16)
    attended = product(context_low, output_weight) + output_bias.astype(jnp.float32)
    first_out, first_normed, first_inverse = layer_norm(
        hidden_state + attended, first_gain, first_shift
    )
    first_low = first_out.astype(jnp.bfloat16)
    inner_pre = product(first_low, inner_weight) + inner_bias.astype(jnp.float32)
    inner_low = gelu_tanh(inner_pre).astype(jnp.bfloat16)
    outer_out = product(inner_low, outer_weight) + outer_bias.astype(jnp.float32)
    result, second_normed, second_inverse = layer_norm(
        first_out + outer_out, second_gain, second_shift
    )
    kept_values = (
        rows_low,
        query_rows,
        key_rows,
        value_rows,
        log_total,
        context_low,
        first_normed,
        first_inverse,
        first_low,
        inner_pre,
        inner_low,
        second_normed,
        second_inverse,
    )
    return (result, kept_values)


def layer_backward(weights, kept_values, upstream):
    (
        query_weight,
        query_bias,
        key_weight,
        value_weight,
        value_bias,
        output_weight,
        output_bias,
        first_gain,
        first_shift,
        inner_weight,
        inner_bias,
        outer_weight,
        outer_bias,
        second_gain,
        second_shift,
    ) = weights
    (
        rows_low,
        query_rows,
        key_rows,
        value_rows,
        log_total,
        context_low,
        first_normed,
        first_inverse,
        first_low,
        inner_pre,
        inner_low,
        second_normed,
        second_inverse,
    ) = kept_values
    second_gain_grad = jnp.sum(upstream * second_normed, axis=0)
    second_shift_grad = jnp.sum(upstream, axis=0)
    second_grad = norm_backward(upstream, second_normed, second_inverse, second_gain)
    outer_low = second_grad.astype(jnp.bfloat16)
    outer_bias_grad = column_sums(outer_low)
    outer_weight_grad = product_tn(inner_low, outer_low)
    active_grad = product_nt(outer_low, outer_weight)
    gelu_pull = jax.vjp(gelu_tanh, inner_pre)[1]
    inner_grad = gelu_pull(active_grad)[0].astype(jnp.bfloat16)
    inner_bias_grad = column_sums(inner_grad)
    inner_weight_grad = product_tn(first_low, inner_grad)
    first_grad = second_grad + product_nt(inner_grad, inner_weight)
    first_gain_grad = jnp.sum(first_grad * first_normed, axis=0)
    first_shift_grad = jnp.sum(first_grad, axis=0)
    attended_grad = norm_backward(first_grad, first_normed, first_inverse, first_gain)
    attended_low = attended_grad.astype(jnp.bfloat16)
    output_bias_grad = column_sums(attended_low)
    output_weight_grad = product_tn(context_low, attended_low)
    context_grad = product_nt(attended_low, output_weight).astype(jnp.bfloat16)
    query_grad, key_grad, value_grad = lax.map(
        attend_backward,
        (
            by_sequence(query_rows),
            by_sequence(key_rows),
            by_sequence(value_rows),
            log_total,
            by_sequence(context_grad),
        ),
    )
    query_grad = flatten_rows(query_grad)
    key_grad = flatten_rows(key_grad)
    value_grad = flatten_rows(value_grad)
    below_grad = (
        attended_grad
        + product_nt(query_grad, query_weight)
        + product_nt(key_grad, key_weight)
        + product_nt(value_grad, value_weight)
    )
    weight_grads = (
        product_tn(rows_low, query_grad),
        column_sums(query_grad),
        product_tn(rows_low, key_grad),
        product_tn(rows_low, value_grad),
        column_sums(value_grad),
        output_weight_grad,
        output_bias_grad,
        first_gain_grad,
        first_shift_grad,
        inner_weight_grad,
        inner_bias_grad,
        outer_weight_grad,
        outer_bias_grad,
        second_gain_grad,
        second_shift_grad,
    )
    return (below_grad, weight_grads)


def per_device(
    inputs,
    cotangent,
    masked,
    query_weight,
    query_bias,
    key_weight,
    value_weight,
    value_bias,
    output_weight,
    output_bias,
    first_gain,
    first_shift,
    inner_weight,
    inner_bias,
    outer_weight,
    outer_bias,
    second_gain,
    second_shift,
):
    hidden_state = inputs.astype(jnp.float32)
    kept_inputs = []
    for applied in range(LAYERS):
        resident = (
            lax.all_gather(query_weight, ("dp", "fsdp"), axis=0, tiled=True),
            lax.all_gather(query_bias, ("dp", "fsdp"), axis=0, tiled=True),
            lax.all_gather(key_weight, ("dp", "fsdp"), axis=0, tiled=True),
            lax.all_gather(value_weight, ("dp", "fsdp"), axis=0, tiled=True),
            lax.all_gather(value_bias, ("dp", "fsdp"), axis=0, tiled=True),
            lax.all_gather(output_weight, ("dp", "fsdp"), axis=0, tiled=True),
            lax.all_gather(output_bias, ("dp", "fsdp"), axis=0, tiled=True),
            lax.all_gather(first_gain, ("dp", "fsdp"), axis=0, tiled=True),
            lax.all_gather(first_shift, ("dp", "fsdp"), axis=0, tiled=True),
            lax.all_gather(inner_weight, ("dp", "fsdp"), axis=0, tiled=True),
            lax.all_gather(inner_bias, ("dp", "fsdp"), axis=0, tiled=True),
            lax.all_gather(outer_weight, ("dp", "fsdp"), axis=0, tiled=True),
            lax.all_gather(outer_bias, ("dp", "fsdp"), axis=0, tiled=True),
            lax.all_gather(second_gain, ("dp", "fsdp"), axis=0, tiled=True),
            lax.all_gather(second_shift, ("dp", "fsdp"), axis=0, tiled=True),
        )
        kept_inputs.append(hidden_state)
        hidden_state = layer_forward(resident, hidden_state)[0]
    outputs = hidden_state.astype(jnp.bfloat16)
    upstream = cotangent.astype(jnp.float32) * masked.reshape(-1, 1).astype(jnp.float32)
    collected = None
    for applied in range(LAYERS - 1, -1, -1):
        resident = (
            lax.all_gather(query_weight, ("dp", "fsdp"), axis=0, tiled=True),
            lax.all_gather(query_bias, ("dp", "fsdp"), axis=0, tiled=True),
            lax.all_gather(key_weight, ("dp", "fsdp"), axis=0, tiled=True),
            lax.all_gather(value_weight, ("dp", "fsdp"), axis=0, tiled=True),
            lax.all_gather(value_bias, ("dp", "fsdp"), axis=0, tiled=True),
            lax.all_gather(output_weight, ("dp", "fsdp"), axis=0, tiled=True),
            lax.all_gather(output_bias, ("dp", "fsdp"), axis=0, tiled=True),
            lax.all_gather(first_gain, ("dp", "fsdp"), axis=0, tiled=True),
            lax.all_gather(first_shift, ("dp", "fsdp"), axis=0, tiled=True),
            lax.all_gather(inner_weight, ("dp", "fsdp"), axis=0, tiled=True),
            lax.all_gather(inner_bias, ("dp", "fsdp"), axis=0, tiled=True),
            lax.all_gather(outer_weight, ("dp", "fsdp"), axis=0, tiled=True),
            lax.all_gather(outer_bias, ("dp", "fsdp"), axis=0, tiled=True),
            lax.all_gather(second_gain, ("dp", "fsdp"), axis=0, tiled=True),
            lax.all_gather(second_shift, ("dp", "fsdp"), axis=0, tiled=True),
        )
        kept_values = layer_forward(resident, kept_inputs[applied])[1]
        upstream, weight_grads = layer_backward(resident, kept_values, upstream)
        collected = (
            weight_grads
            if collected is None
            else tuple((earlier + later for earlier, later in zip(collected, weight_grads)))
        )
    collected = (
        lax.psum_scatter(collected[0], ("dp", "fsdp"), scatter_dimension=0, tiled=True),
        lax.psum_scatter(collected[1], ("dp", "fsdp"), scatter_dimension=0, tiled=True),
        lax.psum_scatter(collected[2], ("dp", "fsdp"), scatter_dimension=0, tiled=True),
        lax.psum_scatter(collected[3], ("dp", "fsdp"), scatter_dimension=0, tiled=True),
        lax.psum_scatter(collected[4], ("dp", "fsdp"), scatter_dimension=0, tiled=True),
        lax.psum_scatter(collected[5], ("dp", "fsdp"), scatter_dimension=0, tiled=True),
        lax.psum_scatter(collected[6], ("dp", "fsdp"), scatter_dimension=0, tiled=True),
        lax.psum_scatter(collected[7], ("dp", "fsdp"), scatter_dimension=0, tiled=True),
        lax.psum_scatter(collected[8], ("dp", "fsdp"), scatter_dimension=0, tiled=True),
        lax.psum_scatter(collected[9], ("dp", "fsdp"), scatter_dimension=0, tiled=True),
        lax.psum_scatter(collected[10], ("dp", "fsdp"), scatter_dimension=0, tiled=True),
        lax.psum_scatter(collected[11], ("dp", "fsdp"), scatter_dimension=0, tiled=True),
        lax.psum_scatter(collected[12], ("dp", "fsdp"), scatter_dimension=0, tiled=True),
        lax.psum_scatter(collected[13], ("dp", "fsdp"), scatter_dimension=0, tiled=True),
        lax.psum_scatter(collected[14], ("dp", "fsdp"), scatter_dimension=0, tiled=True),
    )
    return (outputs, upstream.astype(jnp.bfloat16)) + tuple(collected)


def solution(mesh):
    in_specs = (
        P(("dp", "fsdp"), None),
        P(("dp", "fsdp"), None),
        P(("dp", "fsdp"), None),
        P(("dp", "fsdp"), None),
        P(("dp", "fsdp")),
        P(("dp", "fsdp"), None),
        P(("dp", "fsdp"), None),
        P(("dp", "fsdp")),
        P(("dp", "fsdp"), None),
        P(("dp", "fsdp")),
        P(("dp", "fsdp")),
        P(("dp", "fsdp")),
        P(("dp", "fsdp"), None),
        P(("dp", "fsdp")),
        P(("dp", "fsdp"), None),
        P(("dp", "fsdp")),
        P(("dp", "fsdp")),
        P(("dp", "fsdp")),
    )
    out_specs = (
        P(("dp", "fsdp"), None),
        P(("dp", "fsdp"), None),
        P(("dp", "fsdp"), None),
        P(("dp", "fsdp")),
        P(("dp", "fsdp"), None),
        P(("dp", "fsdp"), None),
        P(("dp", "fsdp")),
        P(("dp", "fsdp"), None),
        P(("dp", "fsdp")),
        P(("dp", "fsdp")),
        P(("dp", "fsdp")),
        P(("dp", "fsdp"), None),
        P(("dp", "fsdp")),
        P(("dp", "fsdp"), None),
        P(("dp", "fsdp")),
        P(("dp", "fsdp")),
        P(("dp", "fsdp")),
    )
    return jax.shard_map(
        per_device, mesh=mesh, in_specs=in_specs, out_specs=out_specs, check_vma=False
    )
```

profile of v0, /device:TPU:0, one launch (start us, length us, event | category | flops | bytes accessed | tf_op | source)
XLA Modules:
  0.0 1297.5 jit_solution(730865034362673800)
XLA Ops:
  18.8 42.5 %all-reduce.19 = (bf16[768]{0:T(1024)(128)(2,1)S(1)}, bf16[768]{0:T(1024)(128)(2,1)S(1)}, bf16[768]{0:T(1024)(128)(2,1)S(1)}, bf16[768]{0:T(1024)(128)(2,1)S(1)}...) all-reduce(bf16[768]{0:T(1024)(128)(2,1)S(1)} %dynamic-update-slice, ...), channel_id=1, replica_groups=mesh['dp'=8,'fsdp'=4] {'dp','fsdp'}, use_global_device_ids=true, to_apply=%add | all-reduce | flops 9216 | bytes 36864
  70.5 53.4 %all-gather.9.cloned.1.call-done = bf16[768,768]{1,0:T(8,128)(2,1)} async-done(((bf16[24,768]{1,0:T(8,128)(2,1)}), bf16[768,768]{1,0:T(8,128)(2,1)}) %all-gather.9.cloned.1.call-update) | async-done | bytes 1179664 | tf_op jit(solution)/shard_map/all_gather | solution.py:295
  126.3 53.5 %all-gather.11.cloned.1.call-done = bf16[768,768]{1,0:T(8,128)(2,1)} async-done(((bf16[24,768]{1,0:T(8,128)(2,1)}), bf16[768,768]{1,0:T(8,128)(2,1)}) %all-gather.11.cloned.1.call-update) | async-done | bytes 1179664 | tf_op jit(solution)/shard_map/all_gather | solution.py:297
  191.4 44.0 %all-gather.13.cloned.1.call-done = bf16[768,768]{1,0:T(8,128)(2,1)} async-done(((bf16[24,768]{1,0:T(8,128)(2,1)}), bf16[768,768]{1,0:T(8,128)(2,1)}) %all-gather.13.cloned.1.call-update) | async-done | bytes 1179664 | tf_op jit(solution)/shard_map/all_gather | solution.py:300
  238.8 61.9 %all-gather.15.cloned.1.call-done = bf16[768,3072]{1,0:T(8,128)(2,1)} async-done(((bf16[24,3072]{1,0:T(8,128)(2,1)}), bf16[768,3072]{1,0:T(8,128)(2,1)}) %all-gather.15.cloned.1.call-update) | async-done | bytes 4718608 | tf_op jit(solution)/shard_map/all_gather | solution.py:304
  300.7 7.0 fusion.102
  307.6 57.7 %all-gather.17.cloned.1.call-done = bf16[3072,768]{1,0:T(8,128)(2,1)} async-done(((bf16[96,768]{1,0:T(8,128)(2,1)}), bf16[3072,768]{1,0:T(8,128)(2,1)}) %all-gather.17.cloned.1.call-update) | async-done | bytes 4718608 | tf_op jit(solution)/shard_map/all_gather | solution.py:306
  365.4 8.1 fusion.105
  401.6 5.7 fusion.99
  452.1 7.1 convert_reduce_fusion.2
  468.2 7.9 convert_reduce_fusion.11
  476.2 9.2 multiply_reduce_fusion.2
  485.4 7.1 multiply_convert_fusion.2
  502.6 7.1 convert_reduce_fusion.1
  515.8 7.1 convert_reduce_fusion.10
  523.0 9.3 multiply_reduce_fusion.1
  532.3 7.3 multiply_convert_fusion.1
  550.9 8.8 convert_reduce_fusion
  568.3 13.0 %multiply_reduce_fusion = (f32[12,512]{1,0:T(8,128)S(1)}, f32[12,512,512]{1,2,0:T(8,128)}) fusion(f32[12,512,512]{1,2,0:T(8,128)} %copy-done, f32[12,512]{1,0:T(8,128)S(1)} %copy-done.79, bf16[512,12,64]{0,2,1:T(8,128)(2,1)} %bitcast.181, bf16[512,12,64]{0,2,1:T(8,128)(2,1)} %bitcast.208), kind=kOutput, calls=%fused_computation.1 | convolution fusion | flops 415229952 | bytes 26787840 | tf_op jit(solution)/shard_map/while/body/eval_jaxpr/qhd,khd->hqk/dot_general | solution.py:96
  581.4 6.9 multiply_convert_fusion
  609.4 7.2 convert_reduce_fusion.9
  632.9 5.6 fusion.97
  638.5 8.3 add_add_fusion.1
  648.3 6.2 fusion.81
  654.4 10.5 fusion.72
  664.9 13.5 %add_add_fusion = f32[3072,768]{1,0:T(8,128)} fusion(f32[3072,768]{1,0:T(8,128)S(1)} %fusion.81, f32[3072,768]{1,0:T(8,128)} %fusion.72, f32[512,768]{1,0:T(8,128)S(1)} %copy-done.56, f32[512,3072]{1,0:T(8,128)} %fusion.102, f32[3072]{0:T(1024)S(1)} %copy-done.88), kind=kOutput, calls=%fused_computation.21 | convolution fusion | flops 2436759552 | bytes 36188160 | tf_op jit(solution)/shard_map/dot_general | solution.py:19
  679.4 40.1 %all-reduce.18 = (f32[768]{0:T(1024)S(1)}, f32[768]{0:T(1024)S(1)}, f32[768]{0:T(1024)S(1)}, f32[768]{0:T(1024)S(1)}, f32[768]{0:T(1024)S(1)}, /*index=5*/f32[30...) all-reduce(f32[768]{0:T(1024)S(1)} %add.600, ...), channel_id=3, replica_groups=mesh['dp'=8,'fsdp'=4] {'dp','fsdp'}, use_global_device_ids=true, to_apply=%region_37.38.clone | all-reduce | flops 9216 | bytes 73728
  730.3 67.8 %reduce-scatter.9.cloned.1.call-done = f32[24,768]{1,0:T(8,128)} async-done(((f32[768,768]{1,0:T(8,128)}), f32[24,768]{1,0:T(8,128)}) %reduce-scatter.9.cloned.1.call-update) | async-done | bytes 73744 | tf_op jit(solution)/shard_map/reduce_scatter | solution.py:344
  798.1 104.4 %reduce-scatter.11.cloned.1.call-done = f32[24,768]{1,0:T(8,128)} async-done(((f32[768,768]{1,0:T(8,128)}), f32[24,768]{1,0:T(8,128)}) %reduce-scatter.11.cloned.1.call-update) | async-done | bytes 73744 | tf_op jit(solution)/shard_map/reduce_scatter | solution.py:345
  902.6 104.3 %reduce-scatter.13.cloned.1.call-done = f32[24,768]{1,0:T(8,128)} async-done(((f32[768,768]{1,0:T(8,128)}), f32[24,768]{1,0:T(8,128)}) %reduce-scatter.13.cloned.1.call-update) | async-done | bytes 73744 | tf_op jit(solution)/shard_map/reduce_scatter | solution.py:347
  1006.9 142.0 %reduce-scatter.15.cloned.1.call-done = f32[24,3072]{1,0:T(8,128)} async-done(((f32[768,3072]{1,0:T(8,128)}), f32[24,3072]{1,0:T(8,128)}) %reduce-scatter.15.cloned.1.call-update) | async-done | bytes 294928 | tf_op jit(solution)/shard_map/reduce_scatter | solution.py:351
  1149.0 141.5 %reduce-scatter.17.cloned.1.call-done = f32[96,768]{1,0:T(8,128)} async-done(((f32[3072,768]{1,0:T(8,128)}), f32[96,768]{1,0:T(8,128)}) %reduce-scatter.17.cloned.1.call-update) | async-done | bytes 294928 | tf_op jit(solution)/shard_map/reduce_scatter | solution.py:353
  (550 shorter events, 204.5 us)
Async XLA Ops:
  7.2 60.7 %all-gather.7.cloned.1.call-start = ((), (), s32[]{:S(2)}) async-start(), calls=%async_computation.6 | async-start | bytes 1216512 | tf_op jit(solution)/shard_map/all_gather | solution.py:298
  7.9 116.0 %all-gather.9.cloned.1.call-start = ((), (), s32[]{:S(2)}) async-start(), calls=%async_computation.7 | async-start | bytes 1216512 | tf_op jit(solution)/shard_map/all_gather | solution.py:295
  8.7 171.1 %all-gather.11.cloned.1.call-start = ((), (), s32[]{:S(2)}) async-start(), calls=%async_computation.8 | async-start | bytes 1216512 | tf_op jit(solution)/shard_map/all_gather | solution.py:297
  9.4 226.0 %all-gather.13.cloned.1.call-start = ((), (), s32[]{:S(2)}) async-start(), calls=%async_computation.9 | async-start | bytes 1216512 | tf_op jit(solution)/shard_map/all_gather | solution.py:300
  10.0 290.7 %all-gather.15.cloned.1.call-start = ((), (), s32[]{:S(2)}) async-start(), calls=%async_computation.10 | async-start | bytes 4866048 | tf_op jit(solution)/shard_map/all_gather | solution.py:304
  10.6 354.8 %all-gather.17.cloned.1.call-start = ((), (), s32[]{:S(2)}) async-start(), calls=%async_computation.11 | async-start | bytes 4866048 | tf_op jit(solution)/shard_map/all_gather | solution.py:306
  11.1 719.2 %reduce-scatter.7.cloned.1.call-start = ((), (), s32[]{:S(2)}) async-start(), calls=%async_computation.12 | async-start | bytes 2433024 | tf_op jit(solution)/shard_map/reduce_scatter | solution.py:342
  61.3 304.1 %copy-start.123 = (f32[768]{0:T(1024)}, f32[768]{0:T(1024)S(1)}, u32[]{:S(2)}) copy-start(f32[768]{0:T(1024)S(1)} %convert_element_type.448) | copy-start | bytes 9220
  61.3 174.1 %copy-start.126 = (f32[768]{0:T(1024)}, f32[768]{0:T(1024)S(1)}, u32[]{:S(2)}) copy-start(f32[768]{0:T(1024)S(1)} %convert_element_type.442) | copy-start | bytes 9220
  61.3 62.6 %copy-start.129 = (f32[768]{0:T(1024)}, f32[768]{0:T(1024)S(1)}, u32[]{:S(2)}) copy-start(f32[768]{0:T(1024)S(1)} %convert_element_type.435) | copy-start | bytes 9220
  61.4 304.0 %copy-start.105 = (f32[768]{0:T(1024)}, f32[768]{0:T(1024)S(1)}, u32[]{:S(2)}) copy-start(f32[768]{0:T(1024)S(1)} %convert_element_type.444) | copy-start | bytes 9220
  61.4 304.0 %copy-start.86 = (f32[3072]{0:T(1024)}, f32[3072]{0:T(1024)S(1)}, u32[]{:S(2)}) copy-start(f32[3072]{0:T(1024)S(1)} %convert_element_type.446) | copy-start | bytes 36868
  70.1 53.8 %copy-start.40 = (bf16[512,768]{1,0:T(8,128)(2,1)S(1)}, bf16[512,768]{1,0:T(8,128)(2,1)}, u32[]{:S(2)}) copy-start(bf16[512,768]{1,0:T(8,128)(2,1)} %param.18) | copy-start | bytes 2359300
  70.4 115.6 %copy-start.57 = (bf16[512,768]{0,1:T(8,128)(2,1)}, bf16[512,768]{0,1:T(8,128)(2,1)S(1)}, u32[]{:S(2)}) copy-start(bf16[512,768]{0,1:T(8,128)(2,1)S(1)} %copy.101) | copy-start | bytes 2359300
  126.2 55.8 %copy-start.35 = (bf16[512,768]{0,1:T(8,128)(2,1)}, bf16[512,768]{0,1:T(8,128)(2,1)S(1)}, u32[]{:S(2)}) copy-start(bf16[512,768]{0,1:T(8,128)(2,1)S(1)} %copy.102) | copy-start | bytes 2359300
  188.5 46.9 %copy-start.41 = (bf16[512,768]{1,0:T(8,128)(2,1)S(1)}, bf16[512,768]{1,0:T(8,128)(2,1)}, u32[]{:S(2)}) copy-start(bf16[512,768]{1,0:T(8,128)(2,1)} %param.18) | copy-start | bytes 2359300
  191.4 46.2 %copy-start.74 = (bf16[12,64,512]{2,1,0:T(8,128)(2,1)}, bf16[12,64,512]{2,1,0:T(8,128)(2,1)S(1)}, u32[]{:S(2)}) copy-start(bf16[12,64,512]{2,1,0:T(8,128)(2,1)S(1)} %fusion.56) | copy-start | bytes 2359300
  237.6 127.7 %copy-start.6 = (f32[512,768]{1,0:T(8,128)}, f32[512,768]{1,0:T(8,128)S(1)}, u32[]{:S(2)}) copy-start(f32[512,768]{1,0:T(8,128)S(1)} %get-tuple-element.255) | copy-start | bytes 4718596
  237.7 127.7 %copy-start.89 = (f32[512]{0:T(512)}, f32[512]{0:T(512)S(1)}, u32[]{:S(2)}) copy-start(f32[512]{0:T(512)S(1)} %broadcast_multiply_fusion.17) | copy-start | bytes 6148
  238.0 127.4 %copy-start.99 = (f32[512]{0:T(512)}, f32[512]{0:T(512)S(1)}, u32[]{:S(2)}) copy-start(f32[512]{0:T(512)S(1)} %add_rsqrt_fusion.5) | copy-start | bytes 6148
  373.5 26.3 %copy-start.4 = (f32[512,768]{1,0:T(8,128)}, f32[512,768]{1,0:T(8,128)S(1)}, u32[]{:S(2)}) copy-start(f32[512,768]{1,0:T(8,128)S(1)} %get-tuple-element.257) | copy-start | bytes 4718596
  373.5 26.3 %copy-start.84 = (f32[512]{0:T(512)}, f32[512]{0:T(512)S(1)}, u32[]{:S(2)}) copy-start(f32[512]{0:T(512)S(1)} %broadcast_multiply_fusion.16) | copy-start | bytes 6148
  436.5 26.3 %copy-start.54 = (f32[512,768]{1,0:T(8,128)}, f32[512,768]{1,0:T(8,128)S(1)}, u32[]{:S(2)}) copy-start(f32[512,768]{1,0:T(8,128)S(1)} %get-tuple-element.267) | copy-start | bytes 4718596
  436.6 26.3 %copy-start.103 = (f32[512]{0:T(512)}, f32[512]{0:T(512)S(1)}, u32[]{:S(2)}) copy-start(f32[512]{0:T(512)S(1)} %broadcast_multiply_fusion.13) | copy-start | bytes 6148
  464.0 34.9 %copy-start.8 = (f32[512,768]{1,0:T(8,128)}, f32[512,768]{1,0:T(8,128)S(1)}, u32[]{:S(2)}) copy-start(f32[512,768]{1,0:T(8,128)S(1)} %get-tuple-element.248) | copy-start | bytes 4718596
  514.5 33.3 %copy-start.9 = (f32[512,768]{1,0:T(8,128)}, f32[512,768]{1,0:T(8,128)S(1)}, u32[]{:S(2)}) copy-start(f32[512,768]{1,0:T(8,128)S(1)} %get-tuple-element.246) | copy-start | bytes 4718596
  595.6 202.6 %reduce-scatter.9.cloned.1.call-start = ((), (), s32[]{:S(2)}) async-start(), calls=%async_computation.13 | async-start | bytes 2433024 | tf_op jit(solution)/shard_map/reduce_scatter | solution.py:344
  607.0 295.6 %reduce-scatter.11.cloned.1.call-start = ((), (), s32[]{:S(2)}) async-start(), calls=%async_computation.14 | async-start | bytes 2433024 | tf_op jit(solution)/shard_map/reduce_scatter | solution.py:345
  620.6 386.3 %reduce-scatter.13.cloned.1.call-start = ((), (), s32[]{:S(2)}) async-start(), calls=%async_computation.15 | async-start | bytes 2433024 | tf_op jit(solution)/shard_map/reduce_scatter | solution.py:347
  626.7 522.2 %reduce-scatter.15.cloned.1.call-start = ((), (), s32[]{:S(2)}) async-start(), calls=%async_computation.16 | async-start | bytes 9732096 | tf_op jit(solution)/shard_map/reduce_scatter | solution.py:351
  646.9 643.6 %reduce-scatter.17.cloned.1.call-start = ((), (), s32[]{:S(2)}) async-start(), calls=%async_computation.17 | async-start | bytes 9732096 | tf_op jit(solution)/shard_map/reduce_scatter | solution.py:353
  678.5 46.2 %copy-start.68 = (bf16[12,64,512]{2,1,0:T(8,128)(2,1)S(1)}, bf16[12,64,512]{2,1,0:T(8,128)(2,1)}, u32[]{:S(2)}) copy-start(bf16[12,64,512]{2,1,0:T(8,128)(2,1)} %copy-done.67) | copy-start | bytes 2359300
  (158 other events, 740.0 us)
Sparse Core Ops, SparseCore 0:
  10.9 56.8 all-gather.6
  70.7 53.1 all-gather.8
  126.8 52.8 all-gather.10
  182.5 52.8 all-gather.12
  238.2 62.4 all-gather.14
  303.4 61.8 all-gather.16
  595.7 97.8 reduce-scatter.6
  699.5 98.6 reduce-scatter.8
  804.0 98.5 reduce-scatter.10
  908.3 98.5 reduce-scatter.12
  1013.4 135.5 reduce-scatter.14
  1155.3 135.1 reduce-scatter.16
where the time goes:
time: 1310 us; the launch traced here: 1300 us
  waiting for transfers between devices  840 us (64%)
  matrix products  263 us (20%)
  blocking collectives  82.6 us (6%)
  local copies, waits for them, and re-layouts  53.5 us (4%)
  other arithmetic  40.3 us (3%)
  between operations  16.7 us (1%)
    reduce_scatter x1, waiting for transfers between devices, per_device(): lax.psum_scatter(collected[9], ('dp', 'fsdp'), scatter_dimension=0, tiled...  142 us
    reduce_scatter x1, waiting for transfers between devices, per_device(): lax.psum_scatter(collected[11], ('dp', 'fsdp'), scatter_dimension=0, tile...  141 us
    reduce_scatter x1, waiting for transfers between devices, per_device(): lax.psum_scatter(collected[3], ('dp', 'fsdp'), scatter_dimension=0, tiled...  104 us
    reduce_scatter x1, waiting for transfers between devices, per_device(): lax.psum_scatter(collected[5], ('dp', 'fsdp'), scatter_dimension=0, tiled...  104 us
    unnamed x2, blocking collectives  82.6 us
    dot_general x18, matrix products, product_tn(): lax.dot_general(left, right, (((0,), (0,)), ((), ())), preferred_element_...  71.3 us
    reduce_scatter x1, waiting for transfers between devices, per_device(): lax.psum_scatter(collected[2], ('dp', 'fsdp'), scatter_dimension=0, tiled...  67.8 us
    all_gather x1, waiting for transfers between devices, per_device(): lax.all_gather(inner_weight, ('dp', 'fsdp'), axis=0, tiled=True)  61.9 us
  transfers between devices with their start and end apart: 12, of which 11 were waited for; matrix products, arithmetic and copies ran while one was open for 9% of the time, Pallas kernels for 0%

commit v1 on v0

--- a/solution.py
+++ b/solution.py
@@ -1,3 +1,5 @@
+import functools
+
 import jax
 import jax.numpy as jnp
 from jax import lax
@@ -144,8 +146,8 @@
     value_rows = (product(rows_low, value_weight) + value_bias.astype(jnp.float32)).astype(
         jnp.bfloat16
     )
-    context, log_total = lax.map(
-        attend_forward, (by_sequence(query_rows), by_sequence(key_rows), by_sequence(value_rows))
+    context, log_total = jax.vmap(attend_forward)(
+        (by_sequence(query_rows), by_sequence(key_rows), by_sequence(value_rows))
     )
     context_low = flatten_rows(context).astype(jnp.bfloat16)
     attended = product(context_low, output_weight) + output_bias.astype(jnp.float32)
@@ -229,8 +231,7 @@
     output_bias_grad = column_sums(attended_low)
     output_weight_grad = product_tn(context_low, attended_low)
     context_grad = product_nt(attended_low, output_weight).astype(jnp.bfloat16)
-    query_grad, key_grad, value_grad = lax.map(
-        attend_backward,
+    query_grad, key_grad, value_grad = jax.vmap(attend_backward)(
         (
             by_sequence(query_rows),
             by_sequence(key_rows),
@@ -268,93 +269,213 @@
     return (below_grad, weight_grads)
 
 
+AXES = ("dp", "fsdp")
+
+
+def pack_weights(weights):
+    (
+        query_weight,
+        query_bias,
+        key_weight,
+        value_weight,
+        value_bias,
+        output_weight,
+        output_bias,
+        first_gain,
+        first_shift,
+        inner_weight,
+        inner_bias,
+        outer_weight,
+        outer_bias,
+        second_gain,
+        second_shift,
+    ) = weights
+    width = query_weight.shape[1]
+    rows = query_weight.shape[0]
+    vectors = jnp.concatenate(
+        [
+            query_bias,
+            value_bias,
+            output_bias,
+            first_gain,
+            first_shift,
+            outer_bias,
+            second_gain,
+            second_shift,
+            inner_bias,
+        ]
+    )
+    vectors = jnp.pad(vectors, (0, width - vectors.shape[0]))[None, :]
+    return jnp.concatenate(
+        [
+            query_weight,
+            key_weight,
+            value_weight,
+            output_weight,
+            inner_weight.reshape(-1, width),
+            outer_weight,
+            vectors,
+        ],
+        axis=0,
+    )
+
+
+def unpack_rows(packed, rows, ff_rows):
+    width = packed.shape[-1]
+    at = 0
+    pieces = []
+    for count in (rows, rows, rows, rows, ff_rows, ff_rows):
+        pieces.append(packed[..., at : at + count, :])
+        at += count
+    vectors = packed[..., at, :]
+    return pieces, vectors
+
+
+def gather_weights(weights):
+    rows = weights[0].shape[0]
+    ff_rows = weights[11].shape[0]
+    width = weights[0].shape[1]
+    packed = lax.all_gather(pack_weights(weights), AXES, axis=0, tiled=False)
+    shards = packed.shape[0]
+    (qw, kw, vw, ow, iw, uw), vectors = unpack_rows(packed, rows, ff_rows)
+    full_rows = shards * rows
+
+    def square(piece):
+        return piece.reshape(full_rows, width)
+
+    inner_weight = iw.reshape(shards, rows, -1).reshape(full_rows, -1)
+    outer_weight = uw.reshape(shards * ff_rows, width)
+    at = 0
+    found = []
+    for count in (rows,) * 8 + (ff_rows,):
+        found.append(vectors[:, at : at + count].reshape(-1))
+        at += count
+    (qb, vb, ob, g1, s1, ub, g2, s2, ib) = found
+    return (
+        square(qw),
+        qb,
+        square(kw),
+        square(vw),
+        vb,
+        square(ow),
+        ob,
+        g1,
+        s1,
+        inner_weight,
+        ib,
+        outer_weight,
+        ub,
+        g2,
+        s2,
+    )
+
+
+def scatter_grads(grads, shards):
+    (
+        query_weight_grad,
+        query_bias_grad,
+        key_weight_grad,
+        value_weight_grad,
+        value_bias_grad,
+        output_weight_grad,
+        output_bias_grad,
+        first_gain_grad,
+        first_shift_grad,
+        inner_weight_grad,
+        inner_bias_grad,
+        outer_weight_grad,
+        outer_bias_grad,
+        second_gain_grad,
+        second_shift_grad,
+    ) = grads
+    width = query_weight_grad.shape[1]
+    rows = query_weight_grad.shape[0] // shards
+    ff_rows = outer_weight_grad.shape[0] // shards
+
+    def blocks(grad):
+        return grad.reshape(shards, -1, width)
+
+    vectors = jnp.concatenate(
+        [
+            v.reshape(shards, -1)
+            for v in (
+                query_bias_grad,
+                value_bias_grad,
+                output_bias_grad,
+                first_gain_grad,
+                first_shift_grad,
+                outer_bias_grad,
+                second_gain_grad,
+                second_shift_grad,
+                inner_bias_grad,
+            )
+        ],
+        axis=1,
+    )
+    vectors = jnp.pad(vectors, ((0, 0), (0, width - vectors.shape[1])))[:, None, :]
+    packed = jnp.concatenate(
+        [
+            blocks(query_weight_grad),
+            blocks(key_weight_grad),
+            blocks(value_weight_grad),
+            blocks(output_weight_grad),
+            blocks(inner_weight_grad.reshape(shards, rows, -1)),
+            blocks(outer_weight_grad),
+            vectors,
+        ],
+        axis=1,
+    )
+    mine = lax.psum_scatter(packed, AXES, scatter_dimension=0, tiled=True)[0]
+    (qw, kw, vw, ow, iw, uw), vec = unpack_rows(mine, rows, ff_rows)
+    at = 0
+    found = []
+    for count in (rows,) * 8 + (ff_rows,):
+        found.append(vec[at : at + count])
+        at += count
+    (qb, vb, ob, g1, s1, ub, g2, s2, ib) = found
+    return (
+        qw,
+        qb,
+        kw,
+        vw,
+        vb,
+        ow,
+        ob,
+        g1,
+        s1,
+        iw.reshape(rows, -1),
+        ib,
+        uw,
+        ub,
+        g2,
+        s2,
+    )
+
+
 def per_device(
+    shards,
     inputs,
     cotangent,
     masked,
-    query_weight,
-    query_bias,
-    key_weight,
-    value_weight,
-    value_bias,
-    output_weight,
-    output_bias,
-    first_gain,
-    first_shift,
-    inner_weight,
-    inner_bias,
-    outer_weight,
-    outer_bias,
-    second_gain,
-    second_shift,
+    *weights,
 ):
+    resident = gather_weights(weights)
     hidden_state = inputs.astype(jnp.float32)
-    kept_inputs = []
+    kept = []
     for applied in range(LAYERS):
-        resident = (
-            lax.all_gather(query_weight, ("dp", "fsdp"), axis=0, tiled=True),
-            lax.all_gather(query_bias, ("dp", "fsdp"), axis=0, tiled=True),
-            lax.all_gather(key_weight, ("dp", "fsdp"), axis=0, tiled=True),
-            lax.all_gather(value_weight, ("dp", "fsdp"), axis=0, tiled=True),
-            lax.all_gather(value_bias, ("dp", "fsdp"), axis=0, tiled=True),
-            lax.all_gather(output_weight, ("dp", "fsdp"), axis=0, tiled=True),
-            lax.all_gather(output_bias, ("dp", "fsdp"), axis=0, tiled=True),
-            lax.all_gather(first_gain, ("dp", "fsdp"), axis=0, tiled=True),
-            lax.all_gather(first_shift, ("dp", "fsdp"), axis=0, tiled=True),
-            lax.all_gather(inner_weight, ("dp", "fsdp"), axis=0, tiled=True),
-            lax.all_gather(inner_bias, ("dp", "fsdp"), axis=0, tiled=True),
-            lax.all_gather(outer_weight, ("dp", "fsdp"), axis=0, tiled=True),
-            lax.all_gather(outer_bias, ("dp", "fsdp"), axis=0, tiled=True),
-            lax.all_gather(second_gain, ("dp", "fsdp"), axis=0, tiled=True),
-            lax.all_gather(second_shift, ("dp", "fsdp"), axis=0, tiled=True),
-        )
-        kept_inputs.append(hidden_state)
-        hidden_state = layer_forward(resident, hidden_state)[0]
+        hidden_state, kept_values = layer_forward(resident, hidden_state)
+        kept.append(kept_values)
     outputs = hidden_state.astype(jnp.bfloat16)
     upstream = cotangent.astype(jnp.float32) * masked.reshape(-1, 1).astype(jnp.float32)
     collected = None
     for applied in range(LAYERS - 1, -1, -1):
-        resident = (
-            lax.all_gather(query_weight, ("dp", "fsdp"), axis=0, tiled=True),
-            lax.all_gather(query_bias, ("dp", "fsdp"), axis=0, tiled=True),
-            lax.all_gather(key_weight, ("dp", "fsdp"), axis=0, tiled=True),
-            lax.all_gather(value_weight, ("dp", "fsdp"), axis=0, tiled=True),
-            lax.all_gather(value_bias, ("dp", "fsdp"), axis=0, tiled=True),
-            lax.all_gather(output_weight, ("dp", "fsdp"), axis=0, tiled=True),
-            lax.all_gather(output_bias, ("dp", "fsdp"), axis=0, tiled=True),
-            lax.all_gather(first_gain, ("dp", "fsdp"), axis=0, tiled=True),
-            lax.all_gather(first_shift, ("dp", "fsdp"), axis=0, tiled=True),
-            lax.all_gather(inner_weight, ("dp", "fsdp"), axis=0, tiled=True),
-            lax.all_gather(inner_bias, ("dp", "fsdp"), axis=0, tiled=True),
-            lax.all_gather(outer_weight, ("dp", "fsdp"), axis=0, tiled=True),
-            lax.all_gather(outer_bias, ("dp", "fsdp"), axis=0, tiled=True),
-            lax.all_gather(second_gain, ("dp", "fsdp"), axis=0, tiled=True),
-            lax.all_gather(second_shift, ("dp", "fsdp"), axis=0, tiled=True),
-        )
-        kept_values = layer_forward(resident, kept_inputs[applied])[1]
-        upstream, weight_grads = layer_backward(resident, kept_values, upstream)
+        upstream, weight_grads = layer_backward(resident, kept[applied], upstream)
         collected = (
             weight_grads
             if collected is None
             else tuple((earlier + later for earlier, later in zip(collected, weight_grads)))
         )
-    collected = (
-        lax.psum_scatter(collected[0], ("dp", "fsdp"), scatter_dimension=0, tiled=True),
-        lax.psum_scatter(collected[1], ("dp", "fsdp"), scatter_dimension=0, tiled=True),
-        lax.psum_scatter(collected[2], ("dp", "fsdp"), scatter_dimension=0, tiled=True),
-        lax.psum_scatter(collected[3], ("dp", "fsdp"), scatter_dimension=0, tiled=True),
-        lax.psum_scatter(collected[4], ("dp", "fsdp"), scatter_dimension=0, tiled=True),
-        lax.psum_scatter(collected[5], ("dp", "fsdp"), scatter_dimension=0, tiled=True),
-        lax.psum_scatter(collected[6], ("dp", "fsdp"), scatter_dimension=0, tiled=True),
-        lax.psum_scatter(collected[7], ("dp", "fsdp"), scatter_dimension=0, tiled=True),
-        lax.psum_scatter(collected[8], ("dp", "fsdp"), scatter_dimension=0, tiled=True),
-        lax.psum_scatter(collected[9], ("dp", "fsdp"), scatter_dimension=0, tiled=True),
-        lax.psum_scatter(collected[10], ("dp", "fsdp"), scatter_dimension=0, tiled=True),
-        lax.psum_scatter(collected[11], ("dp", "fsdp"), scatter_dimension=0, tiled=True),
-        lax.psum_scatter(collected[12], ("dp", "fsdp"), scatter_dimension=0, tiled=True),
-        lax.psum_scatter(collected[13], ("dp", "fsdp"), scatter_dimension=0, tiled=True),
-        lax.psum_scatter(collected[14], ("dp", "fsdp"), scatter_dimension=0, tiled=True),
-    )
+    collected = scatter_grads(collected, shards)
     return (outputs, upstream.astype(jnp.bfloat16)) + tuple(collected)
 
 
@@ -398,6 +519,7 @@
         P(("dp", "fsdp")),
         P(("dp", "fsdp")),
     )
+    shards = mesh.shape["dp"] * mesh.shape["fsdp"]
     return jax.shard_map(
-        per_device, mesh=mesh, in_specs=in_specs, out_specs=out_specs, check_vma=False
-    )
+        functools.partial(per_device, shards), mesh=mesh, in_specs=in_specs, out_specs=out_specs, check_vma=False
+    )

time: 1310 us -> 804 us (0.61)
  waiting for transfers between devices: 840 us -> 369 us
  blocking collectives: 82.6 us -> 0 us
  local copies, waits for them, and re-layouts: 53.5 us -> 115 us
    reduce_scatter x6 -> x1, waiting for transfers between devices: 560 us -> 262 us  [scatter_grads(): mine = lax.psum_scatter(packed, AXES, scatter_dimension=0, tiled=True)[0]]
    all_gather x6 -> x1, waiting for transfers between devices: 276 us -> 106 us  [gather_weights(): packed = lax.all_gather(pack_weights(weights), AXES, axis=0, tiled=False)]
    unnamed x2 -> x0, blocking collectives: 82.6 us -> none
    another operation x0 -> x2, local copies, waits for them, and re-layouts: none -> 20.3 us  [the longest x1 11.8 us: blocks(): return grad.reshape(shards, -1, width)]
    slice x0 -> x7, local copies, waits for them, and re-layouts: none -> 19.1 us  [the longest x4 15.3 us: unpack_rows(): pieces.append(packed[..., at:at + count, :])]
    unnamed x383 -> x447, local copies, waits for them, and re-layouts: 36.5 us -> 47.1 us
  transfers between devices with their start and end apart: 12 -> 2, of which waited for: 11 -> 2; matrix products, arithmetic and copies ran while one was open for 9% -> 1% of each run, Pallas kernels for 0% -> 0%
where the time goes in v1:
time: 804 us; the launch traced here: 793 us
  waiting for transfers between devices  369 us (46%)
  matrix products  250 us (31%)
  local copies, waits for them, and re-layouts  115 us (14%)
  other arithmetic  42.8 us (5%)
  between operations  16.8 us (2%)
    reduce_scatter x1, waiting for transfers between devices, scatter_grads(): mine = lax.psum_scatter(packed, AXES, scatter_dimension=0, tiled=True)[0]  262 us
    all_gather x1, waiting for transfers between devices, gather_weights(): packed = lax.all_gather(pack_weights(weights), AXES, axis=0, tiled=False)  106 us
    dot_general x18, matrix products, product_tn(): lax.dot_general(left, right, (((0,), (0,)), ((), ())), preferred_element_...  67.2 us
    dot_general x18, matrix products, product(): return jnp.dot(left, right, preferred_element_type=jnp.float32)  56.6 us
    dot_general x18, matrix products, product_nt(): lax.dot_general(left, right, (((1,), (1,)), ((), ())), preferred_element_...  49.8 us
    unnamed x447, local copies, waits for them, and re-layouts  47.1 us
    dot_general x3, matrix products, attend_backward(): jnp.einsum('qhd,khd->hqk', grad_heads, value_heads, preferred_element_typ...  29.5 us
    convert_element_type x3, other arithmetic, attend_backward(): (probs * (prob_grad - jnp.sum(probs * prob_grad, axis=-1, keepdims=True))...  21.6 us
  transfers between devices with their start and end apart: 2, of which 2 were waited for; matrix products, arithmetic and copies ran while one was open for 1% of the time, Pallas kernels for 0%

profile of v1, /device:TPU:0, one launch (start us, length us, event | category | flops | bytes accessed | tf_op | source)
XLA Modules:
  0.0 793.4 jit_solution(9116649165182260095)
XLA Ops:
  12.3 6.1 concatenate.12
  19.8 106.5 %all-gather.4.cloned.1.call-done = bf16[32,289,768]{2,1,0:T(8,128)(2,1)} async-done(((bf16[1,289,768]{2,1,0:T(8,128)(2,1)}), bf16[32,289,768]{2,1,0:T(8,128)(2,1)}) %all-gather.4.cloned.1.call-update) | async-done | bytes 14204944 | tf_op jit(solution)/shard_map/all_gather | solution.py:338
  127.6 7.9 fusion.104
  135.6 8.5 %reshape_reshape.4 = bf16[768,3072]{1,0:T(8,128)(2,1)} reshape(bf16[32,96,768]{2,1,0:T(8,128)(2,1)} %get-tuple-element.53) | data formatting | bytes 9437184 | tf_op jit(solution)/shard_map/reshape;reshape | solution.py:346
  144.5 3.8 fusion.105
  162.1 15.1 %fusion.102 = f32[512,3072]{1,0:T(8,128)S(1)} fusion(bf16[768,3072]{1,0:T(8,128)(2,1)} %reshape_reshape.4, f32[512,768]{1,0:T(8,128)S(1)} %get-tuple-element.85, f32[768]{0:T(1024)S(1)} %reshape.737, f32[768]{0:T(1024)S(1)} %reshape.736, f32[512]{0:T(512)S(1)} %add_rsqrt_fusion.5, f32[512]{0:T(512)S(1)} %broadcast_multiply_fusion.17), kind=kOutput, calls=%fused_computation.275 | convolution fusion | flops 2417885184 | bytes 12593152 | tf_op jit(solution)/shard_map/dot_general | solution.py:17
  177.4 9.2 %fusion.107 = (f32[512]{0:T(512)S(1)}, f32[512,768]{1,0:T(8,128)S(1)}) fusion(f32[768]{0:T(1024)S(1)} %reshape.739, bf16[3072,768]{1,0:T(8,128)(2,1)} %bitcast.302, f32[512,3072]{1,0:T(8,128)S(1)} %fusion.102, f32[3072]{0:T(1024)S(1)} %reshape.738, f32[768]{0:T(1024)S(1)} %reshape.737, f32[768]{0:T(1024)S(1)} %reshape.736, f32[512]{0:T(512)S(1)} %add_rsqrt_fusion.5, ...), kind=kOutput, calls=%fused_computation.279 | convolution fusion | flops 2434399744 | bytes 14183424 | tf_op jit(solution)/shard_map/dot_general | solution.py:17
  210.9 5.2 fusion.99
  216.2 4.2 fusion.109
  245.5 4.8 fusion.95
  250.3 4.2 fusion.111
  259.3 7.1 convert_reduce_fusion.2
  276.4 7.9 convert_reduce_fusion.11
  284.3 9.2 %multiply_reduce_fusion.2 = (f32[12,512]{1,0:T(8,128)S(1)}, f32[12,512,512]{1,2,0:T(8,128)}) fusion(f32[12,512,512]{1,2,0:T(8,128)} %copy-done.2, f32[12,512]{1,0:T(8,128)S(1)} %copy-done.95, bf16[512,12,64]{0,2,1:T(8,128)(2,1)S(1)} %bitcast.273, bf16[512,12,64]{0,2,1:T(8,128)(2,1)S(1)} %bitcast.319), kind=kOutput, calls=%fused_computation.7 | convolution fusion | flops 415229952 | bytes 26787840 | tf_op jit(solution)/shard_map/vmap(qhd,khd->hqk)/dot_general | solution.py:98
  293.6 7.3 multiply_convert_fusion.2
  311.4 7.1 convert_reduce_fusion.1
  318.6 3.6 multiply_reduce_fusion.10
  326.7 7.1 convert_reduce_fusion.10
  333.8 9.3 %multiply_reduce_fusion.1 = (f32[12,512]{1,0:T(8,128)S(1)}, f32[12,512,512]{1,2,0:T(8,128)}) fusion(f32[12,512,512]{1,2,0:T(8,128)} %copy-done.1, f32[12,512]{1,0:T(8,128)S(1)} %copy-done.96, bf16[512,12,64]{0,2,1:T(8,128)(2,1)S(1)} %bitcast.275, bf16[512,12,64]{0,2,1:T(8,128)(2,1)S(1)} %bitcast.317), kind=kOutput, calls=%fused_computation.4 | convolution fusion | flops 415229952 | bytes 26787840 | tf_op jit(solution)/shard_map/vmap(qhd,khd->hqk)/dot_general | solution.py:98
  343.1 7.3 multiply_convert_fusion.1
  361.4 7.1 convert_reduce_fusion
  377.6 11.0 %multiply_reduce_fusion = (f32[12,512]{1,0:T(8,128)S(1)}, f32[12,512,512]{1,2,0:T(8,128)}) fusion(f32[12,512,512]{1,2,0:T(8,128)} %copy-done, f32[12,512]{1,0:T(8,128)} %log_add_fusion, bf16[512,12,64]{0,2,1:T(8,128)(2,1)S(1)} %bitcast.270, bf16[512,12,64]{0,2,1:T(8,128)(2,1)} %bitcast.347), kind=kOutput, calls=%fused_computation.1 | convolution fusion | flops 415229952 | bytes 26787840 | tf_op jit(solution)/shard_map/vmap(qhd,khd->hqk)/dot_general | solution.py:98
  390.5 6.9 multiply_convert_fusion
  418.8 5.6 fusion.97
  424.4 10.4 %fusion.81 = f32[3072,768]{1,0:T(8,128)} fusion(f32[512,768]{1,0:T(8,128)S(1)} %copy-done.67, f32[512,3072]{1,0:T(8,128)} %copy-done.180, f32[3072]{0:T(1024)S(1)} %copy-done.113), kind=kOutput, calls=%fused_computation.261 | convolution fusion | flops 2432040960 | bytes 17313792 | tf_op jit(solution)/shard_map/dot_general | solution.py:21
  434.8 6.6 fusion.72
  449.8 8.3 %add_add_fusion.1 = f32[768,3072]{1,0:T(8,128)} fusion(f32[768,3072]{1,0:T(8,128)S(1)} %fusion.93, f32[768,3072]{1,0:T(8,128)} %fusion.97, bf16[512,3072]{1,0:T(8,128)(2,1)S(1)} %copy-done.56, f32[512,768]{1,0:T(8,128)S(1)} %copy-done.6, f32[768]{0:T(1024)S(1)} %copy-done.140, f32[768]{0:T(1024)S(1)} %reshape.736, f32[512]{0:T(512)S(1)} %copy-done.131, ...), kind=kOutput, calls=%fused_computation.22 | convolution fusion | flops 2422603776 | bytes 33040384 | tf_op jit(solution)/shard_map/dot_general | solution.py:21
  458.4 11.8 %reshape_reshape.5 = f32[32,96,768]{2,1,0:T(8,128)} reshape(f32[768,3072]{1,0:T(8,128)} %add_add_fusion.1) | data formatting | bytes 18874368 | tf_op jit(solution)/shard_map/reshape;reshape | solution.py:396
  485.9 4.6 constant_dynamic-update-slice_fusion.8
  490.5 12.5 %add_add_fusion = f32[3072,768]{1,0:T(8,128)S(1)} fusion(f32[3072,768]{1,0:T(8,128)} %fusion.81, f32[3072,768]{1,0:T(8,128)} %fusion.72, f32[512,768]{1,0:T(8,128)S(1)} %copy-done.50, f32[512,3072]{1,0:T(8,128)} %copy-done.48, f32[3072]{0:T(1024)S(1)} %copy-done.114), kind=kOutput, calls=%fused_computation.21 | convolution fusion | flops 2436759552 | bytes 36188160 | tf_op jit(solution)/shard_map/dot_general | solution.py:21
  503.1 4.2 constant_dynamic-update-slice_fusion.7
  516.9 262.4 %reduce-scatter.2.cloned.1.call-done = f32[1,289,768]{2,1,0:T(8,128)} async-done(((f32[32,289,768]{2,1,0:T(8,128)}), f32[1,289,768]{2,1,0:T(8,128)}) %reduce-scatter.2.cloned.1.call-update) | async-done | bytes 887824 | tf_op jit(solution)/shard_map/reduce_scatter | solution.py:428
  (609 shorter events, 183.5 us)
Async XLA Ops:
  7.2 119.1 %all-gather.4.cloned.1.call-start = ((), (), s32[]{:S(2)}) async-start(), calls=%async_computation.2 | async-start | bytes 15003648 | tf_op jit(solution)/shard_map/all_gather | solution.py:338
  19.2 760.1 %reduce-scatter.2.cloned.1.call-start = ((), (), s32[]{:S(2)}) async-start(), calls=%async_computation.1 | async-start | bytes 30007296 | tf_op jit(solution)/shard_map/reduce_scatter | solution.py:428
  127.6 49.7 %copy-start.161 = (f32[768]{0:T(1024)}, f32[768]{0:T(1024)S(1)}, u32[]{:S(2)}) copy-start(f32[768]{0:T(1024)S(1)} %reshape.739) | copy-start | bytes 9220
  144.1 16.4 %copy-start.164 = (f32[768]{0:T(1024)}, f32[768]{0:T(1024)S(1)}, u32[]{:S(2)}) copy-start(f32[768]{0:T(1024)S(1)} %reshape.735) | copy-start | bytes 9220
  144.2 43.0 %copy-start.167 = (f32[768]{0:T(1024)}, f32[768]{0:T(1024)S(1)}, u32[]{:S(2)}) copy-start(f32[768]{0:T(1024)S(1)} %reshape.733) | copy-start | bytes 9220
  144.4 32.9 %copy-start.137 = (f32[768]{0:T(1024)}, f32[768]{0:T(1024)S(1)}, u32[]{:S(2)}) copy-start(f32[768]{0:T(1024)S(1)} %reshape.737) | copy-start | bytes 9220
  161.5 15.7 %copy-start.5 = (f32[512,768]{1,0:T(8,128)}, f32[512,768]{1,0:T(8,128)S(1)}, u32[]{:S(2)}) copy-start(f32[512,768]{1,0:T(8,128)S(1)} %get-tuple-element.85) | copy-start | bytes 4718596
  161.6 15.8 %copy-start.115 = (f32[512]{0:T(512)}, f32[512]{0:T(512)S(1)}, u32[]{:S(2)}) copy-start(f32[512]{0:T(512)S(1)} %broadcast_multiply_fusion.17) | copy-start | bytes 6148
  161.9 15.5 %copy-start.129 = (f32[512]{0:T(512)}, f32[512]{0:T(512)S(1)}, u32[]{:S(2)}) copy-start(f32[512]{0:T(512)S(1)} %add_rsqrt_fusion.5) | copy-start | bytes 6148
  162.0 15.4 %copy-start.108 = (f32[3072]{0:T(1024)}, f32[3072]{0:T(1024)S(1)}, u32[]{:S(2)}) copy-start(f32[3072]{0:T(1024)S(1)} %reshape.738) | copy-start | bytes 36868
  186.6 21.5 %copy-start.3 = (f32[512,768]{1,0:T(8,128)}, f32[512,768]{1,0:T(8,128)S(1)}, u32[]{:S(2)}) copy-start(f32[512,768]{1,0:T(8,128)S(1)} %get-tuple-element.87) | copy-start | bytes 4718596
  186.6 21.5 %copy-start.106 = (f32[512]{0:T(512)}, f32[512]{0:T(512)S(1)}, u32[]{:S(2)}) copy-start(f32[512]{0:T(512)S(1)} %broadcast_multiply_fusion.16) | copy-start | bytes 6148
  243.8 26.3 %copy-start.46 = (f32[512,768]{1,0:T(8,128)}, f32[512,768]{1,0:T(8,128)S(1)}, u32[]{:S(2)}) copy-start(f32[512,768]{1,0:T(8,128)S(1)} %get-tuple-element.97) | copy-start | bytes 4718596
  243.8 26.3 %copy-start.135 = (f32[512]{0:T(512)}, f32[512]{0:T(512)S(1)}, u32[]{:S(2)}) copy-start(f32[512]{0:T(512)S(1)} %broadcast_multiply_fusion.13) | copy-start | bytes 6148
  245.5 24.7 %copy-start.159 = (f32[512]{0:T(512)}, f32[512]{0:T(512)S(1)}, u32[]{:S(2)}) copy-start(f32[512]{0:T(512)S(1)} %add_rsqrt_fusion.1) | copy-start | bytes 6148
  276.4 17.1 %slice-start.6 = ((s8[12582912]{0:T(1024)(128)(4,1)}), s8[4194304]{0:T(1024)(128)(4,1)S(1)}, s32[]{:S(2)}) async-start(s8[12582912]{0:T(1024)(128)(4,1)} %bitcast.251), calls=%async_computation.9 | async-start | bytes 8388608
  276.4 17.1 %slice-start.7 = ((s8[12582912]{0:T(1024)(128)(4,1)}), s8[4194304]{0:T(1024)(128)(4,1)S(1)}, s32[]{:S(2)}) async-start(s8[12582912]{0:T(1024)(128)(4,1)} %bitcast.251), calls=%async_computation.10 | async-start | bytes 8388608
  284.3 23.2 %copy-start.29 = (bf16[12,64,512]{2,1,0:T(8,128)(2,1)}, bf16[12,64,512]{2,1,0:T(8,128)(2,1)S(1)}, u32[]{:S(2)}) copy-start(bf16[12,64,512]{2,1,0:T(8,128)(2,1)S(1)} %get-tuple-element.120) | copy-start | bytes 2359300
  323.3 34.2 %copy-start.12 = (f32[512,768]{1,0:T(8,128)}, f32[512,768]{1,0:T(8,128)S(1)}, u32[]{:S(2)}) copy-start(f32[512,768]{1,0:T(8,128)S(1)} %get-tuple-element.48) | copy-start | bytes 4718596
  326.6 16.5 %slice-start.3 = ((s8[12582912]{0:T(1024)(128)(4,1)}), s8[4194304]{0:T(1024)(128)(4,1)S(1)}, s32[]{:S(2)}) async-start(s8[12582912]{0:T(1024)(128)(4,1)} %bitcast.249), calls=%async_computation.6 | async-start | bytes 8388608
  326.6 16.5 %slice-start.4 = ((s8[12582912]{0:T(1024)(128)(4,1)}), s8[4194304]{0:T(1024)(128)(4,1)S(1)}, s32[]{:S(2)}) async-start(s8[12582912]{0:T(1024)(128)(4,1)} %bitcast.249), calls=%async_computation.7 | async-start | bytes 8388608
  333.8 23.7 %copy-start.25 = (bf16[12,64,512]{2,1,0:T(8,128)(2,1)}, bf16[12,64,512]{2,1,0:T(8,128)(2,1)S(1)}, u32[]{:S(2)}) copy-start(bf16[12,64,512]{2,1,0:T(8,128)(2,1)S(1)} %get-tuple-element.122) | copy-start | bytes 2359300
  377.6 12.9 %slice-start.2 = ((s8[12582912]{0:T(1024)(128)(4,1)}), s8[4194304]{0:T(1024)(128)(4,1)S(1)}, s32[]{:S(2)}) async-start(s8[12582912]{0:T(1024)(128)(4,1)} %bitcast.247), calls=%async_computation.5 | async-start | bytes 8388608
  377.6 12.8 %copy-start.94 = (f32[12,512]{1,0:T(8,128)S(1)}, f32[12,512]{1,0:T(8,128)}, u32[]{:S(2)}) copy-start(f32[12,512]{1,0:T(8,128)} %log_add_fusion) | copy-start | bytes 73732
  402.1 39.3 %copy-start.39 = (bf16[12,64,512]{2,1,0:T(8,128)(2,1)}, bf16[12,64,512]{2,1,0:T(8,128)(2,1)S(1)}, u32[]{:S(2)}) copy-start(bf16[12,64,512]{2,1,0:T(8,128)(2,1)S(1)} %get-tuple-element.112) | copy-start | bytes 2359300
  405.3 42.2 %copy-start.27 = (bf16[12,64,512]{2,1,0:T(8,128)(2,1)}, bf16[12,64,512]{2,1,0:T(8,128)(2,1)S(1)}, u32[]{:S(2)}) copy-start(bf16[12,64,512]{2,1,0:T(8,128)(2,1)S(1)} %get-tuple-element.118) | copy-start | bytes 2359300
  418.8 16.0 %slice-start.30 = ((s8[6291456]{0:T(1024)(128)(4,1)}), s8[4194304]{0:T(1024)(128)(4,1)S(1)}, s32[]{:S(2)}) async-start(s8[6291456]{0:T(1024)(128)(4,1)} %bitcast.361), calls=%async_computation.33 | async-start | bytes 8388608
  458.2 12.6 %copy-start.147 = (f32[768]{0:T(1024)S(1)}, f32[768]{0:T(1024)}, u32[]{:S(2)}) copy-start(f32[768]{0:T(1024)} %get-tuple-element.27) | copy-start | bytes 9220
  458.3 12.8 %copy-start.153 = (f32[3072]{0:T(1024)S(1)}, f32[3072]{0:T(1024)}, u32[]{:S(2)}) copy-start(f32[3072]{0:T(1024)} %get-tuple-element.125) | copy-start | bytes 36868
  458.3 12.8 %copy-start.154 = (f32[3072]{0:T(1024)S(1)}, f32[3072]{0:T(1024)}, u32[]{:S(2)}) copy-start(f32[3072]{0:T(1024)} %get-tuple-element.127) | copy-start | bytes 36868
  458.3 12.8 %copy-start.155 = (f32[3072]{0:T(1024)S(1)}, f32[3072]{0:T(1024)}, u32[]{:S(2)}) copy-start(f32[3072]{0:T(1024)} %get-tuple-element.123) | copy-start | bytes 36868
  458.3 13.7 %copy-start.61 = (bf16[12,64,512]{2,1,0:T(8,128)(2,1)S(1)}, bf16[12,64,512]{2,1,0:T(8,128)(2,1)}, u32[]{:S(2)}) copy-start(bf16[12,64,512]{2,1,0:T(8,128)(2,1)} %copy-done.60) | copy-start | bytes 2359300
  (187 other events, 962.4 us)
Sparse Core Ops, SparseCore 0:
  19.3 106.9 all-gather.3
  510.5 268.7 reduce-scatter.1

commit v2 on v1

--- a/solution.py
+++ b/solution.py
@@ -425,7 +425,9 @@
         ],
         axis=1,
     )
-    mine = lax.psum_scatter(packed, AXES, scatter_dimension=0, tiled=True)[0]
+    mine = lax.psum_scatter(
+        packed.astype(jnp.bfloat16), AXES, scatter_dimension=0, tiled=True
+    )[0].astype(jnp.float32)
     (qw, kw, vw, ow, iw, uw), vec = unpack_rows(mine, rows, ff_rows)
     at = 0
     found = []

time: 804 us -> 686 us (0.85)
  waiting for transfers between devices: 369 us -> 265 us
  local copies, waits for them, and re-layouts: 115 us -> 98.1 us
    reduce_scatter x1, waiting for transfers between devices: 262 us -> 158 us  [scatter_grads(): lax.psum_scatter(packed.astype(jnp.bfloat16), AXES, scatter_dimension=0,...]
    unnamed x447 -> x443, local copies, waits for them, and re-layouts: 47.1 us -> 40.2 us
where the time goes in v2:
time: 686 us; the launch traced here: 676 us
  waiting for transfers between devices  265 us (39%)
  matrix products  252 us (37%)
  local copies, waits for them, and re-layouts  98.1 us (14%)
  other arithmetic  44 us (6%)
  between operations  16.8 us (2%)
    reduce_scatter x1, waiting for transfers between devices, scatter_grads(): lax.psum_scatter(packed.astype(jnp.bfloat16), AXES, scatter_dimension=0,...  158 us
    all_gather x1, waiting for transfers between devices, gather_weights(): packed = lax.all_gather(pack_weights(weights), AXES, axis=0, tiled=False)  107 us
    dot_general x18, matrix products, product_tn(): lax.dot_general(left, right, (((0,), (0,)), ((), ())), preferred_element_...  69.2 us
    dot_general x18, matrix products, product(): return jnp.dot(left, right, preferred_element_type=jnp.float32)  56.5 us
    dot_general x18, matrix products, product_nt(): lax.dot_general(left, right, (((1,), (1,)), ((), ())), preferred_element_...  49.8 us
    unnamed x443, local copies, waits for them, and re-layouts  40.2 us
    dot_general x3, matrix products, attend_backward(): jnp.einsum('qhd,khd->hqk', grad_heads, value_heads, preferred_element_typ...  29.5 us
    convert_element_type x3, other arithmetic, attend_backward(): (probs * (prob_grad - jnp.sum(probs * prob_grad, axis=-1, keepdims=True))...  21.6 us
  transfers between devices with their start and end apart: 2, of which 2 were waited for; matrix products, arithmetic and copies ran while one was open for 1% of the time, Pallas kernels for 0%

profile of v2, /device:TPU:0, one launch (start us, length us, event | category | flops | bytes accessed | tf_op | source)
XLA Modules:
  0.0 675.6 jit_solution(9091946308658620056)
XLA Ops:
  12.3 6.1 concatenate.14
  19.8 106.5 %all-gather.4.cloned.1.call-done = bf16[32,289,768]{2,1,0:T(8,128)(2,1)} async-done(((bf16[1,289,768]{2,1,0:T(8,128)(2,1)}), bf16[32,289,768]{2,1,0:T(8,128)(2,1)}) %all-gather.4.cloned.1.call-update) | async-done | bytes 14204944 | tf_op jit(solution)/shard_map/all_gather | solution.py:338
  127.6 8.0 %fusion.107 = (bf16[32,96,768]{2,1,0:T(8,128)(2,1)}, bf16[32,96,768]{2,1,0:T(8,128)(2,1)}) fusion(bf16[32,289,768]{2,1,0:T(8,128)(2,1)} %all-gather.4.cloned.1.call-done), kind=kLoop, calls=%fused_computation.282 | loop fusion | bytes 18874368 | tf_op jit(solution)/shard_map/slice | solution.py:328
  135.7 8.5 %reshape_reshape.5 = bf16[768,3072]{1,0:T(8,128)(2,1)} reshape(bf16[32,96,768]{2,1,0:T(8,128)(2,1)} %get-tuple-element.53) | data formatting | bytes 9437184 | tf_op jit(solution)/shard_map/reshape;reshape | solution.py:346
  144.6 3.8 fusion.108
  162.3 15.1 %fusion.105 = f32[512,3072]{1,0:T(8,128)S(1)} fusion(bf16[768,3072]{1,0:T(8,128)(2,1)} %reshape_reshape.5, f32[512,768]{1,0:T(8,128)S(1)} %get-tuple-element.85, f32[768]{0:T(1024)S(1)} %reshape.750, f32[768]{0:T(1024)S(1)} %reshape.749, f32[512]{0:T(512)S(1)} %add_rsqrt_fusion.5, f32[512]{0:T(512)S(1)} %broadcast_multiply_fusion.17), kind=kOutput, calls=%fused_computation.281 | convolution fusion | flops 2417885184 | bytes 12593152 | tf_op jit(solution)/shard_map/dot_general | solution.py:17
  177.5 9.2 %fusion.110 = (f32[512]{0:T(512)S(1)}, f32[512,768]{1,0:T(8,128)S(1)}) fusion(f32[768]{0:T(1024)S(1)} %reshape.752, bf16[3072,768]{1,0:T(8,128)(2,1)} %bitcast.312, f32[512,3072]{1,0:T(8,128)S(1)} %fusion.105, f32[3072]{0:T(1024)S(1)} %reshape.751, f32[768]{0:T(1024)S(1)} %reshape.750, f32[768]{0:T(1024)S(1)} %reshape.749, f32[512]{0:T(512)S(1)} %add_rsqrt_fusion.5, ...), kind=kOutput, calls=%fused_computation.285 | convolution fusion | flops 2434399744 | bytes 14183424 | tf_op jit(solution)/shard_map/dot_general | solution.py:17
  211.0 5.2 fusion.102
  216.3 4.2 fusion.112
  245.5 4.8 fusion.98
  250.3 4.2 fusion.114
  259.3 7.1 %convert_reduce_fusion.2 = (f32[3072]{0:T(1024)}, bf16[512,3072]{1,0:T(8,128)(2,1)S(1)}) fusion(f32[512,3072]{1,0:T(8,128)S(1)} %fusion.98, f32[3072]{0:T(1024)S(1)} %copy-done.109, bf16[3072,768]{1,0:T(8,128)(2,1)S(1)} %bitcast.319, f32[512,768]{1,0:T(8,128)S(1)} %get-tuple-element.44), kind=kOutput, calls=%fused_computation.58 | convolution fusion | flops 2452485120 | bytes 15753216 | tf_op jit(solution)/shard_map/dot_general | solution.py:27
  266.5 3.6 multiply_reduce_fusion.11
  276.4 7.9 %convert_reduce_fusion.11 = (f32[12,64]{1,0:T(8,128)}, bf16[12,64,512]{2,1,0:T(8,128)(2,1)S(1)}) fusion(bf16[512,12,64]{0,2,1:T(8,128)(2,1)} %bitcast.278, f32[12,512,512]{1,2,0:T(8,128)} %copy-done.2, f32[12,512]{1,0:T(8,128)} %log_add_fusion.2), kind=kOutput, calls=%fused_computation.92 | convolution fusion | flops 413269248 | bytes 14183424 | tf_op jit(solution)/shard_map/vmap(hqk,qhd->khd)/dot_general | solution.py:101
  284.3 9.2 %multiply_reduce_fusion.2 = (f32[12,512]{1,0:T(8,128)S(1)}, f32[12,512,512]{1,2,0:T(8,128)}) fusion(f32[12,512,512]{1,2,0:T(8,128)} %copy-done.2, f32[12,512]{1,0:T(8,128)S(1)} %copy-done.95, bf16[512,12,64]{0,2,1:T(8,128)(2,1)S(1)} %bitcast.279, bf16[512,12,64]{0,2,1:T(8,128)(2,1)S(1)} %bitcast.329), kind=kOutput, calls=%fused_computation.7 | convolution fusion | flops 415229952 | bytes 26787840 | tf_op jit(solution)/shard_map/vmap(qhd,khd->hqk)/dot_general | solution.py:98
  293.5 7.3 %multiply_convert_fusion.2 = bf16[12,512,512]{1,2,0:T(8,128)(2,1)S(1)} fusion(f32[12,512,512]{1,2,0:T(8,128)} %get-tuple-element.102, f32[12,512,512]{1,2,0:T(8,128)S(1)} %bitcast.262, f32[12,512]{1,0:T(8,128)S(1)} %get-tuple-element.101, f32[12,512]{1,0:T(8,128)S(1)} %copy-done.95), kind=kLoop, calls=%fused_computation.6 | loop fusion | flops 15728640 | bytes 31506432 | tf_op jit(solution)/shard_map/vmap()/convert_element_type | solution.py:104
  311.3 7.1 %convert_reduce_fusion.1 = (f32[3072]{0:T(1024)}, bf16[512,3072]{1,0:T(8,128)(2,1)S(1)}) fusion(f32[512,3072]{1,0:T(8,128)S(1)} %bitcast.370, f32[3072]{0:T(1024)S(1)} %copy-done.110, bf16[3072,768]{1,0:T(8,128)(2,1)S(1)} %bitcast.322, f32[512,768]{1,0:T(8,128)S(1)} %get-tuple-element.42), kind=kOutput, calls=%fused_computation.57 | convolution fusion | flops 2452485120 | bytes 15753216 | tf_op jit(solution)/shard_map/dot_general | solution.py:27
  318.5 3.6 multiply_reduce_fusion.10
  326.6 7.1 %convert_reduce_fusion.10 = (f32[12,64]{1,0:T(8,128)S(1)}, bf16[12,64,512]{2,1,0:T(8,128)(2,1)S(1)}) fusion(bf16[512,12,64]{0,2,1:T(8,128)(2,1)S(1)} %bitcast.280, f32[12,512,512]{1,2,0:T(8,128)} %copy-done.1, f32[12,512]{1,0:T(8,128)} %log_add_fusion.1), kind=kOutput, calls=%fused_computation.91 | convolution fusion | flops 413269248 | bytes 14183424 | tf_op jit(solution)/shard_map/vmap(hqk,qhd->khd)/dot_general | solution.py:101
  333.8 9.3 %multiply_reduce_fusion.1 = (f32[12,512]{1,0:T(8,128)S(1)}, f32[12,512,512]{1,2,0:T(8,128)}) fusion(f32[12,512,512]{1,2,0:T(8,128)} %copy-done.1, f32[12,512]{1,0:T(8,128)S(1)} %copy-done.96, bf16[512,12,64]{0,2,1:T(8,128)(2,1)S(1)} %bitcast.281, bf16[512,12,64]{0,2,1:T(8,128)(2,1)S(1)} %bitcast.327), kind=kOutput, calls=%fused_computation.4 | convolution fusion | flops 415229952 | bytes 26787840 | tf_op jit(solution)/shard_map/vmap(qhd,khd->hqk)/dot_general | solution.py:98
  343.1 7.3 %multiply_convert_fusion.1 = bf16[12,512,512]{1,2,0:T(8,128)(2,1)S(1)} fusion(f32[12,512,512]{1,2,0:T(8,128)} %get-tuple-element.106, f32[12,512,512]{1,2,0:T(8,128)S(1)} %bitcast.260, f32[12,512]{1,0:T(8,128)S(1)} %get-tuple-element.105, f32[12,512]{1,0:T(8,128)S(1)} %copy-done.96), kind=kLoop, calls=%fused_computation.3 | loop fusion | flops 15728640 | bytes 31506432 | tf_op jit(solution)/shard_map/vmap()/convert_element_type | solution.py:104
  361.4 7.1 %convert_reduce_fusion = (f32[3072]{0:T(1024)}, bf16[512,3072]{1,0:T(8,128)(2,1)S(1)}) fusion(f32[512,3072]{1,0:T(8,128)S(1)} %bitcast.301, f32[3072]{0:T(1024)S(1)} %copy-done.111, bf16[3072,768]{1,0:T(8,128)(2,1)S(1)} %bitcast.325, f32[512,768]{1,0:T(8,128)S(1)} %get-tuple-element.46), kind=kOutput, calls=%fused_computation.56 | convolution fusion | flops 2452485120 | bytes 15753216 | tf_op jit(solution)/shard_map/dot_general | solution.py:27
  368.6 3.6 multiply_reduce_fusion.9
  377.7 11.0 %multiply_reduce_fusion = (f32[12,512]{1,0:T(8,128)S(1)}, f32[12,512,512]{1,2,0:T(8,128)}) fusion(f32[12,512,512]{1,2,0:T(8,128)} %copy-done, f32[12,512]{1,0:T(8,128)} %log_add_fusion, bf16[512,12,64]{0,2,1:T(8,128)(2,1)S(1)} %bitcast.276, bf16[512,12,64]{0,2,1:T(8,128)(2,1)} %bitcast.357), kind=kOutput, calls=%fused_computation.1 | convolution fusion | flops 415229952 | bytes 26787840 | tf_op jit(solution)/shard_map/vmap(qhd,khd->hqk)/dot_general | solution.py:98
  390.5 6.9 %multiply_convert_fusion = bf16[12,512,512]{1,2,0:T(8,128)(2,1)S(1)} fusion(f32[12,512,512]{1,2,0:T(8,128)} %get-tuple-element.110, f32[12,512,512]{1,2,0:T(8,128)S(1)} %bitcast.258, f32[12,512]{1,0:T(8,128)S(1)} %get-tuple-element.109, f32[12,512]{1,0:T(8,128)S(1)} %copy-done.94), kind=kLoop, calls=%fused_computation | loop fusion | flops 15728640 | bytes 31506432 | tf_op jit(solution)/shard_map/vmap()/convert_element_type | solution.py:104
  418.8 5.6 fusion.100
  424.4 10.3 %fusion.84 = f32[3072,768]{1,0:T(8,128)} fusion(f32[512,768]{1,0:T(8,128)S(1)} %copy-done.66, f32[512,3072]{1,0:T(8,128)} %copy-done.179, f32[3072]{0:T(1024)S(1)} %copy-done.112), kind=kOutput, calls=%fused_computation.267 | convolution fusion | flops 2432040960 | bytes 17313792 | tf_op jit(solution)/shard_map/dot_general | solution.py:21
  434.7 6.6 fusion.75
  449.7 10.3 %add_convert_fusion.1 = bf16[768,3072]{1,0:T(8,128)(2,1)} fusion(f32[768,3072]{1,0:T(8,128)S(1)} %fusion.96, f32[768,3072]{1,0:T(8,128)} %fusion.100, bf16[512,3072]{1,0:T(8,128)(2,1)} %copy-done.56, f32[512,768]{1,0:T(8,128)S(1)} %copy-done.6, f32[768]{0:T(1024)S(1)} %copy-done.139, f32[768]{0:T(1024)S(1)} %reshape.749, f32[512]{0:T(512)S(1)} %copy-done.130, ...), kind=kOutput, calls=%fused_computation.22 | convolution fusion | flops 2424963072 | bytes 28321792 | tf_op jit(solution)/shard_map/dot_general | solution.py:21
  460.3 8.7 %reshape_reshape.6 = bf16[32,96,768]{2,1,0:T(8,128)(2,1)} reshape(bf16[768,3072]{1,0:T(8,128)(2,1)} %add_convert_fusion.1) | data formatting | bytes 9437184 | tf_op jit(solution)/shard_map/reshape;reshape | solution.py:396
  484.0 12.3 %add_convert_fusion = bf16[3072,768]{1,0:T(8,128)(2,1)S(1)} fusion(f32[3072,768]{1,0:T(8,128)} %fusion.84, f32[3072,768]{1,0:T(8,128)} %fusion.75, f32[512,768]{1,0:T(8,128)S(1)} %copy-done.44, f32[512,3072]{1,0:T(8,128)} %copy-done.50, f32[3072]{0:T(1024)S(1)} %copy-done.113), kind=kOutput, calls=%fused_computation.21 | convolution fusion | flops 2439118848 | bytes 31469568 | tf_op jit(solution)/shard_map/dot_general | solution.py:21
  505.9 158.0 %reduce-scatter.2.cloned.1.call-done = bf16[1,289,768]{2,1,0:T(8,128)(2,1)} async-done(((bf16[32,289,768]{2,1,0:T(8,128)(2,1)}), bf16[1,289,768]{2,1,0:T(8,128)(2,1)}) %reduce-scatter.2.cloned.1.call-update) | async-done | bytes 443920 | tf_op jit(solution)/shard_map/reduce_scatter | solution.py:428
  (606 shorter events, 173.0 us)
Async XLA Ops:
  7.2 12.1 %copy-start.177 = (s32[1,512]{1,0:T(1,128)S(1)}, s32[1,512]{1,0:T(1,128)}, u32[]{:S(2)}) copy-start(s32[1,512]{1,0:T(1,128)} %param.20) | copy-start | bytes 6148
  7.2 119.1 %all-gather.4.cloned.1.call-start = ((), (), s32[]{:S(2)}) async-start(), calls=%async_computation.2 | async-start | bytes 15003648 | tf_op jit(solution)/shard_map/all_gather | solution.py:338
  19.2 644.7 %reduce-scatter.2.cloned.1.call-start = ((), (), s32[]{:S(2)}) async-start(), calls=%async_computation.1 | async-start | bytes 15003648 | tf_op jit(solution)/shard_map/reduce_scatter | solution.py:428
  127.6 49.8 %copy-start.164 = (f32[768]{0:T(1024)}, f32[768]{0:T(1024)S(1)}, u32[]{:S(2)}) copy-start(f32[768]{0:T(1024)S(1)} %reshape.752) | copy-start | bytes 9220
  144.2 16.5 %copy-start.169 = (f32[768]{0:T(1024)}, f32[768]{0:T(1024)S(1)}, u32[]{:S(2)}) copy-start(f32[768]{0:T(1024)S(1)} %reshape.748) | copy-start | bytes 9220
  144.3 43.0 %copy-start.172 = (f32[768]{0:T(1024)}, f32[768]{0:T(1024)S(1)}, u32[]{:S(2)}) copy-start(f32[768]{0:T(1024)S(1)} %reshape.746) | copy-start | bytes 9220
  144.5 32.9 %copy-start.136 = (f32[768]{0:T(1024)}, f32[768]{0:T(1024)S(1)}, u32[]{:S(2)}) copy-start(f32[768]{0:T(1024)S(1)} %reshape.750) | copy-start | bytes 9220
  161.7 15.8 %copy-start.5 = (f32[512,768]{1,0:T(8,128)}, f32[512,768]{1,0:T(8,128)S(1)}, u32[]{:S(2)}) copy-start(f32[512,768]{1,0:T(8,128)S(1)} %get-tuple-element.85) | copy-start | bytes 4718596
  161.7 15.8 %copy-start.114 = (f32[512]{0:T(512)}, f32[512]{0:T(512)S(1)}, u32[]{:S(2)}) copy-start(f32[512]{0:T(512)S(1)} %broadcast_multiply_fusion.17) | copy-start | bytes 6148
  162.0 15.5 %copy-start.128 = (f32[512]{0:T(512)}, f32[512]{0:T(512)S(1)}, u32[]{:S(2)}) copy-start(f32[512]{0:T(512)S(1)} %add_rsqrt_fusion.5) | copy-start | bytes 6148
  162.1 15.4 %copy-start.107 = (f32[3072]{0:T(1024)}, f32[3072]{0:T(1024)S(1)}, u32[]{:S(2)}) copy-start(f32[3072]{0:T(1024)S(1)} %reshape.751) | copy-start | bytes 36868
  186.7 21.4 %copy-start.3 = (f32[512,768]{1,0:T(8,128)}, f32[512,768]{1,0:T(8,128)S(1)}, u32[]{:S(2)}) copy-start(f32[512,768]{1,0:T(8,128)S(1)} %get-tuple-element.87) | copy-start | bytes 4718596
  186.7 21.4 %copy-start.105 = (f32[512]{0:T(512)}, f32[512]{0:T(512)S(1)}, u32[]{:S(2)}) copy-start(f32[512]{0:T(512)S(1)} %broadcast_multiply_fusion.16) | copy-start | bytes 6148
  243.8 26.3 %copy-start.48 = (f32[512,768]{1,0:T(8,128)}, f32[512,768]{1,0:T(8,128)S(1)}, u32[]{:S(2)}) copy-start(f32[512,768]{1,0:T(8,128)S(1)} %get-tuple-element.97) | copy-start | bytes 4718596
  243.8 26.3 %copy-start.134 = (f32[512]{0:T(512)}, f32[512]{0:T(512)S(1)}, u32[]{:S(2)}) copy-start(f32[512]{0:T(512)S(1)} %broadcast_multiply_fusion.13) | copy-start | bytes 6148
  245.5 24.7 %copy-start.158 = (f32[512]{0:T(512)}, f32[512]{0:T(512)S(1)}, u32[]{:S(2)}) copy-start(f32[512]{0:T(512)S(1)} %add_rsqrt_fusion.1) | copy-start | bytes 6148
  255.6 10.8 %slice-start.13 = ((s8[4718592]{0:T(1024)(128)(4,1)}), s8[4194304]{0:T(1024)(128)(4,1)S(1)}, s32[]{:S(2)}) async-start(s8[4718592]{0:T(1024)(128)(4,1)} %bitcast.305), calls=%async_computation.16 | async-start | bytes 8388608
  276.4 17.1 %slice-start.6 = ((s8[12582912]{0:T(1024)(128)(4,1)}), s8[4194304]{0:T(1024)(128)(4,1)S(1)}, s32[]{:S(2)}) async-start(s8[12582912]{0:T(1024)(128)(4,1)} %bitcast.261), calls=%async_computation.9 | async-start | bytes 8388608
  276.4 17.1 %slice-start.7 = ((s8[12582912]{0:T(1024)(128)(4,1)}), s8[4194304]{0:T(1024)(128)(4,1)S(1)}, s32[]{:S(2)}) async-start(s8[12582912]{0:T(1024)(128)(4,1)} %bitcast.261), calls=%async_computation.10 | async-start | bytes 8388608
  284.3 23.2 %copy-start.29 = (bf16[12,64,512]{2,1,0:T(8,128)(2,1)}, bf16[12,64,512]{2,1,0:T(8,128)(2,1)S(1)}, u32[]{:S(2)}) copy-start(bf16[12,64,512]{2,1,0:T(8,128)(2,1)S(1)} %get-tuple-element.120) | copy-start | bytes 2359300
  323.2 34.2 %copy-start.12 = (f32[512,768]{1,0:T(8,128)}, f32[512,768]{1,0:T(8,128)S(1)}, u32[]{:S(2)}) copy-start(f32[512,768]{1,0:T(8,128)S(1)} %get-tuple-element.48) | copy-start | bytes 4718596
  326.6 16.5 %slice-start.3 = ((s8[12582912]{0:T(1024)(128)(4,1)}), s8[4194304]{0:T(1024)(128)(4,1)S(1)}, s32[]{:S(2)}) async-start(s8[12582912]{0:T(1024)(128)(4,1)} %bitcast.259), calls=%async_computation.6 | async-start | bytes 8388608
  326.6 16.5 %slice-start.4 = ((s8[12582912]{0:T(1024)(128)(4,1)}), s8[4194304]{0:T(1024)(128)(4,1)S(1)}, s32[]{:S(2)}) async-start(s8[12582912]{0:T(1024)(128)(4,1)} %bitcast.259), calls=%async_computation.7 | async-start | bytes 8388608
  333.7 23.7 %copy-start.25 = (bf16[12,64,512]{2,1,0:T(8,128)(2,1)}, bf16[12,64,512]{2,1,0:T(8,128)(2,1)S(1)}, u32[]{:S(2)}) copy-start(bf16[12,64,512]{2,1,0:T(8,128)(2,1)S(1)} %get-tuple-element.122) | copy-start | bytes 2359300
  358.0 10.5 %slice-start.17 = ((s8[4718592]{0:T(1024)(128)(4,1)}), s8[4194304]{0:T(1024)(128)(4,1)S(1)}, s32[]{:S(2)}) async-start(s8[4718592]{0:T(1024)(128)(4,1)} %bitcast.309), calls=%async_computation.20 | async-start | bytes 8388608
  377.6 11.0 %slice-start = ((s8[12582912]{0:T(1024)(128)(4,1)}), s8[4194304]{0:T(1024)(128)(4,1)S(1)}, s32[]{:S(2)}) async-start(s8[12582912]{0:T(1024)(128)(4,1)} %bitcast.257), calls=%async_computation.3 | async-start | bytes 8388608
  377.6 11.0 %slice-start.1 = ((s8[12582912]{0:T(1024)(128)(4,1)}), s8[4194304]{0:T(1024)(128)(4,1)S(1)}, s32[]{:S(2)}) async-start(s8[12582912]{0:T(1024)(128)(4,1)} %bitcast.257), calls=%async_computation.4 | async-start | bytes 8388608
  377.6 12.9 %slice-start.2 = ((s8[12582912]{0:T(1024)(128)(4,1)}), s8[4194304]{0:T(1024)(128)(4,1)S(1)}, s32[]{:S(2)}) async-start(s8[12582912]{0:T(1024)(128)(4,1)} %bitcast.257), calls=%async_computation.5 | async-start | bytes 8388608
  377.6 12.8 %copy-start.94 = (f32[12,512]{1,0:T(8,128)S(1)}, f32[12,512]{1,0:T(8,128)}, u32[]{:S(2)}) copy-start(f32[12,512]{1,0:T(8,128)} %log_add_fusion) | copy-start | bytes 73732
  402.1 39.2 %copy-start.39 = (bf16[12,64,512]{2,1,0:T(8,128)(2,1)}, bf16[12,64,512]{2,1,0:T(8,128)(2,1)S(1)}, u32[]{:S(2)}) copy-start(bf16[12,64,512]{2,1,0:T(8,128)(2,1)S(1)} %get-tuple-element.112) | copy-start | bytes 2359300
  405.3 42.0 %copy-start.27 = (bf16[12,64,512]{2,1,0:T(8,128)(2,1)}, bf16[12,64,512]{2,1,0:T(8,128)(2,1)S(1)}, u32[]{:S(2)}) copy-start(bf16[12,64,512]{2,1,0:T(8,128)(2,1)S(1)} %get-tuple-element.118) | copy-start | bytes 2359300
  418.8 15.9 %slice-start.29 = ((s8[6291456]{0:T(1024)(128)(4,1)}), s8[4194304]{0:T(1024)(128)(4,1)S(1)}, s32[]{:S(2)}) async-start(s8[6291456]{0:T(1024)(128)(4,1)} %bitcast.371), calls=%async_computation.32 | async-start | bytes 8388608
  (185 other events, 871.1 us)
Sparse Core Ops, SparseCore 0:
  19.3 106.9 all-gather.3
  499.7 164.1 reduce-scatter.1

commit v3 on v2

--- a/solution.py
+++ b/solution.py
@@ -4,6 +4,9 @@
 import jax.numpy as jnp
 from jax import lax
 from jax.sharding import PartitionSpec as P
+
+from jax.experimental import pallas as pl
+from jax.experimental.pallas import tpu as pltpu
 
 HEADS = 12
 SEQ = 512
@@ -65,59 +68,130 @@
     return blocks.reshape(-1, blocks.shape[-1])
 
 
-def attend_forward(triple):
-    query_rows, key_rows, value_rows = triple
-    query_heads = by_heads(query_rows)
-    key_heads = by_heads(key_rows)
-    value_heads = by_heads(value_rows)
-    scale = query_heads.shape[-1] ** (-0.5)
-    scores = (
-        jnp.einsum("qhd,khd->hqk", query_heads, key_heads, preferred_element_type=jnp.float32)
-        * scale
-    )
-    top_score = jnp.max(scores, axis=-1, keepdims=True)
-    weights = jnp.exp(scores - top_score)
-    totals = jnp.sum(weights, axis=-1, keepdims=True)
-    probs = (weights / totals).astype(jnp.bfloat16)
-    context = jnp.einsum("hqk,khd->qhd", probs, value_heads, preferred_element_type=jnp.float32)
-    return (context.reshape(query_rows.shape), (top_score + jnp.log(totals))[..., 0])
-
-
-def attend_backward(packed):
-    query_rows, key_rows, value_rows, log_total, context_grad = packed
-    query_heads = by_heads(query_rows)
-    key_heads = by_heads(key_rows)
-    value_heads = by_heads(value_rows)
-    grad_heads = by_heads(context_grad)
-    scale = query_heads.shape[-1] ** (-0.5)
-    scores = (
-        jnp.einsum("qhd,khd->hqk", query_heads, key_heads, preferred_element_type=jnp.float32)
-        * scale
-    )
-    probs = jnp.exp(scores - log_total[..., None])
-    prob_grad = jnp.einsum(
-        "qhd,khd->hqk", grad_heads, value_heads, preferred_element_type=jnp.float32
-    )
-    value_grad = jnp.einsum(
-        "hqk,qhd->khd", probs.astype(jnp.bfloat16), grad_heads, preferred_element_type=jnp.float32
-    )
-    score_grad = (probs * (prob_grad - jnp.sum(probs * prob_grad, axis=-1, keepdims=True))).astype(
-        jnp.bfloat16
-    )
-    query_grad = (
-        jnp.einsum("hqk,khd->qhd", score_grad, key_heads, preferred_element_type=jnp.float32)
-        * scale
-    )
-    key_grad = (
-        jnp.einsum("hqk,qhd->khd", score_grad, query_heads, preferred_element_type=jnp.float32)
-        * scale
-    )
-    row_shape = query_rows.shape
-    return (
-        query_grad.reshape(row_shape).astype(jnp.bfloat16),
-        key_grad.reshape(row_shape).astype(jnp.bfloat16),
-        value_grad.reshape(row_shape).astype(jnp.bfloat16),
-    )
+HEAD = 64
+PAIR = 128
+NT = (((1,), (1,)), ((), ()))
+TN = (((0,), (0,)), ((), ()))
+
+
+def _head_masks(shape):
+    lane = lax.broadcasted_iota(jnp.int32, shape, 1)
+    first = lane < HEAD
+    return first, jnp.logical_not(first)
+
+
+def attention_forward_kernel(q_ref, k_ref, v_ref, ctx_ref, lt_ref):
+    scale = HEAD ** (-0.5)
+    q = q_ref[...]
+    k = k_ref[...]
+    v = v_ref[...]
+    masks = _head_masks(q.shape)
+    zero = jnp.zeros_like(q)
+    context = None
+    total = None
+    for mask in masks:
+        scores = lax.dot_general(
+            jnp.where(mask, q, zero), k, NT, preferred_element_type=jnp.float32
+        ) * scale
+        top = jnp.max(scores, axis=-1, keepdims=True)
+        weights = jnp.exp(scores - top)
+        sums = jnp.sum(weights, axis=-1, keepdims=True)
+        probs = (weights / sums).astype(jnp.bfloat16)
+        part = jnp.dot(probs, v, preferred_element_type=jnp.float32)
+        log_total = jnp.broadcast_to(top + jnp.log(sums), part.shape)
+        context = part if context is None else jnp.where(mask, part, context)
+        total = log_total if total is None else jnp.where(mask, log_total, total)
+    ctx_ref[...] = context.astype(ctx_ref.dtype)
+    lt_ref[...] = total
+
+
+def attention_backward_kernel(q_ref, k_ref, v_ref, lt_ref, g_ref, dq_ref, dk_ref, dv_ref):
+    scale = HEAD ** (-0.5)
+    q = q_ref[...]
+    k = k_ref[...]
+    v = v_ref[...]
+    g = g_ref[...]
+    lt_all = lt_ref[...]
+    masks = _head_masks(q.shape)
+    zero = jnp.zeros_like(q)
+    dq = dk = dv = None
+    for mask in masks:
+        scores = lax.dot_general(
+            jnp.where(mask, q, zero), k, NT, preferred_element_type=jnp.float32
+        ) * scale
+        lt = jnp.max(jnp.where(mask, lt_all, -jnp.inf), axis=-1, keepdims=True)
+        probs = jnp.exp(scores - lt)
+        prob_grad = lax.dot_general(
+            jnp.where(mask, g, zero), v, NT, preferred_element_type=jnp.float32
+        )
+        value_part = lax.dot_general(
+            probs.astype(jnp.bfloat16), g, TN, preferred_element_type=jnp.float32
+        )
+        score_grad = (
+            probs * (prob_grad - jnp.sum(probs * prob_grad, axis=-1, keepdims=True))
+        ).astype(jnp.bfloat16)
+        query_part = jnp.dot(score_grad, k, preferred_element_type=jnp.float32) * scale
+        key_part = lax.dot_general(score_grad, q, TN, preferred_element_type=jnp.float32) * scale
+        if dq is None:
+            dq, dk, dv = query_part, key_part, value_part
+        else:
+            dq = jnp.where(mask, query_part, dq)
+            dk = jnp.where(mask, key_part, dk)
+            dv = jnp.where(mask, value_part, dv)
+    dq_ref[...] = dq.astype(dq_ref.dtype)
+    dk_ref[...] = dk.astype(dk_ref.dtype)
+    dv_ref[...] = dv.astype(dv_ref.dtype)
+
+
+def _grid(rows):
+    tokens, width = rows.shape
+    return (tokens // SEQ, width // PAIR)
+
+
+def _spec():
+    return pl.BlockSpec((SEQ, PAIR), lambda s, h: (s, h))
+
+
+def attention_forward(query_rows, key_rows, value_rows):
+    tokens, width = query_rows.shape
+    grid = _grid(query_rows)
+    steps = grid[0] * grid[1]
+    flops = steps * 2 * (2 * 2 * SEQ * SEQ * PAIR)
+    return pl.pallas_call(
+        attention_forward_kernel,
+        grid=grid,
+        in_specs=[_spec(), _spec(), _spec()],
+        out_specs=[_spec(), _spec()],
+        out_shape=[
+            jax.ShapeDtypeStruct((tokens, width), jnp.bfloat16),
+            jax.ShapeDtypeStruct((tokens, width), jnp.float32),
+        ],
+        compiler_params=pltpu.CompilerParams(dimension_semantics=("parallel", "parallel")),
+        cost_estimate=pl.CostEstimate(
+            flops=flops, transcendentals=steps * 2 * SEQ * SEQ, bytes_accessed=tokens * width * 12
+        ),
+        name="attention_forward",
+    )(query_rows, key_rows, value_rows)
+
+
+def attention_backward(query_rows, key_rows, value_rows, log_total, context_grad):
+    tokens, width = query_rows.shape
+    grid = _grid(query_rows)
+    steps = grid[0] * grid[1]
+    flops = steps * 2 * (5 * 2 * SEQ * SEQ * PAIR)
+    shape = jax.ShapeDtypeStruct((tokens, width), jnp.bfloat16)
+    return pl.pallas_call(
+        attention_backward_kernel,
+        grid=grid,
+        in_specs=[_spec()] * 5,
+        out_specs=[_spec()] * 3,
+        out_shape=[shape, shape, shape],
+        compiler_params=pltpu.CompilerParams(dimension_semantics=("parallel", "parallel")),
+        cost_estimate=pl.CostEstimate(
+            flops=flops, transcendentals=steps * 2 * SEQ * SEQ, bytes_accessed=tokens * width * 18
+        ),
+        name="attention_backward",
+    )(query_rows, key_rows, value_rows, log_total, context_grad)
 
 
 def layer_forward(weights, hidden_state):
@@ -146,10 +220,7 @@
     value_rows = (product(rows_low, value_weight) + value_bias.astype(jnp.float32)).astype(
         jnp.bfloat16
     )
-    context, log_total = jax.vmap(attend_forward)(
-        (by_sequence(query_rows), by_sequence(key_rows), by_sequence(value_rows))
-    )
-    context_low = flatten_rows(context).astype(jnp.bfloat16)
+    context_low, log_total = attention_forward(query_rows, key_rows, value_rows)
     attended = product(context_low, output_weight) + output_bias.astype(jnp.float32)
     first_out, first_normed, first_inverse = layer_norm(
         hidden_state + attended, first_gain, first_shift
@@ -231,18 +302,9 @@
     output_bias_grad = column_sums(attended_low)
     output_weight_grad = product_tn(context_low, attended_low)
     context_grad = product_nt(attended_low, output_weight).astype(jnp.bfloat16)
-    query_grad, key_grad, value_grad = jax.vmap(attend_backward)(
-        (
-            by_sequence(query_rows),
-            by_sequence(key_rows),
-            by_sequence(value_rows),
-            log_total,
-            by_sequence(context_grad),
-        ),
-    )
-    query_grad = flatten_rows(query_grad)
-    key_grad = flatten_rows(key_grad)
-    value_grad = flatten_rows(value_grad)
+    query_grad, key_grad, value_grad = attention_backward(
+        query_rows, key_rows, value_rows, log_total, context_grad
+    )
     below_grad = (
         attended_grad
         + product_nt(query_grad, query_weight)

time: 686 us -> 650 us (0.948)
  Pallas kernels: 0 us -> 72.8 us
  matrix products: 252 us -> 186 us
  local copies, waits for them, and re-layouts: 98.1 us -> 79 us
  other arithmetic: 44 us -> 27.5 us
    dot_general x18 -> x0, matrix products: 76.6 us -> none  [the longest x3 29.5 us: attend_backward(): jnp.einsum('qhd,khd->hqk', grad_heads, value_heads, preferred_element_typ...]
    pallas_call x0 -> x6, Pallas kernels: none -> 72.8 us  [the longest x3 42.1 us: attention_backward(): pl.pallas_call(attention_backward_kernel, grid=grid, in_specs=[_spec()] *...]
    convert_element_type x3 -> x0, other arithmetic: 21.6 us -> none  [attend_backward(): (probs * (prob_grad - jnp.sum(probs * prob_grad, axis=-1, keepdims=True))...]
    unnamed x443 -> x279, local copies, waits for them, and re-layouts: 40.2 us -> 22.4 us
    convert_element_type x9 -> x0, local copies, waits for them, and re-layouts: 14.9 us -> none  [the longest x3 5.13 us: layer_backward(): context_grad = product_nt(attended_low, output_weight).astype(jnp.bfloat16)]
    add x9, local copies, waits for them, and re-layouts: 0.8 us -> 11.7 us  [per_device(): earlier + later]
    dot_general x18, matrix products: 49.8 us -> 59 us  [product_nt(): lax.dot_general(left, right, (((1,), (1,)), ((), ())), preferred_element_...]
    another operation x7, other arithmetic: 0.05 us -> 8.34 us
where the time goes in v3:
time: 650 us; the launch traced here: 645 us
  waiting for transfers between devices  264 us (41%)
  matrix products  186 us (29%)
  local copies, waits for them, and re-layouts  79 us (12%)
  Pallas kernels  72.8 us (11%)
  other arithmetic  27.5 us (4%)
  between operations  15.7 us (2%)
    reduce_scatter x1, waiting for transfers between devices, scatter_grads(): lax.psum_scatter(packed.astype(jnp.bfloat16), AXES, scatter_dimension=0,...  158 us
    all_gather x1, waiting for transfers between devices, gather_weights(): packed = lax.all_gather(pack_weights(weights), AXES, axis=0, tiled=False)  106 us
    dot_general x18, matrix products, product_tn(): lax.dot_general(left, right, (((0,), (0,)), ((), ())), preferred_element_...  73.8 us
    dot_general x18, matrix products, product_nt(): lax.dot_general(left, right, (((1,), (1,)), ((), ())), preferred_element_...  59 us
    dot_general x18, matrix products, product(): return jnp.dot(left, right, preferred_element_type=jnp.float32)  53.1 us
    pallas_call x3, Pallas kernels, attention_backward(): pl.pallas_call(attention_backward_kernel, grid=grid, in_specs=[_spec()] *...  42.1 us
    pallas_call x3, Pallas kernels, attention_forward(): pl.pallas_call(attention_forward_kernel, grid=grid, in_specs=[_spec(), _s...  30.8 us
    unnamed x279, local copies, waits for them, and re-layouts  22.4 us
  transfers between devices with their start and end apart: 2, of which 2 were waited for; matrix products, arithmetic and copies ran while one was open for 1% of the time, Pallas kernels for 0%

profile of v3, /device:TPU:0, one launch (start us, length us, event | category | flops | bytes accessed | tf_op | source)
XLA Modules:
  0.0 645.4 jit_solution(3993269365691479833)
XLA Ops:
  12.3 6.1 concatenate.14
  19.8 106.5 %all-gather.4.cloned.1.call-done = bf16[32,289,768]{2,1,0:T(8,128)(2,1)} async-done(((bf16[1,289,768]{2,1,0:T(8,128)(2,1)}), bf16[32,289,768]{2,1,0:T(8,128)(2,1)}) %all-gather.4.cloned.1.call-update) | async-done | bytes 14204944 | tf_op jit(solution)/shard_map/all_gather | solution.py:400
  129.1 3.7 fusion.72
  137.9 10.6 %attention_forward.3 = (bf16[512,768]{1,0:T(8,128)(2,1)}, f32[512,768]{1,0:T(8,128)}) custom-call(bf16[512,768]{1,0:T(8,128)(2,1)} %fusion.32.q_ref, bf16[512,768]{1,0:T(8,128)(2,1)} %fusion.34.k_ref, bf16[512,768]{1,0:T(8,128)(2,1)} %fusion.33.v_ref), custom_call_target="tpu_custom_call" | custom-call | flops 1610612736 | bytes 4718592 | tf_op jit(solution)/shard_map/attention_forward/pallas_call | solution.py:160
  151.7 8.0 %fusion.71 = (bf16[32,96,768]{2,1,0:T(8,128)(2,1)}, bf16[32,96,768]{2,1,0:T(8,128)(2,1)}) fusion(bf16[32,289,768]{2,1,0:T(8,128)(2,1)} %all-gather.4.cloned.1.call-done), kind=kLoop, calls=%fused_computation.228 | loop fusion | bytes 18874368 | tf_op jit(solution)/shard_map/slice | solution.py:390
  159.7 8.5 %reshape_reshape.7 = bf16[768,3072]{1,0:T(8,128)(2,1)} reshape(bf16[32,96,768]{2,1,0:T(8,128)(2,1)} %get-tuple-element.83) | data formatting | bytes 9437184 | tf_op jit(solution)/shard_map/reshape;reshape | solution.py:408
  168.4 4.8 fusion.69
  173.3 6.1 fusion.74
  185.7 10.1 %attention_forward.4 = (bf16[512,768]{1,0:T(8,128)(2,1)}, f32[512,768]{1,0:T(8,128)}) custom-call(bf16[512,768]{1,0:T(8,128)(2,1)} %add_convert_fusion.8.q_ref, bf16[512,768]{1,0:T(8,128)(2,1)} %convolution_convert_fusion.5.k_ref, bf16[512,768]{1,0:T(8,128)(2,1)} %add_convert_fusion.7.v_ref), custom_call_target="tpu_custom_call" | custom-call | flops 1610612736 | bytes 4718592 | tf_op jit(solution)/shard_map/attention_forward/pallas_call | solution.py:160
  198.7 5.7 fusion.66
  204.5 4.2 fusion.76
  214.9 10.1 %attention_forward.5 = (bf16[512,768]{1,0:T(8,128)(2,1)}, f32[512,768]{1,0:T(8,128)}) custom-call(bf16[512,768]{1,0:T(8,128)(2,1)} %add_convert_fusion.6.q_ref, bf16[512,768]{1,0:T(8,128)(2,1)} %convolution_convert_fusion.4.k_ref, bf16[512,768]{1,0:T(8,128)(2,1)} %add_convert_fusion.5.v_ref), custom_call_target="tpu_custom_call" | custom-call | flops 1610612736 | bytes 4718592 | tf_op jit(solution)/shard_map/attention_forward/pallas_call | solution.py:160
  228.8 5.0 fusion.62
  233.9 4.2 fusion.78
  242.9 7.1 %convert_reduce_fusion.2 = (f32[3072]{0:T(1024)}, bf16[512,3072]{1,0:T(8,128)(2,1)S(1)}) fusion(f32[512,3072]{1,0:T(8,128)S(1)} %fusion.62, f32[3072]{0:T(1024)S(1)} %copy-done.72, bf16[3072,768]{1,0:T(8,128)(2,1)S(1)} %bitcast.177, f32[512,768]{1,0:T(8,128)S(1)} %get-tuple-element.74), kind=kOutput, calls=%fused_computation.31 | convolution fusion | flops 2452485120 | bytes 15753216 | tf_op jit(solution)/shard_map/dot_general | solution.py:30
  250.1 3.7 multiply_reduce_fusion.5
  256.8 14.1 %attention_backward.3 = (bf16[512,768]{1,0:T(8,128)(2,1)}, bf16[512,768]{1,0:T(8,128)(2,1)}, bf16[512,768]{1,0:T(8,128)(2,1)}) custom-call(bf16[512,768]{1,0:T(8,128)(2,1)} %add_convert_fusion.6.q_ref, bf16[512,768]{1,0:T(8,128)(2,1)} %convolution_convert_fusion.4.k_ref, bf16[512,768]{1,0:T(8,128)(2,1)} %add_convert_fusion.5.v_ref, ...), custom_call_target="tpu_custom_call" | custom-call | flops 4026531840 | bytes 7077888 | tf_op jit(solution)/shard_map/attention_backward/pallas_call | solution.py:183
  279.0 10.2 %convert_reduce_fusion.1 = (f32[3072]{0:T(1024)}, bf16[512,3072]{1,0:T(8,128)(2,1)S(1)}) fusion(f32[512,3072]{1,0:T(8,128)} %copy-done.113, f32[3072]{0:T(1024)S(1)} %copy-done.73, bf16[3072,768]{1,0:T(8,128)(2,1)} %bitcast.168, f32[512,768]{1,0:T(8,128)S(1)} %get-tuple-element.72), kind=kOutput, calls=%fused_computation.30 | convolution fusion | flops 2452485120 | bytes 15753216 | tf_op jit(solution)/shard_map/dot_general | solution.py:30
  289.2 6.3 fusion.45
  295.5 6.4 fusion.54
  302.0 3.7 multiply_reduce_fusion.4
  305.7 5.7 fusion.64
  311.4 5.5 fusion.60
  326.7 13.8 %attention_backward.4 = (bf16[512,768]{1,0:T(8,128)(2,1)}, bf16[512,768]{1,0:T(8,128)(2,1)}, bf16[512,768]{1,0:T(8,128)(2,1)}) custom-call(bf16[512,768]{1,0:T(8,128)(2,1)} %add_convert_fusion.8.q_ref, bf16[512,768]{1,0:T(8,128)(2,1)} %convolution_convert_fusion.5.k_ref, bf16[512,768]{1,0:T(8,128)(2,1)} %add_convert_fusion.7.v_ref, ...), custom_call_target="tpu_custom_call" | custom-call | flops 4026531840 | bytes 7077888 | tf_op jit(solution)/shard_map/attention_backward/pallas_call | solution.py:183
  348.5 10.2 %convert_reduce_fusion = (f32[3072]{0:T(1024)}, bf16[512,3072]{1,0:T(8,128)(2,1)S(1)}) fusion(f32[512,3072]{1,0:T(8,128)} %copy-done.28, f32[3072]{0:T(1024)S(1)} %copy-done.74, bf16[3072,768]{1,0:T(8,128)(2,1)} %bitcast.169, f32[512,768]{1,0:T(8,128)S(1)} %get-tuple-element.76), kind=kOutput, calls=%fused_computation.29 | convolution fusion | flops 2452485120 | bytes 15753216 | tf_op jit(solution)/shard_map/dot_general | solution.py:30
  358.8 3.6 multiply_reduce_fusion.3
  365.4 14.2 %attention_backward.5 = (bf16[512,768]{1,0:T(8,128)(2,1)}, bf16[512,768]{1,0:T(8,128)(2,1)}, bf16[512,768]{1,0:T(8,128)(2,1)}) custom-call(bf16[512,768]{1,0:T(8,128)(2,1)} %fusion.32.q_ref, bf16[512,768]{1,0:T(8,128)(2,1)} %fusion.34.k_ref, bf16[512,768]{1,0:T(8,128)(2,1)} %fusion.33.v_ref, f32[512,768]{1,0:T(8,128)} %get-tuple-element.43.lt_ref, ...), custom_call_target="tpu_custom_call" | custom-call | flops 4026531840 | bytes 7077888 | tf_op jit(solution)/shard_map/attention_backward/pallas_call | solution.py:183
  381.4 3.4 fusion.90
  414.0 13.1 %add_convert_fusion.1 = bf16[768,3072]{1,0:T(8,128)(2,1)} fusion(f32[768,3072]{1,0:T(8,128)} %fusion.60, f32[768,3072]{1,0:T(8,128)} %fusion.64, bf16[512,3072]{1,0:T(8,128)(2,1)} %copy-done.37, f32[512,768]{1,0:T(8,128)} %copy-done.6, f32[768]{0:T(1024)} %copy-done.89, f32[768]{0:T(1024)S(1)} %reshape.371, f32[512]{0:T(512)} %copy-done.83, ...), kind=kOutput, calls=%fused_computation.1 | convolution fusion | flops 2424963072 | bytes 28321792 | tf_op jit(solution)/shard_map/dot_general | solution.py:24
  427.1 8.6 %reshape_reshape.8 = bf16[32,96,768]{2,1,0:T(8,128)(2,1)} reshape(bf16[768,3072]{1,0:T(8,128)(2,1)} %add_convert_fusion.1) | data formatting | bytes 9437184 | tf_op jit(solution)/shard_map/reshape;reshape | solution.py:458
  440.4 12.9 %add_convert_fusion = bf16[3072,768]{1,0:T(8,128)(2,1)S(1)} fusion(f32[3072,768]{1,0:T(8,128)} %fusion.54, f32[3072,768]{1,0:T(8,128)} %fusion.45, f32[512,768]{1,0:T(8,128)} %copy-done.23, f32[512,3072]{1,0:T(8,128)} %copy-done.28, f32[3072]{0:T(1024)S(1)} %copy-done.75), kind=kOutput, calls=%fused_computation | convolution fusion | flops 2439118848 | bytes 31469568 | tf_op jit(solution)/shard_map/dot_general | solution.py:24
  475.7 158.0 %reduce-scatter.2.cloned.1.call-done = bf16[1,289,768]{2,1,0:T(8,128)(2,1)} async-done(((bf16[32,289,768]{2,1,0:T(8,128)(2,1)}), bf16[1,289,768]{2,1,0:T(8,128)(2,1)}) %reduce-scatter.2.cloned.1.call-update) | async-done | bytes 443920 | tf_op jit(solution)/shard_map/reduce_scatter | solution.py:490
  (410 shorter events, 135.7 us)
Async XLA Ops:
  7.2 12.1 %copy-start.112 = (s32[1,512]{1,0:T(1,128)S(1)}, s32[1,512]{1,0:T(1,128)}, u32[]{:S(2)}) copy-start(s32[1,512]{1,0:T(1,128)} %param.20) | copy-start | bytes 6148
  7.2 119.1 %all-gather.4.cloned.1.call-start = ((), (), s32[]{:S(2)}) async-start(), calls=%async_computation.2 | async-start | bytes 15003648 | tf_op jit(solution)/shard_map/all_gather | solution.py:400
  19.2 614.5 %reduce-scatter.2.cloned.1.call-start = ((), (), s32[]{:S(2)}) async-start(), calls=%async_computation.1 | async-start | bytes 15003648 | tf_op jit(solution)/shard_map/reduce_scatter | solution.py:490
  129.0 19.4 %copy-start.102 = (f32[768]{0:T(1024)}, f32[768]{0:T(1024)S(1)}, u32[]{:S(2)}) copy-start(f32[768]{0:T(1024)S(1)} %reshape.370) | copy-start | bytes 9220
  150.8 17.6 %copy-start.6 = (f32[512,768]{1,0:T(8,128)}, f32[512,768]{1,0:T(8,128)S(1)}, u32[]{:S(2)}) copy-start(f32[512,768]{1,0:T(8,128)S(1)} %get-tuple-element.113) | copy-start | bytes 4718596
  150.9 22.4 %copy-start.76 = (f32[512]{0:T(512)}, f32[512]{0:T(512)S(1)}, u32[]{:S(2)}) copy-start(f32[512]{0:T(512)S(1)} %broadcast_multiply_fusion.17) | copy-start | bytes 6148
  151.2 22.1 %copy-start.83 = (f32[512]{0:T(512)}, f32[512]{0:T(512)S(1)}, u32[]{:S(2)}) copy-start(f32[512]{0:T(512)S(1)} %add_rsqrt_fusion.5) | copy-start | bytes 6148
  151.7 52.7 %copy-start.89 = (f32[768]{0:T(1024)}, f32[768]{0:T(1024)S(1)}, u32[]{:S(2)}) copy-start(f32[768]{0:T(1024)S(1)} %reshape.372) | copy-start | bytes 9220
  168.3 36.1 %copy-start.110 = (f32[768]{0:T(1024)}, f32[768]{0:T(1024)S(1)}, u32[]{:S(2)}) copy-start(f32[768]{0:T(1024)S(1)} %reshape.374) | copy-start | bytes 9220
  168.4 36.0 %copy-start.71 = (f32[3072]{0:T(1024)}, f32[3072]{0:T(1024)S(1)}, u32[]{:S(2)}) copy-start(f32[3072]{0:T(1024)S(1)} %reshape.373) | copy-start | bytes 36868
  179.8 16.1 %copy-start.78 = (f32[512]{0:T(512)}, f32[512]{0:T(512)S(1)}, u32[]{:S(2)}) copy-start(f32[512]{0:T(512)S(1)} %add_rsqrt_fusion.4) | copy-start | bytes 6148
  185.7 10.1 %copy-start.103 = (f32[768]{0:T(1024)S(1)}, f32[768]{0:T(1024)}, u32[]{:S(2)}) copy-start(f32[768]{0:T(1024)} %copy-done.102) | copy-start | bytes 9220
  225.0 8.8 %slice-start.10 = ((s8[4718592]{0:T(1024)(128)(4,1)}), s8[4194304]{0:T(1024)(128)(4,1)S(1)}, s32[]{:S(2)}) async-start(s8[4718592]{0:T(1024)(128)(4,1)} %bitcast.174), calls=%async_computation.13 | async-start | bytes 8388608
  228.1 25.6 %copy-start.26 = (f32[512,768]{1,0:T(8,128)}, f32[512,768]{1,0:T(8,128)S(1)}, u32[]{:S(2)}) copy-start(f32[512,768]{1,0:T(8,128)S(1)} %get-tuple-element.121) | copy-start | bytes 4718596
  228.1 25.6 %copy-start.87 = (f32[512]{0:T(512)}, f32[512]{0:T(512)S(1)}, u32[]{:S(2)}) copy-start(f32[512]{0:T(512)S(1)} %broadcast_multiply_fusion.13) | copy-start | bytes 6148
  228.8 25.0 %copy-start.100 = (f32[512]{0:T(512)}, f32[512]{0:T(512)S(1)}, u32[]{:S(2)}) copy-start(f32[512]{0:T(512)S(1)} %add_rsqrt_fusion.1) | copy-start | bytes 6148
  233.9 9.0 %copy-start.114 = (f32[512,3072]{1,0:T(8,128)}, f32[512,3072]{1,0:T(8,128)S(1)}, u32[]{:S(2)}) copy-start(f32[512,3072]{1,0:T(8,128)S(1)} %fusion.62) | copy-start | bytes 18874372
  240.7 9.3 %slice-start.2 = ((s8[4718592]{0:T(1024)(128)(4,1)}), s8[4194304]{0:T(1024)(128)(4,1)S(1)}, s32[]{:S(2)}) async-start(s8[4718592]{0:T(1024)(128)(4,1)} %bitcast.161), calls=%async_computation.5 | async-start | bytes 8388608
  277.9 11.3 %slice-start.12 = ((s8[6291456]{0:T(1024)(128)(4,1)}), s8[4194304]{0:T(1024)(128)(4,1)S(1)}, s32[]{:S(2)}) async-start(s8[6291456]{0:T(1024)(128)(4,1)} %bitcast.201), calls=%async_computation.15 | async-start | bytes 8388608
  277.9 17.5 %slice-start.14 = ((s8[6291456]{0:T(1024)(128)(4,1)}), s8[4194304]{0:T(1024)(128)(4,1)S(1)}, s32[]{:S(2)}) async-start(s8[6291456]{0:T(1024)(128)(4,1)} %bitcast.203), calls=%async_computation.17 | async-start | bytes 8388608
  279.0 10.2 %slice-start.13 = ((s8[6291456]{0:T(1024)(128)(4,1)}), s8[2097152]{0:T(1024)(128)(4,1)S(1)}, s32[]{:S(2)}) async-start(s8[6291456]{0:T(1024)(128)(4,1)} %bitcast.201), calls=%async_computation.16 | async-start | bytes 4194304
  279.0 16.4 %slice-start.15 = ((s8[6291456]{0:T(1024)(128)(4,1)}), s8[2097152]{0:T(1024)(128)(4,1)S(1)}, s32[]{:S(2)}) async-start(s8[6291456]{0:T(1024)(128)(4,1)} %bitcast.203), calls=%async_computation.18 | async-start | bytes 4194304
  289.2 12.7 %slice-start.4 = ((s8[4718592]{0:T(1024)(128)(4,1)}), s8[4194304]{0:T(1024)(128)(4,1)S(1)}, s32[]{:S(2)}) async-start(s8[4718592]{0:T(1024)(128)(4,1)} %bitcast.163), calls=%async_computation.7 | async-start | bytes 8388608
  345.4 13.3 %slice-start.6 = ((s8[4718592]{0:T(1024)(128)(4,1)}), s8[4194304]{0:T(1024)(128)(4,1)S(1)}, s32[]{:S(2)}) async-start(s8[4718592]{0:T(1024)(128)(4,1)} %bitcast.165), calls=%async_computation.9 | async-start | bytes 8388608
  348.5 10.2 %copy-start.23 = (f32[512,768]{1,0:T(8,128)}, f32[512,768]{1,0:T(8,128)S(1)}, u32[]{:S(2)}) copy-start(f32[512,768]{1,0:T(8,128)S(1)} %get-tuple-element.76) | copy-start | bytes 4718596
  348.5 10.2 %copy-start.7 = (f32[512,768]{1,0:T(8,128)S(1)}, f32[512,768]{1,0:T(8,128)}, u32[]{:S(2)}) copy-start(f32[512,768]{1,0:T(8,128)} %copy-done.6) | copy-start | bytes 4718596
  348.5 10.2 %slice-start.7 = ((s8[4718592]{0:T(1024)(128)(4,1)}), s8[524288]{0:T(1024)(128)(4,1)S(1)}, s32[]{:S(2)}) async-start(s8[4718592]{0:T(1024)(128)(4,1)} %bitcast.165), calls=%async_computation.10 | async-start | bytes 1048576
  348.5 10.3 %copy-start.77 = (f32[512]{0:T(512)S(1)}, f32[512]{0:T(512)}, u32[]{:S(2)}) copy-start(f32[512]{0:T(512)} %copy-done.76) | copy-start | bytes 6148
  348.5 10.3 %copy-start.84 = (f32[512]{0:T(512)S(1)}, f32[512]{0:T(512)}, u32[]{:S(2)}) copy-start(f32[512]{0:T(512)} %copy-done.83) | copy-start | bytes 6148
  365.4 16.0 %copy-start.21 = (bf16[512,768]{1,0:T(8,128)(2,1)S(1)}, bf16[512,768]{1,0:T(8,128)(2,1)}, u32[]{:S(2)}) copy-start(bf16[512,768]{1,0:T(8,128)(2,1)} %param.18) | copy-start | bytes 2359300
  440.4 12.9 %copy-start.9 = (f32[512,768]{1,0:T(8,128)S(1)}, f32[512,768]{1,0:T(8,128)}, u32[]{:S(2)}) copy-start(f32[512,768]{1,0:T(8,128)} %copy-done.8) | copy-start | bytes 4718596
  440.4 12.9 %copy-start.60 = (bf16[512,768]{1,0:T(8,128)(2,1)S(1)}, bf16[512,768]{1,0:T(8,128)(2,1)}, u32[]{:S(2)}) copy-start(bf16[512,768]{1,0:T(8,128)(2,1)} %get-tuple-element.32) | copy-start | bytes 2359300
  (103 other events, 307.3 us)
Sparse Core Ops, SparseCore 0:
  19.3 106.9 all-gather.3
  469.5 164.1 reduce-scatter.1

commit v4 on v3

v4 whole, which is shorter than its diff:
```python
import functools

import jax
import jax.numpy as jnp
from jax import lax
from jax.experimental import pallas as pl
from jax.experimental.pallas import tpu as pltpu
from jax.sharding import PartitionSpec as P

SEQ = 512
HEAD = 64
PAIR = 128
LAYERS = 3
AXES = ("dp", "fsdp")
NT = (((1,), (1,)), ((), ()))
TN = (((0,), (0,)), ((), ()))
norm_epsilon = 1e-05


def product(left, right):
    return jnp.dot(left, right, preferred_element_type=jnp.float32)


def product_nt(left, right):
    return lax.dot_general(left, right, NT, preferred_element_type=jnp.float32)


def gelu_tanh(values):
    return jax.nn.gelu(values, approximate=True)


def layer_norm(summed, gain, shift):
    centre = summed - jnp.mean(summed, axis=-1, keepdims=True)
    inverse = lax.rsqrt(jnp.mean(centre * centre, axis=-1, keepdims=True) + norm_epsilon)
    normed = centre * inverse
    return (normed * gain + shift, normed, inverse)


def norm_backward(upstream, normed, inverse, gain):
    scaled = upstream * gain
    return inverse * (
        scaled
        - jnp.mean(scaled, axis=-1, keepdims=True)
        - normed * jnp.mean(scaled * normed, axis=-1, keepdims=True)
    )


def _head_masks(shape):
    lane = lax.broadcasted_iota(jnp.int32, shape, 1)
    first = lane < HEAD
    return first, jnp.logical_not(first)


def attention_forward_kernel(qkv_ref, ctx_ref, lt_ref):
    scale = HEAD ** (-0.5)
    q = qkv_ref[:, 0:PAIR]
    k = qkv_ref[:, PAIR : 2 * PAIR]
    v = qkv_ref[:, 2 * PAIR : 3 * PAIR]
    masks = _head_masks(q.shape)
    zero = jnp.zeros_like(q)
    context = None
    total = None
    for mask in masks:
        scores = product_nt(jnp.where(mask, q, zero), k) * scale
        top = jnp.max(scores, axis=-1, keepdims=True)
        weights = jnp.exp(scores - top)
        sums = jnp.sum(weights, axis=-1, keepdims=True)
        probs = (weights / sums).astype(jnp.bfloat16)
        part = jnp.dot(probs, v, preferred_element_type=jnp.float32)
        log_total = jnp.broadcast_to(top + jnp.log(sums), part.shape)
        context = part if context is None else jnp.where(mask, part, context)
        total = log_total if total is None else jnp.where(mask, log_total, total)
    ctx_ref[...] = context.astype(ctx_ref.dtype)
    lt_ref[...] = total


def attention_backward_kernel(qkv_ref, lt_ref, g_ref, out_ref):
    scale = HEAD ** (-0.5)
    q = qkv_ref[:, 0:PAIR]
    k = qkv_ref[:, PAIR : 2 * PAIR]
    v = qkv_ref[:, 2 * PAIR : 3 * PAIR]
    g = g_ref[...]
    lt_all = lt_ref[...]
    masks = _head_masks(q.shape)
    zero = jnp.zeros_like(q)
    dq = dk = dv = None
    for mask in masks:
        scores = product_nt(jnp.where(mask, q, zero), k) * scale
        lt = jnp.max(jnp.where(mask, lt_all, -jnp.inf), axis=-1, keepdims=True)
        probs = jnp.exp(scores - lt)
        prob_grad = product_nt(jnp.where(mask, g, zero), v)
        value_part = lax.dot_general(
            probs.astype(jnp.bfloat16), g, TN, preferred_element_type=jnp.float32
        )
        score_grad = (
            probs * (prob_grad - jnp.sum(probs * prob_grad, axis=-1, keepdims=True))
        ).astype(jnp.bfloat16)
        query_part = jnp.dot(score_grad, k, preferred_element_type=jnp.float32) * scale
        key_part = lax.dot_general(score_grad, q, TN, preferred_element_type=jnp.float32) * scale
        if dq is None:
            dq, dk, dv = query_part, key_part, value_part
        else:
            dq = jnp.where(mask, query_part, dq)
            dk = jnp.where(mask, key_part, dk)
            dv = jnp.where(mask, value_part, dv)
    out_ref[:, 0:PAIR] = dq.astype(out_ref.dtype)
    out_ref[:, PAIR : 2 * PAIR] = dk.astype(out_ref.dtype)
    out_ref[:, 2 * PAIR : 3 * PAIR] = dv.astype(out_ref.dtype)


def attention_forward(qkv):
    tokens, width = qkv.shape
    grid = (tokens // SEQ, width // (3 * PAIR))
    steps = grid[0] * grid[1]
    pair = pl.BlockSpec((SEQ, PAIR), lambda s, h: (s, h))
    return pl.pallas_call(
        attention_forward_kernel,
        grid=grid,
        in_specs=[pl.BlockSpec((SEQ, 3 * PAIR), lambda s, h: (s, h))],
        out_specs=[pair, pair],
        out_shape=[
            jax.ShapeDtypeStruct((tokens, width // 3), jnp.bfloat16),
            jax.ShapeDtypeStruct((tokens, width // 3), jnp.float32),
        ],
        compiler_params=pltpu.CompilerParams(dimension_semantics=("parallel", "parallel")),
        cost_estimate=pl.CostEstimate(
            flops=steps * 8 * SEQ * SEQ * PAIR,
            transcendentals=steps * 2 * SEQ * SEQ,
            bytes_accessed=tokens * width * 4,
        ),
        name="attention_forward",
    )(qkv)


def attention_backward(qkv, log_total, context_grad):
    tokens, width = qkv.shape
    grid = (tokens // SEQ, width // (3 * PAIR))
    steps = grid[0] * grid[1]
    pair = pl.BlockSpec((SEQ, PAIR), lambda s, h: (s, h))
    triple = pl.BlockSpec((SEQ, 3 * PAIR), lambda s, h: (s, h))
    return pl.pallas_call(
        attention_backward_kernel,
        grid=grid,
        in_specs=[triple, pair, pair],
        out_specs=triple,
        out_shape=jax.ShapeDtypeStruct((tokens, width), jnp.bfloat16),
        compiler_params=pltpu.CompilerParams(dimension_semantics=("parallel", "parallel")),
        cost_estimate=pl.CostEstimate(
            flops=steps * 20 * SEQ * SEQ * PAIR,
            transcendentals=steps * 2 * SEQ * SEQ,
            bytes_accessed=tokens * width * 6,
        ),
        name="attention_backward",
    )(qkv, log_total, context_grad)


def weight_grad_kernel(*refs):
    count = (len(refs) - 2) // 2
    xs, gs = refs[:count], refs[count : 2 * count]
    out_ref, sum_ref = refs[-2], refs[-1]
    acc = None
    sums = None
    for x_ref, g_ref in zip(xs, gs):
        g = g_ref[...]
        part = lax.dot_general(x_ref[...], g, TN, preferred_element_type=jnp.float32)
        col = jnp.sum(g.astype(jnp.float32), axis=0, keepdims=True)
        acc = part if acc is None else acc + part
        sums = col if sums is None else sums + col
    out_ref[...] = acc.astype(out_ref.dtype)
    sum_ref[...] = sums


def weight_grad(xs, gs, block=768):
    tokens, depth = xs[0].shape
    width = gs[0].shape[1]
    bk = min(block, depth)
    bn = min(block, width)
    grid = (depth // bk, width // bn)
    count = len(xs)
    in_specs = [pl.BlockSpec((tokens, bk), lambda i, j: (0, i))] * count + [
        pl.BlockSpec((tokens, bn), lambda i, j: (0, j))
    ] * count
    return pl.pallas_call(
        weight_grad_kernel,
        grid=grid,
        in_specs=in_specs,
        out_specs=[
            pl.BlockSpec((bk, bn), lambda i, j: (i, j)),
            pl.BlockSpec((1, bn), lambda i, j: (0, j)),
        ],
        out_shape=[
            jax.ShapeDtypeStruct((depth, width), jnp.bfloat16),
            jax.ShapeDtypeStruct((1, width), jnp.float32),
        ],
        compiler_params=pltpu.CompilerParams(
            dimension_semantics=("arbitrary", "arbitrary"), vmem_limit_bytes=48 * 1024 * 1024
        ),
        cost_estimate=pl.CostEstimate(
            flops=2 * count * tokens * depth * width,
            transcendentals=0,
            bytes_accessed=2 * count * tokens * (depth + width) + 2 * depth * width,
        ),
        name="weight_grad",
    )(*xs, *gs)


def interleave_qkv(q, k, v):
    pieces = []
    for h in range(q.shape[-1] // PAIR):
        cols = slice(h * PAIR, (h + 1) * PAIR)
        pieces += [q[..., cols], k[..., cols], v[..., cols]]
    return jnp.concatenate(pieces, axis=-1)


def split_qkv(packed):
    pairs = packed.shape[-1] // (3 * PAIR)
    parts = [[], [], []]
    for h in range(pairs):
        for which in range(3):
            start = (3 * h + which) * PAIR
            parts[which].append(packed[..., start : start + PAIR])
    return [jnp.concatenate(p, axis=-1) for p in parts]


def pack_weights(weights):
    (qw, qb, kw, vw, vb, ow, ob, g1, s1, iw, ib, uw, ub, g2, s2) = weights
    rows, width = qw.shape
    wide = iw.shape[1]
    vectors = jnp.concatenate([qb, vb, ob, g1, s1, ub, g2, s2, ib])
    vectors = jnp.pad(vectors, (0, wide - vectors.shape[0]))[None, :]
    return jnp.concatenate(
        [
            jnp.concatenate([interleave_qkv(qw, kw, vw), ow], axis=1),
            iw,
            uw.reshape(rows, wide),
            vectors,
        ],
        axis=0,
    )


def gather_weights(weights):
    rows, width = weights[0].shape
    ff_rows, wide = weights[11].shape[0], weights[9].shape[1]
    packed = lax.all_gather(pack_weights(weights), AXES, axis=0, tiled=False)
    shards = packed.shape[0]
    attn = packed[:, 0:rows].reshape(shards * rows, wide)
    inner = packed[:, rows : 2 * rows].reshape(shards * rows, wide)
    outer = packed[:, 2 * rows : 3 * rows].reshape(shards * ff_rows, width)
    vectors = packed[:, 3 * rows, :].astype(jnp.float32)
    found = []
    at = 0
    for count in (rows,) * 8 + (ff_rows,):
        found.append(vectors[:, at : at + count].reshape(-1))
        at += count
    (qb, vb, ob, g1, s1, ub, g2, s2, ib) = found
    return dict(
        qkv=attn[:, : 3 * width],
        qkv_bias=interleave_qkv(qb, jnp.zeros_like(qb), vb),
        out=attn[:, 3 * width :],
        out_bias=ob,
        g1=g1,
        s1=s1,
        inner=inner,
        inner_bias=ib,
        outer=outer,
        outer_bias=ub,
        g2=g2,
        s2=s2,
    )


def layer_forward(w, hidden_state):
    rows_low = hidden_state.astype(jnp.bfloat16)
    qkv = (product(rows_low, w["qkv"]) + w["qkv_bias"]).astype(jnp.bfloat16)
    context_low, log_total = attention_forward(qkv)
    attended = product(context_low, w["out"]) + w["out_bias"]
    first_out, first_normed, first_inverse = layer_norm(hidden_state + attended, w["g1"], w["s1"])
    first_low = first_out.astype(jnp.bfloat16)
    inner_pre = product(first_low, w["inner"]) + w["inner_bias"]
    inner_low = gelu_tanh(inner_pre).astype(jnp.bfloat16)
    outer_out = product(inner_low, w["outer"]) + w["outer_bias"]
    result, second_normed, second_inverse = layer_norm(first_out + outer_out, w["g2"], w["s2"])
    kept = dict(
        rows_low=rows_low,
        qkv=qkv,
        log_total=log_total,
        context_low=context_low,
        first_normed=first_normed,
        first_inverse=first_inverse,
        first_low=first_low,
        inner_pre=inner_pre,
        inner_low=inner_low,
        second_normed=second_normed,
        second_inverse=second_inverse,
    )
    return result, kept


def layer_backward(w, kept, upstream):
    second_gain_grad = jnp.sum(upstream * kept["second_normed"], axis=0)
    second_shift_grad = jnp.sum(upstream, axis=0)
    second_grad = norm_backward(upstream, kept["second_normed"], kept["second_inverse"], w["g2"])
    outer_low = second_grad.astype(jnp.bfloat16)
    active_grad = product_nt(outer_low, w["outer"])
    gelu_pull = jax.vjp(gelu_tanh, kept["inner_pre"])[1]
    inner_grad = gelu_pull(active_grad)[0].astype(jnp.bfloat16)
    first_grad = second_grad + product_nt(inner_grad, w["inner"])
    first_gain_grad = jnp.sum(first_grad * kept["first_normed"], axis=0)
    first_shift_grad = jnp.sum(first_grad, axis=0)
    attended_grad = norm_backward(first_grad, kept["first_normed"], kept["first_inverse"], w["g1"])
    attended_low = attended_grad.astype(jnp.bfloat16)
    context_grad = product_nt(attended_low, w["out"]).astype(jnp.bfloat16)
    qkv_grad = attention_backward(kept["qkv"], kept["log_total"], context_grad)
    below_grad = attended_grad + product_nt(qkv_grad, w["qkv"])
    saved = dict(
        outer_low=outer_low,
        inner_grad=inner_grad,
        attended_low=attended_low,
        qkv_grad=qkv_grad,
    )
    norms = (second_gain_grad, second_shift_grad, first_gain_grad, first_shift_grad)
    return below_grad, saved, norms


def scatter_grads(kept, saved, norms, shards):
    def across(source, name):
        return [item[name] for item in source]

    qkv_w, qkv_b = weight_grad(across(kept, "rows_low"), across(saved, "qkv_grad"))
    out_w, out_b = weight_grad(across(kept, "context_low"), across(saved, "attended_low"))
    inner_w, inner_b = weight_grad(across(kept, "first_low"), across(saved, "inner_grad"))
    outer_w, outer_b = weight_grad(across(kept, "inner_low"), across(saved, "outer_low"))
    rows, wide = inner_w.shape
    q_b, _, v_b = split_qkv(qkv_b[0])
    s2g, s2s, s1g, s1s = [sum(parts) for parts in zip(*norms)]
    columns = jnp.stack(
        [q_b, v_b, out_b[0], s1g, s1s, outer_b[0], s2g, s2s], axis=1
    )
    columns = jnp.concatenate([columns, inner_b[0].reshape(rows, -1)], axis=1)
    columns = jnp.pad(columns, ((0, 0), (0, PAIR - columns.shape[1]))).astype(jnp.bfloat16)
    packed = jnp.concatenate(
        [qkv_w, out_w, inner_w, outer_w.reshape(rows, wide), columns], axis=1
    )
    mine = lax.psum_scatter(packed, AXES, scatter_dimension=0, tiled=True).astype(jnp.float32)
    width = out_w.shape[1]
    at = 0
    pieces = []
    for count in (3 * width, width, wide, wide, PAIR):
        pieces.append(mine[:, at : at + count])
        at += count
    qkv_mine, out_mine, inner_mine, outer_mine, col_mine = pieces
    q_w, k_w, v_w = split_qkv(qkv_mine)
    c = [col_mine[:, i] for i in range(8)]
    ib_mine = col_mine[:, 8:12].reshape(-1)
    return (
        q_w,
        c[0],
        k_w,
        v_w,
        c[1],
        out_mine,
        c[2],
        c[3],
        c[4],
        inner_mine,
        ib_mine,
        outer_mine.reshape(-1, width),
        c[5],
        c[6],
        c[7],
    )


def per_device(shards, inputs, cotangent, masked, *weights):
    w = gather_weights(weights)
    hidden_state = inputs.astype(jnp.float32)
    kept = []
    for applied in range(LAYERS):
        hidden_state, kept_values = layer_forward(w, hidden_state)
        kept.append(kept_values)
    outputs = hidden_state.astype(jnp.bfloat16)
    upstream = cotangent.astype(jnp.float32) * masked.reshape(-1, 1).astype(jnp.float32)
    saved = [None] * LAYERS
    norms = [None] * LAYERS
    for applied in range(LAYERS - 1, -1, -1):
        upstream, saved[applied], norms[applied] = layer_backward(w, kept[applied], upstream)
    collected = scatter_grads(kept, saved, norms, shards)
    return (outputs, upstream.astype(jnp.bfloat16)) + tuple(collected)


def solution(mesh):
    rows = P(AXES, None)
    vec = P(AXES)
    in_specs = (rows, rows, rows, rows, vec, rows, rows, vec, rows, vec, vec, vec, rows, vec, rows, vec, vec, vec)
    out_specs = (rows, rows, rows, vec, rows, rows, vec, rows, vec, vec, vec, rows, vec, rows, vec, vec, vec)
    shards = mesh.shape["dp"] * mesh.shape["fsdp"]
    return jax.shard_map(
        functools.partial(per_device, shards),
        mesh=mesh,
        in_specs=in_specs,
        out_specs=out_specs,
        check_vma=False,
    )
```

time: 650 us -> 606 us (0.932)
  matrix products: 186 us -> 111 us
  Pallas kernels: 72.8 us -> 104 us
  other arithmetic: 27.5 us -> 17.8 us
    reduce_scatter x1 -> x0, waiting for transfers between devices: 158 us -> none  [scatter_grads(): lax.psum_scatter(packed.astype(jnp.bfloat16), AXES, scatter_dimension=0,...]
    unnamed x2 -> x3, waiting for transfers between devices: 0.03 us -> 151 us
    dot_general x36 -> x12, matrix products: 133 us -> 63.3 us  [product_nt(): return lax.dot_general(left, right, NT, preferred_element_type=jnp.float32)]
    pallas_call x6 -> x10, Pallas kernels: 72.8 us -> 104 us  [the longest x3 41.2 us: attention_backward(): pl.pallas_call(attention_backward_kernel, grid=grid, in_specs=[triple, pa...]
    reshape x2 -> x7, local copies, waits for them, and re-layouts: 1.8 us -> 19.7 us  [the longest x1 8.68 us: gather_weights(): outer = packed[:, 2 * rows:3 * rows].reshape(shards * ff_rows, width)]
    unnamed x279 -> x247, local copies, waits for them, and re-layouts: 22.4 us -> 39.6 us
    another operation x2 -> x5, local copies, waits for them, and re-layouts: 17.1 us -> 1.13 us  [the longest x4 0.7 us: scatter_grads(): jnp.stack([q_b, v_b, out_b[0], s1g, s1s, outer_b[0], s2g, s2s], axis=1)]
    reduce_sum x11 -> x1, other arithmetic: 13.4 us -> 1.45 us  [layer_backward(): second_gain_grad = jnp.sum(upstream * kept['second_normed'], axis=0)]
where the time goes in v4:
time: 606 us; the launch traced here: 596 us
  waiting for transfers between devices  264 us (44%)
  matrix products  111 us (18%)
  Pallas kernels  104 us (17%)
  local copies, waits for them, and re-layouts  83.3 us (14%)
  other arithmetic  17.8 us (3%)
  between operations  15.9 us (3%)
    unnamed x3, waiting for transfers between devices  151 us
    all_gather x1, waiting for transfers between devices, gather_weights(): packed = lax.all_gather(pack_weights(weights), AXES, axis=0, tiled=False)  112 us
    dot_general x12, matrix products, product_nt(): return lax.dot_general(left, right, NT, preferred_element_type=jnp.float32)  63.3 us
    dot_general x12, matrix products, product(): return jnp.dot(left, right, preferred_element_type=jnp.float32)  47.6 us
    pallas_call x3, Pallas kernels, attention_backward(): pl.pallas_call(attention_backward_kernel, grid=grid, in_specs=[triple, pa...  41.2 us
    unnamed x247, local copies, waits for them, and re-layouts  39.6 us
    pallas_call x4, Pallas kernels, weight_grad(): pl.pallas_call(weight_grad_kernel, grid=grid, in_specs=in_specs, out_spec...  33.1 us
    pallas_call x3, Pallas kernels, attention_forward(): pl.pallas_call(attention_forward_kernel, grid=grid, in_specs=[pl.BlockSpe...  30.1 us
  transfers between devices with their start and end apart: 2, of which 2 were waited for; matrix products, arithmetic and copies ran while one was open for 1% of the time, Pallas kernels for 0%

profile of v4, /device:TPU:0, one launch (start us, length us, event | category | flops | bytes accessed | tf_op | source)
XLA Modules:
  0.0 595.9 jit_solution(681278818746478110)
XLA Ops:
  7.2 6.1 %concatenate.37 = bf16[288]{0:T(512)(128)(2,1)S(1)} concatenate(bf16[24]{0:T(256)(128)(2,1)} %param.22, bf16[24]{0:T(256)(128)(2,1)} %param.25, bf16[24]{0:T(256)(128)(2,1)} %param.27, bf16[24]{0:T(256)(128)(2,1)} %param.28, bf16[24]{0:T(256)(128)(2,1)} %param.29, bf16[24]{0:T(256)(128)(2,1)} %param.33, bf16[24]{0:T(256)(128)(2,1)} %param.34, bf16[24]{0:T(256)(128)(2,1)} %param.35, ...), dimensions={0} | concatenate | bytes 1152 | tf_op jit(solution)/shard_map/concatenate | solution.py:229
  29.6 112.3 %all-gather.4.cloned.1.call-done = bf16[32,73,3072]{2,1,0:T(8,128)(2,1)} async-done(((bf16[1,73,3072]{2,1,0:T(8,128)(2,1)}), bf16[32,73,3072]{2,1,0:T(8,128)(2,1)}) %all-gather.4.cloned.1.call-update) | async-done | bytes 14352400 | tf_op jit(solution)/shard_map/all_gather | solution.py:245
  144.5 9.6 %fusion.62 = (bf16[32,24,3072]{2,1,0:T(8,128)(2,1)}, bf16[32,24,3072]{2,1,0:T(8,128)(2,1)}, bf16[32,24,3072]{2,1,0:T(8,128)(2,1)S(1)}) fusion(bf16[32,73,3072]{2,1,0:T(8,128)(2,1)} %all-gather.4.cloned.1.call-done), kind=kLoop, calls=%fused_computation.237 | loop fusion | bytes 28311552 | tf_op jit(solution)/shard_map/slice | solution.py:249
  156.2 3.5 fusion.24.qkv_ref
  159.7 10.0 %attention_forward.3 = (bf16[512,768]{1,0:T(8,128)(2,1)}, f32[512,768]{1,0:T(8,128)}) custom-call(bf16[512,2304]{1,0:T(8,128)(2,1)} %fusion.24.qkv_ref), custom_call_target="tpu_custom_call" | custom-call | flops 1610612736 | bytes 4718592 | tf_op jit(solution)/shard_map/attention_forward/pallas_call | solution.py:116
  172.6 8.7 %reshape.313 = bf16[3072,768]{1,0:T(8,128)(2,1)} reshape(bf16[32,24,3072]{2,1,0:T(8,128)(2,1)} %get-tuple-element.87) | data formatting | bytes 9437184 | tf_op jit(solution)/shard_map/reshape | solution.py:249
  181.8 8.7 %multiply_convert_fusion.2 = (bf16[512,3072]{1,0:T(8,128)(2,1)S(1)}, f32[512,3072]{1,0:T(8,128)}) fusion(f32[3072]{0:T(1024)S(1)} %add.356, bf16[512,768]{1,0:T(8,128)(2,1)S(1)} %fusion.43.refs_0_, bf16[768,3072]{1,0:T(8,128)(2,1)} %bitcast.92), kind=kOutput, calls=%fused_computation.29 | convolution fusion | flops 2431647744 | bytes 14954496 | tf_op jit(solution)/shard_map/dot_general | solution.py:21
  194.0 3.5 fusion.21.qkv_ref
  198.4 10.2 %attention_forward.4 = (bf16[512,768]{1,0:T(8,128)(2,1)}, f32[512,768]{1,0:T(8,128)}) custom-call(bf16[512,2304]{1,0:T(8,128)(2,1)} %fusion.21.qkv_ref), custom_call_target="tpu_custom_call" | custom-call | flops 1610612736 | bytes 4718592 | tf_op jit(solution)/shard_map/attention_forward/pallas_call | solution.py:116
  211.9 5.9 multiply_convert_fusion.1
  221.3 3.5 fusion.22.qkv_ref
  225.7 10.0 %attention_forward.5 = (bf16[512,768]{1,0:T(8,128)(2,1)}, f32[512,768]{1,0:T(8,128)}) custom-call(bf16[512,2304]{1,0:T(8,128)(2,1)} %fusion.22.qkv_ref), custom_call_target="tpu_custom_call" | custom-call | flops 1610612736 | bytes 4718592 | tf_op jit(solution)/shard_map/attention_forward/pallas_call | solution.py:116
  238.9 6.8 %multiply_convert_fusion = (bf16[512,3072]{1,0:T(8,128)(2,1)S(1)}, f32[512,3072]{1,0:T(8,128)S(1)}) fusion(f32[3072]{0:T(1024)S(1)} %add.356, bf16[512,768]{1,0:T(8,128)(2,1)S(1)} %fusion.47.refs_2_, bf16[768,3072]{1,0:T(8,128)(2,1)} %bitcast.93), kind=kOutput, calls=%fused_computation.27 | convolution fusion | flops 2431647744 | bytes 14954496 | tf_op jit(solution)/shard_map/dot_general | solution.py:21
  254.3 6.3 %fusion.20.refs_5_ = bf16[512,3072]{1,0:T(8,128)(2,1)S(1)} fusion(f32[512,3072]{1,0:T(8,128)S(1)} %get-tuple-element.147, f32[3072]{0:T(1024)S(1)} %add.356, bf16[512,768]{1,0:T(8,128)(2,1)S(1)} %get-tuple-element.90.refs_5_, bf16[3072,768]{1,0:T(8,128)(2,1)S(1)} %bitcast.111), kind=kOutput, calls=%fused_computation.26 | convolution fusion | flops 2448949248 | bytes 14954496 | tf_op jit(solution)/shard_map/dot_general | solution.py:25
  260.6 3.9 multiply_reduce_fusion.3
  269.2 13.8 %attention_backward.3.refs_5_ = bf16[512,2304]{1,0:T(8,128)(2,1)} custom-call(bf16[512,2304]{1,0:T(8,128)(2,1)} %fusion.22.qkv_ref, f32[512,768]{1,0:T(8,128)} %get-tuple-element.34.lt_ref, bf16[512,768]{1,0:T(8,128)(2,1)} %convolution_convert_fusion.2.g_ref), custom_call_target="tpu_custom_call" | custom-call | flops 4026531840 | bytes 7077888 | tf_op jit(solution)/shard_map/attention_backward/pallas_call | solution.py:141
  283.0 6.8 %multiply_reduce_fusion.1 = (f32[768]{0:T(1024)}, f32[512]{0:T(512)S(1)}, f32[512]{0:T(512)S(1)}, f32[768]{0:T(1024)}, f32[512,768]{1,0:T(8,128)S(1)}) fusion(f32[512,768]{1,0:T(8,128)} %copy-done.29, f32[512]{0:T(512)S(1)} %add_rsqrt_fusion.2, f32[512]{0:T(512)S(1)} %broadcast_multiply_fusion.14, f32[768]{0:T(1024)S(1)} %mul.415, ...), kind=kOutput, calls=%fused_computation.38 | convolution fusion | flops 1815868928 | bytes 10634240 | tf_op jit(solution)/shard_map/dot_general | solution.py:25
  291.3 8.1 %fusion.13.refs_4_ = bf16[512,3072]{1,0:T(8,128)(2,1)S(1)} fusion(f32[512,3072]{1,0:T(8,128)} %get-tuple-element.141, f32[3072]{0:T(1024)S(1)} %copy-done.53, bf16[512,768]{1,0:T(8,128)(2,1)S(1)} %get-tuple-element.83.refs_4_, bf16[3072,768]{1,0:T(8,128)(2,1)S(1)} %bitcast.113), kind=kOutput, calls=%fused_computation.19 | convolution fusion | flops 2448949248 | bytes 14954496 | tf_op jit(solution)/shard_map/dot_general | solution.py:25
  299.4 3.6 multiply_reduce_fusion.4
  308.0 13.6 %attention_backward.4.refs_4_ = bf16[512,2304]{1,0:T(8,128)(2,1)} custom-call(bf16[512,2304]{1,0:T(8,128)(2,1)} %fusion.21.qkv_ref, f32[512,768]{1,0:T(8,128)} %get-tuple-element.35.lt_ref, bf16[512,768]{1,0:T(8,128)(2,1)} %convolution_convert_fusion.1.g_ref), custom_call_target="tpu_custom_call" | custom-call | flops 4026531840 | bytes 7077888 | tf_op jit(solution)/shard_map/attention_backward/pallas_call | solution.py:141
  321.6 6.7 %multiply_reduce_fusion.2 = (f32[768]{0:T(1024)}, f32[512]{0:T(512)S(1)}, f32[512]{0:T(512)S(1)}, f32[768]{0:T(1024)}, f32[512,768]{1,0:T(8,128)S(1)}) fusion(f32[512,768]{1,0:T(8,128)} %copy-done.25, f32[512]{0:T(512)S(1)} %copy-done.46, f32[512]{0:T(512)S(1)} %copy-done.39, f32[768]{0:T(1024)S(1)} %copy-done.35, f32[512,768]{1,0:T(8,128)} %get-tuple-element.82, ...), kind=kOutput, calls=%fused_computation.39 | convolution fusion | flops 1815868928 | bytes 10634240 | tf_op jit(solution)/shard_map/dot_general | solution.py:25
  328.9 9.4 %fusion.6.refs_3_ = bf16[512,3072]{1,0:T(8,128)(2,1)S(1)} fusion(f32[512,3072]{1,0:T(8,128)} %get-tuple-element.135, f32[3072]{0:T(1024)S(1)} %copy-done.53, bf16[512,768]{1,0:T(8,128)(2,1)S(1)} %get-tuple-element.79.refs_3_, bf16[3072,768]{1,0:T(8,128)(2,1)} %reshape.313), kind=kOutput, calls=%fused_computation.12 | convolution fusion | flops 2448949248 | bytes 14954496 | tf_op jit(solution)/shard_map/dot_general | solution.py:25
  338.4 3.5 multiply_reduce_fusion.5
  349.4 11.1 %weight_grad.6 = (bf16[768,3072]{1,0:T(8,128)(2,1)}, f32[1,3072]{1,0:T(1,128)S(1)}) custom-call(bf16[512,768]{1,0:T(8,128)(2,1)S(1)} %copy-done.5, bf16[512,768]{1,0:T(8,128)(2,1)S(1)} %copy-done.9, bf16[512,768]{1,0:T(8,128)(2,1)S(1)} %copy-done.11, bf16[512,3072]{1,0:T(8,128)(2,1)S(1)} %fusion.6.refs_3_, bf16[512,3072]{1,0:T(8,128)(2,1)} %copy-done.70, ...), custom_call_target="tpu_custom_call" | custom-call | flops 7247757312 | bytes 16515072 | tf_op jit(solution)/shard_map/weight_grad/pallas_call | solution.py:183
  360.5 11.0 %weight_grad.7 = (bf16[3072,768]{1,0:T(8,128)(2,1)}, f32[1,768]{1,0:T(1,128)S(1)}) custom-call(bf16[512,3072]{1,0:T(8,128)(2,1)S(1)} %copy-done.22, bf16[512,3072]{1,0:T(8,128)(2,1)} %copy-done.72, bf16[512,3072]{1,0:T(8,128)(2,1)} %copy-done.73, bf16[512,768]{1,0:T(8,128)(2,1)S(1)} %get-tuple-element.79.refs_3_, ...), custom_call_target="tpu_custom_call" | custom-call | flops 7247757312 | bytes 16515072 | tf_op jit(solution)/shard_map/weight_grad/pallas_call | solution.py:183
  371.5 13.7 %attention_backward.5.refs_3_ = bf16[512,2304]{1,0:T(8,128)(2,1)} custom-call(bf16[512,2304]{1,0:T(8,128)(2,1)} %fusion.24.qkv_ref, f32[512,768]{1,0:T(8,128)} %get-tuple-element.36.lt_ref, bf16[512,768]{1,0:T(8,128)(2,1)} %convolution_convert_fusion.g_ref), custom_call_target="tpu_custom_call" | custom-call | flops 4026531840 | bytes 7077888 | tf_op jit(solution)/shard_map/attention_backward/pallas_call | solution.py:141
  388.0 8.9 %weight_grad.4 = (bf16[768,2304]{1,0:T(8,128)(2,1)}, f32[1,2304]{1,0:T(1,128)S(1)}) custom-call(bf16[512,768]{1,0:T(8,128)(2,1)S(1)} %copy-done.15, bf16[512,768]{1,0:T(8,128)(2,1)S(1)} %copy-done.3, bf16[512,768]{1,0:T(8,128)(2,1)S(1)} %copy-done.7, bf16[512,2304]{1,0:T(8,128)(2,1)S(1)} %copy-done.19, bf16[512,2304]{1,0:T(8,128)(2,1)} %attention_backward.4.refs_4_, ...), custom_call_target="tpu_custom_call" | custom-call | flops 5435817984 | bytes 12976128 | tf_op jit(solution)/shard_map/weight_grad/pallas_call | solution.py:183
  396.9 4.0 constant_dynamic-update-slice_fusion.23
  401.1 8.5 %reshape.314 = bf16[768,3072]{1,0:T(8,128)(2,1)} reshape(bf16[3072,768]{1,0:T(8,128)(2,1)} %get-tuple-element.40) | data formatting | bytes 9437184 | tf_op jit(solution)/shard_map/reshape | solution.py:343
  415.2 5.4 constant_dynamic-update-slice_fusion.21
  426.3 5.6 add_convert_fusion
  432.0 151.2 %reduce-scatter.4.cloned.1.call-done = bf16[24,9344]{1,0:T(8,128)(2,1)} async-done(((bf16[768,9344]{1,0:T(8,128)(2,1)}), bf16[24,9344]{1,0:T(8,128)(2,1)}) %reduce-scatter.4.cloned.1.call-update) | async-done | bytes 448528
  (361 shorter events, 86.1 us)
Async XLA Ops:
  7.2 22.4 %copy-start.69 = (s32[1,512]{1,0:T(1,128)S(1)}, s32[1,512]{1,0:T(1,128)}, u32[]{:S(2)}) copy-start(s32[1,512]{1,0:T(1,128)} %param.20) | copy-start | bytes 6148
  7.2 134.7 %all-gather.4.cloned.1.call-start = ((), (), s32[]{:S(2)}) async-start(), calls=%async_computation.1 | async-start | bytes 16220160 | tf_op jit(solution)/shard_map/all_gather | solution.py:245
  29.5 553.7 %reduce-scatter.4.cloned.1.call-start = ((), (), s32[]{:S(2)}) async-start(), calls=%async_computation.2 | async-start | bytes 14800896
  143.9 110.4 %copy-start.52 = (f32[3072]{0:T(1024)}, f32[3072]{0:T(1024)S(1)}, u32[]{:S(2)}) copy-start(f32[3072]{0:T(1024)S(1)} %add.356) | copy-start | bytes 36868
  144.4 11.8 %copy-start.14 = (bf16[512,768]{1,0:T(8,128)(2,1)S(1)}, bf16[512,768]{1,0:T(8,128)(2,1)}, u32[]{:S(2)}) copy-start(bf16[512,768]{1,0:T(8,128)(2,1)} %refs_0_) | copy-start | bytes 2359300
  172.2 18.3 %copy-start.23 = (f32[512,768]{1,0:T(8,128)}, f32[512,768]{1,0:T(8,128)S(1)}, u32[]{:S(2)}) copy-start(f32[512,768]{1,0:T(8,128)S(1)} %get-tuple-element.133) | copy-start | bytes 4718596
  172.2 18.3 %copy-start.36 = (f32[512]{0:T(512)}, f32[512]{0:T(512)S(1)}, u32[]{:S(2)}) copy-start(f32[512]{0:T(512)S(1)} %broadcast_multiply_fusion.17) | copy-start | bytes 6148
  172.5 18.0 %copy-start.43 = (f32[512]{0:T(512)}, f32[512]{0:T(512)S(1)}, u32[]{:S(2)}) copy-start(f32[512]{0:T(512)S(1)} %add_rsqrt_fusion.5) | copy-start | bytes 6148
  181.4 101.6 %copy-start.34 = (f32[768]{0:T(1024)}, f32[768]{0:T(1024)S(1)}, u32[]{:S(2)}) copy-start(f32[768]{0:T(1024)S(1)} %mul.415) | copy-start | bytes 9220
  181.8 12.2 %slice-start.2 = ((s8[4718592]{0:T(1024)(128)(4,1)}), s8[4194304]{0:T(1024)(128)(4,1)S(1)}, s32[]{:S(2)}) async-start(s8[4718592]{0:T(1024)(128)(4,1)} %bitcast.86), calls=%async_computation.5 | async-start | bytes 8388608
  193.3 15.2 %copy-start.25 = (f32[512,768]{1,0:T(8,128)}, f32[512,768]{1,0:T(8,128)S(1)}, u32[]{:S(2)}) copy-start(f32[512,768]{1,0:T(8,128)S(1)} %get-tuple-element.137) | copy-start | bytes 4718596
  193.4 15.2 %copy-start.38 = (f32[512]{0:T(512)}, f32[512]{0:T(512)S(1)}, u32[]{:S(2)}) copy-start(f32[512]{0:T(512)S(1)} %broadcast_multiply_fusion.16) | copy-start | bytes 6148
  193.7 14.9 %copy-start.45 = (f32[512]{0:T(512)}, f32[512]{0:T(512)S(1)}, u32[]{:S(2)}) copy-start(f32[512]{0:T(512)S(1)} %add_rsqrt_fusion.4) | copy-start | bytes 6148
  198.4 13.5 %slice-start.6 = ((s8[4718592]{0:T(1024)(128)(4,1)}), s8[524288]{0:T(1024)(128)(4,1)S(1)}, s32[]{:S(2)}) async-start(s8[4718592]{0:T(1024)(128)(4,1)} %bitcast.94), calls=%async_computation.9 | async-start | bytes 1048576
  220.6 15.1 %copy-start.29 = (f32[512,768]{1,0:T(8,128)}, f32[512,768]{1,0:T(8,128)S(1)}, u32[]{:S(2)}) copy-start(f32[512,768]{1,0:T(8,128)S(1)} %get-tuple-element.143) | copy-start | bytes 4718596
  220.7 62.3 %copy-start.42 = (f32[512]{0:T(512)}, f32[512]{0:T(512)S(1)}, u32[]{:S(2)}) copy-start(f32[512]{0:T(512)S(1)} %broadcast_multiply_fusion.14) | copy-start | bytes 6148
  221.0 62.0 %copy-start.49 = (f32[512]{0:T(512)}, f32[512]{0:T(512)S(1)}, u32[]{:S(2)}) copy-start(f32[512]{0:T(512)S(1)} %add_rsqrt_fusion.2) | copy-start | bytes 6148
  269.2 22.0 %slice-start.20 = ((s8[4718592]{0:T(1024)(128)(4,1)}), s8[524288]{0:T(1024)(128)(4,1)S(1)}, s32[]{:S(2)}) async-start(s8[4718592]{0:T(1024)(128)(4,1)} %bitcast.112), calls=%async_computation.23 | async-start | bytes 1048576
  307.9 13.6 %copy-start.35 = (f32[768]{0:T(1024)S(1)}, f32[768]{0:T(1024)}, u32[]{:S(2)}) copy-start(f32[768]{0:T(1024)} %copy-done.34) | copy-start | bytes 9220
  308.0 13.6 %copy-start.39 = (f32[512]{0:T(512)S(1)}, f32[512]{0:T(512)}, u32[]{:S(2)}) copy-start(f32[512]{0:T(512)} %copy-done.38) | copy-start | bytes 6148
  308.0 13.6 %copy-start.46 = (f32[512]{0:T(512)S(1)}, f32[512]{0:T(512)}, u32[]{:S(2)}) copy-start(f32[512]{0:T(512)} %copy-done.45) | copy-start | bytes 6148
  371.5 13.7 %copy-start.3 = (bf16[512,768]{1,0:T(8,128)(2,1)S(1)}, bf16[512,768]{1,0:T(8,128)(2,1)}, u32[]{:S(2)}) copy-start(bf16[512,768]{1,0:T(8,128)(2,1)} %copy-done.2) | copy-start | bytes 2359300
  371.5 13.7 %copy-start.7 = (bf16[512,768]{1,0:T(8,128)(2,1)S(1)}, bf16[512,768]{1,0:T(8,128)(2,1)}, u32[]{:S(2)}) copy-start(bf16[512,768]{1,0:T(8,128)(2,1)} %copy-done.6) | copy-start | bytes 2359300
  401.0 11.6 %copy-start.55 = (f32[768]{0:T(1024)S(1)}, f32[768]{0:T(1024)}, u32[]{:S(2)}) copy-start(f32[768]{0:T(1024)} %get-tuple-element.66) | copy-start | bytes 9220
  401.0 11.6 %copy-start.58 = (f32[768]{0:T(1024)S(1)}, f32[768]{0:T(1024)}, u32[]{:S(2)}) copy-start(f32[768]{0:T(1024)} %get-tuple-element.49) | copy-start | bytes 9220
  401.0 11.6 %copy-start.59 = (f32[768]{0:T(1024)S(1)}, f32[768]{0:T(1024)}, u32[]{:S(2)}) copy-start(f32[768]{0:T(1024)} %get-tuple-element.64) | copy-start | bytes 9220
  401.0 12.1 %copy-start.50 = (f32[768]{0:T(1024)S(1)}, f32[768]{0:T(1024)}, u32[]{:S(2)}) copy-start(f32[768]{0:T(1024)} %get-tuple-element.55) | copy-start | bytes 9220
  401.1 12.1 %copy-start.51 = (f32[768]{0:T(1024)S(1)}, f32[768]{0:T(1024)}, u32[]{:S(2)}) copy-start(f32[768]{0:T(1024)} %get-tuple-element.76) | copy-start | bytes 9220
  401.1 12.1 %copy-start.56 = (f32[768]{0:T(1024)S(1)}, f32[768]{0:T(1024)}, u32[]{:S(2)}) copy-start(f32[768]{0:T(1024)} %get-tuple-element.45) | copy-start | bytes 9220
  401.1 12.1 %copy-start.57 = (f32[768]{0:T(1024)S(1)}, f32[768]{0:T(1024)}, u32[]{:S(2)}) copy-start(f32[768]{0:T(1024)} %get-tuple-element.62) | copy-start | bytes 9220
  401.1 12.1 %copy-start.60 = (f32[768]{0:T(1024)S(1)}, f32[768]{0:T(1024)}, u32[]{:S(2)}) copy-start(f32[768]{0:T(1024)} %get-tuple-element.47) | copy-start | bytes 9220
  401.1 12.1 %copy-start.61 = (f32[768]{0:T(1024)S(1)}, f32[768]{0:T(1024)}, u32[]{:S(2)}) copy-start(f32[768]{0:T(1024)} %get-tuple-element.63) | copy-start | bytes 9220
  (66 other events, 377.5 us)
Sparse Core Ops, SparseCore 0:
  29.6 112.2 all-gather.3
  424.8 158.3 reduce-scatter.3

commit v5 on v4

--- a/solution.py
+++ b/solution.py
@@ -170,28 +170,49 @@
     sum_ref[...] = sums
 
 
-def weight_grad(xs, gs, block=768):
+def weight_grad(xs, gs, into=None, at=0, stack=False, columns=None, block=768):
     tokens, depth = xs[0].shape
     width = gs[0].shape[1]
     bk = min(block, depth)
     bn = min(block, width)
     grid = (depth // bk, width // bn)
     count = len(xs)
+    if stack:
+        place = lambda i, j: (0, at + i * grid[1] + j)
+        shape = (bk, depth // bk * width)
+    else:
+        place = lambda i, j: (i, at + j)
+        shape = (depth, width)
+    if into is not None:
+        target = into.shape
+    elif columns is not None:
+        target = (shape[0], columns)
+    else:
+        target = shape
     in_specs = [pl.BlockSpec((tokens, bk), lambda i, j: (0, i))] * count + [
         pl.BlockSpec((tokens, bn), lambda i, j: (0, j))
     ] * count
+    args = list(xs) + list(gs)
+    aliases = {}
+    kernel = weight_grad_kernel
+    if into is not None:
+        in_specs.append(pl.BlockSpec(memory_space=pl.ANY))
+        args.append(into)
+        aliases = {len(args) - 1: 0}
+        kernel = lambda *refs: weight_grad_kernel(*refs[: 2 * count], *refs[2 * count + 1 :])
     return pl.pallas_call(
-        weight_grad_kernel,
+        kernel,
         grid=grid,
         in_specs=in_specs,
         out_specs=[
-            pl.BlockSpec((bk, bn), lambda i, j: (i, j)),
+            pl.BlockSpec((bk, bn), place),
             pl.BlockSpec((1, bn), lambda i, j: (0, j)),
         ],
         out_shape=[
-            jax.ShapeDtypeStruct((depth, width), jnp.bfloat16),
+            jax.ShapeDtypeStruct(target, jnp.bfloat16),
             jax.ShapeDtypeStruct((1, width), jnp.float32),
         ],
+        input_output_aliases=aliases,
         compiler_params=pltpu.CompilerParams(
             dimension_semantics=("arbitrary", "arbitrary"), vmem_limit_bytes=48 * 1024 * 1024
         ),
@@ -201,15 +222,14 @@
             bytes_accessed=2 * count * tokens * (depth + width) + 2 * depth * width,
         ),
         name="weight_grad",
-    )(*xs, *gs)
+    )(*args)
 
 
 def interleave_qkv(q, k, v):
-    pieces = []
-    for h in range(q.shape[-1] // PAIR):
-        cols = slice(h * PAIR, (h + 1) * PAIR)
-        pieces += [q[..., cols], k[..., cols], v[..., cols]]
-    return jnp.concatenate(pieces, axis=-1)
+    lead = q.shape[:-1]
+    pairs = q.shape[-1] // PAIR
+    stacked = jnp.stack([q, k, v], axis=-2).reshape(lead + (3, pairs, PAIR))
+    return jnp.swapaxes(stacked, -3, -2).reshape(lead + (3 * pairs * PAIR,))
 
 
 def split_qkv(packed):
@@ -222,16 +242,31 @@
     return [jnp.concatenate(p, axis=-1) for p in parts]
 
 
+def to_hidden_order(values, groups=4):
+    lead, n = values.shape[:-1], values.shape[-1]
+    return jnp.swapaxes(values.reshape(lead + (n // groups, groups)), -1, -2).reshape(lead + (n,))
+
+
+def from_hidden_order(values, groups=4):
+    lead, n = values.shape[:-1], values.shape[-1]
+    return jnp.swapaxes(values.reshape(lead + (groups, n // groups)), -1, -2).reshape(lead + (n,))
+
+
 def pack_weights(weights):
     (qw, qb, kw, vw, vb, ow, ob, g1, s1, iw, ib, uw, ub, g2, s2) = weights
     rows, width = qw.shape
     wide = iw.shape[1]
-    vectors = jnp.concatenate([qb, vb, ob, g1, s1, ub, g2, s2, ib])
-    vectors = jnp.pad(vectors, (0, wide - vectors.shape[0]))[None, :]
+    vectors = None
+    at = 0
+    for piece in (qb, vb, ob, g1, s1, ub, g2, s2, ib):
+        placed = jnp.pad(piece, (at, wide - at - piece.shape[0]))
+        vectors = placed if vectors is None else vectors + placed
+        at += piece.shape[0]
+    vectors = vectors[None, :]
     return jnp.concatenate(
         [
             jnp.concatenate([interleave_qkv(qw, kw, vw), ow], axis=1),
-            iw,
+            to_hidden_order(iw),
             uw.reshape(rows, wide),
             vectors,
         ],
@@ -246,7 +281,11 @@
     shards = packed.shape[0]
     attn = packed[:, 0:rows].reshape(shards * rows, wide)
     inner = packed[:, rows : 2 * rows].reshape(shards * rows, wide)
-    outer = packed[:, 2 * rows : 3 * rows].reshape(shards * ff_rows, width)
+    outer_rows = packed[:, 2 * rows : 3 * rows].reshape(shards * rows, wide)
+    groups = wide // width
+    outer = jnp.concatenate(
+        [outer_rows[:, c * width : (c + 1) * width] for c in range(groups)], axis=0
+    )
     vectors = packed[:, 3 * rows, :].astype(jnp.float32)
     found = []
     at = 0
@@ -262,7 +301,7 @@
         g1=g1,
         s1=s1,
         inner=inner,
-        inner_bias=ib,
+        inner_bias=ib.reshape(shards, rows, groups).transpose(2, 0, 1).reshape(-1),
         outer=outer,
         outer_bias=ub,
         g2=g2,
@@ -327,26 +366,37 @@
     def across(source, name):
         return [item[name] for item in source]
 
-    qkv_w, qkv_b = weight_grad(across(kept, "rows_low"), across(saved, "qkv_grad"))
-    out_w, out_b = weight_grad(across(kept, "context_low"), across(saved, "attended_low"))
-    inner_w, inner_b = weight_grad(across(kept, "first_low"), across(saved, "inner_grad"))
-    outer_w, outer_b = weight_grad(across(kept, "inner_low"), across(saved, "outer_low"))
-    rows, wide = inner_w.shape
+    width = kept[0]["context_low"].shape[1]
+    three = kept[0]["qkv"].shape[1]
+    wide = kept[0]["inner_low"].shape[1]
+    blocks = (three + width + 2 * wide) // width
+    packed, qkv_b = weight_grad(
+        across(kept, "rows_low"), across(saved, "qkv_grad"), columns=blocks * width + PAIR
+    )
+    at = three // width
+    packed, out_b = weight_grad(
+        across(kept, "context_low"), across(saved, "attended_low"), into=packed, at=at
+    )
+    at += 1
+    packed, inner_b = weight_grad(
+        across(kept, "first_low"), across(saved, "inner_grad"), into=packed, at=at
+    )
+    at += wide // width
+    packed, outer_b = weight_grad(
+        across(kept, "inner_low"), across(saved, "outer_low"), into=packed, at=at, stack=True
+    )
+    rows = width
     q_b, _, v_b = split_qkv(qkv_b[0])
     s2g, s2s, s1g, s1s = [sum(parts) for parts in zip(*norms)]
-    columns = jnp.stack(
-        [q_b, v_b, out_b[0], s1g, s1s, outer_b[0], s2g, s2s], axis=1
-    )
-    columns = jnp.concatenate([columns, inner_b[0].reshape(rows, -1)], axis=1)
+    columns = jnp.stack([q_b, v_b, out_b[0], s1g, s1s, outer_b[0], s2g, s2s], axis=1)
+    inner_cols = inner_b[0].reshape(wide // rows, rows).T
+    columns = jnp.concatenate([columns, inner_cols], axis=1)
     columns = jnp.pad(columns, ((0, 0), (0, PAIR - columns.shape[1]))).astype(jnp.bfloat16)
-    packed = jnp.concatenate(
-        [qkv_w, out_w, inner_w, outer_w.reshape(rows, wide), columns], axis=1
-    )
+    packed = lax.dynamic_update_slice(packed, columns, (0, blocks * width))
     mine = lax.psum_scatter(packed, AXES, scatter_dimension=0, tiled=True).astype(jnp.float32)
-    width = out_w.shape[1]
     at = 0
     pieces = []
-    for count in (3 * width, width, wide, wide, PAIR):
+    for count in (three, width, wide, wide, PAIR):
         pieces.append(mine[:, at : at + count])
         at += count
     qkv_mine, out_mine, inner_mine, outer_mine, col_mine = pieces
@@ -363,7 +413,7 @@
         c[2],
         c[3],
         c[4],
-        inner_mine,
+        from_hidden_order(inner_mine),
         ib_mine,
         outer_mine.reshape(-1, width),
         c[5],

time: 606 us -> 583 us (0.962)
  local copies, waits for them, and re-layouts: 83.3 us -> 43.1 us
  matrix products: 111 us -> 130 us
    dot_general x12, matrix products: 63.3 us -> 83.1 us  [product_nt(): return lax.dot_general(left, right, NT, preferred_element_type=jnp.float32)]
    unnamed x247 -> x191, local copies, waits for them, and re-layouts: 39.6 us -> 20.8 us
    reshape x4 -> x3, local copies, waits for them, and re-layouts: 17.3 us -> 0.95 us  [the longest x2 0.85 us: from_hidden_order(): values.reshape(lead + (groups, n // groups))]
    concatenate x5 -> x2, local copies, waits for them, and re-layouts: 8.42 us -> 0.25 us  [scatter_grads(): columns = jnp.concatenate([columns, inner_cols], axis=1)]
    slice x1 -> x3, local copies, waits for them, and re-layouts: 9.59 us -> 13.5 us  [the longest x1 9.59 us: gather_weights(): outer_rows = packed[:, 2 * rows:3 * rows].reshape(shards * rows, wide)]
where the time goes in v5:
time: 583 us; the launch traced here: 573 us
  waiting for transfers between devices  263 us (45%)
  matrix products  130 us (22%)
  Pallas kernels  106 us (18%)
  local copies, waits for them, and re-layouts  43.1 us (7%)
  between operations  16 us (3%)
  other arithmetic  15.1 us (3%)
    unnamed x3, waiting for transfers between devices  150 us
    all_gather x1, waiting for transfers between devices, gather_weights(): packed = lax.all_gather(pack_weights(weights), AXES, axis=0, tiled=False)  112 us
    dot_general x12, matrix products, product_nt(): return lax.dot_general(left, right, NT, preferred_element_type=jnp.float32)  83.1 us
    dot_general x12, matrix products, product(): return jnp.dot(left, right, preferred_element_type=jnp.float32)  46.9 us
    pallas_call x3, Pallas kernels, attention_backward(): pl.pallas_call(attention_backward_kernel, grid=grid, in_specs=[triple, pa...  41 us
    pallas_call x4, Pallas kernels, weight_grad(): pl.pallas_call(kernel, grid=grid, in_specs=in_specs, out_specs=[pl.BlockS...  34.8 us
    pallas_call x3, Pallas kernels, attention_forward(): pl.pallas_call(attention_forward_kernel, grid=grid, in_specs=[pl.BlockSpe...  30.2 us
    unnamed x191, local copies, waits for them, and re-layouts  20.8 us
  transfers between devices with their start and end apart: 2, of which 2 were waited for; matrix products, arithmetic and copies ran while one was open for 1% of the time, Pallas kernels for 0%

profile of v5, /device:TPU:0, one launch (start us, length us, event | category | flops | bytes accessed | tf_op | source)
XLA Modules:
  0.0 572.8 jit_solution(4506653746779054629)
XLA Ops:
  12.6 112.3 %all-gather.4.cloned.1.call-done = bf16[32,73,3072]{2,1,0:T(8,128)(2,1)} async-done(((bf16[1,73,3072]{2,1,0:T(8,128)(2,1)}), bf16[32,73,3072]{2,1,0:T(8,128)(2,1)}) %all-gather.4.cloned.1.call-update) | async-done | bytes 14352400 | tf_op jit(solution)/shard_map/all_gather | solution.py:280
  128.1 9.6 %fusion.65 = (bf16[32,24,3072]{2,1,0:T(8,128)(2,1)}, bf16[32,24,3072]{2,1,0:T(8,128)(2,1)}, bf16[32,24,3072]{2,1,0:T(8,128)(2,1)S(1)}) fusion(bf16[32,73,3072]{2,1,0:T(8,128)(2,1)} %all-gather.4.cloned.1.call-done), kind=kLoop, calls=%fused_computation.202 | loop fusion | bytes 28311552 | tf_op jit(solution)/shard_map/slice | solution.py:284
  139.9 3.4 fusion.24.qkv_ref
  143.3 10.0 %attention_forward.3 = (bf16[512,768]{1,0:T(8,128)(2,1)}, f32[512,768]{1,0:T(8,128)}) custom-call(bf16[512,2304]{1,0:T(8,128)(2,1)} %fusion.24.qkv_ref), custom_call_target="tpu_custom_call" | custom-call | flops 1610612736 | bytes 4718592 | tf_op jit(solution)/shard_map/attention_forward/pallas_call | solution.py:116
  159.6 8.6 %multiply_convert_fusion.2 = (bf16[512,3072]{1,0:T(8,128)(2,1)S(1)}, f32[512,3072]{1,0:T(8,128)}) fusion(f32[3072]{0:T(1024)S(1)} %add.407, bf16[512,768]{1,0:T(8,128)(2,1)S(1)} %fusion.43.refs_0_, bf16[768,3072]{1,0:T(8,128)(2,1)} %bitcast.104), kind=kOutput, calls=%fused_computation.29 | convolution fusion | flops 2431647744 | bytes 14954496 | tf_op jit(solution)/shard_map/dot_general | solution.py:21
  171.6 3.5 fusion.21.qkv_ref
  176.0 10.2 %attention_forward.4 = (bf16[512,768]{1,0:T(8,128)(2,1)}, f32[512,768]{1,0:T(8,128)}) custom-call(bf16[512,2304]{1,0:T(8,128)(2,1)} %fusion.21.qkv_ref), custom_call_target="tpu_custom_call" | custom-call | flops 1610612736 | bytes 4718592 | tf_op jit(solution)/shard_map/attention_forward/pallas_call | solution.py:116
  189.5 5.8 %multiply_convert_fusion.1 = (bf16[512,3072]{1,0:T(8,128)(2,1)S(1)}, f32[512,3072]{1,0:T(8,128)}) fusion(f32[3072]{0:T(1024)S(1)} %add.407, bf16[512,768]{1,0:T(8,128)(2,1)S(1)} %fusion.45.refs_1_, bf16[768,3072]{1,0:T(8,128)(2,1)S(1)} %bitcast.107), kind=kOutput, calls=%fused_computation.28 | convolution fusion | flops 2431647744 | bytes 14954496 | tf_op jit(solution)/shard_map/dot_general | solution.py:21
  198.9 3.4 fusion.22.qkv_ref
  203.2 10.0 %attention_forward.5 = (bf16[512,768]{1,0:T(8,128)(2,1)}, f32[512,768]{1,0:T(8,128)}) custom-call(bf16[512,2304]{1,0:T(8,128)(2,1)} %fusion.22.qkv_ref), custom_call_target="tpu_custom_call" | custom-call | flops 1610612736 | bytes 4718592 | tf_op jit(solution)/shard_map/attention_forward/pallas_call | solution.py:116
  216.6 6.1 %multiply_convert_fusion = (bf16[512,3072]{1,0:T(8,128)(2,1)S(1)}, f32[512,3072]{1,0:T(8,128)}) fusion(f32[3072]{0:T(1024)S(1)} %add.407, bf16[512,768]{1,0:T(8,128)(2,1)S(1)} %fusion.47.refs_2_, bf16[768,3072]{1,0:T(8,128)(2,1)S(1)} %bitcast.110), kind=kOutput, calls=%fused_computation.27 | convolution fusion | flops 2431647744 | bytes 14954496 | tf_op jit(solution)/shard_map/dot_general | solution.py:21
  222.7 2.8 fusion.74
  229.2 15.3 %fusion.20.refs_5_ = bf16[512,3072]{1,0:T(8,128)(2,1)S(1)} fusion(f32[512,3072]{1,0:T(8,128)} %get-tuple-element.185, f32[3072]{0:T(1024)S(1)} %add.407, bf16[512,768]{1,0:T(8,128)(2,1)S(1)} %get-tuple-element.128.refs_5_, bf16[768,768]{1,0:T(8,128)(2,1)S(1)} %copy-done.42, bf16[768,768]{1,0:T(8,128)(2,1)S(1)} %copy-done.47, ...), kind=kOutput, calls=%fused_computation.26 | convolution fusion | flops 2467823616 | bytes 14954496 | tf_op jit(solution)/shard_map/dot_general | solution.py:25
  244.6 3.5 multiply_reduce_fusion.3
  249.7 3.0 convolution_convert_fusion.2.g_ref
  252.7 13.6 %attention_backward.3.refs_5_ = bf16[512,2304]{1,0:T(8,128)(2,1)} custom-call(bf16[512,2304]{1,0:T(8,128)(2,1)} %fusion.22.qkv_ref, f32[512,768]{1,0:T(8,128)} %get-tuple-element.34.lt_ref, bf16[512,768]{1,0:T(8,128)(2,1)} %convolution_convert_fusion.2.g_ref), custom_call_target="tpu_custom_call" | custom-call | flops 4026531840 | bytes 7077888 | tf_op jit(solution)/shard_map/attention_backward/pallas_call | solution.py:141
  266.3 5.8 %multiply_reduce_fusion.1 = (f32[768]{0:T(1024)S(1)}, f32[512]{0:T(512)S(1)}, f32[512]{0:T(512)S(1)}, f32[768]{0:T(1024)S(1)}, f32[512,768]{1,0:T(8,128)S(1)}) fusion(f32[512,768]{1,0:T(8,128)S(1)} %get-tuple-element.181, f32[512]{0:T(512)S(1)} %add_rsqrt_fusion.2, f32[512]{0:T(512)S(1)} %broadcast_multiply_fusion.14, f32[768]{0:T(1024)S(1)} %mul.415, ...), kind=kOutput, calls=%fused_computation.39 | convolution fusion | flops 1815868928 | bytes 10634240 | tf_op jit(solution)/shard_map/dot_general | solution.py:25
  273.4 15.7 %fusion.13.refs_4_ = bf16[512,3072]{1,0:T(8,128)(2,1)S(1)} fusion(f32[512,3072]{1,0:T(8,128)} %get-tuple-element.179, f32[3072]{0:T(1024)S(1)} %add.407, bf16[512,768]{1,0:T(8,128)(2,1)S(1)} %get-tuple-element.117.refs_4_, bf16[768,768]{1,0:T(8,128)(2,1)S(1)} %copy-done.43, bf16[768,768]{1,0:T(8,128)(2,1)S(1)} %copy-done.48, ...), kind=kOutput, calls=%fused_computation.19 | convolution fusion | flops 2467823616 | bytes 14954496 | tf_op jit(solution)/shard_map/dot_general | solution.py:25
  289.2 3.1 multiply_reduce_fusion.4
  294.0 3.0 convolution_convert_fusion.1.g_ref
  297.0 13.7 %attention_backward.4.refs_4_ = bf16[512,2304]{1,0:T(8,128)(2,1)} custom-call(bf16[512,2304]{1,0:T(8,128)(2,1)} %fusion.21.qkv_ref, f32[512,768]{1,0:T(8,128)} %get-tuple-element.35.lt_ref, bf16[512,768]{1,0:T(8,128)(2,1)} %convolution_convert_fusion.1.g_ref), custom_call_target="tpu_custom_call" | custom-call | flops 4026531840 | bytes 7077888 | tf_op jit(solution)/shard_map/attention_backward/pallas_call | solution.py:141
  310.7 6.2 %multiply_reduce_fusion.2 = (f32[768]{0:T(1024)S(1)}, f32[512]{0:T(512)S(1)}, f32[512]{0:T(512)S(1)}, f32[768]{0:T(1024)S(1)}, f32[512,768]{1,0:T(8,128)S(1)}) fusion(f32[512,768]{1,0:T(8,128)} %copy-done.28, f32[512]{0:T(512)S(1)} %add_rsqrt_fusion.4, f32[512]{0:T(512)S(1)} %broadcast_multiply_fusion.16, f32[768]{0:T(1024)S(1)} %mul.415, ...), kind=kOutput, calls=%fused_computation.40 | convolution fusion | flops 1815868928 | bytes 10634240 | tf_op jit(solution)/shard_map/dot_general | solution.py:25
  318.2 15.8 %fusion.6.refs_3_ = bf16[512,3072]{1,0:T(8,128)(2,1)S(1)} fusion(f32[512,3072]{1,0:T(8,128)} %get-tuple-element.173, f32[3072]{0:T(1024)S(1)} %add.407, bf16[512,768]{1,0:T(8,128)(2,1)S(1)} %get-tuple-element.113.refs_3_, bf16[768,768]{1,0:T(8,128)(2,1)S(1)} %copy-done.44, bf16[768,768]{1,0:T(8,128)(2,1)S(1)} %copy-done.49, ...), kind=kOutput, calls=%fused_computation.12 | convolution fusion | flops 2467823616 | bytes 14954496 | tf_op jit(solution)/shard_map/dot_general | solution.py:25
  334.0 3.1 multiply_reduce_fusion.5
  338.9 3.0 convolution_convert_fusion.g_ref
  341.8 13.7 %attention_backward.5.refs_3_ = bf16[512,2304]{1,0:T(8,128)(2,1)} custom-call(bf16[512,2304]{1,0:T(8,128)(2,1)} %fusion.24.qkv_ref, f32[512,768]{1,0:T(8,128)} %get-tuple-element.36.lt_ref, bf16[512,768]{1,0:T(8,128)(2,1)} %convolution_convert_fusion.g_ref), custom_call_target="tpu_custom_call" | custom-call | flops 4026531840 | bytes 7077888 | tf_op jit(solution)/shard_map/attention_backward/pallas_call | solution.py:141
  360.6 9.0 %weight_grad.4 = (bf16[768,9344]{1,0:T(8,128)(2,1)}, f32[1,2304]{1,0:T(1,128)S(1)}) custom-call(bf16[512,768]{1,0:T(8,128)(2,1)S(1)} %copy-done.18, bf16[512,768]{1,0:T(8,128)(2,1)S(1)} %copy-done.12, bf16[512,768]{1,0:T(8,128)(2,1)S(1)} %copy-done.16, bf16[512,2304]{1,0:T(8,128)(2,1)S(1)} %copy-done.23, bf16[512,2304]{1,0:T(8,128)(2,1)} %attention_backward.4.refs_4_, ...), custom_call_target="tpu_custom_call" | custom-call | flops 5435817984 | bytes 12976128 | tf_op jit(solution)/shard_map/weight_grad/pallas_call | solution.py:203
  369.6 3.2 weight_grad.5
  374.7 11.2 %weight_grad.6 = (bf16[768,9344]{1,0:T(8,128)(2,1)}, f32[1,3072]{1,0:T(1,128)S(1)}) custom-call(bf16[512,768]{1,0:T(8,128)(2,1)S(1)} %copy-done.8, bf16[512,768]{1,0:T(8,128)(2,1)S(1)} %copy-done.10, bf16[512,768]{1,0:T(8,128)(2,1)S(1)} %copy-done.14, bf16[512,3072]{1,0:T(8,128)(2,1)S(1)} %copy-done.22, ...), custom_call_target="tpu_custom_call", output_to_operand_aliasing={{0}: (6, {})} | custom-call | flops 7247757312 | bytes 16515072 | tf_op jit(solution)/shard_map/weight_grad/pallas_call | solution.py:203
  386.0 11.3 %weight_grad.7 = (bf16[768,9344]{1,0:T(8,128)(2,1)}, f32[1,768]{1,0:T(1,128)S(1)}) custom-call(bf16[512,3072]{1,0:T(8,128)(2,1)S(1)} %copy-done.20, bf16[512,3072]{1,0:T(8,128)(2,1)} %copy-done.68, bf16[512,3072]{1,0:T(8,128)(2,1)} %copy-done.69, bf16[512,768]{1,0:T(8,128)(2,1)S(1)} %copy-done.6, ...), custom_call_target="tpu_custom_call", output_to_operand_aliasing={{0}: (6, {})} | custom-call | flops 7247757312 | bytes 16515072 | tf_op jit(solution)/shard_map/weight_grad/pallas_call | solution.py:203
  402.6 5.6 add_convert_fusion
  408.2 150.3 %reduce-scatter.4.cloned.1.call-done = bf16[24,9344]{1,0:T(8,128)(2,1)} async-done(((bf16[768,9344]{1,0:T(8,128)(2,1)}), bf16[24,9344]{1,0:T(8,128)(2,1)}) %reduce-scatter.4.cloned.1.call-update) | async-done | bytes 448528
  (318 shorter events, 62.0 us)
Async XLA Ops:
  7.2 117.6 %all-gather.4.cloned.1.call-start = ((), (), s32[]{:S(2)}) async-start(), calls=%async_computation.1 | async-start | bytes 16220160 | tf_op jit(solution)/shard_map/all_gather | solution.py:280
  12.4 546.1 %reduce-scatter.4.cloned.1.call-start = ((), (), s32[]{:S(2)}) async-start(), calls=%async_computation.2 | async-start | bytes 14800896
  128.1 11.8 %copy-start.17 = (bf16[512,768]{1,0:T(8,128)(2,1)S(1)}, bf16[512,768]{1,0:T(8,128)(2,1)}, u32[]{:S(2)}) copy-start(bf16[512,768]{1,0:T(8,128)(2,1)} %refs_0_) | copy-start | bytes 2359300
  156.2 12.0 %copy-start.26 = (f32[512,768]{1,0:T(8,128)}, f32[512,768]{1,0:T(8,128)S(1)}, u32[]{:S(2)}) copy-start(f32[512,768]{1,0:T(8,128)S(1)} %get-tuple-element.171) | copy-start | bytes 4718596
  159.5 8.6 %copy-start.7 = (bf16[512,768]{1,0:T(8,128)(2,1)}, bf16[512,768]{1,0:T(8,128)(2,1)S(1)}, u32[]{:S(2)}) copy-start(bf16[512,768]{1,0:T(8,128)(2,1)S(1)} %fusion.43.refs_0_) | copy-start | bytes 2359300
  159.5 8.6 %copy-start.35 = (bf16[768,768]{1,0:T(8,128)(2,1)S(1)}, bf16[768,768]{1,0:T(8,128)(2,1)}, u32[]{:S(2)}) copy-start(bf16[768,768]{1,0:T(8,128)(2,1)} %get-tuple-element.124) | copy-start | bytes 3538948
  159.5 8.6 %copy-start.40 = (bf16[768,768]{1,0:T(8,128)(2,1)S(1)}, bf16[768,768]{1,0:T(8,128)(2,1)}, u32[]{:S(2)}) copy-start(bf16[768,768]{1,0:T(8,128)(2,1)} %get-tuple-element.125) | copy-start | bytes 3538948
  159.5 8.6 %copy-start.45 = (bf16[768,768]{1,0:T(8,128)(2,1)S(1)}, bf16[768,768]{1,0:T(8,128)(2,1)}, u32[]{:S(2)}) copy-start(bf16[768,768]{1,0:T(8,128)(2,1)} %get-tuple-element.126) | copy-start | bytes 3538948
  159.5 8.6 %copy-start.50 = (bf16[768,768]{1,0:T(8,128)(2,1)S(1)}, bf16[768,768]{1,0:T(8,128)(2,1)}, u32[]{:S(2)}) copy-start(bf16[768,768]{1,0:T(8,128)(2,1)} %get-tuple-element.127) | copy-start | bytes 3538948
  159.6 12.1 %slice-start = ((s8[4718592]{0:T(1024)(128)(4,1)}), s8[4194304]{0:T(1024)(128)(4,1)S(1)}, s32[]{:S(2)}) async-start(s8[4718592]{0:T(1024)(128)(4,1)} %bitcast.98), calls=%async_computation.3 | async-start | bytes 8388608
  171.0 15.2 %copy-start.28 = (f32[512,768]{1,0:T(8,128)}, f32[512,768]{1,0:T(8,128)S(1)}, u32[]{:S(2)}) copy-start(f32[512,768]{1,0:T(8,128)S(1)} %get-tuple-element.175) | copy-start | bytes 4718596
  176.0 13.4 %slice-start.4 = ((s8[4718592]{0:T(1024)(128)(4,1)}), s8[524288]{0:T(1024)(128)(4,1)S(1)}, s32[]{:S(2)}) async-start(s8[4718592]{0:T(1024)(128)(4,1)} %bitcast.105), calls=%async_computation.7 | async-start | bytes 1048576
  189.5 9.4 %slice-start.2 = ((s8[4718592]{0:T(1024)(128)(4,1)}), s8[4194304]{0:T(1024)(128)(4,1)S(1)}, s32[]{:S(2)}) async-start(s8[4718592]{0:T(1024)(128)(4,1)} %bitcast.101), calls=%async_computation.5 | async-start | bytes 8388608
  203.2 13.3 %slice-start.6 = ((s8[4718592]{0:T(1024)(128)(4,1)}), s8[524288]{0:T(1024)(128)(4,1)S(1)}, s32[]{:S(2)}) async-start(s8[4718592]{0:T(1024)(128)(4,1)} %bitcast.108), calls=%async_computation.9 | async-start | bytes 1048576
  227.6 16.9 %slice-start.8 = ((s8[4718592]{0:T(1024)(128)(4,1)}), s8[4194304]{0:T(1024)(128)(4,1)S(1)}, s32[]{:S(2)}) async-start(s8[4718592]{0:T(1024)(128)(4,1)} %bitcast.111), calls=%async_computation.11 | async-start | bytes 8388608
  229.2 15.4 %slice-start.9 = ((s8[4718592]{0:T(1024)(128)(4,1)}), s8[524288]{0:T(1024)(128)(4,1)S(1)}, s32[]{:S(2)}) async-start(s8[4718592]{0:T(1024)(128)(4,1)} %bitcast.111), calls=%async_computation.12 | async-start | bytes 1048576
  272.1 17.0 %slice-start.10 = ((s8[4718592]{0:T(1024)(128)(4,1)}), s8[4194304]{0:T(1024)(128)(4,1)S(1)}, s32[]{:S(2)}) async-start(s8[4718592]{0:T(1024)(128)(4,1)} %bitcast.114), calls=%async_computation.13 | async-start | bytes 8388608
  272.6 16.5 %copy-start.3 = (bf16[512,768]{1,0:T(8,128)(2,1)}, bf16[512,768]{1,0:T(8,128)(2,1)S(1)}, u32[]{:S(2)}) copy-start(bf16[512,768]{1,0:T(8,128)(2,1)S(1)} %get-tuple-element.117.refs_4_) | copy-start | bytes 2359300
  273.4 15.8 %copy-start.31 = (f32[512,768]{1,0:T(8,128)S(1)}, f32[512,768]{1,0:T(8,128)}, u32[]{:S(2)}) copy-start(f32[512,768]{1,0:T(8,128)} %copy-done.30) | copy-start | bytes 4718596
  273.4 15.8 %slice-start.11 = ((s8[4718592]{0:T(1024)(128)(4,1)}), s8[524288]{0:T(1024)(128)(4,1)S(1)}, s32[]{:S(2)}) async-start(s8[4718592]{0:T(1024)(128)(4,1)} %bitcast.114), calls=%async_computation.14 | async-start | bytes 1048576
  316.9 17.1 %slice-start.12 = ((s8[4718592]{0:T(1024)(128)(4,1)}), s8[4194304]{0:T(1024)(128)(4,1)S(1)}, s32[]{:S(2)}) async-start(s8[4718592]{0:T(1024)(128)(4,1)} %bitcast.117), calls=%async_computation.15 | async-start | bytes 8388608
  317.5 16.5 %copy-start.5 = (bf16[512,768]{1,0:T(8,128)(2,1)}, bf16[512,768]{1,0:T(8,128)(2,1)S(1)}, u32[]{:S(2)}) copy-start(bf16[512,768]{1,0:T(8,128)(2,1)S(1)} %get-tuple-element.113.refs_3_) | copy-start | bytes 2359300
  318.2 15.8 %copy-start.27 = (f32[512,768]{1,0:T(8,128)S(1)}, f32[512,768]{1,0:T(8,128)}, u32[]{:S(2)}) copy-start(f32[512,768]{1,0:T(8,128)} %copy-done.26) | copy-start | bytes 4718596
  318.2 15.8 %slice-start.13 = ((s8[4718592]{0:T(1024)(128)(4,1)}), s8[524288]{0:T(1024)(128)(4,1)S(1)}, s32[]{:S(2)}) async-start(s8[4718592]{0:T(1024)(128)(4,1)} %bitcast.117), calls=%async_computation.16 | async-start | bytes 1048576
  360.6 9.0 %copy-start = (bf16[512,768]{1,0:T(8,128)(2,1)S(1)}, bf16[512,768]{1,0:T(8,128)(2,1)}, u32[]{:S(2)}) copy-start(bf16[512,768]{1,0:T(8,128)(2,1)} %get-tuple-element.31.refs_0_) | copy-start | bytes 2359300
  360.6 9.0 %copy-start.1 = (bf16[512,768]{1,0:T(8,128)(2,1)S(1)}, bf16[512,768]{1,0:T(8,128)(2,1)}, u32[]{:S(2)}) copy-start(bf16[512,768]{1,0:T(8,128)(2,1)} %get-tuple-element.32.refs_1_) | copy-start | bytes 2359300
  360.6 9.0 %copy-start.2 = (bf16[512,768]{1,0:T(8,128)(2,1)S(1)}, bf16[512,768]{1,0:T(8,128)(2,1)}, u32[]{:S(2)}) copy-start(bf16[512,768]{1,0:T(8,128)(2,1)} %get-tuple-element.33.refs_2_) | copy-start | bytes 2359300
  374.7 11.2 %copy-start.4 = (bf16[512,768]{1,0:T(8,128)(2,1)S(1)}, bf16[512,768]{1,0:T(8,128)(2,1)}, u32[]{:S(2)}) copy-start(bf16[512,768]{1,0:T(8,128)(2,1)} %copy-done.3) | copy-start | bytes 2359300
  374.7 11.2 %copy-start.6 = (bf16[512,768]{1,0:T(8,128)(2,1)S(1)}, bf16[512,768]{1,0:T(8,128)(2,1)}, u32[]{:S(2)}) copy-start(bf16[512,768]{1,0:T(8,128)(2,1)} %copy-done.5) | copy-start | bytes 2359300
  374.7 11.2 %copy-start.20 = (bf16[512,3072]{1,0:T(8,128)(2,1)S(1)}, bf16[512,3072]{1,0:T(8,128)(2,1)}, u32[]{:S(2)}) copy-start(bf16[512,3072]{1,0:T(8,128)(2,1)} %copy-done.19) | copy-start | bytes 9437188
  385.9 11.4 %copy-start.67 = (bf16[768]{0:T(1024)(128)(2,1)S(1)}, bf16[768]{0:T(1024)(128)(2,1)}, u32[]{:S(2)}) copy-start(bf16[768]{0:T(1024)(128)(2,1)} %custom-call.4) | copy-start | bytes 4612
  386.0 12.6 %copy-start.66 = (bf16[768]{0:T(1024)(128)(2,1)S(1)}, bf16[768]{0:T(1024)(128)(2,1)}, u32[]{:S(2)}) copy-start(bf16[768]{0:T(1024)(128)(2,1)} %custom-call.3) | copy-start | bytes 4612
  (56 other events, 201.5 us)
Sparse Core Ops, SparseCore 0:
  12.5 112.2 all-gather.3
  401.0 157.4 reduce-scatter.3

commit v6 on v5

--- a/solution.py
+++ b/solution.py
@@ -293,7 +293,7 @@
         found.append(vectors[:, at : at + count].reshape(-1))
         at += count
     (qb, vb, ob, g1, s1, ub, g2, s2, ib) = found
-    return dict(
+    found = dict(
         qkv=attn[:, : 3 * width],
         qkv_bias=interleave_qkv(qb, jnp.zeros_like(qb), vb),
         out=attn[:, 3 * width :],
@@ -307,6 +307,7 @@
         g2=g2,
         s2=s2,
     )
+    return lax.optimization_barrier(found)
 
 
 def layer_forward(w, hidden_state):

time: 583 us -> 574 us (0.985)
  matrix products: 130 us -> 108 us
  other arithmetic: 15.1 us -> 21.9 us
  local copies, waits for them, and re-layouts: 43.1 us -> 49 us
    dot_general x12, matrix products: 83.1 us -> 57.9 us  [product_nt(): return lax.dot_general(left, right, NT, preferred_element_type=jnp.float32)]
    unnamed x191 -> x161, local copies, waits for them, and re-layouts: 20.8 us -> 21.2 us
where the time goes in v6:
time: 574 us; the launch traced here: 563 us
  waiting for transfers between devices  263 us (46%)
  matrix products  108 us (19%)
  Pallas kernels  107 us (19%)
  local copies, waits for them, and re-layouts  49 us (9%)
  other arithmetic  21.9 us (4%)
  between operations  15.6 us (3%)
    unnamed x3, waiting for transfers between devices  150 us
    all_gather x1, waiting for transfers between devices, gather_weights(): packed = lax.all_gather(pack_weights(weights), AXES, axis=0, tiled=False)  112 us
    dot_general x12, matrix products, product_nt(): return lax.dot_general(left, right, NT, preferred_element_type=jnp.float32)  57.9 us
    dot_general x12, matrix products, product(): return jnp.dot(left, right, preferred_element_type=jnp.float32)  49.7 us
    pallas_call x3, Pallas kernels, attention_backward(): pl.pallas_call(attention_backward_kernel, grid=grid, in_specs=[triple, pa...  41.6 us
    pallas_call x4, Pallas kernels, weight_grad(): pl.pallas_call(kernel, grid=grid, in_specs=in_specs, out_specs=[pl.BlockS...  34.5 us
    pallas_call x3, Pallas kernels, attention_forward(): pl.pallas_call(attention_forward_kernel, grid=grid, in_specs=[pl.BlockSpe...  30.4 us
    unnamed x161, local copies, waits for them, and re-layouts  21.2 us
  transfers between devices with their start and end apart: 2, of which 2 were waited for; matrix products, arithmetic and copies ran while one was open for 1% of the time, Pallas kernels for 0%

profile of v6, /device:TPU:0, one launch (start us, length us, event | category | flops | bytes accessed | tf_op | source)
XLA Modules:
  0.0 563.4 jit_solution(2532046417200689028)
XLA Ops:
  12.6 112.3 %all-gather.4.cloned.1.call-done = bf16[32,73,3072]{2,1,0:T(8,128)(2,1)} async-done(((bf16[1,73,3072]{2,1,0:T(8,128)(2,1)}), bf16[32,73,3072]{2,1,0:T(8,128)(2,1)}) %all-gather.4.cloned.1.call-update) | async-done | bytes 14352400 | tf_op jit(solution)/shard_map/all_gather | solution.py:280
  127.2 10.2 %fusion.39 = (bf16[32,24,3072]{2,1,0:T(8,128)(2,1)}, bf16[32,24,3072]{2,1,0:T(8,128)(2,1)S(1)}, bf16[32,24,3072]{2,1,0:T(8,128)(2,1)}) fusion(bf16[32,73,3072]{2,1,0:T(8,128)(2,1)} %all-gather.4.cloned.1.call-done), kind=kLoop, calls=%fused_computation.184 | loop fusion | bytes 28311552 | tf_op jit(solution)/shard_map/slice | solution.py:284
  141.2 4.1 fusion.40
  146.3 5.4 pad_maximum_fusion
  151.7 3.4 fusion.24.qkv_ref
  155.1 10.1 %attention_forward.3 = (bf16[512,768]{1,0:T(8,128)(2,1)}, f32[512,768]{1,0:T(8,128)}) custom-call(bf16[512,2304]{1,0:T(8,128)(2,1)} %fusion.24.qkv_ref), custom_call_target="tpu_custom_call" | custom-call | flops 1610612736 | bytes 4718592 | tf_op jit(solution)/shard_map/attention_forward/pallas_call | solution.py:116
  167.8 8.9 %multiply_convert_fusion.2 = (bf16[512,3072]{1,0:T(8,128)(2,1)S(1)}, f32[512,3072]{1,0:T(8,128)}) fusion(f32[3072]{0:T(1024)S(1)} %reshape.358, bf16[512,768]{1,0:T(8,128)(2,1)S(1)} %fusion.28.refs_0_, bf16[768,3072]{1,0:T(8,128)(2,1)} %bitcast.108), kind=kOutput, calls=%fused_computation.29 | convolution fusion | flops 2431647744 | bytes 14954496 | tf_op jit(solution)/shard_map/dot_general | solution.py:21
  182.2 3.4 fusion.21.qkv_ref
  186.5 10.3 %attention_forward.4 = (bf16[512,768]{1,0:T(8,128)(2,1)}, f32[512,768]{1,0:T(8,128)}) custom-call(bf16[512,2304]{1,0:T(8,128)(2,1)} %fusion.21.qkv_ref), custom_call_target="tpu_custom_call" | custom-call | flops 1610612736 | bytes 4718592 | tf_op jit(solution)/shard_map/attention_forward/pallas_call | solution.py:116
  199.9 8.9 %multiply_convert_fusion.1 = (bf16[512,3072]{1,0:T(8,128)(2,1)S(1)}, f32[512,3072]{1,0:T(8,128)}) fusion(f32[3072]{0:T(1024)S(1)} %reshape.358, bf16[512,768]{1,0:T(8,128)(2,1)S(1)} %fusion.30.refs_1_, bf16[768,3072]{1,0:T(8,128)(2,1)} %bitcast.109), kind=kOutput, calls=%fused_computation.28 | convolution fusion | flops 2431647744 | bytes 14954496 | tf_op jit(solution)/shard_map/dot_general | solution.py:21
  214.2 3.4 fusion.22.qkv_ref
  218.5 10.0 %attention_forward.5 = (bf16[512,768]{1,0:T(8,128)(2,1)}, f32[512,768]{1,0:T(8,128)}) custom-call(bf16[512,2304]{1,0:T(8,128)(2,1)} %fusion.22.qkv_ref), custom_call_target="tpu_custom_call" | custom-call | flops 1610612736 | bytes 4718592 | tf_op jit(solution)/shard_map/attention_forward/pallas_call | solution.py:116
  231.6 6.4 %multiply_convert_fusion = (bf16[512,3072]{1,0:T(8,128)(2,1)S(1)}, f32[512,3072]{1,0:T(8,128)S(1)}) fusion(f32[3072]{0:T(1024)S(1)} %reshape.358, bf16[512,768]{1,0:T(8,128)(2,1)S(1)} %fusion.32.refs_2_, bf16[768,3072]{1,0:T(8,128)(2,1)} %bitcast.110), kind=kOutput, calls=%fused_computation.27 | convolution fusion | flops 2431647744 | bytes 14954496 | tf_op jit(solution)/shard_map/dot_general | solution.py:21
  238.1 2.8 fusion.48
  244.5 6.2 %fusion.20.refs_5_ = bf16[512,3072]{1,0:T(8,128)(2,1)S(1)} fusion(f32[512,3072]{1,0:T(8,128)S(1)} %get-tuple-element.209, f32[3072]{0:T(1024)S(1)} %reshape.358, bf16[512,768]{1,0:T(8,128)(2,1)S(1)} %get-tuple-element.152.refs_5_, bf16[3072,768]{1,0:T(8,128)(2,1)S(1)} %bitcast.125), kind=kOutput, calls=%fused_computation.26 | convolution fusion | flops 2448949248 | bytes 14954496 | tf_op jit(solution)/shard_map/dot_general | solution.py:25
  250.8 3.5 multiply_reduce_fusion.3
  257.7 13.8 %attention_backward.3.refs_5_ = bf16[512,2304]{1,0:T(8,128)(2,1)} custom-call(bf16[512,2304]{1,0:T(8,128)(2,1)} %fusion.22.qkv_ref, f32[512,768]{1,0:T(8,128)} %get-tuple-element.58.lt_ref, bf16[512,768]{1,0:T(8,128)(2,1)} %convolution_convert_fusion.2.g_ref), custom_call_target="tpu_custom_call" | custom-call | flops 4026531840 | bytes 7077888 | tf_op jit(solution)/shard_map/attention_backward/pallas_call | solution.py:141
  271.5 6.2 %multiply_reduce_fusion.1 = (f32[768]{0:T(1024)S(1)}, f32[512]{0:T(512)S(1)}, f32[512]{0:T(512)S(1)}, f32[768]{0:T(1024)S(1)}, f32[512,768]{1,0:T(8,128)S(1)}) fusion(f32[512,768]{1,0:T(8,128)} %copy-done.30, f32[512]{0:T(512)S(1)} %add_rsqrt_fusion.2, f32[512]{0:T(512)S(1)} %broadcast_multiply_fusion.14, f32[768]{0:T(1024)S(1)} %reshape.356, ...), kind=kOutput, calls=%fused_computation.39 | convolution fusion | flops 1815868928 | bytes 10634240 | tf_op jit(solution)/shard_map/dot_general | solution.py:25
  278.2 9.5 %fusion.13.refs_4_ = bf16[512,3072]{1,0:T(8,128)(2,1)S(1)} fusion(f32[512,3072]{1,0:T(8,128)} %get-tuple-element.203, f32[3072]{0:T(1024)S(1)} %reshape.358, bf16[512,768]{1,0:T(8,128)(2,1)S(1)} %get-tuple-element.141.refs_4_, bf16[3072,768]{1,0:T(8,128)(2,1)} %pad_maximum_fusion), kind=kOutput, calls=%fused_computation.19 | convolution fusion | flops 2448949248 | bytes 14954496 | tf_op jit(solution)/shard_map/dot_general | solution.py:25
  287.8 3.1 multiply_reduce_fusion.4
  290.9 3.2 fusion.36
  295.8 14.0 %attention_backward.4.refs_4_ = bf16[512,2304]{1,0:T(8,128)(2,1)} custom-call(bf16[512,2304]{1,0:T(8,128)(2,1)} %fusion.21.qkv_ref, f32[512,768]{1,0:T(8,128)} %get-tuple-element.59.lt_ref, bf16[512,768]{1,0:T(8,128)(2,1)} %convolution_convert_fusion.1.g_ref), custom_call_target="tpu_custom_call" | custom-call | flops 4026531840 | bytes 7077888 | tf_op jit(solution)/shard_map/attention_backward/pallas_call | solution.py:141
  309.8 6.2 %multiply_reduce_fusion.2 = (f32[768]{0:T(1024)S(1)}, f32[512]{0:T(512)S(1)}, f32[512]{0:T(512)S(1)}, f32[768]{0:T(1024)S(1)}, f32[512,768]{1,0:T(8,128)S(1)}) fusion(f32[512,768]{1,0:T(8,128)} %copy-done.27, f32[512]{0:T(512)S(1)} %add_rsqrt_fusion.4, f32[512]{0:T(512)S(1)} %broadcast_multiply_fusion.16, f32[768]{0:T(1024)S(1)} %reshape.356, ...), kind=kOutput, calls=%fused_computation.40 | convolution fusion | flops 1815868928 | bytes 10634240 | tf_op jit(solution)/shard_map/dot_general | solution.py:25
  316.5 9.5 %fusion.6.refs_3_ = bf16[512,3072]{1,0:T(8,128)(2,1)S(1)} fusion(f32[512,3072]{1,0:T(8,128)} %get-tuple-element.197, f32[3072]{0:T(1024)S(1)} %reshape.358, bf16[512,768]{1,0:T(8,128)(2,1)S(1)} %get-tuple-element.137.refs_3_, bf16[3072,768]{1,0:T(8,128)(2,1)} %pad_maximum_fusion), kind=kOutput, calls=%fused_computation.12 | convolution fusion | flops 2448949248 | bytes 14954496 | tf_op jit(solution)/shard_map/dot_general | solution.py:25
  326.1 3.1 multiply_reduce_fusion.5
  332.6 13.8 %attention_backward.5.refs_3_ = bf16[512,2304]{1,0:T(8,128)(2,1)} custom-call(bf16[512,2304]{1,0:T(8,128)(2,1)} %fusion.24.qkv_ref, f32[512,768]{1,0:T(8,128)} %get-tuple-element.60.lt_ref, bf16[512,768]{1,0:T(8,128)(2,1)} %convolution_convert_fusion.g_ref), custom_call_target="tpu_custom_call" | custom-call | flops 4026531840 | bytes 7077888 | tf_op jit(solution)/shard_map/attention_backward/pallas_call | solution.py:141
  351.5 9.0 %weight_grad.4 = (bf16[768,9344]{1,0:T(8,128)(2,1)}, f32[1,2304]{1,0:T(1,128)S(1)}) custom-call(bf16[512,768]{1,0:T(8,128)(2,1)S(1)} %copy-done.18, bf16[512,768]{1,0:T(8,128)(2,1)S(1)} %copy-done.12, bf16[512,768]{1,0:T(8,128)(2,1)S(1)} %copy-done.16, bf16[512,2304]{1,0:T(8,128)(2,1)S(1)} %copy-done.23, bf16[512,2304]{1,0:T(8,128)(2,1)} %attention_backward.4.refs_4_, ...), custom_call_target="tpu_custom_call" | custom-call | flops 5435817984 | bytes 12976128 | tf_op jit(solution)/shard_map/weight_grad/pallas_call | solution.py:203
  360.5 3.2 weight_grad.5
  365.6 11.2 %weight_grad.6 = (bf16[768,9344]{1,0:T(8,128)(2,1)}, f32[1,3072]{1,0:T(1,128)S(1)}) custom-call(bf16[512,768]{1,0:T(8,128)(2,1)S(1)} %copy-done.8, bf16[512,768]{1,0:T(8,128)(2,1)S(1)} %copy-done.10, bf16[512,768]{1,0:T(8,128)(2,1)S(1)} %copy-done.14, bf16[512,3072]{1,0:T(8,128)(2,1)S(1)} %copy-done.22, ...), custom_call_target="tpu_custom_call", output_to_operand_aliasing={{0}: (6, {})} | custom-call | flops 7247757312 | bytes 16515072 | tf_op jit(solution)/shard_map/weight_grad/pallas_call | solution.py:203
  376.8 11.1 %weight_grad.7 = (bf16[768,9344]{1,0:T(8,128)(2,1)}, f32[1,768]{1,0:T(1,128)S(1)}) custom-call(bf16[512,3072]{1,0:T(8,128)(2,1)S(1)} %copy-done.20, bf16[512,3072]{1,0:T(8,128)(2,1)} %copy-done.55, bf16[512,3072]{1,0:T(8,128)(2,1)} %copy-done.56, bf16[512,768]{1,0:T(8,128)(2,1)S(1)} %copy-done.6, ...), custom_call_target="tpu_custom_call", output_to_operand_aliasing={{0}: (6, {})} | custom-call | flops 7247757312 | bytes 16515072 | tf_op jit(solution)/shard_map/weight_grad/pallas_call | solution.py:203
  393.4 5.6 add_convert_fusion
  399.0 150.3 %reduce-scatter.4.cloned.1.call-done = bf16[24,9344]{1,0:T(8,128)(2,1)} async-done(((bf16[768,9344]{1,0:T(8,128)(2,1)}), bf16[24,9344]{1,0:T(8,128)(2,1)}) %reduce-scatter.4.cloned.1.call-update) | async-done | bytes 448528
  (291 shorter events, 65.7 us)
Async XLA Ops:
  7.2 117.6 %all-gather.4.cloned.1.call-start = ((), (), s32[]{:S(2)}) async-start(), calls=%async_computation.1 | async-start | bytes 16220160 | tf_op jit(solution)/shard_map/all_gather | solution.py:280
  12.4 536.9 %reduce-scatter.4.cloned.1.call-start = ((), (), s32[]{:S(2)}) async-start(), calls=%async_computation.2 | async-start | bytes 14800896
  127.1 10.2 %copy-start.37 = (f32[32,3072]{0,1:T(8,128)}, f32[32,3072]{0,1:T(8,128)S(1)}, u32[]{:S(2)}) copy-start(f32[32,3072]{0,1:T(8,128)S(1)} %bitcast_convert_fusion) | copy-start | bytes 1179652
  155.1 10.1 %copy-start.38 = (bf16[768,768]{1,0:T(8,128)(2,1)S(1)}, bf16[768,768]{1,0:T(8,128)(2,1)}, u32[]{:S(2)}) copy-start(bf16[768,768]{1,0:T(8,128)(2,1)} %slice.339) | copy-start | bytes 3538948
  167.2 9.6 %copy-start.25 = (f32[512,768]{1,0:T(8,128)}, f32[512,768]{1,0:T(8,128)S(1)}, u32[]{:S(2)}) copy-start(f32[512,768]{1,0:T(8,128)S(1)} %get-tuple-element.195) | copy-start | bytes 4718596
  167.5 9.3 %slice-start.6 = ((s8[4718592]{0:T(1024)(128)(4,1)}), s8[4194304]{0:T(1024)(128)(4,1)S(1)}, s32[]{:S(2)}) async-start(s8[4718592]{0:T(1024)(128)(4,1)} %bitcast.120), calls=%async_computation.9 | async-start | bytes 8388608
  167.8 9.0 %copy-start.7 = (bf16[512,768]{1,0:T(8,128)(2,1)}, bf16[512,768]{1,0:T(8,128)(2,1)S(1)}, u32[]{:S(2)}) copy-start(bf16[512,768]{1,0:T(8,128)(2,1)S(1)} %fusion.28.refs_0_) | copy-start | bytes 2359300
  167.8 9.0 %slice-start.7 = ((s8[4718592]{0:T(1024)(128)(4,1)}), s8[524288]{0:T(1024)(128)(4,1)S(1)}, s32[]{:S(2)}) async-start(s8[4718592]{0:T(1024)(128)(4,1)} %bitcast.120), calls=%async_computation.10 | async-start | bytes 1048576
  179.6 17.2 %copy-start.27 = (f32[512,768]{1,0:T(8,128)}, f32[512,768]{1,0:T(8,128)S(1)}, u32[]{:S(2)}) copy-start(f32[512,768]{1,0:T(8,128)S(1)} %get-tuple-element.199) | copy-start | bytes 4718596
  199.2 88.5 %copy-start.29 = (f32[512,768]{1,0:T(8,128)}, f32[512,768]{1,0:T(8,128)S(1)}, u32[]{:S(2)}) copy-start(f32[512,768]{1,0:T(8,128)S(1)} %get-tuple-element.201) | copy-start | bytes 4718596
  199.6 9.3 %slice-start.8 = ((s8[4718592]{0:T(1024)(128)(4,1)}), s8[4194304]{0:T(1024)(128)(4,1)S(1)}, s32[]{:S(2)}) async-start(s8[4718592]{0:T(1024)(128)(4,1)} %bitcast.122), calls=%async_computation.11 | async-start | bytes 8388608
  199.9 9.0 %copy-start.9 = (bf16[512,768]{1,0:T(8,128)(2,1)}, bf16[512,768]{1,0:T(8,128)(2,1)S(1)}, u32[]{:S(2)}) copy-start(bf16[512,768]{1,0:T(8,128)(2,1)S(1)} %fusion.30.refs_1_) | copy-start | bytes 2359300
  199.9 9.0 %slice-start.9 = ((s8[4718592]{0:T(1024)(128)(4,1)}), s8[524288]{0:T(1024)(128)(4,1)S(1)}, s32[]{:S(2)}) async-start(s8[4718592]{0:T(1024)(128)(4,1)} %bitcast.122), calls=%async_computation.12 | async-start | bytes 1048576
  211.6 16.9 %copy-start.30 = (f32[512,768]{1,0:T(8,128)}, f32[512,768]{1,0:T(8,128)S(1)}, u32[]{:S(2)}) copy-start(f32[512,768]{1,0:T(8,128)S(1)} %get-tuple-element.205) | copy-start | bytes 4718596
  231.3 6.8 %slice-start.10 = ((s8[4718592]{0:T(1024)(128)(4,1)}), s8[4194304]{0:T(1024)(128)(4,1)S(1)}, s32[]{:S(2)}) async-start(s8[4718592]{0:T(1024)(128)(4,1)} %bitcast.124), calls=%async_computation.13 | async-start | bytes 8388608
  231.6 6.4 %slice-start.11 = ((s8[4718592]{0:T(1024)(128)(4,1)}), s8[524288]{0:T(1024)(128)(4,1)S(1)}, s32[]{:S(2)}) async-start(s8[4718592]{0:T(1024)(128)(4,1)} %bitcast.124), calls=%async_computation.14 | async-start | bytes 1048576
  242.9 7.8 %slice-start = ((s8[4718592]{0:T(1024)(128)(4,1)}), s8[4194304]{0:T(1024)(128)(4,1)S(1)}, s32[]{:S(2)}) async-start(s8[4718592]{0:T(1024)(128)(4,1)} %bitcast.111), calls=%async_computation.3 | async-start | bytes 8388608
  277.7 10.0 %slice-start.2 = ((s8[4718592]{0:T(1024)(128)(4,1)}), s8[4194304]{0:T(1024)(128)(4,1)S(1)}, s32[]{:S(2)}) async-start(s8[4718592]{0:T(1024)(128)(4,1)} %bitcast.114), calls=%async_computation.5 | async-start | bytes 8388608
  278.2 9.5 %copy-start.3 = (bf16[512,768]{1,0:T(8,128)(2,1)}, bf16[512,768]{1,0:T(8,128)(2,1)S(1)}, u32[]{:S(2)}) copy-start(bf16[512,768]{1,0:T(8,128)(2,1)S(1)} %get-tuple-element.141.refs_4_) | copy-start | bytes 2359300
  278.2 9.5 %slice-start.3 = ((s8[4718592]{0:T(1024)(128)(4,1)}), s8[524288]{0:T(1024)(128)(4,1)S(1)}, s32[]{:S(2)}) async-start(s8[4718592]{0:T(1024)(128)(4,1)} %bitcast.114), calls=%async_computation.6 | async-start | bytes 1048576
  316.0 10.0 %slice-start.4 = ((s8[4718592]{0:T(1024)(128)(4,1)}), s8[4194304]{0:T(1024)(128)(4,1)S(1)}, s32[]{:S(2)}) async-start(s8[4718592]{0:T(1024)(128)(4,1)} %bitcast.117), calls=%async_computation.7 | async-start | bytes 8388608
  316.5 9.5 %copy-start.5 = (bf16[512,768]{1,0:T(8,128)(2,1)}, bf16[512,768]{1,0:T(8,128)(2,1)S(1)}, u32[]{:S(2)}) copy-start(bf16[512,768]{1,0:T(8,128)(2,1)S(1)} %get-tuple-element.137.refs_3_) | copy-start | bytes 2359300
  316.5 9.5 %copy-start.26 = (f32[512,768]{1,0:T(8,128)S(1)}, f32[512,768]{1,0:T(8,128)}, u32[]{:S(2)}) copy-start(f32[512,768]{1,0:T(8,128)} %copy-done.25) | copy-start | bytes 4718596
  316.5 9.5 %slice-start.5 = ((s8[4718592]{0:T(1024)(128)(4,1)}), s8[524288]{0:T(1024)(128)(4,1)S(1)}, s32[]{:S(2)}) async-start(s8[4718592]{0:T(1024)(128)(4,1)} %bitcast.117), calls=%async_computation.8 | async-start | bytes 1048576
  351.4 9.1 %copy-start = (bf16[512,768]{1,0:T(8,128)(2,1)S(1)}, bf16[512,768]{1,0:T(8,128)(2,1)}, u32[]{:S(2)}) copy-start(bf16[512,768]{1,0:T(8,128)(2,1)} %get-tuple-element.45.refs_0_) | copy-start | bytes 2359300
  351.4 9.1 %copy-start.1 = (bf16[512,768]{1,0:T(8,128)(2,1)S(1)}, bf16[512,768]{1,0:T(8,128)(2,1)}, u32[]{:S(2)}) copy-start(bf16[512,768]{1,0:T(8,128)(2,1)} %get-tuple-element.56.refs_1_) | copy-start | bytes 2359300
  351.4 9.1 %copy-start.2 = (bf16[512,768]{1,0:T(8,128)(2,1)S(1)}, bf16[512,768]{1,0:T(8,128)(2,1)}, u32[]{:S(2)}) copy-start(bf16[512,768]{1,0:T(8,128)(2,1)} %get-tuple-element.57.refs_2_) | copy-start | bytes 2359300
  365.6 11.2 %copy-start.4 = (bf16[512,768]{1,0:T(8,128)(2,1)S(1)}, bf16[512,768]{1,0:T(8,128)(2,1)}, u32[]{:S(2)}) copy-start(bf16[512,768]{1,0:T(8,128)(2,1)} %copy-done.3) | copy-start | bytes 2359300
  365.6 11.2 %copy-start.6 = (bf16[512,768]{1,0:T(8,128)(2,1)S(1)}, bf16[512,768]{1,0:T(8,128)(2,1)}, u32[]{:S(2)}) copy-start(bf16[512,768]{1,0:T(8,128)(2,1)} %copy-done.5) | copy-start | bytes 2359300
  365.6 11.2 %copy-start.20 = (bf16[512,3072]{1,0:T(8,128)(2,1)S(1)}, bf16[512,3072]{1,0:T(8,128)(2,1)}, u32[]{:S(2)}) copy-start(bf16[512,3072]{1,0:T(8,128)(2,1)} %copy-done.19) | copy-start | bytes 9437188
  376.8 11.2 %copy-start.54 = (bf16[768]{0:T(1024)(128)(2,1)S(1)}, bf16[768]{0:T(1024)(128)(2,1)}, u32[]{:S(2)}) copy-start(bf16[768]{0:T(1024)(128)(2,1)} %custom-call.4) | copy-start | bytes 4612
  376.8 12.3 %copy-start.53 = (bf16[768]{0:T(1024)(128)(2,1)S(1)}, bf16[768]{0:T(1024)(128)(2,1)}, u32[]{:S(2)}) copy-start(bf16[768]{0:T(1024)(128)(2,1)} %custom-call.3) | copy-start | bytes 4612
  (42 other events, 117.5 us)
Sparse Core Ops, SparseCore 0:
  12.5 112.2 all-gather.3
  391.9 157.4 reduce-scatter.3

commit v7 on v5

--- a/solution.py
+++ b/solution.py
@@ -256,52 +256,45 @@
     (qw, qb, kw, vw, vb, ow, ob, g1, s1, iw, ib, uw, ub, g2, s2) = weights
     rows, width = qw.shape
     wide = iw.shape[1]
-    vectors = None
-    at = 0
-    for piece in (qb, vb, ob, g1, s1, ub, g2, s2, ib):
-        placed = jnp.pad(piece, (at, wide - at - piece.shape[0]))
-        vectors = placed if vectors is None else vectors + placed
-        at += piece.shape[0]
-    vectors = vectors[None, :]
+    columns = jnp.stack([qb, vb, ob, g1, s1, ub, g2, s2], axis=1)
+    columns = jnp.concatenate([columns, ib.reshape(rows, -1)], axis=1)
+    columns = jnp.pad(columns, ((0, 0), (0, PAIR - columns.shape[1])))
     return jnp.concatenate(
-        [
-            jnp.concatenate([interleave_qkv(qw, kw, vw), ow], axis=1),
-            to_hidden_order(iw),
-            uw.reshape(rows, wide),
-            vectors,
-        ],
-        axis=0,
+        [interleave_qkv(qw, kw, vw), ow, to_hidden_order(iw), uw.reshape(rows, wide), columns],
+        axis=1,
     )
 
 
 def gather_weights(weights):
     rows, width = weights[0].shape
-    ff_rows, wide = weights[11].shape[0], weights[9].shape[1]
-    packed = lax.all_gather(pack_weights(weights), AXES, axis=0, tiled=False)
-    shards = packed.shape[0]
-    attn = packed[:, 0:rows].reshape(shards * rows, wide)
-    inner = packed[:, rows : 2 * rows].reshape(shards * rows, wide)
-    outer_rows = packed[:, 2 * rows : 3 * rows].reshape(shards * rows, wide)
+    wide = weights[9].shape[1]
+    packed = lax.all_gather(pack_weights(weights), AXES, axis=0, tiled=True)
+    full = packed.shape[0]
+    shards = full // rows
+    three = 3 * width
+    at = 0
+    pieces = []
+    for count in (three, width, wide, wide, PAIR):
+        pieces.append(packed[:, at : at + count])
+        at += count
+    qkv, out, inner, outer_rows, cols = pieces
     groups = wide // width
     outer = jnp.concatenate(
         [outer_rows[:, c * width : (c + 1) * width] for c in range(groups)], axis=0
     )
-    vectors = packed[:, 3 * rows, :].astype(jnp.float32)
-    found = []
-    at = 0
-    for count in (rows,) * 8 + (ff_rows,):
-        found.append(vectors[:, at : at + count].reshape(-1))
-        at += count
-    (qb, vb, ob, g1, s1, ub, g2, s2, ib) = found
+    outer = lax.optimization_barrier(outer)
+    cols = cols.astype(jnp.float32)
+    (qb, vb, ob, g1, s1, ub, g2, s2) = [cols[:, i] for i in range(8)]
+    ib = cols[:, 8 : 8 + groups].reshape(shards, rows, groups)
     return dict(
-        qkv=attn[:, : 3 * width],
+        qkv=qkv,
         qkv_bias=interleave_qkv(qb, jnp.zeros_like(qb), vb),
-        out=attn[:, 3 * width :],
+        out=out,
         out_bias=ob,
         g1=g1,
         s1=s1,
         inner=inner,
-        inner_bias=ib.reshape(shards, rows, groups).transpose(2, 0, 1).reshape(-1),
+        inner_bias=ib.transpose(2, 0, 1).reshape(-1),
         outer=outer,
         outer_bias=ub,
         g2=g2,

time: 583 us -> 563 us (0.966)
  local copies, waits for them, and re-layouts: 43.1 us -> 32.6 us
  waiting for transfers between devices: 263 us -> 257 us
    dot_general x12, matrix products: 46.9 us -> 58.9 us  [product(): return jnp.dot(left, right, preferred_element_type=jnp.float32)]
    dot_general x12, matrix products: 83.1 us -> 71.5 us  [product_nt(): return lax.dot_general(left, right, NT, preferred_element_type=jnp.float32)]
    slice x12 -> x2, local copies, waits for them, and re-layouts: 11.8 us -> 1.77 us  [the longest x1 1.61 us: gather_weights(): qb, vb, ob, g1, s1, ub, g2, s2 = [cols[:, i] for i in range(8)]]
    all_gather x1, waiting for transfers between devices: 112 us -> 106 us  [gather_weights(): packed = lax.all_gather(pack_weights(weights), AXES, axis=0, tiled=True)]
    unnamed x191 -> x150, local copies, waits for them, and re-layouts: 20.8 us -> 17.4 us
where the time goes in v7:
time: 563 us; the launch traced here: 558 us
  waiting for transfers between devices  257 us (46%)
  matrix products  130 us (23%)
  Pallas kernels  106 us (19%)
  local copies, waits for them, and re-layouts  32.6 us (6%)
  other arithmetic  16.1 us (3%)
  between operations  15.4 us (3%)
    unnamed x3, waiting for transfers between devices  151 us
    all_gather x1, waiting for transfers between devices, gather_weights(): packed = lax.all_gather(pack_weights(weights), AXES, axis=0, tiled=True)  106 us
    dot_general x12, matrix products, product_nt(): return lax.dot_general(left, right, NT, preferred_element_type=jnp.float32)  71.5 us
    dot_general x12, matrix products, product(): return jnp.dot(left, right, preferred_element_type=jnp.float32)  58.9 us
    pallas_call x3, Pallas kernels, attention_backward(): pl.pallas_call(attention_backward_kernel, grid=grid, in_specs=[triple, pa...  41.2 us
    pallas_call x4, Pallas kernels, weight_grad(): pl.pallas_call(kernel, grid=grid, in_specs=in_specs, out_specs=[pl.BlockS...  34.8 us
    pallas_call x3, Pallas kernels, attention_forward(): pl.pallas_call(attention_forward_kernel, grid=grid, in_specs=[pl.BlockSpe...  30.3 us
    unnamed x150, local copies, waits for them, and re-layouts  17.4 us
  transfers between devices with their start and end apart: 2, of which 2 were waited for; matrix products, arithmetic and copies ran while one was open for 1% of the time, Pallas kernels for 0%

profile of v7, /device:TPU:0, one launch (start us, length us, event | category | flops | bytes accessed | tf_op | source)
XLA Modules:
  0.0 557.6 jit_solution(15155894405589780552)
XLA Ops:
  14.2 106.0 %all-gather.2.cloned.1.call-done = bf16[768,9344]{1,0:T(8,128)(2,1)} async-done(((bf16[24,9344]{1,0:T(8,128)(2,1)}), bf16[768,9344]{1,0:T(8,128)(2,1)}) %all-gather.2.cloned.1.call-update) | async-done | bytes 14352400 | tf_op jit(solution)/shard_map/all_gather | solution.py:271
  123.4 5.5 fusion.24.qkv_ref
  128.9 10.1 %attention_forward.3 = (bf16[512,768]{1,0:T(8,128)(2,1)}, f32[512,768]{1,0:T(8,128)}) custom-call(bf16[512,2304]{1,0:T(8,128)(2,1)} %fusion.24.qkv_ref), custom_call_target="tpu_custom_call" | custom-call | flops 1610612736 | bytes 4718592 | tf_op jit(solution)/shard_map/attention_forward/pallas_call | solution.py:116
  141.7 2.9 fusion.83
  145.5 10.6 %multiply_convert_fusion.2 = (bf16[512,3072]{1,0:T(8,128)(2,1)S(1)}, f32[512,3072]{1,0:T(8,128)}) fusion(f32[3072]{0:T(1024)S(1)} %add.359, bf16[512,768]{1,0:T(8,128)(2,1)S(1)} %fusion.64.refs_0_, bf16[768,9344]{1,0:T(8,128)(2,1)} %all-gather.2.cloned.1.call-done), kind=kOutput, calls=%fused_computation.29 | convolution fusion | flops 2431647744 | bytes 14954496 | tf_op jit(solution)/shard_map/dot_general | solution.py:21
  159.5 5.5 fusion.21.qkv_ref
  165.9 10.2 %attention_forward.4 = (bf16[512,768]{1,0:T(8,128)(2,1)}, f32[512,768]{1,0:T(8,128)}) custom-call(bf16[512,2304]{1,0:T(8,128)(2,1)} %fusion.21.qkv_ref), custom_call_target="tpu_custom_call" | custom-call | flops 1610612736 | bytes 4718592 | tf_op jit(solution)/shard_map/attention_forward/pallas_call | solution.py:116
  179.2 9.6 %multiply_convert_fusion.1 = (bf16[512,3072]{1,0:T(8,128)(2,1)S(1)}, f32[512,3072]{1,0:T(8,128)}) fusion(f32[3072]{0:T(1024)S(1)} %add.359, bf16[512,768]{1,0:T(8,128)(2,1)S(1)} %fusion.66.refs_1_, bf16[768,9344]{1,0:T(8,128)(2,1)} %all-gather.2.cloned.1.call-done), kind=kOutput, calls=%fused_computation.28 | convolution fusion | flops 2431647744 | bytes 14954496 | tf_op jit(solution)/shard_map/dot_general | solution.py:21
  192.3 5.4 fusion.22.qkv_ref
  198.6 10.0 %attention_forward.5 = (bf16[512,768]{1,0:T(8,128)(2,1)}, f32[512,768]{1,0:T(8,128)}) custom-call(bf16[512,2304]{1,0:T(8,128)(2,1)} %fusion.22.qkv_ref), custom_call_target="tpu_custom_call" | custom-call | flops 1610612736 | bytes 4718592 | tf_op jit(solution)/shard_map/attention_forward/pallas_call | solution.py:116
  211.7 6.7 %multiply_convert_fusion = (bf16[512,3072]{1,0:T(8,128)(2,1)S(1)}, f32[512,3072]{1,0:T(8,128)S(1)}) fusion(f32[3072]{0:T(1024)S(1)} %add.359, bf16[512,768]{1,0:T(8,128)(2,1)S(1)} %fusion.68.refs_2_, bf16[768,9344]{1,0:T(8,128)(2,1)} %all-gather.2.cloned.1.call-done), kind=kOutput, calls=%fused_computation.27 | convolution fusion | flops 2431647744 | bytes 14954496 | tf_op jit(solution)/shard_map/dot_general | solution.py:21
  224.9 6.2 %fusion.20.refs_5_ = bf16[512,3072]{1,0:T(8,128)(2,1)S(1)} fusion(f32[512,3072]{1,0:T(8,128)S(1)} %get-tuple-element.199, f32[3072]{0:T(1024)S(1)} %add.359, bf16[512,768]{1,0:T(8,128)(2,1)S(1)} %get-tuple-element.150.refs_5_, bf16[3072,768]{1,0:T(8,128)(2,1)S(1)} %bitcast.91), kind=kOutput, calls=%fused_computation.26 | convolution fusion | flops 2448949248 | bytes 14954496 | tf_op jit(solution)/shard_map/dot_general | solution.py:25
  231.2 6.9 %multiply_reduce_fusion.3 = (f32[768]{0:T(1024)S(1)}, f32[512]{0:T(512)S(1)}, f32[512]{0:T(512)S(1)}, f32[768]{0:T(1024)S(1)}, f32[512,768]{1,0:T(8,128)S(1)}) fusion(f32[512,768]{1,0:T(8,128)S(1)} %get-tuple-element.197, f32[512]{0:T(512)S(1)} %add_rsqrt_fusion.1, f32[512]{0:T(512)S(1)} %broadcast_multiply_fusion.13, f32[768]{0:T(1024)S(1)} %get-tuple-element.132, ...), kind=kOutput, calls=%fused_computation.53 | convolution fusion | flops 2423387648 | bytes 13400064 | tf_op jit(solution)/shard_map/dot_general | solution.py:25
  239.8 3.0 convolution_convert_fusion.2.g_ref
  242.7 13.8 %attention_backward.3.refs_5_ = bf16[512,2304]{1,0:T(8,128)(2,1)} custom-call(bf16[512,2304]{1,0:T(8,128)(2,1)} %fusion.22.qkv_ref, f32[512,768]{1,0:T(8,128)} %get-tuple-element.34.lt_ref, bf16[512,768]{1,0:T(8,128)(2,1)} %convolution_convert_fusion.2.g_ref), custom_call_target="tpu_custom_call" | custom-call | flops 4026531840 | bytes 7077888 | tf_op jit(solution)/shard_map/attention_backward/pallas_call | solution.py:141
  256.5 6.2 %multiply_reduce_fusion.1 = (f32[768]{0:T(1024)S(1)}, f32[512]{0:T(512)S(1)}, f32[512]{0:T(512)S(1)}, f32[768]{0:T(1024)S(1)}, f32[512,768]{1,0:T(8,128)S(1)}) fusion(f32[512,768]{1,0:T(8,128)} %copy-done.30, f32[512]{0:T(512)S(1)} %add_rsqrt_fusion.2, f32[512]{0:T(512)S(1)} %broadcast_multiply_fusion.14, f32[768]{0:T(1024)S(1)} %get-tuple-element.128, ...), kind=kOutput, calls=%fused_computation.51 | convolution fusion | flops 1815868928 | bytes 10634240 | tf_op jit(solution)/shard_map/dot_general | solution.py:25
  263.2 9.2 %fusion.13.refs_4_ = bf16[512,3072]{1,0:T(8,128)(2,1)S(1)} fusion(f32[512,3072]{1,0:T(8,128)} %get-tuple-element.193, f32[3072]{0:T(1024)S(1)} %add.359, bf16[512,768]{1,0:T(8,128)(2,1)S(1)} %get-tuple-element.142.refs_4_, bf16[3072,768]{1,0:T(8,128)(2,1)} %copy-done.32), kind=kOutput, calls=%fused_computation.19 | convolution fusion | flops 2448949248 | bytes 14954496 | tf_op jit(solution)/shard_map/dot_general | solution.py:25
  272.4 6.6 %multiply_reduce_fusion.4 = (f32[768]{0:T(1024)S(1)}, f32[512]{0:T(512)S(1)}, f32[512]{0:T(512)S(1)}, f32[768]{0:T(1024)S(1)}, f32[512,768]{1,0:T(8,128)S(1)}) fusion(f32[512,768]{1,0:T(8,128)S(1)} %get-tuple-element.191, f32[512]{0:T(512)S(1)} %add_rsqrt_fusion.3, f32[512]{0:T(512)S(1)} %broadcast_multiply_fusion.15, f32[768]{0:T(1024)S(1)} %get-tuple-element.132, ...), kind=kOutput, calls=%fused_computation.54 | convolution fusion | flops 2419848704 | bytes 12600320 | tf_op jit(solution)/shard_map/dot_general | solution.py:25
  279.0 3.1 fusion.80
  282.1 3.0 convolution_convert_fusion.1.g_ref
  285.1 13.8 %attention_backward.4.refs_4_ = bf16[512,2304]{1,0:T(8,128)(2,1)} custom-call(bf16[512,2304]{1,0:T(8,128)(2,1)} %fusion.21.qkv_ref, f32[512,768]{1,0:T(8,128)} %get-tuple-element.35.lt_ref, bf16[512,768]{1,0:T(8,128)(2,1)} %convolution_convert_fusion.1.g_ref), custom_call_target="tpu_custom_call" | custom-call | flops 4026531840 | bytes 7077888 | tf_op jit(solution)/shard_map/attention_backward/pallas_call | solution.py:141
  299.0 6.2 %multiply_reduce_fusion.2 = (f32[768]{0:T(1024)S(1)}, f32[512]{0:T(512)S(1)}, f32[512]{0:T(512)S(1)}, f32[768]{0:T(1024)S(1)}, f32[512,768]{1,0:T(8,128)S(1)}) fusion(f32[512,768]{1,0:T(8,128)} %copy-done.27, f32[512]{0:T(512)S(1)} %add_rsqrt_fusion.4, f32[512]{0:T(512)S(1)} %broadcast_multiply_fusion.16, f32[768]{0:T(1024)S(1)} %get-tuple-element.128, ...), kind=kOutput, calls=%fused_computation.52 | convolution fusion | flops 1815868928 | bytes 10634240 | tf_op jit(solution)/shard_map/dot_general | solution.py:25
  305.7 9.2 %fusion.6.refs_3_ = bf16[512,3072]{1,0:T(8,128)(2,1)S(1)} fusion(f32[512,3072]{1,0:T(8,128)} %get-tuple-element.187, f32[3072]{0:T(1024)S(1)} %add.359, bf16[512,768]{1,0:T(8,128)(2,1)S(1)} %get-tuple-element.138.refs_3_, bf16[3072,768]{1,0:T(8,128)(2,1)} %copy-done.32), kind=kOutput, calls=%fused_computation.12 | convolution fusion | flops 2448949248 | bytes 14954496 | tf_op jit(solution)/shard_map/dot_general | solution.py:25
  314.9 6.6 %multiply_reduce_fusion.5 = (f32[768]{0:T(1024)S(1)}, f32[512]{0:T(512)S(1)}, f32[512]{0:T(512)S(1)}, f32[768]{0:T(1024)S(1)}, f32[512,768]{1,0:T(8,128)S(1)}) fusion(f32[512,768]{1,0:T(8,128)S(1)} %copy-done.26, f32[512]{0:T(512)S(1)} %add_rsqrt_fusion.5, f32[512]{0:T(512)S(1)} %broadcast_multiply_fusion.17, f32[768]{0:T(1024)S(1)} %get-tuple-element.132, ...), kind=kOutput, calls=%fused_computation.55 | convolution fusion | flops 2419848704 | bytes 12600320 | tf_op jit(solution)/shard_map/dot_general | solution.py:25
  323.2 3.0 convolution_convert_fusion.g_ref
  326.2 13.6 %attention_backward.5.refs_3_ = bf16[512,2304]{1,0:T(8,128)(2,1)} custom-call(bf16[512,2304]{1,0:T(8,128)(2,1)} %fusion.24.qkv_ref, f32[512,768]{1,0:T(8,128)} %get-tuple-element.36.lt_ref, bf16[512,768]{1,0:T(8,128)(2,1)} %convolution_convert_fusion.g_ref), custom_call_target="tpu_custom_call" | custom-call | flops 4026531840 | bytes 7077888 | tf_op jit(solution)/shard_map/attention_backward/pallas_call | solution.py:141
  344.9 9.3 %weight_grad.4 = (bf16[768,9344]{1,0:T(8,128)(2,1)}, f32[1,2304]{1,0:T(1,128)S(1)}) custom-call(bf16[512,768]{1,0:T(8,128)(2,1)S(1)} %copy-done.18, bf16[512,768]{1,0:T(8,128)(2,1)S(1)} %copy-done.12, bf16[512,768]{1,0:T(8,128)(2,1)S(1)} %copy-done.16, bf16[512,2304]{1,0:T(8,128)(2,1)S(1)} %copy-done.23, bf16[512,2304]{1,0:T(8,128)(2,1)} %attention_backward.4.refs_4_, ...), custom_call_target="tpu_custom_call" | custom-call | flops 5435817984 | bytes 12976128 | tf_op jit(solution)/shard_map/weight_grad/pallas_call | solution.py:203
  354.2 3.2 weight_grad.5
  359.3 11.3 %weight_grad.6 = (bf16[768,9344]{1,0:T(8,128)(2,1)}, f32[1,3072]{1,0:T(1,128)S(1)}) custom-call(bf16[512,768]{1,0:T(8,128)(2,1)S(1)} %copy-done.8, bf16[512,768]{1,0:T(8,128)(2,1)S(1)} %copy-done.10, bf16[512,768]{1,0:T(8,128)(2,1)S(1)} %copy-done.14, bf16[512,3072]{1,0:T(8,128)(2,1)S(1)} %copy-done.22, ...), custom_call_target="tpu_custom_call", output_to_operand_aliasing={{0}: (6, {})} | custom-call | flops 7247757312 | bytes 16515072 | tf_op jit(solution)/shard_map/weight_grad/pallas_call | solution.py:203
  370.6 11.1 %weight_grad.7 = (bf16[768,9344]{1,0:T(8,128)(2,1)}, f32[1,768]{1,0:T(1,128)S(1)}) custom-call(bf16[512,3072]{1,0:T(8,128)(2,1)S(1)} %copy-done.20, bf16[512,3072]{1,0:T(8,128)(2,1)} %copy-done.56, bf16[512,3072]{1,0:T(8,128)(2,1)} %copy-done.57, bf16[512,768]{1,0:T(8,128)(2,1)S(1)} %copy-done.6, ...), custom_call_target="tpu_custom_call", output_to_operand_aliasing={{0}: (6, {})} | custom-call | flops 7247757312 | bytes 16515072 | tf_op jit(solution)/shard_map/weight_grad/pallas_call | solution.py:203
  387.4 5.5 add_convert_fusion
  392.9 150.7 %reduce-scatter.4.cloned.1.call-done = bf16[24,9344]{1,0:T(8,128)(2,1)} async-done(((bf16[768,9344]{1,0:T(8,128)(2,1)}), bf16[24,9344]{1,0:T(8,128)(2,1)}) %reduce-scatter.4.cloned.1.call-update) | async-done | bytes 448528
  (263 shorter events, 58.5 us)
Async XLA Ops:
  7.2 113.0 %all-gather.2.cloned.1.call-start = ((), (), s32[]{:S(2)}) async-start(), calls=%async_computation.1 | async-start | bytes 14800896 | tf_op jit(solution)/shard_map/all_gather | solution.py:271
  14.0 529.6 %reduce-scatter.4.cloned.1.call-start = ((), (), s32[]{:S(2)}) async-start(), calls=%async_computation.2 | async-start | bytes 14800896
  141.4 14.7 %copy-start.25 = (f32[512,768]{1,0:T(8,128)}, f32[512,768]{1,0:T(8,128)S(1)}, u32[]{:S(2)}) copy-start(f32[512,768]{1,0:T(8,128)S(1)} %get-tuple-element.185) | copy-start | bytes 4718596
  145.1 10.9 %copy-start.32 = (bf16[3072,768]{1,0:T(8,128)(2,1)}, bf16[3072,768]{1,0:T(8,128)(2,1)S(1)}, u32[]{:S(2)}) copy-start(bf16[3072,768]{1,0:T(8,128)(2,1)S(1)} %pad_maximum_fusion) | copy-start | bytes 14155780
  145.5 10.6 %copy-start.7 = (bf16[512,768]{1,0:T(8,128)(2,1)}, bf16[512,768]{1,0:T(8,128)(2,1)S(1)}, u32[]{:S(2)}) copy-start(bf16[512,768]{1,0:T(8,128)(2,1)S(1)} %fusion.64.refs_0_) | copy-start | bytes 2359300
  158.9 17.2 %copy-start.27 = (f32[512,768]{1,0:T(8,128)}, f32[512,768]{1,0:T(8,128)S(1)}, u32[]{:S(2)}) copy-start(f32[512,768]{1,0:T(8,128)S(1)} %get-tuple-element.189) | copy-start | bytes 4718596
  178.6 93.9 %copy-start.29 = (f32[512,768]{1,0:T(8,128)}, f32[512,768]{1,0:T(8,128)S(1)}, u32[]{:S(2)}) copy-start(f32[512,768]{1,0:T(8,128)S(1)} %get-tuple-element.191) | copy-start | bytes 4718596
  178.9 9.9 %slice-start = ((s8[4718592]{0:T(1024)(128)(4,1)}), s8[4194304]{0:T(1024)(128)(4,1)S(1)}, s32[]{:S(2)}) async-start(s8[4718592]{0:T(1024)(128)(4,1)} %bitcast.88), calls=%async_computation.3 | async-start | bytes 8388608
  179.2 9.6 %copy-start.9 = (bf16[512,768]{1,0:T(8,128)(2,1)}, bf16[512,768]{1,0:T(8,128)(2,1)S(1)}, u32[]{:S(2)}) copy-start(bf16[512,768]{1,0:T(8,128)(2,1)S(1)} %fusion.66.refs_1_) | copy-start | bytes 2359300
  179.2 9.6 %slice-start.1 = ((s8[4718592]{0:T(1024)(128)(4,1)}), s8[524288]{0:T(1024)(128)(4,1)S(1)}, s32[]{:S(2)}) async-start(s8[4718592]{0:T(1024)(128)(4,1)} %bitcast.88), calls=%async_computation.4 | async-start | bytes 1048576
  191.6 17.0 %copy-start.30 = (f32[512,768]{1,0:T(8,128)}, f32[512,768]{1,0:T(8,128)S(1)}, u32[]{:S(2)}) copy-start(f32[512,768]{1,0:T(8,128)S(1)} %get-tuple-element.195) | copy-start | bytes 4718596
  211.4 7.1 %slice-start.2 = ((s8[4718592]{0:T(1024)(128)(4,1)}), s8[4194304]{0:T(1024)(128)(4,1)S(1)}, s32[]{:S(2)}) async-start(s8[4718592]{0:T(1024)(128)(4,1)} %bitcast.90), calls=%async_computation.5 | async-start | bytes 8388608
  211.7 6.8 %copy-start.13 = (bf16[512,768]{1,0:T(8,128)(2,1)}, bf16[512,768]{1,0:T(8,128)(2,1)S(1)}, u32[]{:S(2)}) copy-start(bf16[512,768]{1,0:T(8,128)(2,1)S(1)} %fusion.68.refs_2_) | copy-start | bytes 2359300
  211.7 6.8 %slice-start.3 = ((s8[4718592]{0:T(1024)(128)(4,1)}), s8[524288]{0:T(1024)(128)(4,1)S(1)}, s32[]{:S(2)}) async-start(s8[4718592]{0:T(1024)(128)(4,1)} %bitcast.90), calls=%async_computation.6 | async-start | bytes 1048576
  231.2 6.9 %copy-start.58 = (bf16[512,3072]{1,0:T(8,128)(2,1)}, bf16[512,3072]{1,0:T(8,128)(2,1)S(1)}, u32[]{:S(2)}) copy-start(bf16[512,3072]{1,0:T(8,128)(2,1)S(1)} %fusion.20.refs_5_) | copy-start | bytes 9437188
  256.5 6.2 %copy-start.31 = (f32[512,768]{1,0:T(8,128)S(1)}, f32[512,768]{1,0:T(8,128)}, u32[]{:S(2)}) copy-start(f32[512,768]{1,0:T(8,128)} %copy-done.30) | copy-start | bytes 4718596
  263.2 9.2 %copy-start.3 = (bf16[512,768]{1,0:T(8,128)(2,1)}, bf16[512,768]{1,0:T(8,128)(2,1)S(1)}, u32[]{:S(2)}) copy-start(bf16[512,768]{1,0:T(8,128)(2,1)S(1)} %get-tuple-element.142.refs_4_) | copy-start | bytes 2359300
  272.4 6.6 %copy-start.59 = (bf16[512,3072]{1,0:T(8,128)(2,1)}, bf16[512,3072]{1,0:T(8,128)(2,1)S(1)}, u32[]{:S(2)}) copy-start(bf16[512,3072]{1,0:T(8,128)(2,1)S(1)} %fusion.13.refs_4_) | copy-start | bytes 9437188
  298.9 6.2 %copy-start.28 = (f32[512,768]{1,0:T(8,128)S(1)}, f32[512,768]{1,0:T(8,128)}, u32[]{:S(2)}) copy-start(f32[512,768]{1,0:T(8,128)} %copy-done.27) | copy-start | bytes 4718596
  305.6 9.2 %copy-start.5 = (bf16[512,768]{1,0:T(8,128)(2,1)}, bf16[512,768]{1,0:T(8,128)(2,1)S(1)}, u32[]{:S(2)}) copy-start(bf16[512,768]{1,0:T(8,128)(2,1)S(1)} %get-tuple-element.138.refs_3_) | copy-start | bytes 2359300
  305.7 9.2 %copy-start.26 = (f32[512,768]{1,0:T(8,128)S(1)}, f32[512,768]{1,0:T(8,128)}, u32[]{:S(2)}) copy-start(f32[512,768]{1,0:T(8,128)} %copy-done.25) | copy-start | bytes 4718596
  314.9 6.6 %copy-start.21 = (bf16[512,3072]{1,0:T(8,128)(2,1)}, bf16[512,3072]{1,0:T(8,128)(2,1)S(1)}, u32[]{:S(2)}) copy-start(bf16[512,3072]{1,0:T(8,128)(2,1)S(1)} %fusion.6.refs_3_) | copy-start | bytes 9437188
  344.9 9.3 %copy-start = (bf16[512,768]{1,0:T(8,128)(2,1)S(1)}, bf16[512,768]{1,0:T(8,128)(2,1)}, u32[]{:S(2)}) copy-start(bf16[512,768]{1,0:T(8,128)(2,1)} %get-tuple-element.31.refs_0_) | copy-start | bytes 2359300
  344.9 9.3 %copy-start.1 = (bf16[512,768]{1,0:T(8,128)(2,1)S(1)}, bf16[512,768]{1,0:T(8,128)(2,1)}, u32[]{:S(2)}) copy-start(bf16[512,768]{1,0:T(8,128)(2,1)} %get-tuple-element.32.refs_1_) | copy-start | bytes 2359300
  344.9 9.3 %copy-start.2 = (bf16[512,768]{1,0:T(8,128)(2,1)S(1)}, bf16[512,768]{1,0:T(8,128)(2,1)}, u32[]{:S(2)}) copy-start(bf16[512,768]{1,0:T(8,128)(2,1)} %get-tuple-element.33.refs_2_) | copy-start | bytes 2359300
  354.2 3.2 copy-start.8
  354.2 3.2 copy-start.10
  359.3 11.3 %copy-start.4 = (bf16[512,768]{1,0:T(8,128)(2,1)S(1)}, bf16[512,768]{1,0:T(8,128)(2,1)}, u32[]{:S(2)}) copy-start(bf16[512,768]{1,0:T(8,128)(2,1)} %copy-done.3) | copy-start | bytes 2359300
  359.3 11.3 %copy-start.6 = (bf16[512,768]{1,0:T(8,128)(2,1)S(1)}, bf16[512,768]{1,0:T(8,128)(2,1)}, u32[]{:S(2)}) copy-start(bf16[512,768]{1,0:T(8,128)(2,1)} %copy-done.5) | copy-start | bytes 2359300
  359.3 11.3 %copy-start.20 = (bf16[512,3072]{1,0:T(8,128)(2,1)S(1)}, bf16[512,3072]{1,0:T(8,128)(2,1)}, u32[]{:S(2)}) copy-start(bf16[512,3072]{1,0:T(8,128)(2,1)} %copy-done.19) | copy-start | bytes 9437188
  370.6 11.1 %copy-start.46 = (bf16[768]{0:T(1024)(128)(2,1)S(1)}, bf16[768]{0:T(1024)(128)(2,1)}, u32[]{:S(2)}) copy-start(bf16[768]{0:T(1024)(128)(2,1)} %custom-call.4) | copy-start | bytes 4612
  370.6 12.3 %copy-start.45 = (bf16[768]{0:T(1024)(128)(2,1)S(1)}, bf16[768]{0:T(1024)(128)(2,1)}, u32[]{:S(2)}) copy-start(bf16[768]{0:T(1024)(128)(2,1)} %custom-call.3) | copy-start | bytes 4612
  (34 other events, 70.9 us)
Sparse Core Ops, SparseCore 0:
  14.2 105.9 all-gather.1
  385.9 157.6 reduce-scatter.3

commit v8 on v7

--- a/solution.py
+++ b/solution.py
@@ -80,23 +80,20 @@
     k = qkv_ref[:, PAIR : 2 * PAIR]
     v = qkv_ref[:, 2 * PAIR : 3 * PAIR]
     g = g_ref[...]
-    lt_all = lt_ref[...]
+    lt_t = lt_ref[...].T
     masks = _head_masks(q.shape)
     zero = jnp.zeros_like(q)
     dq = dk = dv = None
-    for mask in masks:
-        scores = product_nt(jnp.where(mask, q, zero), k) * scale
-        lt = jnp.max(jnp.where(mask, lt_all, -jnp.inf), axis=-1, keepdims=True)
-        probs = jnp.exp(scores - lt)
-        prob_grad = product_nt(jnp.where(mask, g, zero), v)
-        value_part = lax.dot_general(
-            probs.astype(jnp.bfloat16), g, TN, preferred_element_type=jnp.float32
-        )
-        score_grad = (
-            probs * (prob_grad - jnp.sum(probs * prob_grad, axis=-1, keepdims=True))
-        ).astype(jnp.bfloat16)
-        query_part = jnp.dot(score_grad, k, preferred_element_type=jnp.float32) * scale
-        key_part = lax.dot_general(score_grad, q, TN, preferred_element_type=jnp.float32) * scale
+    for h, mask in enumerate(masks):
+        lt_row = lt_t[h * HEAD : h * HEAD + 1, :]
+        scores_t = product_nt(jnp.where(mask, k, zero), q) * scale
+        probs_t = jnp.exp(scores_t - lt_row)
+        prob_grad_t = product_nt(jnp.where(mask, v, zero), g)
+        value_part = jnp.dot(probs_t.astype(jnp.bfloat16), g, preferred_element_type=jnp.float32)
+        row_sums = jnp.sum(probs_t * prob_grad_t, axis=0, keepdims=True)
+        score_grad_t = (probs_t * (prob_grad_t - row_sums)).astype(jnp.bfloat16)
+        key_part = jnp.dot(score_grad_t, q, preferred_element_type=jnp.float32) * scale
+        query_part = lax.dot_general(score_grad_t, k, TN, preferred_element_type=jnp.float32) * scale
         if dq is None:
             dq, dk, dv = query_part, key_part, value_part
         else:

time: 563 us -> 560 us (level)
  no operation moved by 1% of the time
where the time goes in v8:
time: 560 us; the launch traced here: 554 us
  waiting for transfers between devices  257 us (46%)
  matrix products  130 us (23%)
  Pallas kernels  103 us (18%)
  local copies, waits for them, and re-layouts  32.4 us (6%)
  other arithmetic  16.1 us (3%)
  between operations  15.7 us (3%)
    unnamed x3, waiting for transfers between devices  151 us
    all_gather x1, waiting for transfers between devices, gather_weights(): packed = lax.all_gather(pack_weights(weights), AXES, axis=0, tiled=True)  106 us
    dot_general x12, matrix products, product_nt(): return lax.dot_general(left, right, NT, preferred_element_type=jnp.float32)  71.5 us
    dot_general x12, matrix products, product(): return jnp.dot(left, right, preferred_element_type=jnp.float32)  58.9 us
    pallas_call x3, Pallas kernels, attention_backward(): pl.pallas_call(attention_backward_kernel, grid=grid, in_specs=[triple, pa...  37.9 us
    pallas_call x4, Pallas kernels, weight_grad(): pl.pallas_call(kernel, grid=grid, in_specs=in_specs, out_specs=[pl.BlockS...  34.8 us
    pallas_call x3, Pallas kernels, attention_forward(): pl.pallas_call(attention_forward_kernel, grid=grid, in_specs=[pl.BlockSpe...  30.3 us
    unnamed x150, local copies, waits for them, and re-layouts  17.4 us
  transfers between devices with their start and end apart: 2, of which 2 were waited for; matrix products, arithmetic and copies ran while one was open for 1% of the time, Pallas kernels for 0%

profile of v8, /device:TPU:0, one launch (start us, length us, event | category | flops | bytes accessed | tf_op | source)
XLA Modules:
  0.0 554.5 jit_solution(15146946998897654240)
XLA Ops:
  14.2 106.0 %all-gather.2.cloned.1.call-done = bf16[768,9344]{1,0:T(8,128)(2,1)} async-done(((bf16[24,9344]{1,0:T(8,128)(2,1)}), bf16[768,9344]{1,0:T(8,128)(2,1)}) %all-gather.2.cloned.1.call-update) | async-done | bytes 14352400 | tf_op jit(solution)/shard_map/all_gather | solution.py:268
  123.4 5.5 fusion.24.qkv_ref
  128.9 10.1 %attention_forward.3 = (bf16[512,768]{1,0:T(8,128)(2,1)}, f32[512,768]{1,0:T(8,128)}) custom-call(bf16[512,2304]{1,0:T(8,128)(2,1)} %fusion.24.qkv_ref), custom_call_target="tpu_custom_call" | custom-call | flops 1610612736 | bytes 4718592 | tf_op jit(solution)/shard_map/attention_forward/pallas_call | solution.py:113
  141.7 2.9 fusion.83
  145.5 10.6 %multiply_convert_fusion.2 = (bf16[512,3072]{1,0:T(8,128)(2,1)S(1)}, f32[512,3072]{1,0:T(8,128)}) fusion(f32[3072]{0:T(1024)S(1)} %add.359, bf16[512,768]{1,0:T(8,128)(2,1)S(1)} %fusion.64.refs_0_, bf16[768,9344]{1,0:T(8,128)(2,1)} %all-gather.2.cloned.1.call-done), kind=kOutput, calls=%fused_computation.29 | convolution fusion | flops 2431647744 | bytes 14954496 | tf_op jit(solution)/shard_map/dot_general | solution.py:21
  159.5 5.5 fusion.21.qkv_ref
  165.9 10.2 %attention_forward.4 = (bf16[512,768]{1,0:T(8,128)(2,1)}, f32[512,768]{1,0:T(8,128)}) custom-call(bf16[512,2304]{1,0:T(8,128)(2,1)} %fusion.21.qkv_ref), custom_call_target="tpu_custom_call" | custom-call | flops 1610612736 | bytes 4718592 | tf_op jit(solution)/shard_map/attention_forward/pallas_call | solution.py:113
  179.2 9.6 %multiply_convert_fusion.1 = (bf16[512,3072]{1,0:T(8,128)(2,1)S(1)}, f32[512,3072]{1,0:T(8,128)}) fusion(f32[3072]{0:T(1024)S(1)} %add.359, bf16[512,768]{1,0:T(8,128)(2,1)S(1)} %fusion.66.refs_1_, bf16[768,9344]{1,0:T(8,128)(2,1)} %all-gather.2.cloned.1.call-done), kind=kOutput, calls=%fused_computation.28 | convolution fusion | flops 2431647744 | bytes 14954496 | tf_op jit(solution)/shard_map/dot_general | solution.py:21
  192.3 5.4 fusion.22.qkv_ref
  198.6 10.0 %attention_forward.5 = (bf16[512,768]{1,0:T(8,128)(2,1)}, f32[512,768]{1,0:T(8,128)}) custom-call(bf16[512,2304]{1,0:T(8,128)(2,1)} %fusion.22.qkv_ref), custom_call_target="tpu_custom_call" | custom-call | flops 1610612736 | bytes 4718592 | tf_op jit(solution)/shard_map/attention_forward/pallas_call | solution.py:113
  211.7 6.7 %multiply_convert_fusion = (bf16[512,3072]{1,0:T(8,128)(2,1)S(1)}, f32[512,3072]{1,0:T(8,128)S(1)}) fusion(f32[3072]{0:T(1024)S(1)} %add.359, bf16[512,768]{1,0:T(8,128)(2,1)S(1)} %fusion.68.refs_2_, bf16[768,9344]{1,0:T(8,128)(2,1)} %all-gather.2.cloned.1.call-done), kind=kOutput, calls=%fused_computation.27 | convolution fusion | flops 2431647744 | bytes 14954496 | tf_op jit(solution)/shard_map/dot_general | solution.py:21
  224.9 6.2 %fusion.20.refs_5_ = bf16[512,3072]{1,0:T(8,128)(2,1)S(1)} fusion(f32[512,3072]{1,0:T(8,128)S(1)} %get-tuple-element.199, f32[3072]{0:T(1024)S(1)} %add.359, bf16[512,768]{1,0:T(8,128)(2,1)S(1)} %get-tuple-element.150.refs_5_, bf16[3072,768]{1,0:T(8,128)(2,1)S(1)} %bitcast.91), kind=kOutput, calls=%fused_computation.26 | convolution fusion | flops 2448949248 | bytes 14954496 | tf_op jit(solution)/shard_map/dot_general | solution.py:25
  231.2 6.9 %multiply_reduce_fusion.3 = (f32[768]{0:T(1024)S(1)}, f32[512]{0:T(512)S(1)}, f32[512]{0:T(512)S(1)}, f32[768]{0:T(1024)S(1)}, f32[512,768]{1,0:T(8,128)S(1)}) fusion(f32[512,768]{1,0:T(8,128)S(1)} %get-tuple-element.197, f32[512]{0:T(512)S(1)} %add_rsqrt_fusion.1, f32[512]{0:T(512)S(1)} %broadcast_multiply_fusion.13, f32[768]{0:T(1024)S(1)} %get-tuple-element.132, ...), kind=kOutput, calls=%fused_computation.53 | convolution fusion | flops 2423387648 | bytes 13400064 | tf_op jit(solution)/shard_map/dot_general | solution.py:25
  239.8 3.0 convolution_convert_fusion.2.g_ref
  242.7 12.7 %attention_backward.3.refs_5_ = bf16[512,2304]{1,0:T(8,128)(2,1)} custom-call(bf16[512,2304]{1,0:T(8,128)(2,1)} %fusion.22.qkv_ref, f32[512,768]{1,0:T(8,128)} %get-tuple-element.34.lt_ref, bf16[512,768]{1,0:T(8,128)(2,1)} %convolution_convert_fusion.2.g_ref), custom_call_target="tpu_custom_call" | custom-call | flops 4026531840 | bytes 7077888 | tf_op jit(solution)/shard_map/attention_backward/pallas_call | solution.py:138
  255.4 6.1 %multiply_reduce_fusion.1 = (f32[768]{0:T(1024)S(1)}, f32[512]{0:T(512)S(1)}, f32[512]{0:T(512)S(1)}, f32[768]{0:T(1024)S(1)}, f32[512,768]{1,0:T(8,128)S(1)}) fusion(f32[512,768]{1,0:T(8,128)} %copy-done.30, f32[512]{0:T(512)S(1)} %add_rsqrt_fusion.2, f32[512]{0:T(512)S(1)} %broadcast_multiply_fusion.14, f32[768]{0:T(1024)S(1)} %get-tuple-element.128, ...), kind=kOutput, calls=%fused_computation.51 | convolution fusion | flops 1815868928 | bytes 10634240 | tf_op jit(solution)/shard_map/dot_general | solution.py:25
  262.1 9.2 %fusion.13.refs_4_ = bf16[512,3072]{1,0:T(8,128)(2,1)S(1)} fusion(f32[512,3072]{1,0:T(8,128)} %get-tuple-element.193, f32[3072]{0:T(1024)S(1)} %add.359, bf16[512,768]{1,0:T(8,128)(2,1)S(1)} %get-tuple-element.142.refs_4_, bf16[3072,768]{1,0:T(8,128)(2,1)} %copy-done.32), kind=kOutput, calls=%fused_computation.19 | convolution fusion | flops 2448949248 | bytes 14954496 | tf_op jit(solution)/shard_map/dot_general | solution.py:25
  271.3 6.6 %multiply_reduce_fusion.4 = (f32[768]{0:T(1024)S(1)}, f32[512]{0:T(512)S(1)}, f32[512]{0:T(512)S(1)}, f32[768]{0:T(1024)S(1)}, f32[512,768]{1,0:T(8,128)S(1)}) fusion(f32[512,768]{1,0:T(8,128)S(1)} %get-tuple-element.191, f32[512]{0:T(512)S(1)} %add_rsqrt_fusion.3, f32[512]{0:T(512)S(1)} %broadcast_multiply_fusion.15, f32[768]{0:T(1024)S(1)} %get-tuple-element.132, ...), kind=kOutput, calls=%fused_computation.54 | convolution fusion | flops 2419848704 | bytes 12600320 | tf_op jit(solution)/shard_map/dot_general | solution.py:25
  277.9 3.1 fusion.80
  281.0 3.0 convolution_convert_fusion.1.g_ref
  284.0 12.7 %attention_backward.4.refs_4_ = bf16[512,2304]{1,0:T(8,128)(2,1)} custom-call(bf16[512,2304]{1,0:T(8,128)(2,1)} %fusion.21.qkv_ref, f32[512,768]{1,0:T(8,128)} %get-tuple-element.35.lt_ref, bf16[512,768]{1,0:T(8,128)(2,1)} %convolution_convert_fusion.1.g_ref), custom_call_target="tpu_custom_call" | custom-call | flops 4026531840 | bytes 7077888 | tf_op jit(solution)/shard_map/attention_backward/pallas_call | solution.py:138
  296.7 6.2 %multiply_reduce_fusion.2 = (f32[768]{0:T(1024)S(1)}, f32[512]{0:T(512)S(1)}, f32[512]{0:T(512)S(1)}, f32[768]{0:T(1024)S(1)}, f32[512,768]{1,0:T(8,128)S(1)}) fusion(f32[512,768]{1,0:T(8,128)} %copy-done.27, f32[512]{0:T(512)S(1)} %add_rsqrt_fusion.4, f32[512]{0:T(512)S(1)} %broadcast_multiply_fusion.16, f32[768]{0:T(1024)S(1)} %get-tuple-element.128, ...), kind=kOutput, calls=%fused_computation.52 | convolution fusion | flops 1815868928 | bytes 10634240 | tf_op jit(solution)/shard_map/dot_general | solution.py:25
  303.5 9.2 %fusion.6.refs_3_ = bf16[512,3072]{1,0:T(8,128)(2,1)S(1)} fusion(f32[512,3072]{1,0:T(8,128)} %get-tuple-element.187, f32[3072]{0:T(1024)S(1)} %add.359, bf16[512,768]{1,0:T(8,128)(2,1)S(1)} %get-tuple-element.138.refs_3_, bf16[3072,768]{1,0:T(8,128)(2,1)} %copy-done.32), kind=kOutput, calls=%fused_computation.12 | convolution fusion | flops 2448949248 | bytes 14954496 | tf_op jit(solution)/shard_map/dot_general | solution.py:25
  312.7 6.6 %multiply_reduce_fusion.5 = (f32[768]{0:T(1024)S(1)}, f32[512]{0:T(512)S(1)}, f32[512]{0:T(512)S(1)}, f32[768]{0:T(1024)S(1)}, f32[512,768]{1,0:T(8,128)S(1)}) fusion(f32[512,768]{1,0:T(8,128)S(1)} %copy-done.26, f32[512]{0:T(512)S(1)} %add_rsqrt_fusion.5, f32[512]{0:T(512)S(1)} %broadcast_multiply_fusion.17, f32[768]{0:T(1024)S(1)} %get-tuple-element.132, ...), kind=kOutput, calls=%fused_computation.55 | convolution fusion | flops 2419848704 | bytes 12600320 | tf_op jit(solution)/shard_map/dot_general | solution.py:25
  321.0 3.0 convolution_convert_fusion.g_ref
  324.0 12.5 %attention_backward.5.refs_3_ = bf16[512,2304]{1,0:T(8,128)(2,1)} custom-call(bf16[512,2304]{1,0:T(8,128)(2,1)} %fusion.24.qkv_ref, f32[512,768]{1,0:T(8,128)} %get-tuple-element.36.lt_ref, bf16[512,768]{1,0:T(8,128)(2,1)} %convolution_convert_fusion.g_ref), custom_call_target="tpu_custom_call" | custom-call | flops 4026531840 | bytes 7077888 | tf_op jit(solution)/shard_map/attention_backward/pallas_call | solution.py:138
  341.6 9.3 %weight_grad.4 = (bf16[768,9344]{1,0:T(8,128)(2,1)}, f32[1,2304]{1,0:T(1,128)S(1)}) custom-call(bf16[512,768]{1,0:T(8,128)(2,1)S(1)} %copy-done.18, bf16[512,768]{1,0:T(8,128)(2,1)S(1)} %copy-done.12, bf16[512,768]{1,0:T(8,128)(2,1)S(1)} %copy-done.16, bf16[512,2304]{1,0:T(8,128)(2,1)S(1)} %copy-done.23, bf16[512,2304]{1,0:T(8,128)(2,1)} %attention_backward.4.refs_4_, ...), custom_call_target="tpu_custom_call" | custom-call | flops 5435817984 | bytes 12976128 | tf_op jit(solution)/shard_map/weight_grad/pallas_call | solution.py:200
  350.9 3.2 weight_grad.5
  356.0 11.3 %weight_grad.6 = (bf16[768,9344]{1,0:T(8,128)(2,1)}, f32[1,3072]{1,0:T(1,128)S(1)}) custom-call(bf16[512,768]{1,0:T(8,128)(2,1)S(1)} %copy-done.8, bf16[512,768]{1,0:T(8,128)(2,1)S(1)} %copy-done.10, bf16[512,768]{1,0:T(8,128)(2,1)S(1)} %copy-done.14, bf16[512,3072]{1,0:T(8,128)(2,1)S(1)} %copy-done.22, ...), custom_call_target="tpu_custom_call", output_to_operand_aliasing={{0}: (6, {})} | custom-call | flops 7247757312 | bytes 16515072 | tf_op jit(solution)/shard_map/weight_grad/pallas_call | solution.py:200
  367.3 11.1 %weight_grad.7 = (bf16[768,9344]{1,0:T(8,128)(2,1)}, f32[1,768]{1,0:T(1,128)S(1)}) custom-call(bf16[512,3072]{1,0:T(8,128)(2,1)S(1)} %copy-done.20, bf16[512,3072]{1,0:T(8,128)(2,1)} %copy-done.56, bf16[512,3072]{1,0:T(8,128)(2,1)} %copy-done.57, bf16[512,768]{1,0:T(8,128)(2,1)S(1)} %copy-done.6, ...), custom_call_target="tpu_custom_call", output_to_operand_aliasing={{0}: (6, {})} | custom-call | flops 7247757312 | bytes 16515072 | tf_op jit(solution)/shard_map/weight_grad/pallas_call | solution.py:200
  384.0 5.5 add_convert_fusion
  389.5 150.7 %reduce-scatter.4.cloned.1.call-done = bf16[24,9344]{1,0:T(8,128)(2,1)} async-done(((bf16[768,9344]{1,0:T(8,128)(2,1)}), bf16[24,9344]{1,0:T(8,128)(2,1)}) %reduce-scatter.4.cloned.1.call-update) | async-done | bytes 448528
  (263 shorter events, 58.3 us)
Async XLA Ops:
  7.2 113.0 %all-gather.2.cloned.1.call-start = ((), (), s32[]{:S(2)}) async-start(), calls=%async_computation.1 | async-start | bytes 14800896 | tf_op jit(solution)/shard_map/all_gather | solution.py:268
  14.0 526.1 %reduce-scatter.4.cloned.1.call-start = ((), (), s32[]{:S(2)}) async-start(), calls=%async_computation.2 | async-start | bytes 14800896
  141.4 14.7 %copy-start.25 = (f32[512,768]{1,0:T(8,128)}, f32[512,768]{1,0:T(8,128)S(1)}, u32[]{:S(2)}) copy-start(f32[512,768]{1,0:T(8,128)S(1)} %get-tuple-element.185) | copy-start | bytes 4718596
  145.1 10.9 %copy-start.32 = (bf16[3072,768]{1,0:T(8,128)(2,1)}, bf16[3072,768]{1,0:T(8,128)(2,1)S(1)}, u32[]{:S(2)}) copy-start(bf16[3072,768]{1,0:T(8,128)(2,1)S(1)} %pad_maximum_fusion) | copy-start | bytes 14155780
  145.5 10.6 %copy-start.7 = (bf16[512,768]{1,0:T(8,128)(2,1)}, bf16[512,768]{1,0:T(8,128)(2,1)S(1)}, u32[]{:S(2)}) copy-start(bf16[512,768]{1,0:T(8,128)(2,1)S(1)} %fusion.64.refs_0_) | copy-start | bytes 2359300
  158.9 17.2 %copy-start.27 = (f32[512,768]{1,0:T(8,128)}, f32[512,768]{1,0:T(8,128)S(1)}, u32[]{:S(2)}) copy-start(f32[512,768]{1,0:T(8,128)S(1)} %get-tuple-element.189) | copy-start | bytes 4718596
  178.6 92.8 %copy-start.29 = (f32[512,768]{1,0:T(8,128)}, f32[512,768]{1,0:T(8,128)S(1)}, u32[]{:S(2)}) copy-start(f32[512,768]{1,0:T(8,128)S(1)} %get-tuple-element.191) | copy-start | bytes 4718596
  178.9 9.9 %slice-start = ((s8[4718592]{0:T(1024)(128)(4,1)}), s8[4194304]{0:T(1024)(128)(4,1)S(1)}, s32[]{:S(2)}) async-start(s8[4718592]{0:T(1024)(128)(4,1)} %bitcast.88), calls=%async_computation.3 | async-start | bytes 8388608
  179.2 9.6 %copy-start.9 = (bf16[512,768]{1,0:T(8,128)(2,1)}, bf16[512,768]{1,0:T(8,128)(2,1)S(1)}, u32[]{:S(2)}) copy-start(bf16[512,768]{1,0:T(8,128)(2,1)S(1)} %fusion.66.refs_1_) | copy-start | bytes 2359300
  179.2 9.6 %slice-start.1 = ((s8[4718592]{0:T(1024)(128)(4,1)}), s8[524288]{0:T(1024)(128)(4,1)S(1)}, s32[]{:S(2)}) async-start(s8[4718592]{0:T(1024)(128)(4,1)} %bitcast.88), calls=%async_computation.4 | async-start | bytes 1048576
  191.6 17.0 %copy-start.30 = (f32[512,768]{1,0:T(8,128)}, f32[512,768]{1,0:T(8,128)S(1)}, u32[]{:S(2)}) copy-start(f32[512,768]{1,0:T(8,128)S(1)} %get-tuple-element.195) | copy-start | bytes 4718596
  211.4 7.1 %slice-start.2 = ((s8[4718592]{0:T(1024)(128)(4,1)}), s8[4194304]{0:T(1024)(128)(4,1)S(1)}, s32[]{:S(2)}) async-start(s8[4718592]{0:T(1024)(128)(4,1)} %bitcast.90), calls=%async_computation.5 | async-start | bytes 8388608
  211.7 6.8 %copy-start.13 = (bf16[512,768]{1,0:T(8,128)(2,1)}, bf16[512,768]{1,0:T(8,128)(2,1)S(1)}, u32[]{:S(2)}) copy-start(bf16[512,768]{1,0:T(8,128)(2,1)S(1)} %fusion.68.refs_2_) | copy-start | bytes 2359300
  211.7 6.8 %slice-start.3 = ((s8[4718592]{0:T(1024)(128)(4,1)}), s8[524288]{0:T(1024)(128)(4,1)S(1)}, s32[]{:S(2)}) async-start(s8[4718592]{0:T(1024)(128)(4,1)} %bitcast.90), calls=%async_computation.6 | async-start | bytes 1048576
  231.2 6.9 %copy-start.58 = (bf16[512,3072]{1,0:T(8,128)(2,1)}, bf16[512,3072]{1,0:T(8,128)(2,1)S(1)}, u32[]{:S(2)}) copy-start(bf16[512,3072]{1,0:T(8,128)(2,1)S(1)} %fusion.20.refs_5_) | copy-start | bytes 9437188
  255.4 6.2 %copy-start.31 = (f32[512,768]{1,0:T(8,128)S(1)}, f32[512,768]{1,0:T(8,128)}, u32[]{:S(2)}) copy-start(f32[512,768]{1,0:T(8,128)} %copy-done.30) | copy-start | bytes 4718596
  262.1 9.2 %copy-start.3 = (bf16[512,768]{1,0:T(8,128)(2,1)}, bf16[512,768]{1,0:T(8,128)(2,1)S(1)}, u32[]{:S(2)}) copy-start(bf16[512,768]{1,0:T(8,128)(2,1)S(1)} %get-tuple-element.142.refs_4_) | copy-start | bytes 2359300
  271.3 6.6 %copy-start.59 = (bf16[512,3072]{1,0:T(8,128)(2,1)}, bf16[512,3072]{1,0:T(8,128)(2,1)S(1)}, u32[]{:S(2)}) copy-start(bf16[512,3072]{1,0:T(8,128)(2,1)S(1)} %fusion.13.refs_4_) | copy-start | bytes 9437188
  296.7 6.2 %copy-start.28 = (f32[512,768]{1,0:T(8,128)S(1)}, f32[512,768]{1,0:T(8,128)}, u32[]{:S(2)}) copy-start(f32[512,768]{1,0:T(8,128)} %copy-done.27) | copy-start | bytes 4718596
  303.4 9.2 %copy-start.5 = (bf16[512,768]{1,0:T(8,128)(2,1)}, bf16[512,768]{1,0:T(8,128)(2,1)S(1)}, u32[]{:S(2)}) copy-start(bf16[512,768]{1,0:T(8,128)(2,1)S(1)} %get-tuple-element.138.refs_3_) | copy-start | bytes 2359300
  303.4 9.3 %copy-start.26 = (f32[512,768]{1,0:T(8,128)S(1)}, f32[512,768]{1,0:T(8,128)}, u32[]{:S(2)}) copy-start(f32[512,768]{1,0:T(8,128)} %copy-done.25) | copy-start | bytes 4718596
  312.7 6.6 %copy-start.21 = (bf16[512,3072]{1,0:T(8,128)(2,1)}, bf16[512,3072]{1,0:T(8,128)(2,1)S(1)}, u32[]{:S(2)}) copy-start(bf16[512,3072]{1,0:T(8,128)(2,1)S(1)} %fusion.6.refs_3_) | copy-start | bytes 9437188
  341.6 9.3 %copy-start = (bf16[512,768]{1,0:T(8,128)(2,1)S(1)}, bf16[512,768]{1,0:T(8,128)(2,1)}, u32[]{:S(2)}) copy-start(bf16[512,768]{1,0:T(8,128)(2,1)} %get-tuple-element.31.refs_0_) | copy-start | bytes 2359300
  341.6 9.3 %copy-start.1 = (bf16[512,768]{1,0:T(8,128)(2,1)S(1)}, bf16[512,768]{1,0:T(8,128)(2,1)}, u32[]{:S(2)}) copy-start(bf16[512,768]{1,0:T(8,128)(2,1)} %get-tuple-element.32.refs_1_) | copy-start | bytes 2359300
  341.6 9.3 %copy-start.2 = (bf16[512,768]{1,0:T(8,128)(2,1)S(1)}, bf16[512,768]{1,0:T(8,128)(2,1)}, u32[]{:S(2)}) copy-start(bf16[512,768]{1,0:T(8,128)(2,1)} %get-tuple-element.33.refs_2_) | copy-start | bytes 2359300
  350.9 3.2 copy-start.8
  350.9 3.2 copy-start.10
  356.0 11.3 %copy-start.4 = (bf16[512,768]{1,0:T(8,128)(2,1)S(1)}, bf16[512,768]{1,0:T(8,128)(2,1)}, u32[]{:S(2)}) copy-start(bf16[512,768]{1,0:T(8,128)(2,1)} %copy-done.3) | copy-start | bytes 2359300
  356.0 11.3 %copy-start.6 = (bf16[512,768]{1,0:T(8,128)(2,1)S(1)}, bf16[512,768]{1,0:T(8,128)(2,1)}, u32[]{:S(2)}) copy-start(bf16[512,768]{1,0:T(8,128)(2,1)} %copy-done.5) | copy-start | bytes 2359300
  356.0 11.3 %copy-start.20 = (bf16[512,3072]{1,0:T(8,128)(2,1)S(1)}, bf16[512,3072]{1,0:T(8,128)(2,1)}, u32[]{:S(2)}) copy-start(bf16[512,3072]{1,0:T(8,128)(2,1)} %copy-done.19) | copy-start | bytes 9437188
  367.3 11.1 %copy-start.46 = (bf16[768]{0:T(1024)(128)(2,1)S(1)}, bf16[768]{0:T(1024)(128)(2,1)}, u32[]{:S(2)}) copy-start(bf16[768]{0:T(1024)(128)(2,1)} %custom-call.4) | copy-start | bytes 4612
  367.3 12.3 %copy-start.45 = (bf16[768]{0:T(1024)(128)(2,1)S(1)}, bf16[768]{0:T(1024)(128)(2,1)}, u32[]{:S(2)}) copy-start(bf16[768]{0:T(1024)(128)(2,1)} %custom-call.3) | copy-start | bytes 4612
  (34 other events, 70.9 us)
Sparse Core Ops, SparseCore 0:
  14.2 105.9 all-gather.1
  382.4 157.6 reduce-scatter.3

commit v9 on v8

--- a/solution.py
+++ b/solution.py
@@ -2,6 +2,7 @@
 
 import jax
 import jax.numpy as jnp
+import numpy as np
 from jax import lax
 from jax.experimental import pallas as pl
 from jax.experimental.pallas import tpu as pltpu
@@ -26,7 +27,12 @@
 
 
 def gelu_tanh(values):
-    return jax.nn.gelu(values, approximate=True)
+    root = np.sqrt(2 / np.pi).astype(np.float32)
+    cube = values * values * values
+    bent = jnp.tanh(root * (values + 0.044715 * cube))
+    cdf = 0.5 * (1.0 + bent)
+    slope = cdf + values * (0.5 * (1.0 - bent * bent) * root * (1.0 + 3 * 0.044715 * values * values))
+    return values * cdf, slope
 
 
 def layer_norm(summed, gain, shift):
@@ -307,7 +313,8 @@
     first_out, first_normed, first_inverse = layer_norm(hidden_state + attended, w["g1"], w["s1"])
     first_low = first_out.astype(jnp.bfloat16)
     inner_pre = product(first_low, w["inner"]) + w["inner_bias"]
-    inner_low = gelu_tanh(inner_pre).astype(jnp.bfloat16)
+    inner_act, inner_slope = gelu_tanh(inner_pre)
+    inner_low = inner_act.astype(jnp.bfloat16)
     outer_out = product(inner_low, w["outer"]) + w["outer_bias"]
     result, second_normed, second_inverse = layer_norm(first_out + outer_out, w["g2"], w["s2"])
     kept = dict(
@@ -318,7 +325,7 @@
         first_normed=first_normed,
         first_inverse=first_inverse,
         first_low=first_low,
-        inner_pre=inner_pre,
+        inner_slope=inner_slope,
         inner_low=inner_low,
         second_normed=second_normed,
         second_inverse=second_inverse,
@@ -332,8 +339,7 @@
     second_grad = norm_backward(upstream, kept["second_normed"], kept["second_inverse"], w["g2"])
     outer_low = second_grad.astype(jnp.bfloat16)
     active_grad = product_nt(outer_low, w["outer"])
-    gelu_pull = jax.vjp(gelu_tanh, kept["inner_pre"])[1]
-    inner_grad = gelu_pull(active_grad)[0].astype(jnp.bfloat16)
+    inner_grad = (active_grad * kept["inner_slope"]).astype(jnp.bfloat16)
     first_grad = second_grad + product_nt(inner_grad, w["inner"])
     first_gain_grad = jnp.sum(first_grad * kept["first_normed"], axis=0)
     first_shift_grad = jnp.sum(first_grad, axis=0)

time: 560 us -> 558 us (level)
  no operation moved by 1% of the time
where the time goes in v9:
time: 558 us; the launch traced here: 553 us
  waiting for transfers between devices  257 us (46%)
  matrix products  129 us (23%)
  Pallas kernels  103 us (18%)
  local copies, waits for them, and re-layouts  32.1 us (6%)
  other arithmetic  16.1 us (3%)
  between operations  15.7 us (3%)
    unnamed x3, waiting for transfers between devices  152 us
    all_gather x1, waiting for transfers between devices, gather_weights(): packed = lax.all_gather(pack_weights(weights), AXES, axis=0, tiled=True)  106 us
    dot_general x12, matrix products, product_nt(): return lax.dot_general(left, right, NT, preferred_element_type=jnp.float32)  69.7 us
    dot_general x12, matrix products, product(): return jnp.dot(left, right, preferred_element_type=jnp.float32)  58.9 us
    pallas_call x3, Pallas kernels, attention_backward(): pl.pallas_call(attention_backward_kernel, grid=grid, in_specs=[triple, pa...  38 us
    pallas_call x4, Pallas kernels, weight_grad(): pl.pallas_call(kernel, grid=grid, in_specs=in_specs, out_specs=[pl.BlockS...  34.8 us
    pallas_call x3, Pallas kernels, attention_forward(): pl.pallas_call(attention_forward_kernel, grid=grid, in_specs=[pl.BlockSpe...  30.3 us
    unnamed x150, local copies, waits for them, and re-layouts  17.4 us
  transfers between devices with their start and end apart: 2, of which 2 were waited for; matrix products, arithmetic and copies ran while one was open for 1% of the time, Pallas kernels for 0%

profile of v9, /device:TPU:0, one launch (start us, length us, event | category | flops | bytes accessed | tf_op | source)
XLA Modules:
  0.0 553.1 jit_solution(8177570313191126159)
XLA Ops:
  14.2 106.0 %all-gather.2.cloned.1.call-done = bf16[768,9344]{1,0:T(8,128)(2,1)} async-done(((bf16[24,9344]{1,0:T(8,128)(2,1)}), bf16[768,9344]{1,0:T(8,128)(2,1)}) %all-gather.2.cloned.1.call-update) | async-done | bytes 14352400 | tf_op jit(solution)/shard_map/all_gather | solution.py:274
  123.4 5.5 fusion.33.qkv_ref
  128.9 10.1 %attention_forward.3 = (bf16[512,768]{1,0:T(8,128)(2,1)}, f32[512,768]{1,0:T(8,128)}) custom-call(bf16[512,2304]{1,0:T(8,128)(2,1)} %fusion.33.qkv_ref), custom_call_target="tpu_custom_call" | custom-call | flops 1610612736 | bytes 4718592 | tf_op jit(solution)/shard_map/attention_forward/pallas_call | solution.py:119
  141.7 2.9 fusion.92
  145.5 10.6 %multiply_convert_fusion.2 = (bf16[512,3072]{1,0:T(8,128)(2,1)S(1)}, f32[512,3072]{1,0:T(8,128)}) fusion(f32[3072]{0:T(1024)S(1)} %add.368, bf16[512,768]{1,0:T(8,128)(2,1)S(1)} %fusion.73.refs_0_, bf16[768,9344]{1,0:T(8,128)(2,1)} %all-gather.2.cloned.1.call-done), kind=kOutput, calls=%fused_computation.40 | convolution fusion | flops 2431647744 | bytes 14954496 | tf_op jit(solution)/shard_map/dot_general | solution.py:22
  159.5 5.5 fusion.30.qkv_ref
  165.9 10.2 %attention_forward.4 = (bf16[512,768]{1,0:T(8,128)(2,1)}, f32[512,768]{1,0:T(8,128)}) custom-call(bf16[512,2304]{1,0:T(8,128)(2,1)} %fusion.30.qkv_ref), custom_call_target="tpu_custom_call" | custom-call | flops 1610612736 | bytes 4718592 | tf_op jit(solution)/shard_map/attention_forward/pallas_call | solution.py:119
  179.2 9.6 %multiply_convert_fusion.1 = (bf16[512,3072]{1,0:T(8,128)(2,1)S(1)}, f32[512,3072]{1,0:T(8,128)}) fusion(f32[3072]{0:T(1024)S(1)} %add.368, bf16[512,768]{1,0:T(8,128)(2,1)S(1)} %fusion.75.refs_1_, bf16[768,9344]{1,0:T(8,128)(2,1)} %all-gather.2.cloned.1.call-done), kind=kOutput, calls=%fused_computation.38 | convolution fusion | flops 2431647744 | bytes 14954496 | tf_op jit(solution)/shard_map/dot_general | solution.py:22
  192.3 5.4 fusion.31.qkv_ref
  198.6 10.0 %attention_forward.5 = (bf16[512,768]{1,0:T(8,128)(2,1)}, f32[512,768]{1,0:T(8,128)}) custom-call(bf16[512,2304]{1,0:T(8,128)(2,1)} %fusion.31.qkv_ref), custom_call_target="tpu_custom_call" | custom-call | flops 1610612736 | bytes 4718592 | tf_op jit(solution)/shard_map/attention_forward/pallas_call | solution.py:119
  211.7 6.7 %multiply_convert_fusion = (bf16[512,3072]{1,0:T(8,128)(2,1)S(1)}, f32[512,3072]{1,0:T(8,128)S(1)}) fusion(f32[3072]{0:T(1024)S(1)} %add.368, bf16[512,768]{1,0:T(8,128)(2,1)S(1)} %fusion.77.refs_2_, bf16[768,9344]{1,0:T(8,128)(2,1)} %all-gather.2.cloned.1.call-done), kind=kOutput, calls=%fused_computation.36 | convolution fusion | flops 2431647744 | bytes 14954496 | tf_op jit(solution)/shard_map/dot_general | solution.py:22
  224.9 5.7 %fusion.17.refs_5_ = bf16[512,3072]{1,0:T(8,128)(2,1)S(1)} fusion(f32[512,3072]{1,0:T(8,128)S(1)} %get-tuple-element.199, bf16[512,768]{1,0:T(8,128)(2,1)S(1)} %get-tuple-element.150.refs_5_, bf16[3072,768]{1,0:T(8,128)(2,1)S(1)} %bitcast.91, f32[3072]{0:T(1024)S(1)} %add.368), kind=kOutput, calls=%fused_computation.23 | convolution fusion | flops 2445803520 | bytes 14954496 | tf_op jit(solution)/shard_map/dot_general | solution.py:26
  230.6 6.9 %multiply_reduce_fusion.3 = (f32[768]{0:T(1024)S(1)}, f32[512]{0:T(512)S(1)}, f32[512]{0:T(512)S(1)}, f32[768]{0:T(1024)S(1)}, f32[512,768]{1,0:T(8,128)S(1)}) fusion(f32[512,768]{1,0:T(8,128)S(1)} %get-tuple-element.197, f32[512]{0:T(512)S(1)} %add_rsqrt_fusion.1, f32[512]{0:T(512)S(1)} %broadcast_multiply_fusion.13, f32[768]{0:T(1024)S(1)} %get-tuple-element.132, ...), kind=kOutput, calls=%fused_computation.65 | convolution fusion | flops 2423387648 | bytes 13400064 | tf_op jit(solution)/shard_map/dot_general | solution.py:26
  239.2 3.0 convolution_convert_fusion.2.g_ref
  242.2 12.7 %attention_backward.3.refs_5_ = bf16[512,2304]{1,0:T(8,128)(2,1)} custom-call(bf16[512,2304]{1,0:T(8,128)(2,1)} %fusion.31.qkv_ref, f32[512,768]{1,0:T(8,128)} %get-tuple-element.34.lt_ref, bf16[512,768]{1,0:T(8,128)(2,1)} %convolution_convert_fusion.2.g_ref), custom_call_target="tpu_custom_call" | custom-call | flops 4026531840 | bytes 7077888 | tf_op jit(solution)/shard_map/attention_backward/pallas_call | solution.py:144
  254.9 6.1 %multiply_reduce_fusion.1 = (f32[768]{0:T(1024)S(1)}, f32[512]{0:T(512)S(1)}, f32[512]{0:T(512)S(1)}, f32[768]{0:T(1024)S(1)}, f32[512,768]{1,0:T(8,128)S(1)}) fusion(f32[512,768]{1,0:T(8,128)} %copy-done.30, f32[512]{0:T(512)S(1)} %add_rsqrt_fusion.2, f32[512]{0:T(512)S(1)} %broadcast_multiply_fusion.14, f32[768]{0:T(1024)S(1)} %get-tuple-element.128, ...), kind=kOutput, calls=%fused_computation.63 | convolution fusion | flops 1815868928 | bytes 10634240 | tf_op jit(solution)/shard_map/dot_general | solution.py:26
  261.6 8.6 %fusion.23.refs_4_ = bf16[512,3072]{1,0:T(8,128)(2,1)S(1)} fusion(f32[512,3072]{1,0:T(8,128)} %get-tuple-element.193, bf16[512,768]{1,0:T(8,128)(2,1)S(1)} %get-tuple-element.142.refs_4_, bf16[3072,768]{1,0:T(8,128)(2,1)} %copy-done.32, f32[3072]{0:T(1024)S(1)} %add.368), kind=kOutput, calls=%fused_computation.29 | convolution fusion | flops 2445803520 | bytes 14954496 | tf_op jit(solution)/shard_map/dot_general | solution.py:26
  270.2 6.6 %multiply_reduce_fusion.4 = (f32[768]{0:T(1024)S(1)}, f32[512]{0:T(512)S(1)}, f32[512]{0:T(512)S(1)}, f32[768]{0:T(1024)S(1)}, f32[512,768]{1,0:T(8,128)S(1)}) fusion(f32[512,768]{1,0:T(8,128)S(1)} %get-tuple-element.191, f32[512]{0:T(512)S(1)} %add_rsqrt_fusion.3, f32[512]{0:T(512)S(1)} %broadcast_multiply_fusion.15, f32[768]{0:T(1024)S(1)} %get-tuple-element.132, ...), kind=kOutput, calls=%fused_computation.66 | convolution fusion | flops 2419848704 | bytes 12600320 | tf_op jit(solution)/shard_map/dot_general | solution.py:26
  276.8 3.1 fusion.89
  279.9 3.0 convolution_convert_fusion.1.g_ref
  282.8 12.7 %attention_backward.4.refs_4_ = bf16[512,2304]{1,0:T(8,128)(2,1)} custom-call(bf16[512,2304]{1,0:T(8,128)(2,1)} %fusion.30.qkv_ref, f32[512,768]{1,0:T(8,128)} %get-tuple-element.35.lt_ref, bf16[512,768]{1,0:T(8,128)(2,1)} %convolution_convert_fusion.1.g_ref), custom_call_target="tpu_custom_call" | custom-call | flops 4026531840 | bytes 7077888 | tf_op jit(solution)/shard_map/attention_backward/pallas_call | solution.py:144
  295.6 6.2 %multiply_reduce_fusion.2 = (f32[768]{0:T(1024)S(1)}, f32[512]{0:T(512)S(1)}, f32[512]{0:T(512)S(1)}, f32[768]{0:T(1024)S(1)}, f32[512,768]{1,0:T(8,128)S(1)}) fusion(f32[512,768]{1,0:T(8,128)} %copy-done.27, f32[512]{0:T(512)S(1)} %add_rsqrt_fusion.4, f32[512]{0:T(512)S(1)} %broadcast_multiply_fusion.16, f32[768]{0:T(1024)S(1)} %get-tuple-element.128, ...), kind=kOutput, calls=%fused_computation.64 | convolution fusion | flops 1815868928 | bytes 10634240 | tf_op jit(solution)/shard_map/dot_general | solution.py:26
  302.3 8.6 %fusion.29.refs_3_ = bf16[512,3072]{1,0:T(8,128)(2,1)S(1)} fusion(f32[512,3072]{1,0:T(8,128)} %get-tuple-element.187, bf16[512,768]{1,0:T(8,128)(2,1)S(1)} %get-tuple-element.138.refs_3_, bf16[3072,768]{1,0:T(8,128)(2,1)} %copy-done.32, f32[3072]{0:T(1024)S(1)} %add.368), kind=kOutput, calls=%fused_computation.35 | convolution fusion | flops 2445803520 | bytes 14954496 | tf_op jit(solution)/shard_map/dot_general | solution.py:26
  310.9 6.6 %multiply_reduce_fusion.5 = (f32[768]{0:T(1024)S(1)}, f32[512]{0:T(512)S(1)}, f32[512]{0:T(512)S(1)}, f32[768]{0:T(1024)S(1)}, f32[512,768]{1,0:T(8,128)S(1)}) fusion(f32[512,768]{1,0:T(8,128)S(1)} %copy-done.26, f32[512]{0:T(512)S(1)} %add_rsqrt_fusion.5, f32[512]{0:T(512)S(1)} %broadcast_multiply_fusion.17, f32[768]{0:T(1024)S(1)} %get-tuple-element.132, ...), kind=kOutput, calls=%fused_computation.67 | convolution fusion | flops 2419848704 | bytes 12600320 | tf_op jit(solution)/shard_map/dot_general | solution.py:26
  319.2 3.0 convolution_convert_fusion.g_ref
  322.3 12.5 %attention_backward.5.refs_3_ = bf16[512,2304]{1,0:T(8,128)(2,1)} custom-call(bf16[512,2304]{1,0:T(8,128)(2,1)} %fusion.33.qkv_ref, f32[512,768]{1,0:T(8,128)} %get-tuple-element.36.lt_ref, bf16[512,768]{1,0:T(8,128)(2,1)} %convolution_convert_fusion.g_ref), custom_call_target="tpu_custom_call" | custom-call | flops 4026531840 | bytes 7077888 | tf_op jit(solution)/shard_map/attention_backward/pallas_call | solution.py:144
  339.9 9.2 %weight_grad.4 = (bf16[768,9344]{1,0:T(8,128)(2,1)}, f32[1,2304]{1,0:T(1,128)S(1)}) custom-call(bf16[512,768]{1,0:T(8,128)(2,1)S(1)} %copy-done.18, bf16[512,768]{1,0:T(8,128)(2,1)S(1)} %copy-done.12, bf16[512,768]{1,0:T(8,128)(2,1)S(1)} %copy-done.16, bf16[512,2304]{1,0:T(8,128)(2,1)S(1)} %copy-done.23, bf16[512,2304]{1,0:T(8,128)(2,1)} %attention_backward.4.refs_4_, ...), custom_call_target="tpu_custom_call" | custom-call | flops 5435817984 | bytes 12976128 | tf_op jit(solution)/shard_map/weight_grad/pallas_call | solution.py:206
  349.1 3.2 weight_grad.5
  354.2 11.3 %weight_grad.6 = (bf16[768,9344]{1,0:T(8,128)(2,1)}, f32[1,3072]{1,0:T(1,128)S(1)}) custom-call(bf16[512,768]{1,0:T(8,128)(2,1)S(1)} %copy-done.8, bf16[512,768]{1,0:T(8,128)(2,1)S(1)} %copy-done.10, bf16[512,768]{1,0:T(8,128)(2,1)S(1)} %copy-done.14, bf16[512,3072]{1,0:T(8,128)(2,1)S(1)} %copy-done.22, ...), custom_call_target="tpu_custom_call", output_to_operand_aliasing={{0}: (6, {})} | custom-call | flops 7247757312 | bytes 16515072 | tf_op jit(solution)/shard_map/weight_grad/pallas_call | solution.py:206
  365.6 11.1 %weight_grad.7 = (bf16[768,9344]{1,0:T(8,128)(2,1)}, f32[1,768]{1,0:T(1,128)S(1)}) custom-call(bf16[512,3072]{1,0:T(8,128)(2,1)S(1)} %copy-done.20, bf16[512,3072]{1,0:T(8,128)(2,1)} %copy-done.56, bf16[512,3072]{1,0:T(8,128)(2,1)} %copy-done.57, bf16[512,768]{1,0:T(8,128)(2,1)S(1)} %copy-done.6, ...), custom_call_target="tpu_custom_call", output_to_operand_aliasing={{0}: (6, {})} | custom-call | flops 7247757312 | bytes 16515072 | tf_op jit(solution)/shard_map/weight_grad/pallas_call | solution.py:206
  381.9 5.5 add_convert_fusion
  387.4 151.5 %reduce-scatter.4.cloned.1.call-done = bf16[24,9344]{1,0:T(8,128)(2,1)} async-done(((bf16[768,9344]{1,0:T(8,128)(2,1)}), bf16[24,9344]{1,0:T(8,128)(2,1)}) %reduce-scatter.4.cloned.1.call-update) | async-done | bytes 448528
  (263 shorter events, 58.1 us)
Async XLA Ops:
  7.2 113.0 %all-gather.2.cloned.1.call-start = ((), (), s32[]{:S(2)}) async-start(), calls=%async_computation.1 | async-start | bytes 14800896 | tf_op jit(solution)/shard_map/all_gather | solution.py:274
  14.0 524.9 %reduce-scatter.4.cloned.1.call-start = ((), (), s32[]{:S(2)}) async-start(), calls=%async_computation.2 | async-start | bytes 14800896
  141.4 14.7 %copy-start.25 = (f32[512,768]{1,0:T(8,128)}, f32[512,768]{1,0:T(8,128)S(1)}, u32[]{:S(2)}) copy-start(f32[512,768]{1,0:T(8,128)S(1)} %get-tuple-element.185) | copy-start | bytes 4718596
  145.1 10.9 %copy-start.32 = (bf16[3072,768]{1,0:T(8,128)(2,1)}, bf16[3072,768]{1,0:T(8,128)(2,1)S(1)}, u32[]{:S(2)}) copy-start(bf16[3072,768]{1,0:T(8,128)(2,1)S(1)} %pad_maximum_fusion) | copy-start | bytes 14155780
  145.5 10.6 %copy-start.7 = (bf16[512,768]{1,0:T(8,128)(2,1)}, bf16[512,768]{1,0:T(8,128)(2,1)S(1)}, u32[]{:S(2)}) copy-start(bf16[512,768]{1,0:T(8,128)(2,1)S(1)} %fusion.73.refs_0_) | copy-start | bytes 2359300
  158.9 17.2 %copy-start.27 = (f32[512,768]{1,0:T(8,128)}, f32[512,768]{1,0:T(8,128)S(1)}, u32[]{:S(2)}) copy-start(f32[512,768]{1,0:T(8,128)S(1)} %get-tuple-element.189) | copy-start | bytes 4718596
  178.6 91.6 %copy-start.29 = (f32[512,768]{1,0:T(8,128)}, f32[512,768]{1,0:T(8,128)S(1)}, u32[]{:S(2)}) copy-start(f32[512,768]{1,0:T(8,128)S(1)} %get-tuple-element.191) | copy-start | bytes 4718596
  178.9 9.9 %slice-start = ((s8[4718592]{0:T(1024)(128)(4,1)}), s8[4194304]{0:T(1024)(128)(4,1)S(1)}, s32[]{:S(2)}) async-start(s8[4718592]{0:T(1024)(128)(4,1)} %bitcast.88), calls=%async_computation.3 | async-start | bytes 8388608
  179.2 9.6 %copy-start.9 = (bf16[512,768]{1,0:T(8,128)(2,1)}, bf16[512,768]{1,0:T(8,128)(2,1)S(1)}, u32[]{:S(2)}) copy-start(bf16[512,768]{1,0:T(8,128)(2,1)S(1)} %fusion.75.refs_1_) | copy-start | bytes 2359300
  179.2 9.6 %slice-start.1 = ((s8[4718592]{0:T(1024)(128)(4,1)}), s8[524288]{0:T(1024)(128)(4,1)S(1)}, s32[]{:S(2)}) async-start(s8[4718592]{0:T(1024)(128)(4,1)} %bitcast.88), calls=%async_computation.4 | async-start | bytes 1048576
  191.6 17.0 %copy-start.30 = (f32[512,768]{1,0:T(8,128)}, f32[512,768]{1,0:T(8,128)S(1)}, u32[]{:S(2)}) copy-start(f32[512,768]{1,0:T(8,128)S(1)} %get-tuple-element.195) | copy-start | bytes 4718596
  211.4 7.1 %slice-start.2 = ((s8[4718592]{0:T(1024)(128)(4,1)}), s8[4194304]{0:T(1024)(128)(4,1)S(1)}, s32[]{:S(2)}) async-start(s8[4718592]{0:T(1024)(128)(4,1)} %bitcast.90), calls=%async_computation.5 | async-start | bytes 8388608
  211.7 6.8 %copy-start.13 = (bf16[512,768]{1,0:T(8,128)(2,1)}, bf16[512,768]{1,0:T(8,128)(2,1)S(1)}, u32[]{:S(2)}) copy-start(bf16[512,768]{1,0:T(8,128)(2,1)S(1)} %fusion.77.refs_2_) | copy-start | bytes 2359300
  211.7 6.8 %slice-start.3 = ((s8[4718592]{0:T(1024)(128)(4,1)}), s8[524288]{0:T(1024)(128)(4,1)S(1)}, s32[]{:S(2)}) async-start(s8[4718592]{0:T(1024)(128)(4,1)} %bitcast.90), calls=%async_computation.6 | async-start | bytes 1048576
  230.6 6.9 %copy-start.58 = (bf16[512,3072]{1,0:T(8,128)(2,1)}, bf16[512,3072]{1,0:T(8,128)(2,1)S(1)}, u32[]{:S(2)}) copy-start(bf16[512,3072]{1,0:T(8,128)(2,1)S(1)} %fusion.17.refs_5_) | copy-start | bytes 9437188
  254.9 6.2 %copy-start.31 = (f32[512,768]{1,0:T(8,128)S(1)}, f32[512,768]{1,0:T(8,128)}, u32[]{:S(2)}) copy-start(f32[512,768]{1,0:T(8,128)} %copy-done.30) | copy-start | bytes 4718596
  261.6 8.6 %copy-start.3 = (bf16[512,768]{1,0:T(8,128)(2,1)}, bf16[512,768]{1,0:T(8,128)(2,1)S(1)}, u32[]{:S(2)}) copy-start(bf16[512,768]{1,0:T(8,128)(2,1)S(1)} %get-tuple-element.142.refs_4_) | copy-start | bytes 2359300
  270.2 6.6 %copy-start.59 = (bf16[512,3072]{1,0:T(8,128)(2,1)}, bf16[512,3072]{1,0:T(8,128)(2,1)S(1)}, u32[]{:S(2)}) copy-start(bf16[512,3072]{1,0:T(8,128)(2,1)S(1)} %fusion.23.refs_4_) | copy-start | bytes 9437188
  295.6 6.2 %copy-start.28 = (f32[512,768]{1,0:T(8,128)S(1)}, f32[512,768]{1,0:T(8,128)}, u32[]{:S(2)}) copy-start(f32[512,768]{1,0:T(8,128)} %copy-done.27) | copy-start | bytes 4718596
  302.3 8.6 %copy-start.5 = (bf16[512,768]{1,0:T(8,128)(2,1)}, bf16[512,768]{1,0:T(8,128)(2,1)S(1)}, u32[]{:S(2)}) copy-start(bf16[512,768]{1,0:T(8,128)(2,1)S(1)} %get-tuple-element.138.refs_3_) | copy-start | bytes 2359300
  302.3 8.6 %copy-start.26 = (f32[512,768]{1,0:T(8,128)S(1)}, f32[512,768]{1,0:T(8,128)}, u32[]{:S(2)}) copy-start(f32[512,768]{1,0:T(8,128)} %copy-done.25) | copy-start | bytes 4718596
  310.9 6.6 %copy-start.21 = (bf16[512,3072]{1,0:T(8,128)(2,1)}, bf16[512,3072]{1,0:T(8,128)(2,1)S(1)}, u32[]{:S(2)}) copy-start(bf16[512,3072]{1,0:T(8,128)(2,1)S(1)} %fusion.29.refs_3_) | copy-start | bytes 9437188
  339.8 9.2 %copy-start = (bf16[512,768]{1,0:T(8,128)(2,1)S(1)}, bf16[512,768]{1,0:T(8,128)(2,1)}, u32[]{:S(2)}) copy-start(bf16[512,768]{1,0:T(8,128)(2,1)} %get-tuple-element.31.refs_0_) | copy-start | bytes 2359300
  339.8 9.3 %copy-start.1 = (bf16[512,768]{1,0:T(8,128)(2,1)S(1)}, bf16[512,768]{1,0:T(8,128)(2,1)}, u32[]{:S(2)}) copy-start(bf16[512,768]{1,0:T(8,128)(2,1)} %get-tuple-element.32.refs_1_) | copy-start | bytes 2359300
  339.9 9.3 %copy-start.2 = (bf16[512,768]{1,0:T(8,128)(2,1)S(1)}, bf16[512,768]{1,0:T(8,128)(2,1)}, u32[]{:S(2)}) copy-start(bf16[512,768]{1,0:T(8,128)(2,1)} %get-tuple-element.33.refs_2_) | copy-start | bytes 2359300
  349.1 3.2 copy-start.8
  349.1 3.2 copy-start.10
  354.2 11.3 %copy-start.4 = (bf16[512,768]{1,0:T(8,128)(2,1)S(1)}, bf16[512,768]{1,0:T(8,128)(2,1)}, u32[]{:S(2)}) copy-start(bf16[512,768]{1,0:T(8,128)(2,1)} %copy-done.3) | copy-start | bytes 2359300
  354.2 11.3 %copy-start.6 = (bf16[512,768]{1,0:T(8,128)(2,1)S(1)}, bf16[512,768]{1,0:T(8,128)(2,1)}, u32[]{:S(2)}) copy-start(bf16[512,768]{1,0:T(8,128)(2,1)} %copy-done.5) | copy-start | bytes 2359300
  354.2 11.3 %copy-start.20 = (bf16[512,3072]{1,0:T(8,128)(2,1)S(1)}, bf16[512,3072]{1,0:T(8,128)(2,1)}, u32[]{:S(2)}) copy-start(bf16[512,3072]{1,0:T(8,128)(2,1)} %copy-done.19) | copy-start | bytes 9437188
  365.5 11.1 %copy-start.46 = (bf16[768]{0:T(1024)(128)(2,1)S(1)}, bf16[768]{0:T(1024)(128)(2,1)}, u32[]{:S(2)}) copy-start(bf16[768]{0:T(1024)(128)(2,1)} %custom-call.4) | copy-start | bytes 4612
  365.5 12.3 %copy-start.45 = (bf16[768]{0:T(1024)(128)(2,1)S(1)}, bf16[768]{0:T(1024)(128)(2,1)}, u32[]{:S(2)}) copy-start(bf16[768]{0:T(1024)(128)(2,1)} %custom-call.3) | copy-start | bytes 4612
  (34 other events, 70.9 us)
Sparse Core Ops, SparseCore 0:
  14.2 105.9 all-gather.1
  380.4 158.4 reduce-scatter.3

commit v10 on v9

--- a/solution.py
+++ b/solution.py
@@ -236,13 +236,16 @@
 
 
 def split_qkv(packed):
+    lead = packed.shape[:-1]
     pairs = packed.shape[-1] // (3 * PAIR)
-    parts = [[], [], []]
-    for h in range(pairs):
-        for which in range(3):
-            start = (3 * h + which) * PAIR
-            parts[which].append(packed[..., start : start + PAIR])
-    return [jnp.concatenate(p, axis=-1) for p in parts]
+    grouped = packed.reshape(lead + (pairs, 3, PAIR))
+    return [grouped[..., which, :].reshape(lead + (pairs * PAIR,)) for which in range(3)]
+
+
+def as_columns(vectors, count):
+    rows = jnp.stack(vectors, axis=0)
+    rows = jnp.pad(rows, ((0, count - rows.shape[0]), (0, 0)))
+    return rows.T
 
 
 def to_hidden_order(values, groups=4):
@@ -259,9 +262,8 @@
     (qw, qb, kw, vw, vb, ow, ob, g1, s1, iw, ib, uw, ub, g2, s2) = weights
     rows, width = qw.shape
     wide = iw.shape[1]
-    columns = jnp.stack([qb, vb, ob, g1, s1, ub, g2, s2], axis=1)
-    columns = jnp.concatenate([columns, ib.reshape(rows, -1)], axis=1)
-    columns = jnp.pad(columns, ((0, 0), (0, PAIR - columns.shape[1])))
+    inner_rows = ib.reshape(rows, -1).T
+    columns = as_columns([qb, vb, ob, g1, s1, ub, g2, s2] + list(inner_rows), PAIR)
     return jnp.concatenate(
         [interleave_qkv(qw, kw, vw), ow, to_hidden_order(iw), uw.reshape(rows, wide), columns],
         axis=1,
@@ -384,10 +386,10 @@
     rows = width
     q_b, _, v_b = split_qkv(qkv_b[0])
     s2g, s2s, s1g, s1s = [sum(parts) for parts in zip(*norms)]
-    columns = jnp.stack([q_b, v_b, out_b[0], s1g, s1s, outer_b[0], s2g, s2s], axis=1)
-    inner_cols = inner_b[0].reshape(wide // rows, rows).T
-    columns = jnp.concatenate([columns, inner_cols], axis=1)
-    columns = jnp.pad(columns, ((0, 0), (0, PAIR - columns.shape[1]))).astype(jnp.bfloat16)
+    inner_rows = list(inner_b[0].reshape(wide // rows, rows))
+    columns = as_columns(
+        [q_b, v_b, out_b[0], s1g, s1s, outer_b[0], s2g, s2s] + inner_rows, PAIR
+    ).astype(jnp.bfloat16)
     packed = lax.dynamic_update_slice(packed, columns, (0, blocks * width))
     mine = lax.psum_scatter(packed, AXES, scatter_dimension=0, tiled=True).astype(jnp.float32)
     at = 0

time: 558 us -> 563 us (level)
  local copies, waits for them, and re-layouts: 32.1 us -> 39.2 us
    unnamed x150 -> x104, local copies, waits for them, and re-layouts: 17.4 us -> 15.7 us
where the time goes in v10:
time: 563 us; the launch traced here: 558 us
  waiting for transfers between devices  257 us (46%)
  matrix products  129 us (23%)
  Pallas kernels  103 us (18%)
  local copies, waits for them, and re-layouts  39.2 us (7%)
  between operations  15.5 us (3%)
  other arithmetic  15 us (3%)
    unnamed x3, waiting for transfers between devices  151 us
    all_gather x1, waiting for transfers between devices, gather_weights(): packed = lax.all_gather(pack_weights(weights), AXES, axis=0, tiled=True)  106 us
    dot_general x12, matrix products, product_nt(): return lax.dot_general(left, right, NT, preferred_element_type=jnp.float32)  69.7 us
    dot_general x12, matrix products, product(): return jnp.dot(left, right, preferred_element_type=jnp.float32)  58.9 us
    pallas_call x3, Pallas kernels, attention_backward(): pl.pallas_call(attention_backward_kernel, grid=grid, in_specs=[triple, pa...  37.9 us
    pallas_call x4, Pallas kernels, weight_grad(): pl.pallas_call(kernel, grid=grid, in_specs=in_specs, out_specs=[pl.BlockS...  34.4 us
    pallas_call x3, Pallas kernels, attention_forward(): pl.pallas_call(attention_forward_kernel, grid=grid, in_specs=[pl.BlockSpe...  30.3 us
    unnamed x104, local copies, waits for them, and re-layouts  15.7 us
  transfers between devices with their start and end apart: 2, of which 2 were waited for; matrix products, arithmetic and copies ran while one was open for 1% of the time, Pallas kernels for 0%

profile of v10, /device:TPU:0, one launch (start us, length us, event | category | flops | bytes accessed | tf_op | source)
XLA Modules:
  0.0 557.7 jit_solution(8636167926001719579)
XLA Ops:
  19.9 106.0 %all-gather.2.cloned.1.call-done = bf16[768,9344]{1,0:T(8,128)(2,1)} async-done(((bf16[24,9344]{1,0:T(8,128)(2,1)}), bf16[768,9344]{1,0:T(8,128)(2,1)}) %all-gather.2.cloned.1.call-update) | async-done | bytes 14352400 | tf_op jit(solution)/shard_map/all_gather | solution.py:276
  129.2 5.5 fusion.33.qkv_ref
  134.6 10.1 %attention_forward.3 = (bf16[512,768]{1,0:T(8,128)(2,1)}, f32[512,768]{1,0:T(8,128)}) custom-call(bf16[512,2304]{1,0:T(8,128)(2,1)} %fusion.33.qkv_ref), custom_call_target="tpu_custom_call" | custom-call | flops 1610612736 | bytes 4718592 | tf_op jit(solution)/shard_map/attention_forward/pallas_call | solution.py:119
  147.5 2.9 fusion.92
  151.2 10.6 %multiply_convert_fusion.2 = (bf16[512,3072]{1,0:T(8,128)(2,1)S(1)}, f32[512,3072]{1,0:T(8,128)}) fusion(f32[3072]{0:T(1024)S(1)} %add.368, bf16[512,768]{1,0:T(8,128)(2,1)S(1)} %fusion.73.refs_0_, bf16[768,9344]{1,0:T(8,128)(2,1)} %all-gather.2.cloned.1.call-done), kind=kOutput, calls=%fused_computation.40 | convolution fusion | flops 2431647744 | bytes 14954496 | tf_op jit(solution)/shard_map/dot_general | solution.py:22
  165.2 5.5 fusion.30.qkv_ref
  171.6 10.2 %attention_forward.4 = (bf16[512,768]{1,0:T(8,128)(2,1)}, f32[512,768]{1,0:T(8,128)}) custom-call(bf16[512,2304]{1,0:T(8,128)(2,1)} %fusion.30.qkv_ref), custom_call_target="tpu_custom_call" | custom-call | flops 1610612736 | bytes 4718592 | tf_op jit(solution)/shard_map/attention_forward/pallas_call | solution.py:119
  185.0 9.6 %multiply_convert_fusion.1 = (bf16[512,3072]{1,0:T(8,128)(2,1)S(1)}, f32[512,3072]{1,0:T(8,128)}) fusion(f32[3072]{0:T(1024)S(1)} %add.368, bf16[512,768]{1,0:T(8,128)(2,1)S(1)} %fusion.75.refs_1_, bf16[768,9344]{1,0:T(8,128)(2,1)} %all-gather.2.cloned.1.call-done), kind=kOutput, calls=%fused_computation.38 | convolution fusion | flops 2431647744 | bytes 14954496 | tf_op jit(solution)/shard_map/dot_general | solution.py:22
  198.0 5.4 fusion.31.qkv_ref
  204.3 10.0 %attention_forward.5 = (bf16[512,768]{1,0:T(8,128)(2,1)}, f32[512,768]{1,0:T(8,128)}) custom-call(bf16[512,2304]{1,0:T(8,128)(2,1)} %fusion.31.qkv_ref), custom_call_target="tpu_custom_call" | custom-call | flops 1610612736 | bytes 4718592 | tf_op jit(solution)/shard_map/attention_forward/pallas_call | solution.py:119
  217.4 6.7 %multiply_convert_fusion = (bf16[512,3072]{1,0:T(8,128)(2,1)S(1)}, f32[512,3072]{1,0:T(8,128)S(1)}) fusion(f32[3072]{0:T(1024)S(1)} %add.368, bf16[512,768]{1,0:T(8,128)(2,1)S(1)} %fusion.77.refs_2_, bf16[768,9344]{1,0:T(8,128)(2,1)} %all-gather.2.cloned.1.call-done), kind=kOutput, calls=%fused_computation.36 | convolution fusion | flops 2431647744 | bytes 14954496 | tf_op jit(solution)/shard_map/dot_general | solution.py:22
  230.7 5.7 %fusion.17.refs_5_ = bf16[512,3072]{1,0:T(8,128)(2,1)S(1)} fusion(f32[512,3072]{1,0:T(8,128)S(1)} %get-tuple-element.178, bf16[512,768]{1,0:T(8,128)(2,1)S(1)} %get-tuple-element.153.refs_5_, bf16[3072,768]{1,0:T(8,128)(2,1)S(1)} %bitcast.83, f32[3072]{0:T(1024)S(1)} %add.368), kind=kOutput, calls=%fused_computation.23 | convolution fusion | flops 2445803520 | bytes 14954496 | tf_op jit(solution)/shard_map/dot_general | solution.py:26
  236.4 6.9 %multiply_reduce_fusion.3 = (f32[768]{0:T(1024)S(1)}, f32[512]{0:T(512)S(1)}, f32[512]{0:T(512)S(1)}, f32[768]{0:T(1024)S(1)}, f32[512,768]{1,0:T(8,128)S(1)}) fusion(f32[512,768]{1,0:T(8,128)S(1)} %get-tuple-element.176, f32[512]{0:T(512)S(1)} %add_rsqrt_fusion.1, f32[512]{0:T(512)S(1)} %broadcast_multiply_fusion.13, f32[768]{0:T(1024)S(1)} %get-tuple-element.132, ...), kind=kOutput, calls=%fused_computation.65 | convolution fusion | flops 2423387648 | bytes 13400064 | tf_op jit(solution)/shard_map/dot_general | solution.py:26
  245.0 3.0 convolution_convert_fusion.2.g_ref
  247.9 12.7 %attention_backward.3.refs_5_ = bf16[512,2304]{1,0:T(8,128)(2,1)} custom-call(bf16[512,2304]{1,0:T(8,128)(2,1)} %fusion.31.qkv_ref, f32[512,768]{1,0:T(8,128)} %get-tuple-element.34.lt_ref, bf16[512,768]{1,0:T(8,128)(2,1)} %convolution_convert_fusion.2.g_ref), custom_call_target="tpu_custom_call" | custom-call | flops 4026531840 | bytes 7077888 | tf_op jit(solution)/shard_map/attention_backward/pallas_call | solution.py:144
  260.6 6.2 %multiply_reduce_fusion.1 = (f32[768]{0:T(1024)S(1)}, f32[512]{0:T(512)S(1)}, f32[512]{0:T(512)S(1)}, f32[768]{0:T(1024)S(1)}, f32[512,768]{1,0:T(8,128)S(1)}) fusion(f32[512,768]{1,0:T(8,128)} %copy-done.30, f32[512]{0:T(512)S(1)} %add_rsqrt_fusion.2, f32[512]{0:T(512)S(1)} %broadcast_multiply_fusion.14, f32[768]{0:T(1024)S(1)} %get-tuple-element.128, ...), kind=kOutput, calls=%fused_computation.63 | convolution fusion | flops 1815868928 | bytes 10634240 | tf_op jit(solution)/shard_map/dot_general | solution.py:26
  267.3 8.5 %fusion.23.refs_4_ = bf16[512,3072]{1,0:T(8,128)(2,1)S(1)} fusion(f32[512,3072]{1,0:T(8,128)} %get-tuple-element.172, bf16[512,768]{1,0:T(8,128)(2,1)S(1)} %get-tuple-element.145.refs_4_, bf16[3072,768]{1,0:T(8,128)(2,1)} %copy-done.32, f32[3072]{0:T(1024)S(1)} %add.368), kind=kOutput, calls=%fused_computation.29 | convolution fusion | flops 2445803520 | bytes 14954496 | tf_op jit(solution)/shard_map/dot_general | solution.py:26
  275.9 6.6 %multiply_reduce_fusion.4 = (f32[768]{0:T(1024)S(1)}, f32[512]{0:T(512)S(1)}, f32[512]{0:T(512)S(1)}, f32[768]{0:T(1024)S(1)}, f32[512,768]{1,0:T(8,128)S(1)}) fusion(f32[512,768]{1,0:T(8,128)S(1)} %get-tuple-element.170, f32[512]{0:T(512)S(1)} %add_rsqrt_fusion.3, f32[512]{0:T(512)S(1)} %broadcast_multiply_fusion.15, f32[768]{0:T(1024)S(1)} %get-tuple-element.132, ...), kind=kOutput, calls=%fused_computation.66 | convolution fusion | flops 2419848704 | bytes 12600320 | tf_op jit(solution)/shard_map/dot_general | solution.py:26
  282.5 3.1 fusion.89
  285.6 3.0 convolution_convert_fusion.1.g_ref
  288.6 12.7 %attention_backward.4.refs_4_ = bf16[512,2304]{1,0:T(8,128)(2,1)} custom-call(bf16[512,2304]{1,0:T(8,128)(2,1)} %fusion.30.qkv_ref, f32[512,768]{1,0:T(8,128)} %get-tuple-element.35.lt_ref, bf16[512,768]{1,0:T(8,128)(2,1)} %convolution_convert_fusion.1.g_ref), custom_call_target="tpu_custom_call" | custom-call | flops 4026531840 | bytes 7077888 | tf_op jit(solution)/shard_map/attention_backward/pallas_call | solution.py:144
  301.3 6.2 %multiply_reduce_fusion.2 = (f32[768]{0:T(1024)S(1)}, f32[512]{0:T(512)S(1)}, f32[512]{0:T(512)S(1)}, f32[768]{0:T(1024)S(1)}, f32[512,768]{1,0:T(8,128)S(1)}) fusion(f32[512,768]{1,0:T(8,128)} %copy-done.27, f32[512]{0:T(512)S(1)} %add_rsqrt_fusion.4, f32[512]{0:T(512)S(1)} %broadcast_multiply_fusion.16, f32[768]{0:T(1024)S(1)} %get-tuple-element.128, ...), kind=kOutput, calls=%fused_computation.64 | convolution fusion | flops 1815868928 | bytes 10634240 | tf_op jit(solution)/shard_map/dot_general | solution.py:26
  308.1 8.6 %fusion.29.refs_3_ = bf16[512,3072]{1,0:T(8,128)(2,1)S(1)} fusion(f32[512,3072]{1,0:T(8,128)} %get-tuple-element.166, bf16[512,768]{1,0:T(8,128)(2,1)S(1)} %get-tuple-element.141.refs_3_, bf16[3072,768]{1,0:T(8,128)(2,1)} %copy-done.32, f32[3072]{0:T(1024)S(1)} %add.368), kind=kOutput, calls=%fused_computation.35 | convolution fusion | flops 2445803520 | bytes 14954496 | tf_op jit(solution)/shard_map/dot_general | solution.py:26
  316.7 6.6 %multiply_reduce_fusion.5 = (f32[768]{0:T(1024)S(1)}, f32[512]{0:T(512)S(1)}, f32[512]{0:T(512)S(1)}, f32[768]{0:T(1024)S(1)}, f32[512,768]{1,0:T(8,128)S(1)}) fusion(f32[512,768]{1,0:T(8,128)S(1)} %copy-done.26, f32[512]{0:T(512)S(1)} %add_rsqrt_fusion.5, f32[512]{0:T(512)S(1)} %broadcast_multiply_fusion.17, f32[768]{0:T(1024)S(1)} %get-tuple-element.132, ...), kind=kOutput, calls=%fused_computation.67 | convolution fusion | flops 2419848704 | bytes 12600320 | tf_op jit(solution)/shard_map/dot_general | solution.py:26
  325.0 3.0 convolution_convert_fusion.g_ref
  328.0 12.5 %attention_backward.5.refs_3_ = bf16[512,2304]{1,0:T(8,128)(2,1)} custom-call(bf16[512,2304]{1,0:T(8,128)(2,1)} %fusion.33.qkv_ref, f32[512,768]{1,0:T(8,128)} %get-tuple-element.36.lt_ref, bf16[512,768]{1,0:T(8,128)(2,1)} %convolution_convert_fusion.g_ref), custom_call_target="tpu_custom_call" | custom-call | flops 4026531840 | bytes 7077888 | tf_op jit(solution)/shard_map/attention_backward/pallas_call | solution.py:144
  345.6 9.2 %weight_grad.4 = (bf16[768,9344]{1,0:T(8,128)(2,1)}, f32[1,2304]{1,0:T(1,128)S(1)}) custom-call(bf16[512,768]{1,0:T(8,128)(2,1)S(1)} %copy-done.18, bf16[512,768]{1,0:T(8,128)(2,1)S(1)} %copy-done.12, bf16[512,768]{1,0:T(8,128)(2,1)S(1)} %copy-done.16, bf16[512,2304]{1,0:T(8,128)(2,1)S(1)} %copy-done.23, bf16[512,2304]{1,0:T(8,128)(2,1)} %attention_backward.4.refs_4_, ...), custom_call_target="tpu_custom_call" | custom-call | flops 5435817984 | bytes 12976128 | tf_op jit(solution)/shard_map/weight_grad/pallas_call | solution.py:206
  354.9 3.1 weight_grad.5
  359.9 11.2 %weight_grad.6 = (bf16[768,9344]{1,0:T(8,128)(2,1)}, f32[1,3072]{1,0:T(1,128)S(1)}) custom-call(bf16[512,768]{1,0:T(8,128)(2,1)S(1)} %copy-done.8, bf16[512,768]{1,0:T(8,128)(2,1)S(1)} %copy-done.10, bf16[512,768]{1,0:T(8,128)(2,1)S(1)} %copy-done.14, bf16[512,3072]{1,0:T(8,128)(2,1)S(1)} %copy-done.22, ...), custom_call_target="tpu_custom_call", output_to_operand_aliasing={{0}: (6, {})} | custom-call | flops 7247757312 | bytes 16515072 | tf_op jit(solution)/shard_map/weight_grad/pallas_call | solution.py:206
  371.1 11.0 %weight_grad.7 = (bf16[768,9344]{1,0:T(8,128)(2,1)}, f32[1,768]{1,0:T(1,128)S(1)}) custom-call(bf16[512,3072]{1,0:T(8,128)(2,1)S(1)} %copy-done.20, bf16[512,3072]{1,0:T(8,128)(2,1)} %copy-done.39, bf16[512,3072]{1,0:T(8,128)(2,1)} %copy-done.40, bf16[512,768]{1,0:T(8,128)(2,1)S(1)} %copy-done.6, ...), custom_call_target="tpu_custom_call", output_to_operand_aliasing={{0}: (6, {})} | custom-call | flops 7247757312 | bytes 16515072 | tf_op jit(solution)/shard_map/weight_grad/pallas_call | solution.py:206
  384.9 5.5 add_convert_fusion
  390.4 150.7 %reduce-scatter.4.cloned.1.call-done = bf16[24,9344]{1,0:T(8,128)(2,1)} async-done(((bf16[768,9344]{1,0:T(8,128)(2,1)}), bf16[24,9344]{1,0:T(8,128)(2,1)}) %reduce-scatter.4.cloned.1.call-update) | async-done | bytes 448528
  (215 shorter events, 64.0 us)
Async XLA Ops:
  7.2 10.6 %copy-start.36 = (bf16[24,3072]{1,0:T(8,128)(2,1)S(1)}, bf16[24,3072]{1,0:T(8,128)(2,1)}, u32[]{:S(2)}) copy-start(bf16[24,3072]{1,0:T(8,128)(2,1)} %param.30) | copy-start | bytes 442372
  7.2 118.7 %all-gather.2.cloned.1.call-start = ((), (), s32[]{:S(2)}) async-start(), calls=%async_computation.1 | async-start | bytes 14800896 | tf_op jit(solution)/shard_map/all_gather | solution.py:276
  19.8 521.3 %reduce-scatter.4.cloned.1.call-start = ((), (), s32[]{:S(2)}) async-start(), calls=%async_computation.2 | async-start | bytes 14800896
  147.1 14.7 %copy-start.25 = (f32[512,768]{1,0:T(8,128)}, f32[512,768]{1,0:T(8,128)S(1)}, u32[]{:S(2)}) copy-start(f32[512,768]{1,0:T(8,128)S(1)} %get-tuple-element.164) | copy-start | bytes 4718596
  150.9 10.9 %copy-start.32 = (bf16[3072,768]{1,0:T(8,128)(2,1)}, bf16[3072,768]{1,0:T(8,128)(2,1)S(1)}, u32[]{:S(2)}) copy-start(bf16[3072,768]{1,0:T(8,128)(2,1)S(1)} %pad_maximum_fusion) | copy-start | bytes 14155780
  151.2 10.6 %copy-start.7 = (bf16[512,768]{1,0:T(8,128)(2,1)}, bf16[512,768]{1,0:T(8,128)(2,1)S(1)}, u32[]{:S(2)}) copy-start(bf16[512,768]{1,0:T(8,128)(2,1)S(1)} %fusion.73.refs_0_) | copy-start | bytes 2359300
  164.6 17.2 %copy-start.27 = (f32[512,768]{1,0:T(8,128)}, f32[512,768]{1,0:T(8,128)S(1)}, u32[]{:S(2)}) copy-start(f32[512,768]{1,0:T(8,128)S(1)} %get-tuple-element.168) | copy-start | bytes 4718596
  184.3 91.6 %copy-start.29 = (f32[512,768]{1,0:T(8,128)}, f32[512,768]{1,0:T(8,128)S(1)}, u32[]{:S(2)}) copy-start(f32[512,768]{1,0:T(8,128)S(1)} %get-tuple-element.170) | copy-start | bytes 4718596
  184.6 9.9 %slice-start = ((s8[4718592]{0:T(1024)(128)(4,1)}), s8[4194304]{0:T(1024)(128)(4,1)S(1)}, s32[]{:S(2)}) async-start(s8[4718592]{0:T(1024)(128)(4,1)} %bitcast.80), calls=%async_computation.3 | async-start | bytes 8388608
  184.9 9.6 %copy-start.9 = (bf16[512,768]{1,0:T(8,128)(2,1)}, bf16[512,768]{1,0:T(8,128)(2,1)S(1)}, u32[]{:S(2)}) copy-start(bf16[512,768]{1,0:T(8,128)(2,1)S(1)} %fusion.75.refs_1_) | copy-start | bytes 2359300
  185.0 9.6 %slice-start.1 = ((s8[4718592]{0:T(1024)(128)(4,1)}), s8[524288]{0:T(1024)(128)(4,1)S(1)}, s32[]{:S(2)}) async-start(s8[4718592]{0:T(1024)(128)(4,1)} %bitcast.80), calls=%async_computation.4 | async-start | bytes 1048576
  197.3 17.0 %copy-start.30 = (f32[512,768]{1,0:T(8,128)}, f32[512,768]{1,0:T(8,128)S(1)}, u32[]{:S(2)}) copy-start(f32[512,768]{1,0:T(8,128)S(1)} %get-tuple-element.174) | copy-start | bytes 4718596
  217.1 7.1 %slice-start.2 = ((s8[4718592]{0:T(1024)(128)(4,1)}), s8[4194304]{0:T(1024)(128)(4,1)S(1)}, s32[]{:S(2)}) async-start(s8[4718592]{0:T(1024)(128)(4,1)} %bitcast.82), calls=%async_computation.5 | async-start | bytes 8388608
  217.4 6.8 %copy-start.13 = (bf16[512,768]{1,0:T(8,128)(2,1)}, bf16[512,768]{1,0:T(8,128)(2,1)S(1)}, u32[]{:S(2)}) copy-start(bf16[512,768]{1,0:T(8,128)(2,1)S(1)} %fusion.77.refs_2_) | copy-start | bytes 2359300
  217.4 6.8 %slice-start.3 = ((s8[4718592]{0:T(1024)(128)(4,1)}), s8[524288]{0:T(1024)(128)(4,1)S(1)}, s32[]{:S(2)}) async-start(s8[4718592]{0:T(1024)(128)(4,1)} %bitcast.82), calls=%async_computation.6 | async-start | bytes 1048576
  236.4 6.9 %copy-start.41 = (bf16[512,3072]{1,0:T(8,128)(2,1)}, bf16[512,3072]{1,0:T(8,128)(2,1)S(1)}, u32[]{:S(2)}) copy-start(bf16[512,3072]{1,0:T(8,128)(2,1)S(1)} %fusion.17.refs_5_) | copy-start | bytes 9437188
  260.6 6.2 %copy-start.31 = (f32[512,768]{1,0:T(8,128)S(1)}, f32[512,768]{1,0:T(8,128)}, u32[]{:S(2)}) copy-start(f32[512,768]{1,0:T(8,128)} %copy-done.30) | copy-start | bytes 4718596
  267.3 8.6 %copy-start.3 = (bf16[512,768]{1,0:T(8,128)(2,1)}, bf16[512,768]{1,0:T(8,128)(2,1)S(1)}, u32[]{:S(2)}) copy-start(bf16[512,768]{1,0:T(8,128)(2,1)S(1)} %get-tuple-element.145.refs_4_) | copy-start | bytes 2359300
  275.9 6.6 %copy-start.42 = (bf16[512,3072]{1,0:T(8,128)(2,1)}, bf16[512,3072]{1,0:T(8,128)(2,1)S(1)}, u32[]{:S(2)}) copy-start(bf16[512,3072]{1,0:T(8,128)(2,1)S(1)} %fusion.23.refs_4_) | copy-start | bytes 9437188
  301.3 6.2 %copy-start.28 = (f32[512,768]{1,0:T(8,128)S(1)}, f32[512,768]{1,0:T(8,128)}, u32[]{:S(2)}) copy-start(f32[512,768]{1,0:T(8,128)} %copy-done.27) | copy-start | bytes 4718596
  308.1 8.6 %copy-start.5 = (bf16[512,768]{1,0:T(8,128)(2,1)}, bf16[512,768]{1,0:T(8,128)(2,1)S(1)}, u32[]{:S(2)}) copy-start(bf16[512,768]{1,0:T(8,128)(2,1)S(1)} %get-tuple-element.141.refs_3_) | copy-start | bytes 2359300
  308.1 8.6 %copy-start.26 = (f32[512,768]{1,0:T(8,128)S(1)}, f32[512,768]{1,0:T(8,128)}, u32[]{:S(2)}) copy-start(f32[512,768]{1,0:T(8,128)} %copy-done.25) | copy-start | bytes 4718596
  316.7 6.6 %copy-start.21 = (bf16[512,3072]{1,0:T(8,128)(2,1)}, bf16[512,3072]{1,0:T(8,128)(2,1)S(1)}, u32[]{:S(2)}) copy-start(bf16[512,3072]{1,0:T(8,128)(2,1)S(1)} %fusion.29.refs_3_) | copy-start | bytes 9437188
  345.6 9.2 %copy-start = (bf16[512,768]{1,0:T(8,128)(2,1)S(1)}, bf16[512,768]{1,0:T(8,128)(2,1)}, u32[]{:S(2)}) copy-start(bf16[512,768]{1,0:T(8,128)(2,1)} %get-tuple-element.31.refs_0_) | copy-start | bytes 2359300
  345.6 9.2 %copy-start.1 = (bf16[512,768]{1,0:T(8,128)(2,1)S(1)}, bf16[512,768]{1,0:T(8,128)(2,1)}, u32[]{:S(2)}) copy-start(bf16[512,768]{1,0:T(8,128)(2,1)} %get-tuple-element.32.refs_1_) | copy-start | bytes 2359300
  345.6 9.2 %copy-start.2 = (bf16[512,768]{1,0:T(8,128)(2,1)S(1)}, bf16[512,768]{1,0:T(8,128)(2,1)}, u32[]{:S(2)}) copy-start(bf16[512,768]{1,0:T(8,128)(2,1)} %get-tuple-element.33.refs_2_) | copy-start | bytes 2359300
  354.8 3.2 copy-start.8
  354.8 3.2 copy-start.10
  359.9 11.2 %copy-start.4 = (bf16[512,768]{1,0:T(8,128)(2,1)S(1)}, bf16[512,768]{1,0:T(8,128)(2,1)}, u32[]{:S(2)}) copy-start(bf16[512,768]{1,0:T(8,128)(2,1)} %copy-done.3) | copy-start | bytes 2359300
  359.9 11.2 %copy-start.6 = (bf16[512,768]{1,0:T(8,128)(2,1)S(1)}, bf16[512,768]{1,0:T(8,128)(2,1)}, u32[]{:S(2)}) copy-start(bf16[512,768]{1,0:T(8,128)(2,1)} %copy-done.5) | copy-start | bytes 2359300
  359.9 11.2 %copy-start.20 = (bf16[512,3072]{1,0:T(8,128)(2,1)S(1)}, bf16[512,3072]{1,0:T(8,128)(2,1)}, u32[]{:S(2)}) copy-start(bf16[512,3072]{1,0:T(8,128)(2,1)} %copy-done.19) | copy-start | bytes 9437188
  541.1 5.0 copy-start.33
  (17 other events, 30.4 us)
Sparse Core Ops, SparseCore 0:
  19.9 105.9 all-gather.1
  383.3 157.6 reduce-scatter.3

commit v11 on v9

--- a/solution.py
+++ b/solution.py
@@ -245,6 +245,18 @@
     return [jnp.concatenate(p, axis=-1) for p in parts]
 
 
+def split_qkv_rows(packed):
+    pairs = packed.shape[-1] // (3 * PAIR)
+    grouped = packed.reshape(pairs, 3, PAIR)
+    return [grouped[:, which, :].reshape(-1) for which in range(3)]
+
+
+def as_columns(vectors, count):
+    rows = jnp.stack(vectors, axis=0)
+    rows = jnp.pad(rows, ((0, count - rows.shape[0]), (0, 0)))
+    return rows.T
+
+
 def to_hidden_order(values, groups=4):
     lead, n = values.shape[:-1], values.shape[-1]
     return jnp.swapaxes(values.reshape(lead + (n // groups, groups)), -1, -2).reshape(lead + (n,))
@@ -382,12 +394,12 @@
         across(kept, "inner_low"), across(saved, "outer_low"), into=packed, at=at, stack=True
     )
     rows = width
-    q_b, _, v_b = split_qkv(qkv_b[0])
+    q_b, _, v_b = split_qkv_rows(qkv_b[0])
     s2g, s2s, s1g, s1s = [sum(parts) for parts in zip(*norms)]
-    columns = jnp.stack([q_b, v_b, out_b[0], s1g, s1s, outer_b[0], s2g, s2s], axis=1)
-    inner_cols = inner_b[0].reshape(wide // rows, rows).T
-    columns = jnp.concatenate([columns, inner_cols], axis=1)
-    columns = jnp.pad(columns, ((0, 0), (0, PAIR - columns.shape[1]))).astype(jnp.bfloat16)
+    inner_rows = list(inner_b[0].reshape(wide // rows, rows))
+    columns = as_columns(
+        [q_b, v_b, out_b[0], s1g, s1s, outer_b[0], s2g, s2s] + inner_rows, PAIR
+    ).astype(jnp.bfloat16)
     packed = lax.dynamic_update_slice(packed, columns, (0, blocks * width))
     mine = lax.psum_scatter(packed, AXES, scatter_dimension=0, tiled=True).astype(jnp.float32)
     at = 0

time: 558 us -> 561 us (level)
    unnamed x150 -> x112, local copies, waits for them, and re-layouts: 17.4 us -> 13.8 us
where the time goes in v11:
time: 561 us; the launch traced here: 555 us
  waiting for transfers between devices  257 us (46%)
  matrix products  129 us (23%)
  Pallas kernels  103 us (18%)
  local copies, waits for them, and re-layouts  35.7 us (6%)
  other arithmetic  16.1 us (3%)
  between operations  15.5 us (3%)
    unnamed x3, waiting for transfers between devices  151 us
    all_gather x1, waiting for transfers between devices, gather_weights(): packed = lax.all_gather(pack_weights(weights), AXES, axis=0, tiled=True)  106 us
    dot_general x12, matrix products, product_nt(): return lax.dot_general(left, right, NT, preferred_element_type=jnp.float32)  69.7 us
    dot_general x12, matrix products, product(): return jnp.dot(left, right, preferred_element_type=jnp.float32)  58.9 us
    pallas_call x3, Pallas kernels, attention_backward(): pl.pallas_call(attention_backward_kernel, grid=grid, in_specs=[triple, pa...  37.9 us
    pallas_call x4, Pallas kernels, weight_grad(): pl.pallas_call(kernel, grid=grid, in_specs=in_specs, out_specs=[pl.BlockS...  34.4 us
    pallas_call x3, Pallas kernels, attention_forward(): pl.pallas_call(attention_forward_kernel, grid=grid, in_specs=[pl.BlockSpe...  30.3 us
    unnamed x112, local copies, waits for them, and re-layouts  13.8 us
  transfers between devices with their start and end apart: 2, of which 2 were waited for; matrix products, arithmetic and copies ran while one was open for 1% of the time, Pallas kernels for 0%

profile of v11, /device:TPU:0, one launch (start us, length us, event | category | flops | bytes accessed | tf_op | source)
XLA Modules:
  0.0 555.3 jit_solution(804181407729167959)
XLA Ops:
  19.9 106.0 %all-gather.2.cloned.1.call-done = bf16[768,9344]{1,0:T(8,128)(2,1)} async-done(((bf16[24,9344]{1,0:T(8,128)(2,1)}), bf16[768,9344]{1,0:T(8,128)(2,1)}) %all-gather.2.cloned.1.call-update) | async-done | bytes 14352400 | tf_op jit(solution)/shard_map/all_gather | solution.py:286
  129.2 5.5 fusion.33.qkv_ref
  134.6 10.1 %attention_forward.3 = (bf16[512,768]{1,0:T(8,128)(2,1)}, f32[512,768]{1,0:T(8,128)}) custom-call(bf16[512,2304]{1,0:T(8,128)(2,1)} %fusion.33.qkv_ref), custom_call_target="tpu_custom_call" | custom-call | flops 1610612736 | bytes 4718592 | tf_op jit(solution)/shard_map/attention_forward/pallas_call | solution.py:119
  147.5 2.9 fusion.92
  151.2 10.6 %multiply_convert_fusion.2 = (bf16[512,3072]{1,0:T(8,128)(2,1)S(1)}, f32[512,3072]{1,0:T(8,128)}) fusion(f32[3072]{0:T(1024)S(1)} %add.368, bf16[512,768]{1,0:T(8,128)(2,1)S(1)} %fusion.73.refs_0_, bf16[768,9344]{1,0:T(8,128)(2,1)} %all-gather.2.cloned.1.call-done), kind=kOutput, calls=%fused_computation.40 | convolution fusion | flops 2431647744 | bytes 14954496 | tf_op jit(solution)/shard_map/dot_general | solution.py:22
  165.2 5.5 fusion.30.qkv_ref
  171.6 10.2 %attention_forward.4 = (bf16[512,768]{1,0:T(8,128)(2,1)}, f32[512,768]{1,0:T(8,128)}) custom-call(bf16[512,2304]{1,0:T(8,128)(2,1)} %fusion.30.qkv_ref), custom_call_target="tpu_custom_call" | custom-call | flops 1610612736 | bytes 4718592 | tf_op jit(solution)/shard_map/attention_forward/pallas_call | solution.py:119
  185.0 9.6 %multiply_convert_fusion.1 = (bf16[512,3072]{1,0:T(8,128)(2,1)S(1)}, f32[512,3072]{1,0:T(8,128)}) fusion(f32[3072]{0:T(1024)S(1)} %add.368, bf16[512,768]{1,0:T(8,128)(2,1)S(1)} %fusion.75.refs_1_, bf16[768,9344]{1,0:T(8,128)(2,1)} %all-gather.2.cloned.1.call-done), kind=kOutput, calls=%fused_computation.38 | convolution fusion | flops 2431647744 | bytes 14954496 | tf_op jit(solution)/shard_map/dot_general | solution.py:22
  198.0 5.4 fusion.31.qkv_ref
  204.3 10.0 %attention_forward.5 = (bf16[512,768]{1,0:T(8,128)(2,1)}, f32[512,768]{1,0:T(8,128)}) custom-call(bf16[512,2304]{1,0:T(8,128)(2,1)} %fusion.31.qkv_ref), custom_call_target="tpu_custom_call" | custom-call | flops 1610612736 | bytes 4718592 | tf_op jit(solution)/shard_map/attention_forward/pallas_call | solution.py:119
  217.4 6.7 %multiply_convert_fusion = (bf16[512,3072]{1,0:T(8,128)(2,1)S(1)}, f32[512,3072]{1,0:T(8,128)S(1)}) fusion(f32[3072]{0:T(1024)S(1)} %add.368, bf16[512,768]{1,0:T(8,128)(2,1)S(1)} %fusion.77.refs_2_, bf16[768,9344]{1,0:T(8,128)(2,1)} %all-gather.2.cloned.1.call-done), kind=kOutput, calls=%fused_computation.36 | convolution fusion | flops 2431647744 | bytes 14954496 | tf_op jit(solution)/shard_map/dot_general | solution.py:22
  230.7 5.7 %fusion.17.refs_5_ = bf16[512,3072]{1,0:T(8,128)(2,1)S(1)} fusion(f32[512,3072]{1,0:T(8,128)S(1)} %get-tuple-element.193, bf16[512,768]{1,0:T(8,128)(2,1)S(1)} %get-tuple-element.150.refs_5_, bf16[3072,768]{1,0:T(8,128)(2,1)S(1)} %bitcast.68, f32[3072]{0:T(1024)S(1)} %add.368), kind=kOutput, calls=%fused_computation.23 | convolution fusion | flops 2445803520 | bytes 14954496 | tf_op jit(solution)/shard_map/dot_general | solution.py:26
  236.4 6.9 %multiply_reduce_fusion.3 = (f32[768]{0:T(1024)S(1)}, f32[512]{0:T(512)S(1)}, f32[512]{0:T(512)S(1)}, f32[768]{0:T(1024)S(1)}, f32[512,768]{1,0:T(8,128)S(1)}) fusion(f32[512,768]{1,0:T(8,128)S(1)} %get-tuple-element.191, f32[512]{0:T(512)S(1)} %add_rsqrt_fusion.1, f32[512]{0:T(512)S(1)} %broadcast_multiply_fusion.13, f32[768]{0:T(1024)S(1)} %get-tuple-element.132, ...), kind=kOutput, calls=%fused_computation.65 | convolution fusion | flops 2423387648 | bytes 13400064 | tf_op jit(solution)/shard_map/dot_general | solution.py:26
  245.0 3.0 convolution_convert_fusion.2.g_ref
  247.9 12.7 %attention_backward.3.refs_5_ = bf16[512,2304]{1,0:T(8,128)(2,1)} custom-call(bf16[512,2304]{1,0:T(8,128)(2,1)} %fusion.31.qkv_ref, f32[512,768]{1,0:T(8,128)} %get-tuple-element.34.lt_ref, bf16[512,768]{1,0:T(8,128)(2,1)} %convolution_convert_fusion.2.g_ref), custom_call_target="tpu_custom_call" | custom-call | flops 4026531840 | bytes 7077888 | tf_op jit(solution)/shard_map/attention_backward/pallas_call | solution.py:144
  260.6 6.2 %multiply_reduce_fusion.1 = (f32[768]{0:T(1024)S(1)}, f32[512]{0:T(512)S(1)}, f32[512]{0:T(512)S(1)}, f32[768]{0:T(1024)S(1)}, f32[512,768]{1,0:T(8,128)S(1)}) fusion(f32[512,768]{1,0:T(8,128)} %copy-done.30, f32[512]{0:T(512)S(1)} %add_rsqrt_fusion.2, f32[512]{0:T(512)S(1)} %broadcast_multiply_fusion.14, f32[768]{0:T(1024)S(1)} %get-tuple-element.128, ...), kind=kOutput, calls=%fused_computation.63 | convolution fusion | flops 1815868928 | bytes 10634240 | tf_op jit(solution)/shard_map/dot_general | solution.py:26
  267.3 8.5 %fusion.23.refs_4_ = bf16[512,3072]{1,0:T(8,128)(2,1)S(1)} fusion(f32[512,3072]{1,0:T(8,128)} %get-tuple-element.187, bf16[512,768]{1,0:T(8,128)(2,1)S(1)} %get-tuple-element.142.refs_4_, bf16[3072,768]{1,0:T(8,128)(2,1)} %copy-done.32, f32[3072]{0:T(1024)S(1)} %add.368), kind=kOutput, calls=%fused_computation.29 | convolution fusion | flops 2445803520 | bytes 14954496 | tf_op jit(solution)/shard_map/dot_general | solution.py:26
  275.9 6.6 %multiply_reduce_fusion.4 = (f32[768]{0:T(1024)S(1)}, f32[512]{0:T(512)S(1)}, f32[512]{0:T(512)S(1)}, f32[768]{0:T(1024)S(1)}, f32[512,768]{1,0:T(8,128)S(1)}) fusion(f32[512,768]{1,0:T(8,128)S(1)} %get-tuple-element.185, f32[512]{0:T(512)S(1)} %add_rsqrt_fusion.3, f32[512]{0:T(512)S(1)} %broadcast_multiply_fusion.15, f32[768]{0:T(1024)S(1)} %get-tuple-element.132, ...), kind=kOutput, calls=%fused_computation.66 | convolution fusion | flops 2419848704 | bytes 12600320 | tf_op jit(solution)/shard_map/dot_general | solution.py:26
  282.5 3.1 fusion.89
  285.6 3.0 convolution_convert_fusion.1.g_ref
  288.6 12.7 %attention_backward.4.refs_4_ = bf16[512,2304]{1,0:T(8,128)(2,1)} custom-call(bf16[512,2304]{1,0:T(8,128)(2,1)} %fusion.30.qkv_ref, f32[512,768]{1,0:T(8,128)} %get-tuple-element.35.lt_ref, bf16[512,768]{1,0:T(8,128)(2,1)} %convolution_convert_fusion.1.g_ref), custom_call_target="tpu_custom_call" | custom-call | flops 4026531840 | bytes 7077888 | tf_op jit(solution)/shard_map/attention_backward/pallas_call | solution.py:144
  301.3 6.2 %multiply_reduce_fusion.2 = (f32[768]{0:T(1024)S(1)}, f32[512]{0:T(512)S(1)}, f32[512]{0:T(512)S(1)}, f32[768]{0:T(1024)S(1)}, f32[512,768]{1,0:T(8,128)S(1)}) fusion(f32[512,768]{1,0:T(8,128)} %copy-done.27, f32[512]{0:T(512)S(1)} %add_rsqrt_fusion.4, f32[512]{0:T(512)S(1)} %broadcast_multiply_fusion.16, f32[768]{0:T(1024)S(1)} %get-tuple-element.128, ...), kind=kOutput, calls=%fused_computation.64 | convolution fusion | flops 1815868928 | bytes 10634240 | tf_op jit(solution)/shard_map/dot_general | solution.py:26
  308.1 8.6 %fusion.29.refs_3_ = bf16[512,3072]{1,0:T(8,128)(2,1)S(1)} fusion(f32[512,3072]{1,0:T(8,128)} %get-tuple-element.181, bf16[512,768]{1,0:T(8,128)(2,1)S(1)} %get-tuple-element.138.refs_3_, bf16[3072,768]{1,0:T(8,128)(2,1)} %copy-done.32, f32[3072]{0:T(1024)S(1)} %add.368), kind=kOutput, calls=%fused_computation.35 | convolution fusion | flops 2445803520 | bytes 14954496 | tf_op jit(solution)/shard_map/dot_general | solution.py:26
  316.7 6.6 %multiply_reduce_fusion.5 = (f32[768]{0:T(1024)S(1)}, f32[512]{0:T(512)S(1)}, f32[512]{0:T(512)S(1)}, f32[768]{0:T(1024)S(1)}, f32[512,768]{1,0:T(8,128)S(1)}) fusion(f32[512,768]{1,0:T(8,128)S(1)} %copy-done.26, f32[512]{0:T(512)S(1)} %add_rsqrt_fusion.5, f32[512]{0:T(512)S(1)} %broadcast_multiply_fusion.17, f32[768]{0:T(1024)S(1)} %get-tuple-element.132, ...), kind=kOutput, calls=%fused_computation.67 | convolution fusion | flops 2419848704 | bytes 12600320 | tf_op jit(solution)/shard_map/dot_general | solution.py:26
  325.0 3.0 convolution_convert_fusion.g_ref
  328.0 12.5 %attention_backward.5.refs_3_ = bf16[512,2304]{1,0:T(8,128)(2,1)} custom-call(bf16[512,2304]{1,0:T(8,128)(2,1)} %fusion.33.qkv_ref, f32[512,768]{1,0:T(8,128)} %get-tuple-element.36.lt_ref, bf16[512,768]{1,0:T(8,128)(2,1)} %convolution_convert_fusion.g_ref), custom_call_target="tpu_custom_call" | custom-call | flops 4026531840 | bytes 7077888 | tf_op jit(solution)/shard_map/attention_backward/pallas_call | solution.py:144
  345.6 9.2 %weight_grad.4 = (bf16[768,9344]{1,0:T(8,128)(2,1)}, f32[1,2304]{1,0:T(1,128)S(1)}) custom-call(bf16[512,768]{1,0:T(8,128)(2,1)S(1)} %copy-done.18, bf16[512,768]{1,0:T(8,128)(2,1)S(1)} %copy-done.12, bf16[512,768]{1,0:T(8,128)(2,1)S(1)} %copy-done.16, bf16[512,2304]{1,0:T(8,128)(2,1)S(1)} %copy-done.23, bf16[512,2304]{1,0:T(8,128)(2,1)} %attention_backward.4.refs_4_, ...), custom_call_target="tpu_custom_call" | custom-call | flops 5435817984 | bytes 12976128 | tf_op jit(solution)/shard_map/weight_grad/pallas_call | solution.py:206
  354.9 3.1 weight_grad.5
  359.9 11.2 %weight_grad.6 = (bf16[768,9344]{1,0:T(8,128)(2,1)}, f32[1,3072]{1,0:T(1,128)S(1)}) custom-call(bf16[512,768]{1,0:T(8,128)(2,1)S(1)} %copy-done.8, bf16[512,768]{1,0:T(8,128)(2,1)S(1)} %copy-done.10, bf16[512,768]{1,0:T(8,128)(2,1)S(1)} %copy-done.14, bf16[512,3072]{1,0:T(8,128)(2,1)S(1)} %copy-done.22, ...), custom_call_target="tpu_custom_call", output_to_operand_aliasing={{0}: (6, {})} | custom-call | flops 7247757312 | bytes 16515072 | tf_op jit(solution)/shard_map/weight_grad/pallas_call | solution.py:206
  371.1 11.0 %weight_grad.7 = (bf16[768,9344]{1,0:T(8,128)(2,1)}, f32[1,768]{1,0:T(1,128)S(1)}) custom-call(bf16[512,3072]{1,0:T(8,128)(2,1)S(1)} %copy-done.20, bf16[512,3072]{1,0:T(8,128)(2,1)} %copy-done.42, bf16[512,3072]{1,0:T(8,128)(2,1)} %copy-done.43, bf16[512,768]{1,0:T(8,128)(2,1)S(1)} %copy-done.6, ...), custom_call_target="tpu_custom_call", output_to_operand_aliasing={{0}: (6, {})} | custom-call | flops 7247757312 | bytes 16515072 | tf_op jit(solution)/shard_map/weight_grad/pallas_call | solution.py:206
  384.9 5.5 add_convert_fusion
  390.4 150.7 %reduce-scatter.4.cloned.1.call-done = bf16[24,9344]{1,0:T(8,128)(2,1)} async-done(((bf16[768,9344]{1,0:T(8,128)(2,1)}), bf16[24,9344]{1,0:T(8,128)(2,1)}) %reduce-scatter.4.cloned.1.call-update) | async-done | bytes 448528
  (221 shorter events, 61.6 us)
Async XLA Ops:
  7.2 10.6 %copy-start.36 = (bf16[24,3072]{1,0:T(8,128)(2,1)S(1)}, bf16[24,3072]{1,0:T(8,128)(2,1)}, u32[]{:S(2)}) copy-start(bf16[24,3072]{1,0:T(8,128)(2,1)} %param.30) | copy-start | bytes 442372
  7.2 118.7 %all-gather.2.cloned.1.call-start = ((), (), s32[]{:S(2)}) async-start(), calls=%async_computation.1 | async-start | bytes 14800896 | tf_op jit(solution)/shard_map/all_gather | solution.py:286
  19.8 521.3 %reduce-scatter.4.cloned.1.call-start = ((), (), s32[]{:S(2)}) async-start(), calls=%async_computation.2 | async-start | bytes 14800896
  147.1 14.7 %copy-start.25 = (f32[512,768]{1,0:T(8,128)}, f32[512,768]{1,0:T(8,128)S(1)}, u32[]{:S(2)}) copy-start(f32[512,768]{1,0:T(8,128)S(1)} %get-tuple-element.179) | copy-start | bytes 4718596
  150.9 10.9 %copy-start.32 = (bf16[3072,768]{1,0:T(8,128)(2,1)}, bf16[3072,768]{1,0:T(8,128)(2,1)S(1)}, u32[]{:S(2)}) copy-start(bf16[3072,768]{1,0:T(8,128)(2,1)S(1)} %pad_maximum_fusion) | copy-start | bytes 14155780
  151.2 10.6 %copy-start.7 = (bf16[512,768]{1,0:T(8,128)(2,1)}, bf16[512,768]{1,0:T(8,128)(2,1)S(1)}, u32[]{:S(2)}) copy-start(bf16[512,768]{1,0:T(8,128)(2,1)S(1)} %fusion.73.refs_0_) | copy-start | bytes 2359300
  164.6 17.2 %copy-start.27 = (f32[512,768]{1,0:T(8,128)}, f32[512,768]{1,0:T(8,128)S(1)}, u32[]{:S(2)}) copy-start(f32[512,768]{1,0:T(8,128)S(1)} %get-tuple-element.183) | copy-start | bytes 4718596
  184.3 91.6 %copy-start.29 = (f32[512,768]{1,0:T(8,128)}, f32[512,768]{1,0:T(8,128)S(1)}, u32[]{:S(2)}) copy-start(f32[512,768]{1,0:T(8,128)S(1)} %get-tuple-element.185) | copy-start | bytes 4718596
  184.6 9.9 %slice-start = ((s8[4718592]{0:T(1024)(128)(4,1)}), s8[4194304]{0:T(1024)(128)(4,1)S(1)}, s32[]{:S(2)}) async-start(s8[4718592]{0:T(1024)(128)(4,1)} %bitcast.65), calls=%async_computation.3 | async-start | bytes 8388608
  184.9 9.6 %copy-start.9 = (bf16[512,768]{1,0:T(8,128)(2,1)}, bf16[512,768]{1,0:T(8,128)(2,1)S(1)}, u32[]{:S(2)}) copy-start(bf16[512,768]{1,0:T(8,128)(2,1)S(1)} %fusion.75.refs_1_) | copy-start | bytes 2359300
  185.0 9.6 %slice-start.1 = ((s8[4718592]{0:T(1024)(128)(4,1)}), s8[524288]{0:T(1024)(128)(4,1)S(1)}, s32[]{:S(2)}) async-start(s8[4718592]{0:T(1024)(128)(4,1)} %bitcast.65), calls=%async_computation.4 | async-start | bytes 1048576
  197.3 17.0 %copy-start.30 = (f32[512,768]{1,0:T(8,128)}, f32[512,768]{1,0:T(8,128)S(1)}, u32[]{:S(2)}) copy-start(f32[512,768]{1,0:T(8,128)S(1)} %get-tuple-element.189) | copy-start | bytes 4718596
  217.1 7.1 %slice-start.2 = ((s8[4718592]{0:T(1024)(128)(4,1)}), s8[4194304]{0:T(1024)(128)(4,1)S(1)}, s32[]{:S(2)}) async-start(s8[4718592]{0:T(1024)(128)(4,1)} %bitcast.67), calls=%async_computation.5 | async-start | bytes 8388608
  217.4 6.8 %copy-start.13 = (bf16[512,768]{1,0:T(8,128)(2,1)}, bf16[512,768]{1,0:T(8,128)(2,1)S(1)}, u32[]{:S(2)}) copy-start(bf16[512,768]{1,0:T(8,128)(2,1)S(1)} %fusion.77.refs_2_) | copy-start | bytes 2359300
  217.4 6.8 %slice-start.3 = ((s8[4718592]{0:T(1024)(128)(4,1)}), s8[524288]{0:T(1024)(128)(4,1)S(1)}, s32[]{:S(2)}) async-start(s8[4718592]{0:T(1024)(128)(4,1)} %bitcast.67), calls=%async_computation.6 | async-start | bytes 1048576
  236.4 6.9 %copy-start.44 = (bf16[512,3072]{1,0:T(8,128)(2,1)}, bf16[512,3072]{1,0:T(8,128)(2,1)S(1)}, u32[]{:S(2)}) copy-start(bf16[512,3072]{1,0:T(8,128)(2,1)S(1)} %fusion.17.refs_5_) | copy-start | bytes 9437188
  260.6 6.2 %copy-start.31 = (f32[512,768]{1,0:T(8,128)S(1)}, f32[512,768]{1,0:T(8,128)}, u32[]{:S(2)}) copy-start(f32[512,768]{1,0:T(8,128)} %copy-done.30) | copy-start | bytes 4718596
  267.3 8.6 %copy-start.3 = (bf16[512,768]{1,0:T(8,128)(2,1)}, bf16[512,768]{1,0:T(8,128)(2,1)S(1)}, u32[]{:S(2)}) copy-start(bf16[512,768]{1,0:T(8,128)(2,1)S(1)} %get-tuple-element.142.refs_4_) | copy-start | bytes 2359300
  275.9 6.6 %copy-start.45 = (bf16[512,3072]{1,0:T(8,128)(2,1)}, bf16[512,3072]{1,0:T(8,128)(2,1)S(1)}, u32[]{:S(2)}) copy-start(bf16[512,3072]{1,0:T(8,128)(2,1)S(1)} %fusion.23.refs_4_) | copy-start | bytes 9437188
  301.3 6.2 %copy-start.28 = (f32[512,768]{1,0:T(8,128)S(1)}, f32[512,768]{1,0:T(8,128)}, u32[]{:S(2)}) copy-start(f32[512,768]{1,0:T(8,128)} %copy-done.27) | copy-start | bytes 4718596
  308.1 8.6 %copy-start.5 = (bf16[512,768]{1,0:T(8,128)(2,1)}, bf16[512,768]{1,0:T(8,128)(2,1)S(1)}, u32[]{:S(2)}) copy-start(bf16[512,768]{1,0:T(8,128)(2,1)S(1)} %get-tuple-element.138.refs_3_) | copy-start | bytes 2359300
  308.1 8.6 %copy-start.26 = (f32[512,768]{1,0:T(8,128)S(1)}, f32[512,768]{1,0:T(8,128)}, u32[]{:S(2)}) copy-start(f32[512,768]{1,0:T(8,128)} %copy-done.25) | copy-start | bytes 4718596
  316.7 6.6 %copy-start.21 = (bf16[512,3072]{1,0:T(8,128)(2,1)}, bf16[512,3072]{1,0:T(8,128)(2,1)S(1)}, u32[]{:S(2)}) copy-start(bf16[512,3072]{1,0:T(8,128)(2,1)S(1)} %fusion.29.refs_3_) | copy-start | bytes 9437188
  345.6 9.2 %copy-start = (bf16[512,768]{1,0:T(8,128)(2,1)S(1)}, bf16[512,768]{1,0:T(8,128)(2,1)}, u32[]{:S(2)}) copy-start(bf16[512,768]{1,0:T(8,128)(2,1)} %get-tuple-element.31.refs_0_) | copy-start | bytes 2359300
  345.6 9.2 %copy-start.1 = (bf16[512,768]{1,0:T(8,128)(2,1)S(1)}, bf16[512,768]{1,0:T(8,128)(2,1)}, u32[]{:S(2)}) copy-start(bf16[512,768]{1,0:T(8,128)(2,1)} %get-tuple-element.32.refs_1_) | copy-start | bytes 2359300
  345.6 9.2 %copy-start.2 = (bf16[512,768]{1,0:T(8,128)(2,1)S(1)}, bf16[512,768]{1,0:T(8,128)(2,1)}, u32[]{:S(2)}) copy-start(bf16[512,768]{1,0:T(8,128)(2,1)} %get-tuple-element.33.refs_2_) | copy-start | bytes 2359300
  354.8 3.2 copy-start.8
  354.8 3.2 copy-start.10
  359.9 11.2 %copy-start.4 = (bf16[512,768]{1,0:T(8,128)(2,1)S(1)}, bf16[512,768]{1,0:T(8,128)(2,1)}, u32[]{:S(2)}) copy-start(bf16[512,768]{1,0:T(8,128)(2,1)} %copy-done.3) | copy-start | bytes 2359300
  359.9 11.2 %copy-start.6 = (bf16[512,768]{1,0:T(8,128)(2,1)S(1)}, bf16[512,768]{1,0:T(8,128)(2,1)}, u32[]{:S(2)}) copy-start(bf16[512,768]{1,0:T(8,128)(2,1)} %copy-done.5) | copy-start | bytes 2359300
  359.9 11.2 %copy-start.20 = (bf16[512,3072]{1,0:T(8,128)(2,1)S(1)}, bf16[512,3072]{1,0:T(8,128)(2,1)}, u32[]{:S(2)}) copy-start(bf16[512,3072]{1,0:T(8,128)(2,1)} %copy-done.19) | copy-start | bytes 9437188
  541.1 3.4 copy-start.34
  (20 other events, 32.5 us)
Sparse Core Ops, SparseCore 0:
  19.9 105.9 all-gather.1
  383.3 157.6 reduce-scatter.3

commit v12 on v9

--- a/solution.py
+++ b/solution.py
@@ -11,6 +11,7 @@
 SEQ = 512
 HEAD = 64
 PAIR = 128
+GROUP = 2
 LAYERS = 3
 AXES = ("dp", "fsdp")
 NT = (((1,), (1,)), ((), ()))
@@ -58,10 +59,15 @@
 
 
 def attention_forward_kernel(qkv_ref, ctx_ref, lt_ref):
+    for p in range(ctx_ref.shape[1] // PAIR):
+        attention_forward_pair(qkv_ref, ctx_ref, lt_ref, 3 * PAIR * p, PAIR * p)
+
+
+def attention_forward_pair(qkv_ref, ctx_ref, lt_ref, at, out_at):
     scale = HEAD ** (-0.5)
-    q = qkv_ref[:, 0:PAIR]
-    k = qkv_ref[:, PAIR : 2 * PAIR]
-    v = qkv_ref[:, 2 * PAIR : 3 * PAIR]
+    q = qkv_ref[:, at : at + PAIR]
+    k = qkv_ref[:, at + PAIR : at + 2 * PAIR]
+    v = qkv_ref[:, at + 2 * PAIR : at + 3 * PAIR]
     masks = _head_masks(q.shape)
     zero = jnp.zeros_like(q)
     context = None
@@ -76,17 +82,22 @@
         log_total = jnp.broadcast_to(top + jnp.log(sums), part.shape)
         context = part if context is None else jnp.where(mask, part, context)
         total = log_total if total is None else jnp.where(mask, log_total, total)
-    ctx_ref[...] = context.astype(ctx_ref.dtype)
-    lt_ref[...] = total
+    ctx_ref[:, out_at : out_at + PAIR] = context.astype(ctx_ref.dtype)
+    lt_ref[:, out_at : out_at + PAIR] = total
 
 
 def attention_backward_kernel(qkv_ref, lt_ref, g_ref, out_ref):
+    for p in range(g_ref.shape[1] // PAIR):
+        attention_backward_pair(qkv_ref, lt_ref, g_ref, out_ref, 3 * PAIR * p, PAIR * p)
+
+
+def attention_backward_pair(qkv_ref, lt_ref, g_ref, out_ref, at, in_at):
     scale = HEAD ** (-0.5)
-    q = qkv_ref[:, 0:PAIR]
-    k = qkv_ref[:, PAIR : 2 * PAIR]
-    v = qkv_ref[:, 2 * PAIR : 3 * PAIR]
-    g = g_ref[...]
-    lt_t = lt_ref[...].T
+    q = qkv_ref[:, at : at + PAIR]
+    k = qkv_ref[:, at + PAIR : at + 2 * PAIR]
+    v = qkv_ref[:, at + 2 * PAIR : at + 3 * PAIR]
+    g = g_ref[:, in_at : in_at + PAIR]
+    lt_t = lt_ref[:, in_at : in_at + PAIR].T
     masks = _head_masks(q.shape)
     zero = jnp.zeros_like(q)
     dq = dk = dv = None
@@ -106,20 +117,21 @@
             dq = jnp.where(mask, query_part, dq)
             dk = jnp.where(mask, key_part, dk)
             dv = jnp.where(mask, value_part, dv)
-    out_ref[:, 0:PAIR] = dq.astype(out_ref.dtype)
-    out_ref[:, PAIR : 2 * PAIR] = dk.astype(out_ref.dtype)
-    out_ref[:, 2 * PAIR : 3 * PAIR] = dv.astype(out_ref.dtype)
+    out_ref[:, at : at + PAIR] = dq.astype(out_ref.dtype)
+    out_ref[:, at + PAIR : at + 2 * PAIR] = dk.astype(out_ref.dtype)
+    out_ref[:, at + 2 * PAIR : at + 3 * PAIR] = dv.astype(out_ref.dtype)
 
 
 def attention_forward(qkv):
     tokens, width = qkv.shape
-    grid = (tokens // SEQ, width // (3 * PAIR))
-    steps = grid[0] * grid[1]
-    pair = pl.BlockSpec((SEQ, PAIR), lambda s, h: (s, h))
+    group = GROUP if (width // (3 * PAIR)) % GROUP == 0 else 1
+    grid = (tokens // SEQ, width // (3 * PAIR * group))
+    steps = grid[0] * grid[1] * group
+    pair = pl.BlockSpec((SEQ, PAIR * group), lambda s, h: (s, h))
     return pl.pallas_call(
         attention_forward_kernel,
         grid=grid,
-        in_specs=[pl.BlockSpec((SEQ, 3 * PAIR), lambda s, h: (s, h))],
+        in_specs=[pl.BlockSpec((SEQ, 3 * PAIR * group), lambda s, h: (s, h))],
         out_specs=[pair, pair],
         out_shape=[
             jax.ShapeDtypeStruct((tokens, width // 3), jnp.bfloat16),
@@ -137,10 +149,11 @@
 
 def attention_backward(qkv, log_total, context_grad):
     tokens, width = qkv.shape
-    grid = (tokens // SEQ, width // (3 * PAIR))
-    steps = grid[0] * grid[1]
-    pair = pl.BlockSpec((SEQ, PAIR), lambda s, h: (s, h))
-    triple = pl.BlockSpec((SEQ, 3 * PAIR), lambda s, h: (s, h))
+    group = GROUP if (width // (3 * PAIR)) % GROUP == 0 else 1
+    grid = (tokens // SEQ, width // (3 * PAIR * group))
+    steps = grid[0] * grid[1] * group
+    pair = pl.BlockSpec((SEQ, PAIR * group), lambda s, h: (s, h))
+    triple = pl.BlockSpec((SEQ, 3 * PAIR * group), lambda s, h: (s, h))
     return pl.pallas_call(
         attention_backward_kernel,
         grid=grid,

time: 558 us -> 552 us (0.989)
  Pallas kernels: 103 us -> 96.4 us
where the time goes in v12:
time: 552 us; the launch traced here: 546 us
  waiting for transfers between devices  257 us (47%)
  matrix products  129 us (23%)
  Pallas kernels  96.4 us (17%)
  local copies, waits for them, and re-layouts  32.1 us (6%)
  other arithmetic  16.1 us (3%)
  between operations  15.6 us (3%)
    unnamed x3, waiting for transfers between devices  151 us
    all_gather x1, waiting for transfers between devices, gather_weights(): packed = lax.all_gather(pack_weights(weights), AXES, axis=0, tiled=True)  106 us
    dot_general x12, matrix products, product_nt(): return lax.dot_general(left, right, NT, preferred_element_type=jnp.float32)  70.5 us
    dot_general x12, matrix products, product(): return jnp.dot(left, right, preferred_element_type=jnp.float32)  58.3 us
    pallas_call x3, Pallas kernels, attention_backward(): pl.pallas_call(attention_backward_kernel, grid=grid, in_specs=[triple, pa...  35.8 us
    pallas_call x4, Pallas kernels, weight_grad(): pl.pallas_call(kernel, grid=grid, in_specs=in_specs, out_specs=[pl.BlockS...  34.8 us
    pallas_call x3, Pallas kernels, attention_forward(): pl.pallas_call(attention_forward_kernel, grid=grid, in_specs=[pl.BlockSpe...  25.8 us
    unnamed x150, local copies, waits for them, and re-layouts  17.4 us
  transfers between devices with their start and end apart: 2, of which 2 were waited for; matrix products, arithmetic and copies ran while one was open for 1% of the time, Pallas kernels for 0%

profile of v12, /device:TPU:0, one launch (start us, length us, event | category | flops | bytes accessed | tf_op | source)
XLA Modules:
  0.0 545.7 jit_solution(9434367047175302557)
XLA Ops:
  14.2 106.0 %all-gather.2.cloned.1.call-done = bf16[768,9344]{1,0:T(8,128)(2,1)} async-done(((bf16[24,9344]{1,0:T(8,128)(2,1)}), bf16[768,9344]{1,0:T(8,128)(2,1)}) %all-gather.2.cloned.1.call-update) | async-done | bytes 14352400 | tf_op jit(solution)/shard_map/all_gather | solution.py:287
  123.4 5.5 fusion.33.qkv_ref
  128.9 8.7 %attention_forward.3 = (bf16[512,768]{1,0:T(8,128)(2,1)}, f32[512,768]{1,0:T(8,128)}) custom-call(bf16[512,2304]{1,0:T(8,128)(2,1)} %fusion.33.qkv_ref), custom_call_target="tpu_custom_call" | custom-call | flops 1610612736 | bytes 4718592 | tf_op jit(solution)/shard_map/attention_forward/pallas_call | solution.py:131
  140.3 2.9 fusion.92
  144.1 10.6 %multiply_convert_fusion.2 = (bf16[512,3072]{1,0:T(8,128)(2,1)S(1)}, f32[512,3072]{1,0:T(8,128)}) fusion(f32[3072]{0:T(1024)S(1)} %add.368, bf16[512,768]{1,0:T(8,128)(2,1)S(1)} %fusion.73.refs_0_, bf16[768,9344]{1,0:T(8,128)(2,1)} %all-gather.2.cloned.1.call-done), kind=kOutput, calls=%fused_computation.40 | convolution fusion | flops 2431647744 | bytes 14954496 | tf_op jit(solution)/shard_map/dot_general | solution.py:23
  158.1 5.5 %fusion.30.qkv_ref = bf16[512,2304]{1,0:T(8,128)(2,1)} fusion(bf16[512,768]{1,0:T(8,128)(2,1)S(1)} %fusion.74.refs_1_, f32[2304]{0:T(1024)S(1)} %add.357, bf16[768,9344]{1,0:T(8,128)(2,1)} %all-gather.2.cloned.1.call-done), kind=kOutput, calls=%fused_computation.46 | convolution fusion | flops 1814298624 | bytes 6693888 | tf_op jit(solution)/shard_map/dot_general | solution.py:23
  164.5 8.5 %attention_forward.4 = (bf16[512,768]{1,0:T(8,128)(2,1)}, f32[512,768]{1,0:T(8,128)}) custom-call(bf16[512,2304]{1,0:T(8,128)(2,1)} %fusion.30.qkv_ref), custom_call_target="tpu_custom_call" | custom-call | flops 1610612736 | bytes 4718592 | tf_op jit(solution)/shard_map/attention_forward/pallas_call | solution.py:131
  176.1 9.6 %multiply_convert_fusion.1 = (bf16[512,3072]{1,0:T(8,128)(2,1)S(1)}, f32[512,3072]{1,0:T(8,128)}) fusion(f32[3072]{0:T(1024)S(1)} %add.368, bf16[512,768]{1,0:T(8,128)(2,1)S(1)} %fusion.75.refs_1_, bf16[768,9344]{1,0:T(8,128)(2,1)} %all-gather.2.cloned.1.call-done), kind=kOutput, calls=%fused_computation.38 | convolution fusion | flops 2431647744 | bytes 14954496 | tf_op jit(solution)/shard_map/dot_general | solution.py:23
  189.2 5.4 fusion.31.qkv_ref
  195.5 8.6 %attention_forward.5 = (bf16[512,768]{1,0:T(8,128)(2,1)}, f32[512,768]{1,0:T(8,128)}) custom-call(bf16[512,2304]{1,0:T(8,128)(2,1)} %fusion.31.qkv_ref), custom_call_target="tpu_custom_call" | custom-call | flops 1610612736 | bytes 4718592 | tf_op jit(solution)/shard_map/attention_forward/pallas_call | solution.py:131
  207.2 6.1 %multiply_convert_fusion = (bf16[512,3072]{1,0:T(8,128)(2,1)S(1)}, f32[512,3072]{1,0:T(8,128)S(1)}) fusion(f32[3072]{0:T(1024)S(1)} %add.368, bf16[512,768]{1,0:T(8,128)(2,1)S(1)} %fusion.77.refs_2_, bf16[768,9344]{1,0:T(8,128)(2,1)} %all-gather.2.cloned.1.call-done), kind=kOutput, calls=%fused_computation.36 | convolution fusion | flops 2431647744 | bytes 14954496 | tf_op jit(solution)/shard_map/dot_general | solution.py:23
  219.8 6.1 %fusion.17.refs_5_ = bf16[512,3072]{1,0:T(8,128)(2,1)S(1)} fusion(f32[512,3072]{1,0:T(8,128)S(1)} %get-tuple-element.199, bf16[512,768]{1,0:T(8,128)(2,1)S(1)} %get-tuple-element.150.refs_5_, bf16[3072,768]{1,0:T(8,128)(2,1)S(1)} %bitcast.91, f32[3072]{0:T(1024)S(1)} %add.368), kind=kOutput, calls=%fused_computation.23 | convolution fusion | flops 2445803520 | bytes 14954496 | tf_op jit(solution)/shard_map/dot_general | solution.py:27
  225.9 6.9 %multiply_reduce_fusion.3 = (f32[768]{0:T(1024)S(1)}, f32[512]{0:T(512)S(1)}, f32[512]{0:T(512)S(1)}, f32[768]{0:T(1024)S(1)}, f32[512,768]{1,0:T(8,128)S(1)}) fusion(f32[512,768]{1,0:T(8,128)S(1)} %get-tuple-element.197, f32[512]{0:T(512)S(1)} %add_rsqrt_fusion.1, f32[512]{0:T(512)S(1)} %broadcast_multiply_fusion.13, f32[768]{0:T(1024)S(1)} %get-tuple-element.132, ...), kind=kOutput, calls=%fused_computation.65 | convolution fusion | flops 2423387648 | bytes 13400064 | tf_op jit(solution)/shard_map/dot_general | solution.py:27
  234.5 3.0 convolution_convert_fusion.2.g_ref
  237.5 11.9 %attention_backward.3.refs_5_ = bf16[512,2304]{1,0:T(8,128)(2,1)} custom-call(bf16[512,2304]{1,0:T(8,128)(2,1)} %fusion.31.qkv_ref, f32[512,768]{1,0:T(8,128)} %get-tuple-element.34.lt_ref, bf16[512,768]{1,0:T(8,128)(2,1)} %convolution_convert_fusion.2.g_ref), custom_call_target="tpu_custom_call" | custom-call | flops 4026531840 | bytes 7077888 | tf_op jit(solution)/shard_map/attention_backward/pallas_call | solution.py:157
  249.4 6.2 %multiply_reduce_fusion.1 = (f32[768]{0:T(1024)S(1)}, f32[512]{0:T(512)S(1)}, f32[512]{0:T(512)S(1)}, f32[768]{0:T(1024)S(1)}, f32[512,768]{1,0:T(8,128)S(1)}) fusion(f32[512,768]{1,0:T(8,128)} %copy-done.30, f32[512]{0:T(512)S(1)} %add_rsqrt_fusion.2, f32[512]{0:T(512)S(1)} %broadcast_multiply_fusion.14, f32[768]{0:T(1024)S(1)} %get-tuple-element.128, ...), kind=kOutput, calls=%fused_computation.63 | convolution fusion | flops 1815868928 | bytes 10634240 | tf_op jit(solution)/shard_map/dot_general | solution.py:27
  256.1 8.7 %fusion.23.refs_4_ = bf16[512,3072]{1,0:T(8,128)(2,1)S(1)} fusion(f32[512,3072]{1,0:T(8,128)} %get-tuple-element.193, bf16[512,768]{1,0:T(8,128)(2,1)S(1)} %get-tuple-element.142.refs_4_, bf16[3072,768]{1,0:T(8,128)(2,1)} %copy-done.32, f32[3072]{0:T(1024)S(1)} %add.368), kind=kOutput, calls=%fused_computation.29 | convolution fusion | flops 2445803520 | bytes 14954496 | tf_op jit(solution)/shard_map/dot_general | solution.py:27
  264.8 6.6 %multiply_reduce_fusion.4 = (f32[768]{0:T(1024)S(1)}, f32[512]{0:T(512)S(1)}, f32[512]{0:T(512)S(1)}, f32[768]{0:T(1024)S(1)}, f32[512,768]{1,0:T(8,128)S(1)}) fusion(f32[512,768]{1,0:T(8,128)S(1)} %get-tuple-element.191, f32[512]{0:T(512)S(1)} %add_rsqrt_fusion.3, f32[512]{0:T(512)S(1)} %broadcast_multiply_fusion.15, f32[768]{0:T(1024)S(1)} %get-tuple-element.132, ...), kind=kOutput, calls=%fused_computation.66 | convolution fusion | flops 2419848704 | bytes 12600320 | tf_op jit(solution)/shard_map/dot_general | solution.py:27
  271.5 3.1 fusion.89
  274.5 3.0 convolution_convert_fusion.1.g_ref
  277.5 12.0 %attention_backward.4.refs_4_ = bf16[512,2304]{1,0:T(8,128)(2,1)} custom-call(bf16[512,2304]{1,0:T(8,128)(2,1)} %fusion.30.qkv_ref, f32[512,768]{1,0:T(8,128)} %get-tuple-element.35.lt_ref, bf16[512,768]{1,0:T(8,128)(2,1)} %convolution_convert_fusion.1.g_ref), custom_call_target="tpu_custom_call" | custom-call | flops 4026531840 | bytes 7077888 | tf_op jit(solution)/shard_map/attention_backward/pallas_call | solution.py:157
  289.5 6.2 %multiply_reduce_fusion.2 = (f32[768]{0:T(1024)S(1)}, f32[512]{0:T(512)S(1)}, f32[512]{0:T(512)S(1)}, f32[768]{0:T(1024)S(1)}, f32[512,768]{1,0:T(8,128)S(1)}) fusion(f32[512,768]{1,0:T(8,128)} %copy-done.27, f32[512]{0:T(512)S(1)} %add_rsqrt_fusion.4, f32[512]{0:T(512)S(1)} %broadcast_multiply_fusion.16, f32[768]{0:T(1024)S(1)} %get-tuple-element.128, ...), kind=kOutput, calls=%fused_computation.64 | convolution fusion | flops 1815868928 | bytes 10634240 | tf_op jit(solution)/shard_map/dot_general | solution.py:27
  296.2 8.8 %fusion.29.refs_3_ = bf16[512,3072]{1,0:T(8,128)(2,1)S(1)} fusion(f32[512,3072]{1,0:T(8,128)} %get-tuple-element.187, bf16[512,768]{1,0:T(8,128)(2,1)S(1)} %get-tuple-element.138.refs_3_, bf16[3072,768]{1,0:T(8,128)(2,1)} %copy-done.32, f32[3072]{0:T(1024)S(1)} %add.368), kind=kOutput, calls=%fused_computation.35 | convolution fusion | flops 2445803520 | bytes 14954496 | tf_op jit(solution)/shard_map/dot_general | solution.py:27
  305.0 6.6 %multiply_reduce_fusion.5 = (f32[768]{0:T(1024)S(1)}, f32[512]{0:T(512)S(1)}, f32[512]{0:T(512)S(1)}, f32[768]{0:T(1024)S(1)}, f32[512,768]{1,0:T(8,128)S(1)}) fusion(f32[512,768]{1,0:T(8,128)S(1)} %copy-done.26, f32[512]{0:T(512)S(1)} %add_rsqrt_fusion.5, f32[512]{0:T(512)S(1)} %broadcast_multiply_fusion.17, f32[768]{0:T(1024)S(1)} %get-tuple-element.132, ...), kind=kOutput, calls=%fused_computation.67 | convolution fusion | flops 2419848704 | bytes 12600320 | tf_op jit(solution)/shard_map/dot_general | solution.py:27
  313.3 3.0 convolution_convert_fusion.g_ref
  316.3 11.9 %attention_backward.5.refs_3_ = bf16[512,2304]{1,0:T(8,128)(2,1)} custom-call(bf16[512,2304]{1,0:T(8,128)(2,1)} %fusion.33.qkv_ref, f32[512,768]{1,0:T(8,128)} %get-tuple-element.36.lt_ref, bf16[512,768]{1,0:T(8,128)(2,1)} %convolution_convert_fusion.g_ref), custom_call_target="tpu_custom_call" | custom-call | flops 4026531840 | bytes 7077888 | tf_op jit(solution)/shard_map/attention_backward/pallas_call | solution.py:157
  333.3 9.0 %weight_grad.4 = (bf16[768,9344]{1,0:T(8,128)(2,1)}, f32[1,2304]{1,0:T(1,128)S(1)}) custom-call(bf16[512,768]{1,0:T(8,128)(2,1)S(1)} %copy-done.18, bf16[512,768]{1,0:T(8,128)(2,1)S(1)} %copy-done.12, bf16[512,768]{1,0:T(8,128)(2,1)S(1)} %copy-done.16, bf16[512,2304]{1,0:T(8,128)(2,1)S(1)} %copy-done.23, bf16[512,2304]{1,0:T(8,128)(2,1)} %attention_backward.4.refs_4_, ...), custom_call_target="tpu_custom_call" | custom-call | flops 5435817984 | bytes 12976128 | tf_op jit(solution)/shard_map/weight_grad/pallas_call | solution.py:219
  342.3 3.2 weight_grad.5
  347.4 11.6 %weight_grad.6 = (bf16[768,9344]{1,0:T(8,128)(2,1)}, f32[1,3072]{1,0:T(1,128)S(1)}) custom-call(bf16[512,768]{1,0:T(8,128)(2,1)S(1)} %copy-done.8, bf16[512,768]{1,0:T(8,128)(2,1)S(1)} %copy-done.10, bf16[512,768]{1,0:T(8,128)(2,1)S(1)} %copy-done.14, bf16[512,3072]{1,0:T(8,128)(2,1)S(1)} %copy-done.22, ...), custom_call_target="tpu_custom_call", output_to_operand_aliasing={{0}: (6, {})} | custom-call | flops 7247757312 | bytes 16515072 | tf_op jit(solution)/shard_map/weight_grad/pallas_call | solution.py:219
  359.0 11.1 %weight_grad.7 = (bf16[768,9344]{1,0:T(8,128)(2,1)}, f32[1,768]{1,0:T(1,128)S(1)}) custom-call(bf16[512,3072]{1,0:T(8,128)(2,1)S(1)} %copy-done.20, bf16[512,3072]{1,0:T(8,128)(2,1)} %copy-done.56, bf16[512,3072]{1,0:T(8,128)(2,1)} %copy-done.57, bf16[512,768]{1,0:T(8,128)(2,1)S(1)} %copy-done.6, ...), custom_call_target="tpu_custom_call", output_to_operand_aliasing={{0}: (6, {})} | custom-call | flops 7247757312 | bytes 16515072 | tf_op jit(solution)/shard_map/weight_grad/pallas_call | solution.py:219
  375.4 5.5 %add_convert_fusion = bf16[512,768]{1,0:T(8,128)(2,1)} fusion(f32[512,768]{1,0:T(8,128)} %get-tuple-element.137, bf16[512,2304]{1,0:T(8,128)(2,1)S(1)} %copy-done.24, bf16[768,9344]{1,0:T(8,128)(2,1)} %all-gather.2.cloned.1.call-done), kind=kOutput, calls=%fused_computation.68 | convolution fusion | flops 1812725760 | bytes 8257536 | tf_op jit(solution)/shard_map/dot_general | solution.py:27
  380.9 150.5 %reduce-scatter.4.cloned.1.call-done = bf16[24,9344]{1,0:T(8,128)(2,1)} async-done(((bf16[768,9344]{1,0:T(8,128)(2,1)}), bf16[24,9344]{1,0:T(8,128)(2,1)}) %reduce-scatter.4.cloned.1.call-update) | async-done | bytes 448528
  (263 shorter events, 58.1 us)
Async XLA Ops:
  7.2 113.0 %all-gather.2.cloned.1.call-start = ((), (), s32[]{:S(2)}) async-start(), calls=%async_computation.1 | async-start | bytes 14800896 | tf_op jit(solution)/shard_map/all_gather | solution.py:287
  14.0 517.4 %reduce-scatter.4.cloned.1.call-start = ((), (), s32[]{:S(2)}) async-start(), calls=%async_computation.2 | async-start | bytes 14800896
  140.0 14.7 %copy-start.25 = (f32[512,768]{1,0:T(8,128)}, f32[512,768]{1,0:T(8,128)S(1)}, u32[]{:S(2)}) copy-start(f32[512,768]{1,0:T(8,128)S(1)} %get-tuple-element.185) | copy-start | bytes 4718596
  143.7 10.9 %copy-start.32 = (bf16[3072,768]{1,0:T(8,128)(2,1)}, bf16[3072,768]{1,0:T(8,128)(2,1)S(1)}, u32[]{:S(2)}) copy-start(bf16[3072,768]{1,0:T(8,128)(2,1)S(1)} %pad_maximum_fusion) | copy-start | bytes 14155780
  144.1 10.6 %copy-start.7 = (bf16[512,768]{1,0:T(8,128)(2,1)}, bf16[512,768]{1,0:T(8,128)(2,1)S(1)}, u32[]{:S(2)}) copy-start(bf16[512,768]{1,0:T(8,128)(2,1)S(1)} %fusion.73.refs_0_) | copy-start | bytes 2359300
  157.5 15.5 %copy-start.27 = (f32[512,768]{1,0:T(8,128)}, f32[512,768]{1,0:T(8,128)S(1)}, u32[]{:S(2)}) copy-start(f32[512,768]{1,0:T(8,128)S(1)} %get-tuple-element.189) | copy-start | bytes 4718596
  175.5 89.4 %copy-start.29 = (f32[512,768]{1,0:T(8,128)}, f32[512,768]{1,0:T(8,128)S(1)}, u32[]{:S(2)}) copy-start(f32[512,768]{1,0:T(8,128)S(1)} %get-tuple-element.191) | copy-start | bytes 4718596
  175.8 9.9 %slice-start = ((s8[4718592]{0:T(1024)(128)(4,1)}), s8[4194304]{0:T(1024)(128)(4,1)S(1)}, s32[]{:S(2)}) async-start(s8[4718592]{0:T(1024)(128)(4,1)} %bitcast.88), calls=%async_computation.3 | async-start | bytes 8388608
  176.1 9.6 %copy-start.9 = (bf16[512,768]{1,0:T(8,128)(2,1)}, bf16[512,768]{1,0:T(8,128)(2,1)S(1)}, u32[]{:S(2)}) copy-start(bf16[512,768]{1,0:T(8,128)(2,1)S(1)} %fusion.75.refs_1_) | copy-start | bytes 2359300
  176.1 9.6 %slice-start.1 = ((s8[4718592]{0:T(1024)(128)(4,1)}), s8[524288]{0:T(1024)(128)(4,1)S(1)}, s32[]{:S(2)}) async-start(s8[4718592]{0:T(1024)(128)(4,1)} %bitcast.88), calls=%async_computation.4 | async-start | bytes 1048576
  188.5 15.5 %copy-start.30 = (f32[512,768]{1,0:T(8,128)}, f32[512,768]{1,0:T(8,128)S(1)}, u32[]{:S(2)}) copy-start(f32[512,768]{1,0:T(8,128)S(1)} %get-tuple-element.195) | copy-start | bytes 4718596
  206.8 6.5 %slice-start.2 = ((s8[4718592]{0:T(1024)(128)(4,1)}), s8[4194304]{0:T(1024)(128)(4,1)S(1)}, s32[]{:S(2)}) async-start(s8[4718592]{0:T(1024)(128)(4,1)} %bitcast.90), calls=%async_computation.5 | async-start | bytes 8388608
  207.2 6.2 %copy-start.13 = (bf16[512,768]{1,0:T(8,128)(2,1)}, bf16[512,768]{1,0:T(8,128)(2,1)S(1)}, u32[]{:S(2)}) copy-start(bf16[512,768]{1,0:T(8,128)(2,1)S(1)} %fusion.77.refs_2_) | copy-start | bytes 2359300
  207.2 6.2 %slice-start.3 = ((s8[4718592]{0:T(1024)(128)(4,1)}), s8[524288]{0:T(1024)(128)(4,1)S(1)}, s32[]{:S(2)}) async-start(s8[4718592]{0:T(1024)(128)(4,1)} %bitcast.90), calls=%async_computation.6 | async-start | bytes 1048576
  225.9 6.9 %copy-start.58 = (bf16[512,3072]{1,0:T(8,128)(2,1)}, bf16[512,3072]{1,0:T(8,128)(2,1)S(1)}, u32[]{:S(2)}) copy-start(bf16[512,3072]{1,0:T(8,128)(2,1)S(1)} %fusion.17.refs_5_) | copy-start | bytes 9437188
  249.4 6.2 %copy-start.31 = (f32[512,768]{1,0:T(8,128)S(1)}, f32[512,768]{1,0:T(8,128)}, u32[]{:S(2)}) copy-start(f32[512,768]{1,0:T(8,128)} %copy-done.30) | copy-start | bytes 4718596
  256.1 8.8 %copy-start.3 = (bf16[512,768]{1,0:T(8,128)(2,1)}, bf16[512,768]{1,0:T(8,128)(2,1)S(1)}, u32[]{:S(2)}) copy-start(bf16[512,768]{1,0:T(8,128)(2,1)S(1)} %get-tuple-element.142.refs_4_) | copy-start | bytes 2359300
  264.8 6.6 %copy-start.59 = (bf16[512,3072]{1,0:T(8,128)(2,1)}, bf16[512,3072]{1,0:T(8,128)(2,1)S(1)}, u32[]{:S(2)}) copy-start(bf16[512,3072]{1,0:T(8,128)(2,1)S(1)} %fusion.23.refs_4_) | copy-start | bytes 9437188
  289.5 6.2 %copy-start.28 = (f32[512,768]{1,0:T(8,128)S(1)}, f32[512,768]{1,0:T(8,128)}, u32[]{:S(2)}) copy-start(f32[512,768]{1,0:T(8,128)} %copy-done.27) | copy-start | bytes 4718596
  296.2 8.8 %copy-start.5 = (bf16[512,768]{1,0:T(8,128)(2,1)}, bf16[512,768]{1,0:T(8,128)(2,1)S(1)}, u32[]{:S(2)}) copy-start(bf16[512,768]{1,0:T(8,128)(2,1)S(1)} %get-tuple-element.138.refs_3_) | copy-start | bytes 2359300
  296.2 8.8 %copy-start.26 = (f32[512,768]{1,0:T(8,128)S(1)}, f32[512,768]{1,0:T(8,128)}, u32[]{:S(2)}) copy-start(f32[512,768]{1,0:T(8,128)} %copy-done.25) | copy-start | bytes 4718596
  305.0 6.6 %copy-start.21 = (bf16[512,3072]{1,0:T(8,128)(2,1)}, bf16[512,3072]{1,0:T(8,128)(2,1)S(1)}, u32[]{:S(2)}) copy-start(bf16[512,3072]{1,0:T(8,128)(2,1)S(1)} %fusion.29.refs_3_) | copy-start | bytes 9437188
  333.3 9.0 %copy-start = (bf16[512,768]{1,0:T(8,128)(2,1)S(1)}, bf16[512,768]{1,0:T(8,128)(2,1)}, u32[]{:S(2)}) copy-start(bf16[512,768]{1,0:T(8,128)(2,1)} %get-tuple-element.31.refs_0_) | copy-start | bytes 2359300
  333.3 9.0 %copy-start.1 = (bf16[512,768]{1,0:T(8,128)(2,1)S(1)}, bf16[512,768]{1,0:T(8,128)(2,1)}, u32[]{:S(2)}) copy-start(bf16[512,768]{1,0:T(8,128)(2,1)} %get-tuple-element.32.refs_1_) | copy-start | bytes 2359300
  333.3 9.0 %copy-start.2 = (bf16[512,768]{1,0:T(8,128)(2,1)S(1)}, bf16[512,768]{1,0:T(8,128)(2,1)}, u32[]{:S(2)}) copy-start(bf16[512,768]{1,0:T(8,128)(2,1)} %get-tuple-element.33.refs_2_) | copy-start | bytes 2359300
  342.3 3.2 copy-start.8
  342.3 3.2 copy-start.10
  347.4 11.6 %copy-start.4 = (bf16[512,768]{1,0:T(8,128)(2,1)S(1)}, bf16[512,768]{1,0:T(8,128)(2,1)}, u32[]{:S(2)}) copy-start(bf16[512,768]{1,0:T(8,128)(2,1)} %copy-done.3) | copy-start | bytes 2359300
  347.4 11.6 %copy-start.6 = (bf16[512,768]{1,0:T(8,128)(2,1)S(1)}, bf16[512,768]{1,0:T(8,128)(2,1)}, u32[]{:S(2)}) copy-start(bf16[512,768]{1,0:T(8,128)(2,1)} %copy-done.5) | copy-start | bytes 2359300
  347.4 11.6 %copy-start.20 = (bf16[512,3072]{1,0:T(8,128)(2,1)S(1)}, bf16[512,3072]{1,0:T(8,128)(2,1)}, u32[]{:S(2)}) copy-start(bf16[512,3072]{1,0:T(8,128)(2,1)} %copy-done.19) | copy-start | bytes 9437188
  359.0 11.1 %copy-start.46 = (bf16[768]{0:T(1024)(128)(2,1)S(1)}, bf16[768]{0:T(1024)(128)(2,1)}, u32[]{:S(2)}) copy-start(bf16[768]{0:T(1024)(128)(2,1)} %custom-call.4) | copy-start | bytes 4612
  359.0 12.3 %copy-start.45 = (bf16[768]{0:T(1024)(128)(2,1)S(1)}, bf16[768]{0:T(1024)(128)(2,1)}, u32[]{:S(2)}) copy-start(bf16[768]{0:T(1024)(128)(2,1)} %custom-call.3) | copy-start | bytes 4612
  (34 other events, 70.9 us)
Sparse Core Ops, SparseCore 0:
  14.2 105.9 all-gather.1
  373.9 157.5 reduce-scatter.3

commit v13 on v12

--- a/solution.py
+++ b/solution.py
@@ -402,7 +402,7 @@
     columns = jnp.concatenate([columns, inner_cols], axis=1)
     columns = jnp.pad(columns, ((0, 0), (0, PAIR - columns.shape[1]))).astype(jnp.bfloat16)
     packed = lax.dynamic_update_slice(packed, columns, (0, blocks * width))
-    mine = lax.psum_scatter(packed, AXES, scatter_dimension=0, tiled=True).astype(jnp.float32)
+    mine = lax.psum_scatter(packed, AXES, scatter_dimension=0, tiled=True)
     at = 0
     pieces = []
     for count in (three, width, wide, wide, PAIR):
@@ -412,7 +412,7 @@
     q_w, k_w, v_w = split_qkv(qkv_mine)
     c = [col_mine[:, i] for i in range(8)]
     ib_mine = col_mine[:, 8:12].reshape(-1)
-    return (
+    found = (
         q_w,
         c[0],
         k_w,
@@ -429,6 +429,7 @@
         c[6],
         c[7],
     )
+    return tuple(piece.astype(jnp.float32) for piece in found)
 
 
 def per_device(shards, inputs, cotangent, masked, *weights):

time: 552 us -> 651 us (1.18)
  waiting for transfers between devices: 257 us -> 348 us
    unnamed x3, waiting for transfers between devices: 151 us -> 242 us
    unnamed x150 -> x136, local copies, waits for them, and re-layouts: 17.4 us -> 21.1 us
where the time goes in v13:
time: 651 us; the launch traced here: 645 us
  waiting for transfers between devices  348 us (53%)
  matrix products  129 us (20%)
  Pallas kernels  96.2 us (15%)
  local copies, waits for them, and re-layouts  35.1 us (5%)
  other arithmetic  22.1 us (3%)
  between operations  15.5 us (2%)
    unnamed x3, waiting for transfers between devices  242 us
    all_gather x1, waiting for transfers between devices, gather_weights(): packed = lax.all_gather(pack_weights(weights), AXES, axis=0, tiled=True)  106 us
    dot_general x12, matrix products, product_nt(): return lax.dot_general(left, right, NT, preferred_element_type=jnp.float32)  70.5 us
    dot_general x12, matrix products, product(): return jnp.dot(left, right, preferred_element_type=jnp.float32)  58.1 us
    pallas_call x3, Pallas kernels, attention_backward(): pl.pallas_call(attention_backward_kernel, grid=grid, in_specs=[triple, pa...  35.8 us
    pallas_call x4, Pallas kernels, weight_grad(): pl.pallas_call(kernel, grid=grid, in_specs=in_specs, out_specs=[pl.BlockS...  34.8 us
    pallas_call x3, Pallas kernels, attention_forward(): pl.pallas_call(attention_forward_kernel, grid=grid, in_specs=[pl.BlockSpe...  25.7 us
    unnamed x136, local copies, waits for them, and re-layouts  21.1 us
  transfers between devices with their start and end apart: 2, of which 2 were waited for; matrix products, arithmetic and copies ran while one was open for 1% of the time, Pallas kernels for 0%

profile of v13, /device:TPU:0, one launch (start us, length us, event | category | flops | bytes accessed | tf_op | source)
XLA Modules:
  0.0 645.2 jit_solution(13898447073696081859)
XLA Ops:
  14.2 106.0 %all-gather.2.cloned.1.call-done = bf16[768,9344]{1,0:T(8,128)(2,1)} async-done(((bf16[24,9344]{1,0:T(8,128)(2,1)}), bf16[768,9344]{1,0:T(8,128)(2,1)}) %all-gather.2.cloned.1.call-update) | async-done | bytes 14352400 | tf_op jit(solution)/shard_map/all_gather | solution.py:287
  123.4 5.4 fusion.33.qkv_ref
  128.8 8.7 %attention_forward.3 = (bf16[512,768]{1,0:T(8,128)(2,1)}, f32[512,768]{1,0:T(8,128)}) custom-call(bf16[512,2304]{1,0:T(8,128)(2,1)} %fusion.33.qkv_ref), custom_call_target="tpu_custom_call" | custom-call | flops 1610612736 | bytes 4718592 | tf_op jit(solution)/shard_map/attention_forward/pallas_call | solution.py:131
  140.3 2.9 fusion.92
  144.0 10.5 %multiply_convert_fusion.2 = (bf16[512,3072]{1,0:T(8,128)(2,1)S(1)}, f32[512,3072]{1,0:T(8,128)}) fusion(f32[3072]{0:T(1024)S(1)} %add.368, bf16[512,768]{1,0:T(8,128)(2,1)S(1)} %fusion.73.refs_0_, bf16[768,9344]{1,0:T(8,128)(2,1)} %all-gather.2.cloned.1.call-done), kind=kOutput, calls=%fused_computation.40 | convolution fusion | flops 2431647744 | bytes 14954496 | tf_op jit(solution)/shard_map/dot_general | solution.py:23
  158.0 5.4 fusion.30.qkv_ref
  164.2 8.5 %attention_forward.4 = (bf16[512,768]{1,0:T(8,128)(2,1)}, f32[512,768]{1,0:T(8,128)}) custom-call(bf16[512,2304]{1,0:T(8,128)(2,1)} %fusion.30.qkv_ref), custom_call_target="tpu_custom_call" | custom-call | flops 1610612736 | bytes 4718592 | tf_op jit(solution)/shard_map/attention_forward/pallas_call | solution.py:131
  175.8 9.6 %multiply_convert_fusion.1 = (bf16[512,3072]{1,0:T(8,128)(2,1)S(1)}, f32[512,3072]{1,0:T(8,128)}) fusion(f32[3072]{0:T(1024)S(1)} %add.368, bf16[512,768]{1,0:T(8,128)(2,1)S(1)} %fusion.75.refs_1_, bf16[768,9344]{1,0:T(8,128)(2,1)} %all-gather.2.cloned.1.call-done), kind=kOutput, calls=%fused_computation.38 | convolution fusion | flops 2431647744 | bytes 14954496 | tf_op jit(solution)/shard_map/dot_general | solution.py:23
  188.9 5.4 fusion.31.qkv_ref
  195.2 8.5 %attention_forward.5 = (bf16[512,768]{1,0:T(8,128)(2,1)}, f32[512,768]{1,0:T(8,128)}) custom-call(bf16[512,2304]{1,0:T(8,128)(2,1)} %fusion.31.qkv_ref), custom_call_target="tpu_custom_call" | custom-call | flops 1610612736 | bytes 4718592 | tf_op jit(solution)/shard_map/attention_forward/pallas_call | solution.py:131
  206.9 6.1 multiply_convert_fusion
  219.5 6.1 fusion.17.refs_5_
  225.6 6.9 %multiply_reduce_fusion.3 = (f32[768]{0:T(1024)S(1)}, f32[512]{0:T(512)S(1)}, f32[512]{0:T(512)S(1)}, f32[768]{0:T(1024)S(1)}, f32[512,768]{1,0:T(8,128)S(1)}) fusion(f32[512,768]{1,0:T(8,128)S(1)} %get-tuple-element.197, f32[512]{0:T(512)S(1)} %add_rsqrt_fusion.1, f32[512]{0:T(512)S(1)} %broadcast_multiply_fusion.13, f32[768]{0:T(1024)S(1)} %get-tuple-element.132, ...), kind=kOutput, calls=%fused_computation.65 | convolution fusion | flops 2423387648 | bytes 13400064 | tf_op jit(solution)/shard_map/dot_general | solution.py:27
  234.2 3.0 convolution_convert_fusion.2.g_ref
  237.2 11.9 %attention_backward.3.refs_5_ = bf16[512,2304]{1,0:T(8,128)(2,1)} custom-call(bf16[512,2304]{1,0:T(8,128)(2,1)} %fusion.31.qkv_ref, f32[512,768]{1,0:T(8,128)} %get-tuple-element.34.lt_ref, bf16[512,768]{1,0:T(8,128)(2,1)} %convolution_convert_fusion.2.g_ref), custom_call_target="tpu_custom_call" | custom-call | flops 4026531840 | bytes 7077888 | tf_op jit(solution)/shard_map/attention_backward/pallas_call | solution.py:157
  249.1 6.2 multiply_reduce_fusion.1
  255.8 8.7 %fusion.23.refs_4_ = bf16[512,3072]{1,0:T(8,128)(2,1)S(1)} fusion(f32[512,3072]{1,0:T(8,128)} %get-tuple-element.193, bf16[512,768]{1,0:T(8,128)(2,1)S(1)} %get-tuple-element.142.refs_4_, bf16[3072,768]{1,0:T(8,128)(2,1)} %copy-done.32, f32[3072]{0:T(1024)S(1)} %add.368), kind=kOutput, calls=%fused_computation.29 | convolution fusion | flops 2445803520 | bytes 14954496 | tf_op jit(solution)/shard_map/dot_general | solution.py:27
  264.6 6.6 %multiply_reduce_fusion.4 = (f32[768]{0:T(1024)S(1)}, f32[512]{0:T(512)S(1)}, f32[512]{0:T(512)S(1)}, f32[768]{0:T(1024)S(1)}, f32[512,768]{1,0:T(8,128)S(1)}) fusion(f32[512,768]{1,0:T(8,128)S(1)} %get-tuple-element.191, f32[512]{0:T(512)S(1)} %add_rsqrt_fusion.3, f32[512]{0:T(512)S(1)} %broadcast_multiply_fusion.15, f32[768]{0:T(1024)S(1)} %get-tuple-element.132, ...), kind=kOutput, calls=%fused_computation.66 | convolution fusion | flops 2419848704 | bytes 12600320 | tf_op jit(solution)/shard_map/dot_general | solution.py:27
  271.2 3.1 fusion.89
  274.2 3.0 convolution_convert_fusion.1.g_ref
  277.2 11.9 %attention_backward.4.refs_4_ = bf16[512,2304]{1,0:T(8,128)(2,1)} custom-call(bf16[512,2304]{1,0:T(8,128)(2,1)} %fusion.30.qkv_ref, f32[512,768]{1,0:T(8,128)} %get-tuple-element.35.lt_ref, bf16[512,768]{1,0:T(8,128)(2,1)} %convolution_convert_fusion.1.g_ref), custom_call_target="tpu_custom_call" | custom-call | flops 4026531840 | bytes 7077888 | tf_op jit(solution)/shard_map/attention_backward/pallas_call | solution.py:157
  289.1 6.2 multiply_reduce_fusion.2
  295.8 8.8 %fusion.29.refs_3_ = bf16[512,3072]{1,0:T(8,128)(2,1)S(1)} fusion(f32[512,3072]{1,0:T(8,128)} %get-tuple-element.187, bf16[512,768]{1,0:T(8,128)(2,1)S(1)} %get-tuple-element.138.refs_3_, bf16[3072,768]{1,0:T(8,128)(2,1)} %copy-done.32, f32[3072]{0:T(1024)S(1)} %add.368), kind=kOutput, calls=%fused_computation.35 | convolution fusion | flops 2445803520 | bytes 14954496 | tf_op jit(solution)/shard_map/dot_general | solution.py:27
  304.7 6.6 %multiply_reduce_fusion.5 = (f32[768]{0:T(1024)S(1)}, f32[512]{0:T(512)S(1)}, f32[512]{0:T(512)S(1)}, f32[768]{0:T(1024)S(1)}, f32[512,768]{1,0:T(8,128)S(1)}) fusion(f32[512,768]{1,0:T(8,128)S(1)} %copy-done.26, f32[512]{0:T(512)S(1)} %add_rsqrt_fusion.5, f32[512]{0:T(512)S(1)} %broadcast_multiply_fusion.17, f32[768]{0:T(1024)S(1)} %get-tuple-element.132, ...), kind=kOutput, calls=%fused_computation.67 | convolution fusion | flops 2419848704 | bytes 12600320 | tf_op jit(solution)/shard_map/dot_general | solution.py:27
  313.0 3.0 convolution_convert_fusion.g_ref
  316.0 11.9 %attention_backward.5.refs_3_ = bf16[512,2304]{1,0:T(8,128)(2,1)} custom-call(bf16[512,2304]{1,0:T(8,128)(2,1)} %fusion.33.qkv_ref, f32[512,768]{1,0:T(8,128)} %get-tuple-element.36.lt_ref, bf16[512,768]{1,0:T(8,128)(2,1)} %convolution_convert_fusion.g_ref), custom_call_target="tpu_custom_call" | custom-call | flops 4026531840 | bytes 7077888 | tf_op jit(solution)/shard_map/attention_backward/pallas_call | solution.py:157
  333.0 9.0 %weight_grad.4 = (bf16[768,9344]{1,0:T(8,128)(2,1)}, f32[1,2304]{1,0:T(1,128)S(1)}) custom-call(bf16[512,768]{1,0:T(8,128)(2,1)S(1)} %copy-done.18, bf16[512,768]{1,0:T(8,128)(2,1)S(1)} %copy-done.12, bf16[512,768]{1,0:T(8,128)(2,1)S(1)} %copy-done.16, bf16[512,2304]{1,0:T(8,128)(2,1)S(1)} %copy-done.23, bf16[512,2304]{1,0:T(8,128)(2,1)} %attention_backward.4.refs_4_, ...), custom_call_target="tpu_custom_call" | custom-call | flops 5435817984 | bytes 12976128 | tf_op jit(solution)/shard_map/weight_grad/pallas_call | solution.py:219
  342.0 3.2 weight_grad.5
  347.1 11.4 %weight_grad.6 = (bf16[768,9344]{1,0:T(8,128)(2,1)}, f32[1,3072]{1,0:T(1,128)S(1)}) custom-call(bf16[512,768]{1,0:T(8,128)(2,1)S(1)} %copy-done.8, bf16[512,768]{1,0:T(8,128)(2,1)S(1)} %copy-done.10, bf16[512,768]{1,0:T(8,128)(2,1)S(1)} %copy-done.14, bf16[512,3072]{1,0:T(8,128)(2,1)S(1)} %copy-done.22, ...), custom_call_target="tpu_custom_call", output_to_operand_aliasing={{0}: (6, {})} | custom-call | flops 7247757312 | bytes 16515072 | tf_op jit(solution)/shard_map/weight_grad/pallas_call | solution.py:219
  358.6 11.1 %weight_grad.7 = (bf16[768,9344]{1,0:T(8,128)(2,1)}, f32[1,768]{1,0:T(1,128)S(1)}) custom-call(bf16[512,3072]{1,0:T(8,128)(2,1)S(1)} %copy-done.20, bf16[512,3072]{1,0:T(8,128)(2,1)} %copy-done.49, bf16[512,3072]{1,0:T(8,128)(2,1)} %copy-done.50, bf16[512,768]{1,0:T(8,128)(2,1)S(1)} %copy-done.6, ...), custom_call_target="tpu_custom_call", output_to_operand_aliasing={{0}: (6, {})} | custom-call | flops 7247757312 | bytes 16515072 | tf_op jit(solution)/shard_map/weight_grad/pallas_call | solution.py:219
  374.9 5.5 add_convert_fusion
  380.5 241.6 %all-reduce.5.cloned.1.call-done = bf16[768,9344]{1,0:T(8,128)(2,1)} async-done(((bf16[768,9344]{1,0:T(8,128)(2,1)}), bf16[768,9344]{1,0:T(8,128)(2,1)}) %all-reduce.5.cloned.1.call-update) | async-done | bytes 14352400
  (251 shorter events, 67.1 us)
Async XLA Ops:
  7.2 113.0 %all-gather.2.cloned.1.call-start = ((), (), s32[]{:S(2)}) async-start(), calls=%async_computation | async-start | bytes 14800896 | tf_op jit(solution)/shard_map/all_gather | solution.py:287
  14.0 608.0 %all-reduce.5.cloned.1.call-start = ((), (), s32[]{:S(2)}) async-start(), calls=%async_computation.1 | async-start | bytes 28704768
  139.9 14.6 %copy-start.25 = (f32[512,768]{1,0:T(8,128)}, f32[512,768]{1,0:T(8,128)S(1)}, u32[]{:S(2)}) copy-start(f32[512,768]{1,0:T(8,128)S(1)} %get-tuple-element.185) | copy-start | bytes 4718596
  143.7 10.8 %copy-start.32 = (bf16[3072,768]{1,0:T(8,128)(2,1)}, bf16[3072,768]{1,0:T(8,128)(2,1)S(1)}, u32[]{:S(2)}) copy-start(bf16[3072,768]{1,0:T(8,128)(2,1)S(1)} %pad_maximum_fusion) | copy-start | bytes 14155780
  144.0 10.5 %copy-start.7 = (bf16[512,768]{1,0:T(8,128)(2,1)}, bf16[512,768]{1,0:T(8,128)(2,1)S(1)}, u32[]{:S(2)}) copy-start(bf16[512,768]{1,0:T(8,128)(2,1)S(1)} %fusion.73.refs_0_) | copy-start | bytes 2359300
  157.3 15.4 %copy-start.27 = (f32[512,768]{1,0:T(8,128)}, f32[512,768]{1,0:T(8,128)S(1)}, u32[]{:S(2)}) copy-start(f32[512,768]{1,0:T(8,128)S(1)} %get-tuple-element.189) | copy-start | bytes 4718596
  175.2 89.4 %copy-start.29 = (f32[512,768]{1,0:T(8,128)}, f32[512,768]{1,0:T(8,128)S(1)}, u32[]{:S(2)}) copy-start(f32[512,768]{1,0:T(8,128)S(1)} %get-tuple-element.191) | copy-start | bytes 4718596
  175.5 9.9 %slice-start = ((s8[4718592]{0:T(1024)(128)(4,1)}), s8[4194304]{0:T(1024)(128)(4,1)S(1)}, s32[]{:S(2)}) async-start(s8[4718592]{0:T(1024)(128)(4,1)} %bitcast.88), calls=%async_computation.2 | async-start | bytes 8388608
  175.8 9.6 %copy-start.9 = (bf16[512,768]{1,0:T(8,128)(2,1)}, bf16[512,768]{1,0:T(8,128)(2,1)S(1)}, u32[]{:S(2)}) copy-start(bf16[512,768]{1,0:T(8,128)(2,1)S(1)} %fusion.75.refs_1_) | copy-start | bytes 2359300
  175.8 9.6 %slice-start.1 = ((s8[4718592]{0:T(1024)(128)(4,1)}), s8[524288]{0:T(1024)(128)(4,1)S(1)}, s32[]{:S(2)}) async-start(s8[4718592]{0:T(1024)(128)(4,1)} %bitcast.88), calls=%async_computation.3 | async-start | bytes 1048576
  188.2 15.5 %copy-start.30 = (f32[512,768]{1,0:T(8,128)}, f32[512,768]{1,0:T(8,128)S(1)}, u32[]{:S(2)}) copy-start(f32[512,768]{1,0:T(8,128)S(1)} %get-tuple-element.195) | copy-start | bytes 4718596
  206.5 6.5 %slice-start.2 = ((s8[4718592]{0:T(1024)(128)(4,1)}), s8[4194304]{0:T(1024)(128)(4,1)S(1)}, s32[]{:S(2)}) async-start(s8[4718592]{0:T(1024)(128)(4,1)} %bitcast.90), calls=%async_computation.4 | async-start | bytes 8388608
  206.8 6.2 copy-start.13
  206.9 6.2 slice-start.3
  225.6 6.9 %copy-start.51 = (bf16[512,3072]{1,0:T(8,128)(2,1)}, bf16[512,3072]{1,0:T(8,128)(2,1)S(1)}, u32[]{:S(2)}) copy-start(bf16[512,3072]{1,0:T(8,128)(2,1)S(1)} %fusion.17.refs_5_) | copy-start | bytes 9437188
  249.1 6.2 copy-start.31
  255.8 8.8 %copy-start.3 = (bf16[512,768]{1,0:T(8,128)(2,1)}, bf16[512,768]{1,0:T(8,128)(2,1)S(1)}, u32[]{:S(2)}) copy-start(bf16[512,768]{1,0:T(8,128)(2,1)S(1)} %get-tuple-element.142.refs_4_) | copy-start | bytes 2359300
  264.5 6.6 %copy-start.52 = (bf16[512,3072]{1,0:T(8,128)(2,1)}, bf16[512,3072]{1,0:T(8,128)(2,1)S(1)}, u32[]{:S(2)}) copy-start(bf16[512,3072]{1,0:T(8,128)(2,1)S(1)} %fusion.23.refs_4_) | copy-start | bytes 9437188
  289.1 6.2 copy-start.28
  295.8 8.8 %copy-start.5 = (bf16[512,768]{1,0:T(8,128)(2,1)}, bf16[512,768]{1,0:T(8,128)(2,1)S(1)}, u32[]{:S(2)}) copy-start(bf16[512,768]{1,0:T(8,128)(2,1)S(1)} %get-tuple-element.138.refs_3_) | copy-start | bytes 2359300
  295.8 8.8 %copy-start.26 = (f32[512,768]{1,0:T(8,128)S(1)}, f32[512,768]{1,0:T(8,128)}, u32[]{:S(2)}) copy-start(f32[512,768]{1,0:T(8,128)} %copy-done.25) | copy-start | bytes 4718596
  304.6 6.6 %copy-start.21 = (bf16[512,3072]{1,0:T(8,128)(2,1)}, bf16[512,3072]{1,0:T(8,128)(2,1)S(1)}, u32[]{:S(2)}) copy-start(bf16[512,3072]{1,0:T(8,128)(2,1)S(1)} %fusion.29.refs_3_) | copy-start | bytes 9437188
  333.0 9.0 %copy-start = (bf16[512,768]{1,0:T(8,128)(2,1)S(1)}, bf16[512,768]{1,0:T(8,128)(2,1)}, u32[]{:S(2)}) copy-start(bf16[512,768]{1,0:T(8,128)(2,1)} %get-tuple-element.31.refs_0_) | copy-start | bytes 2359300
  333.0 9.0 %copy-start.1 = (bf16[512,768]{1,0:T(8,128)(2,1)S(1)}, bf16[512,768]{1,0:T(8,128)(2,1)}, u32[]{:S(2)}) copy-start(bf16[512,768]{1,0:T(8,128)(2,1)} %get-tuple-element.32.refs_1_) | copy-start | bytes 2359300
  333.0 9.0 %copy-start.2 = (bf16[512,768]{1,0:T(8,128)(2,1)S(1)}, bf16[512,768]{1,0:T(8,128)(2,1)}, u32[]{:S(2)}) copy-start(bf16[512,768]{1,0:T(8,128)(2,1)} %get-tuple-element.33.refs_2_) | copy-start | bytes 2359300
  342.0 3.2 copy-start.8
  342.0 3.2 copy-start.10
  347.1 11.4 %copy-start.4 = (bf16[512,768]{1,0:T(8,128)(2,1)S(1)}, bf16[512,768]{1,0:T(8,128)(2,1)}, u32[]{:S(2)}) copy-start(bf16[512,768]{1,0:T(8,128)(2,1)} %copy-done.3) | copy-start | bytes 2359300
  347.1 11.4 %copy-start.6 = (bf16[512,768]{1,0:T(8,128)(2,1)S(1)}, bf16[512,768]{1,0:T(8,128)(2,1)}, u32[]{:S(2)}) copy-start(bf16[512,768]{1,0:T(8,128)(2,1)} %copy-done.5) | copy-start | bytes 2359300
  347.1 11.4 %copy-start.20 = (bf16[512,3072]{1,0:T(8,128)(2,1)S(1)}, bf16[512,3072]{1,0:T(8,128)(2,1)}, u32[]{:S(2)}) copy-start(bf16[512,3072]{1,0:T(8,128)(2,1)} %copy-done.19) | copy-start | bytes 9437188
  358.6 11.2 %copy-start.39 = (bf16[768]{0:T(1024)(128)(2,1)S(1)}, bf16[768]{0:T(1024)(128)(2,1)}, u32[]{:S(2)}) copy-start(bf16[768]{0:T(1024)(128)(2,1)} %custom-call.4) | copy-start | bytes 4612
  358.6 12.4 %copy-start.38 = (bf16[768]{0:T(1024)(128)(2,1)S(1)}, bf16[768]{0:T(1024)(128)(2,1)}, u32[]{:S(2)}) copy-start(bf16[768]{0:T(1024)(128)(2,1)} %custom-call.3) | copy-start | bytes 4612
  (27 other events, 58.2 us)
Sparse Core Ops, SparseCore 0:
  14.2 105.9 all-gather.1
  373.4 248.5 all-reduce.4

commit v14 on v12

--- a/solution.py
+++ b/solution.py
@@ -186,11 +186,16 @@
     sum_ref[...] = sums
 
 
-def weight_grad(xs, gs, into=None, at=0, stack=False, columns=None, block=768):
+def weight_grad(xs, gs, into=None, at=0, stack=False, columns=None, block=768, wide_block=1536):
     tokens, depth = xs[0].shape
     width = gs[0].shape[1]
     bk = min(block, depth)
     bn = min(block, width)
+    if not stack and width % wide_block == 0:
+        bn = wide_block
+    elif not stack and width % (block * 3 // 2) == 0 and width > block:
+        bn = block * 3 // 2
+    at = at * block // bn
     grid = (depth // bk, width // bn)
     count = len(xs)
     if stack:

time: 552 us -> 553 us (level)
  no operation moved by 1% of the time
where the time goes in v14:
time: 553 us; the launch traced here: 547 us
  waiting for transfers between devices  257 us (46%)
  matrix products  129 us (23%)
  Pallas kernels  97.5 us (18%)
  local copies, waits for them, and re-layouts  32.1 us (6%)
  other arithmetic  16.1 us (3%)
  between operations  15.6 us (3%)
    unnamed x3, waiting for transfers between devices  151 us
    all_gather x1, waiting for transfers between devices, gather_weights(): packed = lax.all_gather(pack_weights(weights), AXES, axis=0, tiled=True)  106 us
    dot_general x12, matrix products, product_nt(): return lax.dot_general(left, right, NT, preferred_element_type=jnp.float32)  70.5 us
    dot_general x12, matrix products, product(): return jnp.dot(left, right, preferred_element_type=jnp.float32)  58.3 us
    pallas_call x4, Pallas kernels, weight_grad(): pl.pallas_call(kernel, grid=grid, in_specs=in_specs, out_specs=[pl.BlockS...  36 us
    pallas_call x3, Pallas kernels, attention_backward(): pl.pallas_call(attention_backward_kernel, grid=grid, in_specs=[triple, pa...  35.8 us
    pallas_call x3, Pallas kernels, attention_forward(): pl.pallas_call(attention_forward_kernel, grid=grid, in_specs=[pl.BlockSpe...  25.8 us
    unnamed x150, local copies, waits for them, and re-layouts  17.4 us
  transfers between devices with their start and end apart: 2, of which 2 were waited for; matrix products, arithmetic and copies ran while one was open for 1% of the time, Pallas kernels for 0%

profile of v14, /device:TPU:0, one launch (start us, length us, event | category | flops | bytes accessed | tf_op | source)
XLA Modules:
  0.0 546.8 jit_solution(12065593050982770160)
XLA Ops:
  14.2 106.0 %all-gather.2.cloned.1.call-done = bf16[768,9344]{1,0:T(8,128)(2,1)} async-done(((bf16[24,9344]{1,0:T(8,128)(2,1)}), bf16[768,9344]{1,0:T(8,128)(2,1)}) %all-gather.2.cloned.1.call-update) | async-done | bytes 14352400 | tf_op jit(solution)/shard_map/all_gather | solution.py:292
  123.4 5.5 fusion.33.qkv_ref
  128.9 8.7 %attention_forward.3 = (bf16[512,768]{1,0:T(8,128)(2,1)}, f32[512,768]{1,0:T(8,128)}) custom-call(bf16[512,2304]{1,0:T(8,128)(2,1)} %fusion.33.qkv_ref), custom_call_target="tpu_custom_call" | custom-call | flops 1610612736 | bytes 4718592 | tf_op jit(solution)/shard_map/attention_forward/pallas_call | solution.py:131
  140.3 2.9 fusion.92
  144.1 10.6 %multiply_convert_fusion.2 = (bf16[512,3072]{1,0:T(8,128)(2,1)S(1)}, f32[512,3072]{1,0:T(8,128)}) fusion(f32[3072]{0:T(1024)S(1)} %add.368, bf16[512,768]{1,0:T(8,128)(2,1)S(1)} %fusion.73.refs_0_, bf16[768,9344]{1,0:T(8,128)(2,1)} %all-gather.2.cloned.1.call-done), kind=kOutput, calls=%fused_computation.40 | convolution fusion | flops 2431647744 | bytes 14954496 | tf_op jit(solution)/shard_map/dot_general | solution.py:23
  158.1 5.5 %fusion.30.qkv_ref = bf16[512,2304]{1,0:T(8,128)(2,1)} fusion(bf16[512,768]{1,0:T(8,128)(2,1)S(1)} %fusion.74.refs_1_, f32[2304]{0:T(1024)S(1)} %add.357, bf16[768,9344]{1,0:T(8,128)(2,1)} %all-gather.2.cloned.1.call-done), kind=kOutput, calls=%fused_computation.46 | convolution fusion | flops 1814298624 | bytes 6693888 | tf_op jit(solution)/shard_map/dot_general | solution.py:23
  164.5 8.5 %attention_forward.4 = (bf16[512,768]{1,0:T(8,128)(2,1)}, f32[512,768]{1,0:T(8,128)}) custom-call(bf16[512,2304]{1,0:T(8,128)(2,1)} %fusion.30.qkv_ref), custom_call_target="tpu_custom_call" | custom-call | flops 1610612736 | bytes 4718592 | tf_op jit(solution)/shard_map/attention_forward/pallas_call | solution.py:131
  176.1 9.6 %multiply_convert_fusion.1 = (bf16[512,3072]{1,0:T(8,128)(2,1)S(1)}, f32[512,3072]{1,0:T(8,128)}) fusion(f32[3072]{0:T(1024)S(1)} %add.368, bf16[512,768]{1,0:T(8,128)(2,1)S(1)} %fusion.75.refs_1_, bf16[768,9344]{1,0:T(8,128)(2,1)} %all-gather.2.cloned.1.call-done), kind=kOutput, calls=%fused_computation.38 | convolution fusion | flops 2431647744 | bytes 14954496 | tf_op jit(solution)/shard_map/dot_general | solution.py:23
  189.2 5.4 fusion.31.qkv_ref
  195.5 8.6 %attention_forward.5 = (bf16[512,768]{1,0:T(8,128)(2,1)}, f32[512,768]{1,0:T(8,128)}) custom-call(bf16[512,2304]{1,0:T(8,128)(2,1)} %fusion.31.qkv_ref), custom_call_target="tpu_custom_call" | custom-call | flops 1610612736 | bytes 4718592 | tf_op jit(solution)/shard_map/attention_forward/pallas_call | solution.py:131
  207.2 6.1 %multiply_convert_fusion = (bf16[512,3072]{1,0:T(8,128)(2,1)S(1)}, f32[512,3072]{1,0:T(8,128)S(1)}) fusion(f32[3072]{0:T(1024)S(1)} %add.368, bf16[512,768]{1,0:T(8,128)(2,1)S(1)} %fusion.77.refs_2_, bf16[768,9344]{1,0:T(8,128)(2,1)} %all-gather.2.cloned.1.call-done), kind=kOutput, calls=%fused_computation.36 | convolution fusion | flops 2431647744 | bytes 14954496 | tf_op jit(solution)/shard_map/dot_general | solution.py:23
  219.8 6.1 %fusion.17.refs_5_ = bf16[512,3072]{1,0:T(8,128)(2,1)S(1)} fusion(f32[512,3072]{1,0:T(8,128)S(1)} %get-tuple-element.199, bf16[512,768]{1,0:T(8,128)(2,1)S(1)} %get-tuple-element.150.refs_5_, bf16[3072,768]{1,0:T(8,128)(2,1)S(1)} %bitcast.91, f32[3072]{0:T(1024)S(1)} %add.368), kind=kOutput, calls=%fused_computation.23 | convolution fusion | flops 2445803520 | bytes 14954496 | tf_op jit(solution)/shard_map/dot_general | solution.py:27
  225.9 6.9 %multiply_reduce_fusion.3 = (f32[768]{0:T(1024)S(1)}, f32[512]{0:T(512)S(1)}, f32[512]{0:T(512)S(1)}, f32[768]{0:T(1024)S(1)}, f32[512,768]{1,0:T(8,128)S(1)}) fusion(f32[512,768]{1,0:T(8,128)S(1)} %get-tuple-element.197, f32[512]{0:T(512)S(1)} %add_rsqrt_fusion.1, f32[512]{0:T(512)S(1)} %broadcast_multiply_fusion.13, f32[768]{0:T(1024)S(1)} %get-tuple-element.132, ...), kind=kOutput, calls=%fused_computation.65 | convolution fusion | flops 2423387648 | bytes 13400064 | tf_op jit(solution)/shard_map/dot_general | solution.py:27
  234.5 3.0 convolution_convert_fusion.2.g_ref
  237.5 11.9 %attention_backward.3.refs_5_ = bf16[512,2304]{1,0:T(8,128)(2,1)} custom-call(bf16[512,2304]{1,0:T(8,128)(2,1)} %fusion.31.qkv_ref, f32[512,768]{1,0:T(8,128)} %get-tuple-element.34.lt_ref, bf16[512,768]{1,0:T(8,128)(2,1)} %convolution_convert_fusion.2.g_ref), custom_call_target="tpu_custom_call" | custom-call | flops 4026531840 | bytes 7077888 | tf_op jit(solution)/shard_map/attention_backward/pallas_call | solution.py:157
  249.4 6.2 %multiply_reduce_fusion.1 = (f32[768]{0:T(1024)S(1)}, f32[512]{0:T(512)S(1)}, f32[512]{0:T(512)S(1)}, f32[768]{0:T(1024)S(1)}, f32[512,768]{1,0:T(8,128)S(1)}) fusion(f32[512,768]{1,0:T(8,128)} %copy-done.30, f32[512]{0:T(512)S(1)} %add_rsqrt_fusion.2, f32[512]{0:T(512)S(1)} %broadcast_multiply_fusion.14, f32[768]{0:T(1024)S(1)} %get-tuple-element.128, ...), kind=kOutput, calls=%fused_computation.63 | convolution fusion | flops 1815868928 | bytes 10634240 | tf_op jit(solution)/shard_map/dot_general | solution.py:27
  256.1 8.7 %fusion.23.refs_4_ = bf16[512,3072]{1,0:T(8,128)(2,1)S(1)} fusion(f32[512,3072]{1,0:T(8,128)} %get-tuple-element.193, bf16[512,768]{1,0:T(8,128)(2,1)S(1)} %get-tuple-element.142.refs_4_, bf16[3072,768]{1,0:T(8,128)(2,1)} %copy-done.32, f32[3072]{0:T(1024)S(1)} %add.368), kind=kOutput, calls=%fused_computation.29 | convolution fusion | flops 2445803520 | bytes 14954496 | tf_op jit(solution)/shard_map/dot_general | solution.py:27
  264.8 6.6 %multiply_reduce_fusion.4 = (f32[768]{0:T(1024)S(1)}, f32[512]{0:T(512)S(1)}, f32[512]{0:T(512)S(1)}, f32[768]{0:T(1024)S(1)}, f32[512,768]{1,0:T(8,128)S(1)}) fusion(f32[512,768]{1,0:T(8,128)S(1)} %get-tuple-element.191, f32[512]{0:T(512)S(1)} %add_rsqrt_fusion.3, f32[512]{0:T(512)S(1)} %broadcast_multiply_fusion.15, f32[768]{0:T(1024)S(1)} %get-tuple-element.132, ...), kind=kOutput, calls=%fused_computation.66 | convolution fusion | flops 2419848704 | bytes 12600320 | tf_op jit(solution)/shard_map/dot_general | solution.py:27
  271.5 3.1 fusion.89
  274.5 3.0 convolution_convert_fusion.1.g_ref
  277.5 12.0 %attention_backward.4.refs_4_ = bf16[512,2304]{1,0:T(8,128)(2,1)} custom-call(bf16[512,2304]{1,0:T(8,128)(2,1)} %fusion.30.qkv_ref, f32[512,768]{1,0:T(8,128)} %get-tuple-element.35.lt_ref, bf16[512,768]{1,0:T(8,128)(2,1)} %convolution_convert_fusion.1.g_ref), custom_call_target="tpu_custom_call" | custom-call | flops 4026531840 | bytes 7077888 | tf_op jit(solution)/shard_map/attention_backward/pallas_call | solution.py:157
  289.5 6.2 %multiply_reduce_fusion.2 = (f32[768]{0:T(1024)S(1)}, f32[512]{0:T(512)S(1)}, f32[512]{0:T(512)S(1)}, f32[768]{0:T(1024)S(1)}, f32[512,768]{1,0:T(8,128)S(1)}) fusion(f32[512,768]{1,0:T(8,128)} %copy-done.27, f32[512]{0:T(512)S(1)} %add_rsqrt_fusion.4, f32[512]{0:T(512)S(1)} %broadcast_multiply_fusion.16, f32[768]{0:T(1024)S(1)} %get-tuple-element.128, ...), kind=kOutput, calls=%fused_computation.64 | convolution fusion | flops 1815868928 | bytes 10634240 | tf_op jit(solution)/shard_map/dot_general | solution.py:27
  296.2 8.8 %fusion.29.refs_3_ = bf16[512,3072]{1,0:T(8,128)(2,1)S(1)} fusion(f32[512,3072]{1,0:T(8,128)} %get-tuple-element.187, bf16[512,768]{1,0:T(8,128)(2,1)S(1)} %get-tuple-element.138.refs_3_, bf16[3072,768]{1,0:T(8,128)(2,1)} %copy-done.32, f32[3072]{0:T(1024)S(1)} %add.368), kind=kOutput, calls=%fused_computation.35 | convolution fusion | flops 2445803520 | bytes 14954496 | tf_op jit(solution)/shard_map/dot_general | solution.py:27
  305.0 6.6 %multiply_reduce_fusion.5 = (f32[768]{0:T(1024)S(1)}, f32[512]{0:T(512)S(1)}, f32[512]{0:T(512)S(1)}, f32[768]{0:T(1024)S(1)}, f32[512,768]{1,0:T(8,128)S(1)}) fusion(f32[512,768]{1,0:T(8,128)S(1)} %copy-done.26, f32[512]{0:T(512)S(1)} %add_rsqrt_fusion.5, f32[512]{0:T(512)S(1)} %broadcast_multiply_fusion.17, f32[768]{0:T(1024)S(1)} %get-tuple-element.132, ...), kind=kOutput, calls=%fused_computation.67 | convolution fusion | flops 2419848704 | bytes 12600320 | tf_op jit(solution)/shard_map/dot_general | solution.py:27
  313.3 3.0 convolution_convert_fusion.g_ref
  316.3 11.9 %attention_backward.5.refs_3_ = bf16[512,2304]{1,0:T(8,128)(2,1)} custom-call(bf16[512,2304]{1,0:T(8,128)(2,1)} %fusion.33.qkv_ref, f32[512,768]{1,0:T(8,128)} %get-tuple-element.36.lt_ref, bf16[512,768]{1,0:T(8,128)(2,1)} %convolution_convert_fusion.g_ref), custom_call_target="tpu_custom_call" | custom-call | flops 4026531840 | bytes 7077888 | tf_op jit(solution)/shard_map/attention_backward/pallas_call | solution.py:157
  333.3 9.8 %weight_grad.4 = (bf16[768,9344]{1,0:T(8,128)(2,1)}, f32[1,2304]{1,0:T(1,128)S(1)}) custom-call(bf16[512,768]{1,0:T(8,128)(2,1)S(1)} %copy-done.18, bf16[512,768]{1,0:T(8,128)(2,1)S(1)} %copy-done.12, bf16[512,768]{1,0:T(8,128)(2,1)S(1)} %copy-done.16, bf16[512,2304]{1,0:T(8,128)(2,1)S(1)} %copy-done.23, bf16[512,2304]{1,0:T(8,128)(2,1)} %attention_backward.4.refs_4_, ...), custom_call_target="tpu_custom_call" | custom-call | flops 5435817984 | bytes 12976128 | tf_op jit(solution)/shard_map/weight_grad/pallas_call | solution.py:224
  343.1 3.2 weight_grad.5
  348.2 11.9 %weight_grad.6 = (bf16[768,9344]{1,0:T(8,128)(2,1)}, f32[1,3072]{1,0:T(1,128)S(1)}) custom-call(bf16[512,768]{1,0:T(8,128)(2,1)S(1)} %copy-done.8, bf16[512,768]{1,0:T(8,128)(2,1)S(1)} %copy-done.10, bf16[512,768]{1,0:T(8,128)(2,1)S(1)} %copy-done.14, bf16[512,3072]{1,0:T(8,128)(2,1)S(1)} %copy-done.22, ...), custom_call_target="tpu_custom_call", output_to_operand_aliasing={{0}: (6, {})} | custom-call | flops 7247757312 | bytes 16515072 | tf_op jit(solution)/shard_map/weight_grad/pallas_call | solution.py:224
  360.2 11.1 %weight_grad.7 = (bf16[768,9344]{1,0:T(8,128)(2,1)}, f32[1,768]{1,0:T(1,128)S(1)}) custom-call(bf16[512,3072]{1,0:T(8,128)(2,1)S(1)} %copy-done.20, bf16[512,3072]{1,0:T(8,128)(2,1)} %copy-done.56, bf16[512,3072]{1,0:T(8,128)(2,1)} %copy-done.57, bf16[512,768]{1,0:T(8,128)(2,1)S(1)} %copy-done.6, ...), custom_call_target="tpu_custom_call", output_to_operand_aliasing={{0}: (6, {})} | custom-call | flops 7247757312 | bytes 16515072 | tf_op jit(solution)/shard_map/weight_grad/pallas_call | solution.py:224
  376.5 5.5 %add_convert_fusion = bf16[512,768]{1,0:T(8,128)(2,1)} fusion(f32[512,768]{1,0:T(8,128)} %get-tuple-element.137, bf16[512,2304]{1,0:T(8,128)(2,1)S(1)} %copy-done.24, bf16[768,9344]{1,0:T(8,128)(2,1)} %all-gather.2.cloned.1.call-done), kind=kOutput, calls=%fused_computation.68 | convolution fusion | flops 1812725760 | bytes 8257536 | tf_op jit(solution)/shard_map/dot_general | solution.py:27
  382.0 150.6 %reduce-scatter.4.cloned.1.call-done = bf16[24,9344]{1,0:T(8,128)(2,1)} async-done(((bf16[768,9344]{1,0:T(8,128)(2,1)}), bf16[24,9344]{1,0:T(8,128)(2,1)}) %reduce-scatter.4.cloned.1.call-update) | async-done | bytes 448528
  (263 shorter events, 58.1 us)
Async XLA Ops:
  7.2 113.0 %all-gather.2.cloned.1.call-start = ((), (), s32[]{:S(2)}) async-start(), calls=%async_computation.1 | async-start | bytes 14800896 | tf_op jit(solution)/shard_map/all_gather | solution.py:292
  14.0 518.6 %reduce-scatter.4.cloned.1.call-start = ((), (), s32[]{:S(2)}) async-start(), calls=%async_computation.2 | async-start | bytes 14800896
  140.0 14.7 %copy-start.25 = (f32[512,768]{1,0:T(8,128)}, f32[512,768]{1,0:T(8,128)S(1)}, u32[]{:S(2)}) copy-start(f32[512,768]{1,0:T(8,128)S(1)} %get-tuple-element.185) | copy-start | bytes 4718596
  143.7 10.9 %copy-start.32 = (bf16[3072,768]{1,0:T(8,128)(2,1)}, bf16[3072,768]{1,0:T(8,128)(2,1)S(1)}, u32[]{:S(2)}) copy-start(bf16[3072,768]{1,0:T(8,128)(2,1)S(1)} %pad_maximum_fusion) | copy-start | bytes 14155780
  144.1 10.6 %copy-start.7 = (bf16[512,768]{1,0:T(8,128)(2,1)}, bf16[512,768]{1,0:T(8,128)(2,1)S(1)}, u32[]{:S(2)}) copy-start(bf16[512,768]{1,0:T(8,128)(2,1)S(1)} %fusion.73.refs_0_) | copy-start | bytes 2359300
  157.5 15.5 %copy-start.27 = (f32[512,768]{1,0:T(8,128)}, f32[512,768]{1,0:T(8,128)S(1)}, u32[]{:S(2)}) copy-start(f32[512,768]{1,0:T(8,128)S(1)} %get-tuple-element.189) | copy-start | bytes 4718596
  175.5 89.4 %copy-start.29 = (f32[512,768]{1,0:T(8,128)}, f32[512,768]{1,0:T(8,128)S(1)}, u32[]{:S(2)}) copy-start(f32[512,768]{1,0:T(8,128)S(1)} %get-tuple-element.191) | copy-start | bytes 4718596
  175.8 9.9 %slice-start = ((s8[4718592]{0:T(1024)(128)(4,1)}), s8[4194304]{0:T(1024)(128)(4,1)S(1)}, s32[]{:S(2)}) async-start(s8[4718592]{0:T(1024)(128)(4,1)} %bitcast.88), calls=%async_computation.3 | async-start | bytes 8388608
  176.1 9.6 %copy-start.9 = (bf16[512,768]{1,0:T(8,128)(2,1)}, bf16[512,768]{1,0:T(8,128)(2,1)S(1)}, u32[]{:S(2)}) copy-start(bf16[512,768]{1,0:T(8,128)(2,1)S(1)} %fusion.75.refs_1_) | copy-start | bytes 2359300
  176.1 9.6 %slice-start.1 = ((s8[4718592]{0:T(1024)(128)(4,1)}), s8[524288]{0:T(1024)(128)(4,1)S(1)}, s32[]{:S(2)}) async-start(s8[4718592]{0:T(1024)(128)(4,1)} %bitcast.88), calls=%async_computation.4 | async-start | bytes 1048576
  188.5 15.5 %copy-start.30 = (f32[512,768]{1,0:T(8,128)}, f32[512,768]{1,0:T(8,128)S(1)}, u32[]{:S(2)}) copy-start(f32[512,768]{1,0:T(8,128)S(1)} %get-tuple-element.195) | copy-start | bytes 4718596
  206.8 6.5 %slice-start.2 = ((s8[4718592]{0:T(1024)(128)(4,1)}), s8[4194304]{0:T(1024)(128)(4,1)S(1)}, s32[]{:S(2)}) async-start(s8[4718592]{0:T(1024)(128)(4,1)} %bitcast.90), calls=%async_computation.5 | async-start | bytes 8388608
  207.2 6.2 %copy-start.13 = (bf16[512,768]{1,0:T(8,128)(2,1)}, bf16[512,768]{1,0:T(8,128)(2,1)S(1)}, u32[]{:S(2)}) copy-start(bf16[512,768]{1,0:T(8,128)(2,1)S(1)} %fusion.77.refs_2_) | copy-start | bytes 2359300
  207.2 6.2 %slice-start.3 = ((s8[4718592]{0:T(1024)(128)(4,1)}), s8[524288]{0:T(1024)(128)(4,1)S(1)}, s32[]{:S(2)}) async-start(s8[4718592]{0:T(1024)(128)(4,1)} %bitcast.90), calls=%async_computation.6 | async-start | bytes 1048576
  225.9 6.9 %copy-start.58 = (bf16[512,3072]{1,0:T(8,128)(2,1)}, bf16[512,3072]{1,0:T(8,128)(2,1)S(1)}, u32[]{:S(2)}) copy-start(bf16[512,3072]{1,0:T(8,128)(2,1)S(1)} %fusion.17.refs_5_) | copy-start | bytes 9437188
  249.4 6.2 %copy-start.31 = (f32[512,768]{1,0:T(8,128)S(1)}, f32[512,768]{1,0:T(8,128)}, u32[]{:S(2)}) copy-start(f32[512,768]{1,0:T(8,128)} %copy-done.30) | copy-start | bytes 4718596
  256.1 8.8 %copy-start.3 = (bf16[512,768]{1,0:T(8,128)(2,1)}, bf16[512,768]{1,0:T(8,128)(2,1)S(1)}, u32[]{:S(2)}) copy-start(bf16[512,768]{1,0:T(8,128)(2,1)S(1)} %get-tuple-element.142.refs_4_) | copy-start | bytes 2359300
  264.8 6.6 %copy-start.59 = (bf16[512,3072]{1,0:T(8,128)(2,1)}, bf16[512,3072]{1,0:T(8,128)(2,1)S(1)}, u32[]{:S(2)}) copy-start(bf16[512,3072]{1,0:T(8,128)(2,1)S(1)} %fusion.23.refs_4_) | copy-start | bytes 9437188
  289.5 6.2 %copy-start.28 = (f32[512,768]{1,0:T(8,128)S(1)}, f32[512,768]{1,0:T(8,128)}, u32[]{:S(2)}) copy-start(f32[512,768]{1,0:T(8,128)} %copy-done.27) | copy-start | bytes 4718596
  296.2 8.8 %copy-start.5 = (bf16[512,768]{1,0:T(8,128)(2,1)}, bf16[512,768]{1,0:T(8,128)(2,1)S(1)}, u32[]{:S(2)}) copy-start(bf16[512,768]{1,0:T(8,128)(2,1)S(1)} %get-tuple-element.138.refs_3_) | copy-start | bytes 2359300
  296.2 8.8 %copy-start.26 = (f32[512,768]{1,0:T(8,128)S(1)}, f32[512,768]{1,0:T(8,128)}, u32[]{:S(2)}) copy-start(f32[512,768]{1,0:T(8,128)} %copy-done.25) | copy-start | bytes 4718596
  305.0 6.6 %copy-start.21 = (bf16[512,3072]{1,0:T(8,128)(2,1)}, bf16[512,3072]{1,0:T(8,128)(2,1)S(1)}, u32[]{:S(2)}) copy-start(bf16[512,3072]{1,0:T(8,128)(2,1)S(1)} %fusion.29.refs_3_) | copy-start | bytes 9437188
  333.3 9.8 %copy-start = (bf16[512,768]{1,0:T(8,128)(2,1)S(1)}, bf16[512,768]{1,0:T(8,128)(2,1)}, u32[]{:S(2)}) copy-start(bf16[512,768]{1,0:T(8,128)(2,1)} %get-tuple-element.31.refs_0_) | copy-start | bytes 2359300
  333.3 9.8 %copy-start.1 = (bf16[512,768]{1,0:T(8,128)(2,1)S(1)}, bf16[512,768]{1,0:T(8,128)(2,1)}, u32[]{:S(2)}) copy-start(bf16[512,768]{1,0:T(8,128)(2,1)} %get-tuple-element.32.refs_1_) | copy-start | bytes 2359300
  333.3 9.8 %copy-start.2 = (bf16[512,768]{1,0:T(8,128)(2,1)S(1)}, bf16[512,768]{1,0:T(8,128)(2,1)}, u32[]{:S(2)}) copy-start(bf16[512,768]{1,0:T(8,128)(2,1)} %get-tuple-element.33.refs_2_) | copy-start | bytes 2359300
  343.1 3.2 copy-start.8
  343.1 3.2 copy-start.10
  348.2 11.9 %copy-start.4 = (bf16[512,768]{1,0:T(8,128)(2,1)S(1)}, bf16[512,768]{1,0:T(8,128)(2,1)}, u32[]{:S(2)}) copy-start(bf16[512,768]{1,0:T(8,128)(2,1)} %copy-done.3) | copy-start | bytes 2359300
  348.2 11.9 %copy-start.6 = (bf16[512,768]{1,0:T(8,128)(2,1)S(1)}, bf16[512,768]{1,0:T(8,128)(2,1)}, u32[]{:S(2)}) copy-start(bf16[512,768]{1,0:T(8,128)(2,1)} %copy-done.5) | copy-start | bytes 2359300
  348.2 11.9 %copy-start.20 = (bf16[512,3072]{1,0:T(8,128)(2,1)S(1)}, bf16[512,3072]{1,0:T(8,128)(2,1)}, u32[]{:S(2)}) copy-start(bf16[512,3072]{1,0:T(8,128)(2,1)} %copy-done.19) | copy-start | bytes 9437188
  360.2 11.1 %copy-start.46 = (bf16[768]{0:T(1024)(128)(2,1)S(1)}, bf16[768]{0:T(1024)(128)(2,1)}, u32[]{:S(2)}) copy-start(bf16[768]{0:T(1024)(128)(2,1)} %custom-call.4) | copy-start | bytes 4612
  360.2 12.3 %copy-start.45 = (bf16[768]{0:T(1024)(128)(2,1)S(1)}, bf16[768]{0:T(1024)(128)(2,1)}, u32[]{:S(2)}) copy-start(bf16[768]{0:T(1024)(128)(2,1)} %custom-call.3) | copy-start | bytes 4612
  (34 other events, 70.9 us)
Sparse Core Ops, SparseCore 0:
  14.2 105.9 all-gather.1
  375.0 157.5 reduce-scatter.3

commit v15 on v12

--- a/solution.py
+++ b/solution.py
@@ -410,8 +410,9 @@
         at += count
     qkv_mine, out_mine, inner_mine, outer_mine, col_mine = pieces
     q_w, k_w, v_w = split_qkv(qkv_mine)
-    c = [col_mine[:, i] for i in range(8)]
-    ib_mine = col_mine[:, 8:12].reshape(-1)
+    col_rows = col_mine[:, :12].T
+    c = [col_rows[i] for i in range(8)]
+    ib_mine = col_rows[8:12].T.reshape(-1)
     return (
         q_w,
         c[0],

time: 552 us -> 552 us (level)
  no operation moved by 1% of the time
where the time goes in v15:
time: 552 us; the launch traced here: 546 us
  waiting for transfers between devices  257 us (47%)
  matrix products  129 us (23%)
  Pallas kernels  96.4 us (17%)
  local copies, waits for them, and re-layouts  32.1 us (6%)
  other arithmetic  16.1 us (3%)
  between operations  15.6 us (3%)
    unnamed x3, waiting for transfers between devices  151 us
    all_gather x1, waiting for transfers between devices, gather_weights(): packed = lax.all_gather(pack_weights(weights), AXES, axis=0, tiled=True)  106 us
    dot_general x12, matrix products, product_nt(): return lax.dot_general(left, right, NT, preferred_element_type=jnp.float32)  70.5 us
    dot_general x12, matrix products, product(): return jnp.dot(left, right, preferred_element_type=jnp.float32)  58.3 us
    pallas_call x3, Pallas kernels, attention_backward(): pl.pallas_call(attention_backward_kernel, grid=grid, in_specs=[triple, pa...  35.8 us
    pallas_call x4, Pallas kernels, weight_grad(): pl.pallas_call(kernel, grid=grid, in_specs=in_specs, out_specs=[pl.BlockS...  34.8 us
    pallas_call x3, Pallas kernels, attention_forward(): pl.pallas_call(attention_forward_kernel, grid=grid, in_specs=[pl.BlockSpe...  25.8 us
    unnamed x150, local copies, waits for them, and re-layouts  17.4 us
  transfers between devices with their start and end apart: 2, of which 2 were waited for; matrix products, arithmetic and copies ran while one was open for 1% of the time, Pallas kernels for 0%

profile of v15, /device:TPU:0, one launch (start us, length us, event | category | flops | bytes accessed | tf_op | source)
XLA Modules:
  0.0 545.7 jit_solution(9295958926551895189)
XLA Ops:
  14.2 106.0 %all-gather.2.cloned.1.call-done = bf16[768,9344]{1,0:T(8,128)(2,1)} async-done(((bf16[24,9344]{1,0:T(8,128)(2,1)}), bf16[768,9344]{1,0:T(8,128)(2,1)}) %all-gather.2.cloned.1.call-update) | async-done | bytes 14352400 | tf_op jit(solution)/shard_map/all_gather | solution.py:287
  123.4 5.5 fusion.33.qkv_ref
  128.9 8.7 %attention_forward.3 = (bf16[512,768]{1,0:T(8,128)(2,1)}, f32[512,768]{1,0:T(8,128)}) custom-call(bf16[512,2304]{1,0:T(8,128)(2,1)} %fusion.33.qkv_ref), custom_call_target="tpu_custom_call" | custom-call | flops 1610612736 | bytes 4718592 | tf_op jit(solution)/shard_map/attention_forward/pallas_call | solution.py:131
  140.3 2.9 fusion.92
  144.1 10.6 %multiply_convert_fusion.2 = (bf16[512,3072]{1,0:T(8,128)(2,1)S(1)}, f32[512,3072]{1,0:T(8,128)}) fusion(f32[3072]{0:T(1024)S(1)} %add.368, bf16[512,768]{1,0:T(8,128)(2,1)S(1)} %fusion.73.refs_0_, bf16[768,9344]{1,0:T(8,128)(2,1)} %all-gather.2.cloned.1.call-done), kind=kOutput, calls=%fused_computation.40 | convolution fusion | flops 2431647744 | bytes 14954496 | tf_op jit(solution)/shard_map/dot_general | solution.py:23
  158.1 5.5 %fusion.30.qkv_ref = bf16[512,2304]{1,0:T(8,128)(2,1)} fusion(bf16[512,768]{1,0:T(8,128)(2,1)S(1)} %fusion.74.refs_1_, f32[2304]{0:T(1024)S(1)} %add.357, bf16[768,9344]{1,0:T(8,128)(2,1)} %all-gather.2.cloned.1.call-done), kind=kOutput, calls=%fused_computation.46 | convolution fusion | flops 1814298624 | bytes 6693888 | tf_op jit(solution)/shard_map/dot_general | solution.py:23
  164.5 8.5 %attention_forward.4 = (bf16[512,768]{1,0:T(8,128)(2,1)}, f32[512,768]{1,0:T(8,128)}) custom-call(bf16[512,2304]{1,0:T(8,128)(2,1)} %fusion.30.qkv_ref), custom_call_target="tpu_custom_call" | custom-call | flops 1610612736 | bytes 4718592 | tf_op jit(solution)/shard_map/attention_forward/pallas_call | solution.py:131
  176.1 9.6 %multiply_convert_fusion.1 = (bf16[512,3072]{1,0:T(8,128)(2,1)S(1)}, f32[512,3072]{1,0:T(8,128)}) fusion(f32[3072]{0:T(1024)S(1)} %add.368, bf16[512,768]{1,0:T(8,128)(2,1)S(1)} %fusion.75.refs_1_, bf16[768,9344]{1,0:T(8,128)(2,1)} %all-gather.2.cloned.1.call-done), kind=kOutput, calls=%fused_computation.38 | convolution fusion | flops 2431647744 | bytes 14954496 | tf_op jit(solution)/shard_map/dot_general | solution.py:23
  189.2 5.4 fusion.31.qkv_ref
  195.5 8.6 %attention_forward.5 = (bf16[512,768]{1,0:T(8,128)(2,1)}, f32[512,768]{1,0:T(8,128)}) custom-call(bf16[512,2304]{1,0:T(8,128)(2,1)} %fusion.31.qkv_ref), custom_call_target="tpu_custom_call" | custom-call | flops 1610612736 | bytes 4718592 | tf_op jit(solution)/shard_map/attention_forward/pallas_call | solution.py:131
  207.2 6.1 %multiply_convert_fusion = (bf16[512,3072]{1,0:T(8,128)(2,1)S(1)}, f32[512,3072]{1,0:T(8,128)S(1)}) fusion(f32[3072]{0:T(1024)S(1)} %add.368, bf16[512,768]{1,0:T(8,128)(2,1)S(1)} %fusion.77.refs_2_, bf16[768,9344]{1,0:T(8,128)(2,1)} %all-gather.2.cloned.1.call-done), kind=kOutput, calls=%fused_computation.36 | convolution fusion | flops 2431647744 | bytes 14954496 | tf_op jit(solution)/shard_map/dot_general | solution.py:23
  219.8 6.1 %fusion.17.refs_5_ = bf16[512,3072]{1,0:T(8,128)(2,1)S(1)} fusion(f32[512,3072]{1,0:T(8,128)S(1)} %get-tuple-element.199, bf16[512,768]{1,0:T(8,128)(2,1)S(1)} %get-tuple-element.150.refs_5_, bf16[3072,768]{1,0:T(8,128)(2,1)S(1)} %bitcast.95, f32[3072]{0:T(1024)S(1)} %add.368), kind=kOutput, calls=%fused_computation.23 | convolution fusion | flops 2445803520 | bytes 14954496 | tf_op jit(solution)/shard_map/dot_general | solution.py:27
  225.9 6.9 %multiply_reduce_fusion.3 = (f32[768]{0:T(1024)S(1)}, f32[512]{0:T(512)S(1)}, f32[512]{0:T(512)S(1)}, f32[768]{0:T(1024)S(1)}, f32[512,768]{1,0:T(8,128)S(1)}) fusion(f32[512,768]{1,0:T(8,128)S(1)} %get-tuple-element.197, f32[512]{0:T(512)S(1)} %add_rsqrt_fusion.1, f32[512]{0:T(512)S(1)} %broadcast_multiply_fusion.13, f32[768]{0:T(1024)S(1)} %get-tuple-element.124, ...), kind=kOutput, calls=%fused_computation.65 | convolution fusion | flops 2423387648 | bytes 13400064 | tf_op jit(solution)/shard_map/dot_general | solution.py:27
  234.5 3.0 convolution_convert_fusion.2.g_ref
  237.5 11.9 %attention_backward.3.refs_5_ = bf16[512,2304]{1,0:T(8,128)(2,1)} custom-call(bf16[512,2304]{1,0:T(8,128)(2,1)} %fusion.31.qkv_ref, f32[512,768]{1,0:T(8,128)} %get-tuple-element.34.lt_ref, bf16[512,768]{1,0:T(8,128)(2,1)} %convolution_convert_fusion.2.g_ref), custom_call_target="tpu_custom_call" | custom-call | flops 4026531840 | bytes 7077888 | tf_op jit(solution)/shard_map/attention_backward/pallas_call | solution.py:157
  249.4 6.2 %multiply_reduce_fusion.1 = (f32[768]{0:T(1024)S(1)}, f32[512]{0:T(512)S(1)}, f32[512]{0:T(512)S(1)}, f32[768]{0:T(1024)S(1)}, f32[512,768]{1,0:T(8,128)S(1)}) fusion(f32[512,768]{1,0:T(8,128)} %copy-done.30, f32[512]{0:T(512)S(1)} %add_rsqrt_fusion.2, f32[512]{0:T(512)S(1)} %broadcast_multiply_fusion.14, f32[768]{0:T(1024)S(1)} %get-tuple-element.120, ...), kind=kOutput, calls=%fused_computation.63 | convolution fusion | flops 1815868928 | bytes 10634240 | tf_op jit(solution)/shard_map/dot_general | solution.py:27
  256.1 8.7 %fusion.23.refs_4_ = bf16[512,3072]{1,0:T(8,128)(2,1)S(1)} fusion(f32[512,3072]{1,0:T(8,128)} %get-tuple-element.193, bf16[512,768]{1,0:T(8,128)(2,1)S(1)} %get-tuple-element.142.refs_4_, bf16[3072,768]{1,0:T(8,128)(2,1)} %copy-done.32, f32[3072]{0:T(1024)S(1)} %add.368), kind=kOutput, calls=%fused_computation.29 | convolution fusion | flops 2445803520 | bytes 14954496 | tf_op jit(solution)/shard_map/dot_general | solution.py:27
  264.8 6.6 %multiply_reduce_fusion.4 = (f32[768]{0:T(1024)S(1)}, f32[512]{0:T(512)S(1)}, f32[512]{0:T(512)S(1)}, f32[768]{0:T(1024)S(1)}, f32[512,768]{1,0:T(8,128)S(1)}) fusion(f32[512,768]{1,0:T(8,128)S(1)} %get-tuple-element.191, f32[512]{0:T(512)S(1)} %add_rsqrt_fusion.3, f32[512]{0:T(512)S(1)} %broadcast_multiply_fusion.15, f32[768]{0:T(1024)S(1)} %get-tuple-element.124, ...), kind=kOutput, calls=%fused_computation.66 | convolution fusion | flops 2419848704 | bytes 12600320 | tf_op jit(solution)/shard_map/dot_general | solution.py:27
  271.5 3.1 fusion.89
  274.5 3.0 convolution_convert_fusion.1.g_ref
  277.5 12.0 %attention_backward.4.refs_4_ = bf16[512,2304]{1,0:T(8,128)(2,1)} custom-call(bf16[512,2304]{1,0:T(8,128)(2,1)} %fusion.30.qkv_ref, f32[512,768]{1,0:T(8,128)} %get-tuple-element.35.lt_ref, bf16[512,768]{1,0:T(8,128)(2,1)} %convolution_convert_fusion.1.g_ref), custom_call_target="tpu_custom_call" | custom-call | flops 4026531840 | bytes 7077888 | tf_op jit(solution)/shard_map/attention_backward/pallas_call | solution.py:157
  289.5 6.2 %multiply_reduce_fusion.2 = (f32[768]{0:T(1024)S(1)}, f32[512]{0:T(512)S(1)}, f32[512]{0:T(512)S(1)}, f32[768]{0:T(1024)S(1)}, f32[512,768]{1,0:T(8,128)S(1)}) fusion(f32[512,768]{1,0:T(8,128)} %copy-done.27, f32[512]{0:T(512)S(1)} %add_rsqrt_fusion.4, f32[512]{0:T(512)S(1)} %broadcast_multiply_fusion.16, f32[768]{0:T(1024)S(1)} %get-tuple-element.120, ...), kind=kOutput, calls=%fused_computation.64 | convolution fusion | flops 1815868928 | bytes 10634240 | tf_op jit(solution)/shard_map/dot_general | solution.py:27
  296.2 8.8 %fusion.29.refs_3_ = bf16[512,3072]{1,0:T(8,128)(2,1)S(1)} fusion(f32[512,3072]{1,0:T(8,128)} %get-tuple-element.187, bf16[512,768]{1,0:T(8,128)(2,1)S(1)} %get-tuple-element.138.refs_3_, bf16[3072,768]{1,0:T(8,128)(2,1)} %copy-done.32, f32[3072]{0:T(1024)S(1)} %add.368), kind=kOutput, calls=%fused_computation.35 | convolution fusion | flops 2445803520 | bytes 14954496 | tf_op jit(solution)/shard_map/dot_general | solution.py:27
  305.0 6.6 %multiply_reduce_fusion.5 = (f32[768]{0:T(1024)S(1)}, f32[512]{0:T(512)S(1)}, f32[512]{0:T(512)S(1)}, f32[768]{0:T(1024)S(1)}, f32[512,768]{1,0:T(8,128)S(1)}) fusion(f32[512,768]{1,0:T(8,128)S(1)} %copy-done.26, f32[512]{0:T(512)S(1)} %add_rsqrt_fusion.5, f32[512]{0:T(512)S(1)} %broadcast_multiply_fusion.17, f32[768]{0:T(1024)S(1)} %get-tuple-element.124, ...), kind=kOutput, calls=%fused_computation.67 | convolution fusion | flops 2419848704 | bytes 12600320 | tf_op jit(solution)/shard_map/dot_general | solution.py:27
  313.3 3.0 convolution_convert_fusion.g_ref
  316.3 11.9 %attention_backward.5.refs_3_ = bf16[512,2304]{1,0:T(8,128)(2,1)} custom-call(bf16[512,2304]{1,0:T(8,128)(2,1)} %fusion.33.qkv_ref, f32[512,768]{1,0:T(8,128)} %get-tuple-element.36.lt_ref, bf16[512,768]{1,0:T(8,128)(2,1)} %convolution_convert_fusion.g_ref), custom_call_target="tpu_custom_call" | custom-call | flops 4026531840 | bytes 7077888 | tf_op jit(solution)/shard_map/attention_backward/pallas_call | solution.py:157
  333.3 9.0 %weight_grad.4 = (bf16[768,9344]{1,0:T(8,128)(2,1)}, f32[1,2304]{1,0:T(1,128)S(1)}) custom-call(bf16[512,768]{1,0:T(8,128)(2,1)S(1)} %copy-done.18, bf16[512,768]{1,0:T(8,128)(2,1)S(1)} %copy-done.12, bf16[512,768]{1,0:T(8,128)(2,1)S(1)} %copy-done.16, bf16[512,2304]{1,0:T(8,128)(2,1)S(1)} %copy-done.23, bf16[512,2304]{1,0:T(8,128)(2,1)} %attention_backward.4.refs_4_, ...), custom_call_target="tpu_custom_call" | custom-call | flops 5435817984 | bytes 12976128 | tf_op jit(solution)/shard_map/weight_grad/pallas_call | solution.py:219
  342.3 3.2 weight_grad.5
  347.4 11.6 %weight_grad.6 = (bf16[768,9344]{1,0:T(8,128)(2,1)}, f32[1,3072]{1,0:T(1,128)S(1)}) custom-call(bf16[512,768]{1,0:T(8,128)(2,1)S(1)} %copy-done.8, bf16[512,768]{1,0:T(8,128)(2,1)S(1)} %copy-done.10, bf16[512,768]{1,0:T(8,128)(2,1)S(1)} %copy-done.14, bf16[512,3072]{1,0:T(8,128)(2,1)S(1)} %copy-done.22, ...), custom_call_target="tpu_custom_call", output_to_operand_aliasing={{0}: (6, {})} | custom-call | flops 7247757312 | bytes 16515072 | tf_op jit(solution)/shard_map/weight_grad/pallas_call | solution.py:219
  359.0 11.1 %weight_grad.7 = (bf16[768,9344]{1,0:T(8,128)(2,1)}, f32[1,768]{1,0:T(1,128)S(1)}) custom-call(bf16[512,3072]{1,0:T(8,128)(2,1)S(1)} %copy-done.20, bf16[512,3072]{1,0:T(8,128)(2,1)} %copy-done.56, bf16[512,3072]{1,0:T(8,128)(2,1)} %copy-done.57, bf16[512,768]{1,0:T(8,128)(2,1)S(1)} %copy-done.6, ...), custom_call_target="tpu_custom_call", output_to_operand_aliasing={{0}: (6, {})} | custom-call | flops 7247757312 | bytes 16515072 | tf_op jit(solution)/shard_map/weight_grad/pallas_call | solution.py:219
  375.4 5.5 %add_convert_fusion = bf16[512,768]{1,0:T(8,128)(2,1)} fusion(f32[512,768]{1,0:T(8,128)} %get-tuple-element.137, bf16[512,2304]{1,0:T(8,128)(2,1)S(1)} %copy-done.24, bf16[768,9344]{1,0:T(8,128)(2,1)} %all-gather.2.cloned.1.call-done), kind=kOutput, calls=%fused_computation.68 | convolution fusion | flops 1812725760 | bytes 8257536 | tf_op jit(solution)/shard_map/dot_general | solution.py:27
  380.9 150.5 %reduce-scatter.4.cloned.1.call-done = bf16[24,9344]{1,0:T(8,128)(2,1)} async-done(((bf16[768,9344]{1,0:T(8,128)(2,1)}), bf16[24,9344]{1,0:T(8,128)(2,1)}) %reduce-scatter.4.cloned.1.call-update) | async-done | bytes 448528
  (264 shorter events, 58.1 us)
Async XLA Ops:
  7.2 113.0 %all-gather.2.cloned.1.call-start = ((), (), s32[]{:S(2)}) async-start(), calls=%async_computation.1 | async-start | bytes 14800896 | tf_op jit(solution)/shard_map/all_gather | solution.py:287
  14.0 517.4 %reduce-scatter.4.cloned.1.call-start = ((), (), s32[]{:S(2)}) async-start(), calls=%async_computation.2 | async-start | bytes 14800896
  140.0 14.7 %copy-start.25 = (f32[512,768]{1,0:T(8,128)}, f32[512,768]{1,0:T(8,128)S(1)}, u32[]{:S(2)}) copy-start(f32[512,768]{1,0:T(8,128)S(1)} %get-tuple-element.185) | copy-start | bytes 4718596
  143.7 10.9 %copy-start.32 = (bf16[3072,768]{1,0:T(8,128)(2,1)}, bf16[3072,768]{1,0:T(8,128)(2,1)S(1)}, u32[]{:S(2)}) copy-start(bf16[3072,768]{1,0:T(8,128)(2,1)S(1)} %pad_maximum_fusion) | copy-start | bytes 14155780
  144.1 10.6 %copy-start.7 = (bf16[512,768]{1,0:T(8,128)(2,1)}, bf16[512,768]{1,0:T(8,128)(2,1)S(1)}, u32[]{:S(2)}) copy-start(bf16[512,768]{1,0:T(8,128)(2,1)S(1)} %fusion.73.refs_0_) | copy-start | bytes 2359300
  157.5 15.5 %copy-start.27 = (f32[512,768]{1,0:T(8,128)}, f32[512,768]{1,0:T(8,128)S(1)}, u32[]{:S(2)}) copy-start(f32[512,768]{1,0:T(8,128)S(1)} %get-tuple-element.189) | copy-start | bytes 4718596
  175.5 89.4 %copy-start.29 = (f32[512,768]{1,0:T(8,128)}, f32[512,768]{1,0:T(8,128)S(1)}, u32[]{:S(2)}) copy-start(f32[512,768]{1,0:T(8,128)S(1)} %get-tuple-element.191) | copy-start | bytes 4718596
  175.8 9.9 %slice-start = ((s8[4718592]{0:T(1024)(128)(4,1)}), s8[4194304]{0:T(1024)(128)(4,1)S(1)}, s32[]{:S(2)}) async-start(s8[4718592]{0:T(1024)(128)(4,1)} %bitcast.92), calls=%async_computation.3 | async-start | bytes 8388608
  176.1 9.6 %copy-start.9 = (bf16[512,768]{1,0:T(8,128)(2,1)}, bf16[512,768]{1,0:T(8,128)(2,1)S(1)}, u32[]{:S(2)}) copy-start(bf16[512,768]{1,0:T(8,128)(2,1)S(1)} %fusion.75.refs_1_) | copy-start | bytes 2359300
  176.1 9.6 %slice-start.1 = ((s8[4718592]{0:T(1024)(128)(4,1)}), s8[524288]{0:T(1024)(128)(4,1)S(1)}, s32[]{:S(2)}) async-start(s8[4718592]{0:T(1024)(128)(4,1)} %bitcast.92), calls=%async_computation.4 | async-start | bytes 1048576
  188.5 15.5 %copy-start.30 = (f32[512,768]{1,0:T(8,128)}, f32[512,768]{1,0:T(8,128)S(1)}, u32[]{:S(2)}) copy-start(f32[512,768]{1,0:T(8,128)S(1)} %get-tuple-element.195) | copy-start | bytes 4718596
  206.8 6.5 %slice-start.2 = ((s8[4718592]{0:T(1024)(128)(4,1)}), s8[4194304]{0:T(1024)(128)(4,1)S(1)}, s32[]{:S(2)}) async-start(s8[4718592]{0:T(1024)(128)(4,1)} %bitcast.94), calls=%async_computation.5 | async-start | bytes 8388608
  207.2 6.2 %copy-start.13 = (bf16[512,768]{1,0:T(8,128)(2,1)}, bf16[512,768]{1,0:T(8,128)(2,1)S(1)}, u32[]{:S(2)}) copy-start(bf16[512,768]{1,0:T(8,128)(2,1)S(1)} %fusion.77.refs_2_) | copy-start | bytes 2359300
  207.2 6.2 %slice-start.3 = ((s8[4718592]{0:T(1024)(128)(4,1)}), s8[524288]{0:T(1024)(128)(4,1)S(1)}, s32[]{:S(2)}) async-start(s8[4718592]{0:T(1024)(128)(4,1)} %bitcast.94), calls=%async_computation.6 | async-start | bytes 1048576
  225.9 6.9 %copy-start.58 = (bf16[512,3072]{1,0:T(8,128)(2,1)}, bf16[512,3072]{1,0:T(8,128)(2,1)S(1)}, u32[]{:S(2)}) copy-start(bf16[512,3072]{1,0:T(8,128)(2,1)S(1)} %fusion.17.refs_5_) | copy-start | bytes 9437188
  249.4 6.2 %copy-start.31 = (f32[512,768]{1,0:T(8,128)S(1)}, f32[512,768]{1,0:T(8,128)}, u32[]{:S(2)}) copy-start(f32[512,768]{1,0:T(8,128)} %copy-done.30) | copy-start | bytes 4718596
  256.1 8.8 %copy-start.3 = (bf16[512,768]{1,0:T(8,128)(2,1)}, bf16[512,768]{1,0:T(8,128)(2,1)S(1)}, u32[]{:S(2)}) copy-start(bf16[512,768]{1,0:T(8,128)(2,1)S(1)} %get-tuple-element.142.refs_4_) | copy-start | bytes 2359300
  264.8 6.6 %copy-start.59 = (bf16[512,3072]{1,0:T(8,128)(2,1)}, bf16[512,3072]{1,0:T(8,128)(2,1)S(1)}, u32[]{:S(2)}) copy-start(bf16[512,3072]{1,0:T(8,128)(2,1)S(1)} %fusion.23.refs_4_) | copy-start | bytes 9437188
  289.5 6.2 %copy-start.28 = (f32[512,768]{1,0:T(8,128)S(1)}, f32[512,768]{1,0:T(8,128)}, u32[]{:S(2)}) copy-start(f32[512,768]{1,0:T(8,128)} %copy-done.27) | copy-start | bytes 4718596
  296.2 8.8 %copy-start.5 = (bf16[512,768]{1,0:T(8,128)(2,1)}, bf16[512,768]{1,0:T(8,128)(2,1)S(1)}, u32[]{:S(2)}) copy-start(bf16[512,768]{1,0:T(8,128)(2,1)S(1)} %get-tuple-element.138.refs_3_) | copy-start | bytes 2359300
  296.2 8.8 %copy-start.26 = (f32[512,768]{1,0:T(8,128)S(1)}, f32[512,768]{1,0:T(8,128)}, u32[]{:S(2)}) copy-start(f32[512,768]{1,0:T(8,128)} %copy-done.25) | copy-start | bytes 4718596
  305.0 6.6 %copy-start.21 = (bf16[512,3072]{1,0:T(8,128)(2,1)}, bf16[512,3072]{1,0:T(8,128)(2,1)S(1)}, u32[]{:S(2)}) copy-start(bf16[512,3072]{1,0:T(8,128)(2,1)S(1)} %fusion.29.refs_3_) | copy-start | bytes 9437188
  333.3 9.0 %copy-start = (bf16[512,768]{1,0:T(8,128)(2,1)S(1)}, bf16[512,768]{1,0:T(8,128)(2,1)}, u32[]{:S(2)}) copy-start(bf16[512,768]{1,0:T(8,128)(2,1)} %get-tuple-element.31.refs_0_) | copy-start | bytes 2359300
  333.3 9.0 %copy-start.1 = (bf16[512,768]{1,0:T(8,128)(2,1)S(1)}, bf16[512,768]{1,0:T(8,128)(2,1)}, u32[]{:S(2)}) copy-start(bf16[512,768]{1,0:T(8,128)(2,1)} %get-tuple-element.32.refs_1_) | copy-start | bytes 2359300
  333.3 9.0 %copy-start.2 = (bf16[512,768]{1,0:T(8,128)(2,1)S(1)}, bf16[512,768]{1,0:T(8,128)(2,1)}, u32[]{:S(2)}) copy-start(bf16[512,768]{1,0:T(8,128)(2,1)} %get-tuple-element.33.refs_2_) | copy-start | bytes 2359300
  342.3 3.2 copy-start.8
  342.3 3.2 copy-start.10
  347.4 11.6 %copy-start.4 = (bf16[512,768]{1,0:T(8,128)(2,1)S(1)}, bf16[512,768]{1,0:T(8,128)(2,1)}, u32[]{:S(2)}) copy-start(bf16[512,768]{1,0:T(8,128)(2,1)} %copy-done.3) | copy-start | bytes 2359300
  347.4 11.6 %copy-start.6 = (bf16[512,768]{1,0:T(8,128)(2,1)S(1)}, bf16[512,768]{1,0:T(8,128)(2,1)}, u32[]{:S(2)}) copy-start(bf16[512,768]{1,0:T(8,128)(2,1)} %copy-done.5) | copy-start | bytes 2359300
  347.4 11.6 %copy-start.20 = (bf16[512,3072]{1,0:T(8,128)(2,1)S(1)}, bf16[512,3072]{1,0:T(8,128)(2,1)}, u32[]{:S(2)}) copy-start(bf16[512,3072]{1,0:T(8,128)(2,1)} %copy-done.19) | copy-start | bytes 9437188
  359.0 11.1 %copy-start.46 = (bf16[768]{0:T(1024)(128)(2,1)S(1)}, bf16[768]{0:T(1024)(128)(2,1)}, u32[]{:S(2)}) copy-start(bf16[768]{0:T(1024)(128)(2,1)} %custom-call.4) | copy-start | bytes 4612
  359.0 12.3 %copy-start.45 = (bf16[768]{0:T(1024)(128)(2,1)S(1)}, bf16[768]{0:T(1024)(128)(2,1)}, u32[]{:S(2)}) copy-start(bf16[768]{0:T(1024)(128)(2,1)} %custom-call.3) | copy-start | bytes 4612
  (34 other events, 70.7 us)
Sparse Core Ops, SparseCore 0:
  14.2 105.9 all-gather.1
  373.9 157.5 reduce-scatter.3
